TPU v7x, 32 devices: a whole 2x2x4 slice. The times are simulated.
32 devices in a mesh: groups: 2 (over y), space: 8 (over z, x), tm: 2 (over core).
Axes of the slice: x: 2, y: 2, z: 4, core: 2. Of those that a mesh axis runs over, the one named last changes fastest.
Arguments:
- latents: bfloat16 [4, 16, 4, 256, 256], P('groups', 'space', 'tm'), parts along dimension 0, may hold values from -6 to 6
- cotangent: bfloat16 [4, 16, 4, 256, 256], P('groups', 'space', 'tm'), parts along dimension 0, may hold values from -6 to 6
- valid_frames: int32 [4], P('groups'), parts along dimension 0, may hold values from 1 to 16, as said below
- spatial_weight: bfloat16 [9, 256, 256], replicated, may hold values from -0.125 to 0.125
- temporal_weight: bfloat16 [3, 256, 256], replicated, may hold values from -0.21875 to 0.21875
- cond_weight: bfloat16 [256, 256], replicated, may hold values from -0.375 to 0.375
Outputs:
- output: bfloat16 [4, 16, 4, 256, 256], P('groups', 'space', 'tm'), parts along dimension 0
- grad_latents: bfloat16 [4, 16, 4, 256, 256], P('groups', 'space', 'tm'), parts along dimension 0
- grad_spatial: bfloat16 [18, 256, 256], P('groups'), parts along dimension 0
- grad_temporal: bfloat16 [6, 256, 256], P('groups'), parts along dimension 0
- grad_cond: bfloat16 [512, 256], P('groups'), parts along dimension 0
There are 2 independent parts, one for each index of `groups`. A program takes and returns all parts, laid end to end along the dimension named above; an argument that names none is the same for every part. Nothing has to cross between parts.
Inputs may be any that keep to these rules, and one draw needn't show every extreme that they name: `valid_frames`: the first clip has all 16 frames valid; the others have 1 to 16.
All inputs are finite; a program needn't handle non-finite values.
Results may differ from a plain program's by a relative error of at most 0.0055.
Values may be sent and summed in bfloat16 or wider, within the bound.
No kernel may reach another device: no remote copies, remote signals or barrier semaphores. Data moves between devices by JAX's collectives and lax.ppermute only.
A program may use at most 128 MiB of HBM per device.

v0:
```python
import jax
import jax.numpy as jnp
from jax import lax
from jax.sharding import PartitionSpec as P


def from_root(block, axis, source):
    block = jnp.where(lax.axis_index(axis) == source, block, jnp.zeros_like(block))
    return lax.psum(block, axis)


def shifted(value, axis, by):
    count = lax.axis_size(axis)
    pairs = [(i, i + by) for i in range(count) if 0 <= i + by < count]
    return lax.ppermute(value, axis, pairs)


def spatial_sum(padded, weights, flip):
    rows = padded.shape[2] - 2
    cols = padded.shape[3] - 2
    total = jnp.zeros(padded.shape[:2] + (rows, cols, weights.shape[2]), jnp.float32)
    for row_off in range(3):
        for col_off in range(3):
            if flip:
                piece = padded[
                    :, :, 2 - row_off : 2 - row_off + rows, 2 - col_off : 2 - col_off + cols
                ]
                kernel = weights[3 * row_off + col_off].T
            else:
                piece = padded[:, :, row_off : row_off + rows, col_off : col_off + cols]
                kernel = weights[3 * row_off + col_off]
            total = total + jnp.dot(piece, kernel, preferred_element_type=jnp.float32)
    return total


def lag_forward(padded_act, weights, count):
    total = 0.0
    for lag in range(3):
        total = total + jnp.dot(
            padded_act[:, 2 - lag : 2 - lag + count],
            weights[lag],
            preferred_element_type=jnp.float32,
        )
    return total


def lag_backward(padded_cot, weights, count):
    total = 0.0
    for lag in range(3):
        total = total + jnp.dot(
            padded_cot[:, lag : lag + count], weights[lag].T, preferred_element_type=jnp.float32
        )
    return total


def lag_grads(padded_act, cot, count):
    dims = (((0, 1, 2, 3), (0, 1, 2, 3)), ((), ()))
    terms = []
    for lag in range(3):
        terms.append(
            lax.dot_general(
                padded_act[:, 2 - lag : 2 - lag + count],
                cot,
                dims,
                preferred_element_type=jnp.float32,
            )
        )
    return jnp.stack(terms)


def own_window(whole, rows):
    padded_rows = jnp.pad(whole, ((0, 0), (0, 0), (1, 1), (0, 0), (0, 0)))
    start = lax.axis_index("tm") * rows
    return lax.dynamic_slice_in_dim(padded_rows, start, rows + 2, 2)


def on_device(latents, cotangent, valid_frames, spatial_weight, temporal_weight, cond_weight):
    clips, frames, rows, cols, chans = latents.shape
    slab = lax.axis_index("space")
    frame_ids = slab * frames + jnp.arange(frames, dtype=jnp.int32)
    mask = (frame_ids[None, :] < valid_frames[:, None]).astype(jnp.bfloat16)[:, :, None, None, None]
    mask_f = mask.astype(jnp.float32)
    masked = latents * mask
    first = from_root(masked[:, 0], "space", 0)
    rows_pad = own_window(lax.all_gather(masked, "tm", axis=2, tiled=True), rows)
    padded = jnp.pad(rows_pad, ((0, 0), (0, 0), (0, 0), (1, 1), (0, 0)))
    pre = spatial_sum(padded, spatial_weight, False)
    act = jax.nn.silu(pre).astype(jnp.bfloat16)
    cot = cotangent * mask
    earlier = shifted(act, "space", 1)
    act_pad = jnp.concatenate([earlier, act], axis=1)
    mixed = lag_forward(act_pad, temporal_weight, frames)
    later = shifted(cot, "space", -1)
    cot_pad = jnp.concatenate([cot, later], axis=1)
    dact = lag_backward(cot_pad, temporal_weight, frames)
    temporal_terms = lag_grads(act_pad, cot, frames)
    cond = jnp.dot(first, cond_weight, preferred_element_type=jnp.float32)
    output = ((masked.astype(jnp.float32) + mixed + cond[:, None]) * mask_f).astype(jnp.bfloat16)
    sig = jax.nn.sigmoid(pre)
    dpre = (dact * sig * (1.0 + pre * (1.0 - sig))).astype(jnp.bfloat16)
    cot_sum = lax.psum(jnp.sum(cot, axis=1, dtype=jnp.float32), "space")
    cond_back = jnp.dot(cot_sum, cond_weight.astype(jnp.float32).T, precision=lax.Precision.HIGHEST)
    dpre_rows = own_window(lax.all_gather(dpre, "tm", axis=2, tiled=True), rows)
    dpre_pad = jnp.pad(dpre_rows, ((0, 0), (0, 0), (0, 0), (1, 1), (0, 0)))
    dmasked = spatial_sum(dpre_pad, spatial_weight, True)
    is_first = (frame_ids == 0).astype(jnp.float32)[None, :, None, None, None]
    grad_latents = (
        (cot.astype(jnp.float32) + dmasked + is_first * cond_back[:, None]) * mask_f
    ).astype(jnp.bfloat16)
    dims = (((0, 1, 2, 3), (0, 1, 2, 3)), ((), ()))
    spatial_terms = []
    for row_off in range(3):
        for col_off in range(3):
            piece = padded[:, :, row_off : row_off + rows, col_off : col_off + cols]
            spatial_terms.append(
                lax.dot_general(piece, dpre, dims, preferred_element_type=jnp.float32)
            )
    spatial_terms = jnp.stack(spatial_terms)
    is_owner = (slab == 0).astype(jnp.float32)
    cond_terms = is_owner * lax.dot_general(
        first.astype(jnp.float32),
        cot_sum,
        (((0, 1, 2), (0, 1, 2)), ((), ())),
        precision=lax.Precision.HIGHEST,
    )
    summed = lax.psum((spatial_terms, temporal_terms, cond_terms), ("space", "tm"))
    scale = (clips * frames * rows * cols * lax.axis_size("space") * lax.axis_size("tm")) ** (-0.5)
    grad_spatial = (summed[0] * scale).astype(jnp.bfloat16)
    grad_temporal = (summed[1] * scale).astype(jnp.bfloat16)
    grad_cond = (summed[2] * scale).astype(jnp.bfloat16)
    return (output, grad_latents, grad_spatial, grad_temporal, grad_cond)


def solution(mesh):
    return jax.shard_map(
        on_device,
        mesh=mesh,
        in_specs=(
            P("groups", "space", "tm", None, None),
            P("groups", "space", "tm", None, None),
            P("groups"),
            P(),
            P(),
            P(),
        ),
        out_specs=(
            P("groups", "space", "tm", None, None),
            P("groups", "space", "tm", None, None),
            P("groups", None, None),
            P("groups", None, None),
            P("groups", None),
        ),
        check_vma=False,
    )
```

profile of v0, /device:TPU:0, one launch (start us, length us, event | category | flops | bytes accessed | tf_op | source)
XLA Modules:
  0.0 338.7 jit_solution(10557166967447815481)
XLA Ops:
  8.8 1.4 broadcast_multiply_fusion.1
  11.2 2.7 convert_reduce_fusion
  14.5 1.3 collective-permute-start.1
  15.9 1.8 fusion.75
  17.7 75.7 %all-reduce.9.cloned.1.call-done = bf16[2,2,256,256]{3,2,1,0:T(8,128)(2,1)} async-done(((bf16[2,2,256,256]{3,2,1,0:T(8,128)(2,1)}), bf16[2,2,256,256]{3,2,1,0:T(8,128)(2,1)}) %all-reduce.9.cloned.1.call-update) | async-done | bytes 524304 | tf_op jit(solution)/shard_map/psum | solution.py:9
  93.3 2.3 fusion.47
  95.7 79.6 %all-reduce.11.cloned.1.call-done = f32[2,2,256,256]{3,2,1,0:T(8,128)} async-done(((f32[2,2,256,256]{3,2,1,0:T(8,128)}), f32[2,2,256,256]{3,2,1,0:T(8,128)}) %all-reduce.11.cloned.1.call-update) | async-done | bytes 1048592 | tf_op jit(solution)/shard_map/psum | solution.py:101
  175.3 3.0 fusion.13
  178.2 1.6 fusion.45
  179.9 1.8 fusion.3
  181.7 1.8 pad_dynamic-slice_fusion.1
  187.1 2.1 multiply_convert_fusion.3
  189.9 2.0 multiply_convert_fusion.1
  191.9 1.2 fusion.19
  193.2 3.5 %collective-permute-start = (bf16[2,2,2,256,256]{4,3,2,1,0:T(8,128)(2,1)}, bf16[2,2,2,256,256]{4,3,2,1,0:T(8,128)(2,1)S(1)}, u32[]{:S(2)}, u32[]{:S(2)}) collective-permute-start(bf16[2,2,2,256,256]{4,3,2,1,0:T(8,128)(2,1)} %get-tuple-element.12), channel_id=1, source_target_pairs={{0,2},{2,4},{4,6},{6,8},{8,10},{10,12},{12,14},{1,3},{3,5},{5,7},{... | collective-permute-start | bytes 3145736 | tf_op jit(solution)/shard_map/ppermute | solution.py:15
  196.7 2.4 fusion.12
  199.1 1.2 fusion.18
  200.3 1.2 fusion.17
  201.5 1.2 fusion.11
  202.7 1.2 fusion.16
  203.8 1.2 fusion.15
  205.9 1.2 fusion.10
  207.1 1.2 fusion.14
  208.3 2.7 fusion.77
  211.0 7.8 %collective-permute-done = bf16[2,2,2,256,256]{4,3,2,1,0:T(8,128)(2,1)S(1)} collective-permute-done((bf16[2,2,2,256,256]{4,3,2,1,0:T(8,128)(2,1)}, bf16[2,2,2,256,256]{4,3,2,1,0:T(8,128)(2,1)S(1)}, u32[]{:S(2)}, u32[]{:S(2)}) %collective-permute-start) | collective-permute-done | bytes 1048608 | tf_op jit(solution)/shard_map/ppermute | solution.py:15
  219.8 1.0 pad_maximum_fusion.5
  220.8 1.2 copy-done.8
  224.6 1.7 multiply_convert_fusion.2
  226.3 1.8 pad_dynamic-slice_fusion
  233.1 2.2 fusion.2
  235.3 91.7 %all-reduce.13.cloned.1.call-done = (f32[9,256,256]{2,1,0:T(8,128)}, f32[3,256,256]{2,1,0:T(8,128)}, f32[256,256]{1,0:T(8,128)}) async-done(((f32[9,256,256]{2,1,0:T(8,128)}, f32[3,256,256]{2,1,0:T(8,128)}, f32[256,256]{1,0:T(8,128)}), (f32[9,256,256]{2,1,0:T(8,128)}, f32[3,256,256]{2,1,0:T(8,128)}, f32[256,256]{1,0:T(8,128)})) %all-reduce.13.cloned.1.call-update) | async-done | bytes 3407888 | tf_op jit(solution)/shard_map/psum | solution.py:126
  327.0 3.0 multiply_convert_fusion
  (92 shorter events, 17.6 us)
Async XLA Ops:
  8.0 85.3 %copy-start = (bf16[256,256]{1,0:T(8,128)(2,1)S(1)}, bf16[256,256]{1,0:T(8,128)(2,1)}, u32[]{:S(2)}) copy-start(bf16[256,256]{1,0:T(8,128)(2,1)} %param.11) | copy-start | bytes 393220
  8.0 85.3 %all-reduce.9.cloned.1.call-start = ((), (), s32[]{:S(2)}) async-start(), calls=%async_computation.1 | async-start | bytes 1048576 | tf_op jit(solution)/shard_map/psum | solution.py:9
  10.2 3.7 %copy-start.11 = (bf16[2,2,2,256,256]{4,3,2,1,0:T(8,128)(2,1)}, bf16[2,2,2,256,256]{4,3,2,1,0:T(8,128)(2,1)S(1)}, u32[]{:S(2)}) copy-start(bf16[2,2,2,256,256]{4,3,2,1,0:T(8,128)(2,1)S(1)} %broadcast_multiply_fusion.1) | copy-start | bytes 3145732
  11.1 4.8 %copy-start.21 = (bf16[3,256,256]{2,1,0:T(8,128)(2,1)S(1)}, bf16[3,256,256]{2,1,0:T(8,128)(2,1)}, u32[]{:S(2)}) copy-start(bf16[3,256,256]{2,1,0:T(8,128)(2,1)} %param.10) | copy-start | bytes 1179652
  11.1 164.2 %all-reduce.11.cloned.1.call-start = ((), (), s32[]{:S(2)}) async-start(), calls=%async_computation.3 | async-start | bytes 2097152 | tf_op jit(solution)/shard_map/psum | solution.py:101
  13.9 166.0 %copy-start.4 = (bf16[2,2,2,256,256]{4,3,2,1,0:T(8,128)(2,1)}, bf16[2,2,2,256,256]{4,3,2,1,0:T(8,128)(2,1)S(1)}, u32[]{:S(2)}) copy-start(bf16[2,2,2,256,256]{4,3,2,1,0:T(8,128)(2,1)S(1)} %get-tuple-element.9) | copy-start | bytes 3145732
  13.9 167.8 %all-gather.3.cloned.1.call-start = ((), (), s32[]{:S(2)}) async-start(), calls=%async_computation | async-start | bytes 3145728 | tf_op jit(solution)/shard_map/all_gather | solution.py:85
  14.5 211.8 %all-gather.5.cloned.1.call-start = ((), (), s32[]{:S(2)}) async-start(), calls=%async_computation.2 | async-start | bytes 3145728 | tf_op jit(solution)/shard_map/all_gather | solution.py:103
  14.5 165.3 %collective-permute-start.1 = (bf16[2,2,2,256,256]{4,3,2,1,0:T(8,128)(2,1)S(1)}, bf16[2,2,2,256,256]{4,3,2,1,0:T(8,128)(2,1)S(1)}, u32[]{:S(2)}, u32[]{:S(2)}) collective-permute-start(bf16[2,2,2,256,256]{4,3,2,1,0:T(8,128)(2,1)S(1)} %get-tuple-element.9), channel_id=1, source_target_pairs={{2,0},{4,2},{6,4},{8,6},{10,8},{12,10},{14,12},{3,1},{5,3},{7,5},{... | collective-permute-start | bytes 3145736 | tf_op jit(solution)/shard_map/ppermute | solution.py:15
  175.3 3.0 copy-start.18
  179.8 1.8 copy-start.23
  181.7 1.8 copy-start.14
  187.1 2.2 copy-start.19
  187.1 2.3 copy-start.20
  187.1 2.8 copy-start.24
  193.1 6.0 %copy-start.3 = (bf16[2,2,2,256,256]{4,3,2,1,0:T(8,128)(2,1)S(1)}, bf16[2,2,2,256,256]{4,3,2,1,0:T(8,128)(2,1)}, u32[]{:S(2)}) copy-start(bf16[2,2,2,256,256]{4,3,2,1,0:T(8,128)(2,1)} %copy-done.2) | copy-start | bytes 3145732
  193.2 133.8 %all-reduce.13.cloned.1.call-start = ((), (), s32[]{:S(2)}) async-start(), calls=%async_computation.4 | async-start | bytes 6815744 | tf_op jit(solution)/shard_map/psum | solution.py:126
  193.2 25.7 %collective-permute-start = (bf16[2,2,2,256,256]{4,3,2,1,0:T(8,128)(2,1)}, bf16[2,2,2,256,256]{4,3,2,1,0:T(8,128)(2,1)S(1)}, u32[]{:S(2)}, u32[]{:S(2)}) collective-permute-start(bf16[2,2,2,256,256]{4,3,2,1,0:T(8,128)(2,1)} %get-tuple-element.12), channel_id=1, source_target_pairs={{0,2},{2,4},{4,6},{6,8},{8,10},{10,12},{12,14},{1,3},{3,5},{5,7},{... | collective-permute-start | bytes 3145736 | tf_op jit(solution)/shard_map/ppermute | solution.py:15
  203.8 1.2 copy-start.5
  203.8 1.6 copy-start.7
  220.8 1.2 copy-start.8
  220.8 1.5 copy-start.10
  220.8 1.6 copy-start.22
  222.4 1.2 copy-start.12
  222.4 1.9 copy-start.13
  222.4 2.2 copy-start.17
  226.3 1.9 copy-start.15
  231.6 1.2 copy-start.6
  231.6 1.6 copy-start.16
  327.0 3.0 copy-start.25
  327.0 4.5 %copy-start.1 = (bf16[256,256]{1,0:T(8,128)(2,1)S(1)}, bf16[256,256]{1,0:T(8,128)(2,1)}, u32[]{:S(2)}) copy-start(bf16[256,256]{1,0:T(8,128)(2,1)} %param.11) | copy-start | bytes 393220
  327.0 3.9 %copy-start.26 = (f32[256,256]{1,0:T(8,128)S(1)}, f32[256,256]{1,0:T(8,128)}, u32[]{:S(2)}) copy-start(f32[256,256]{1,0:T(8,128)} %get-tuple-element.7) | copy-start | bytes 786436
  (2 other events, 2.2 us)
Sparse Core Ops, SparseCore 0:
  12.8 80.4 all-reduce.8
  97.8 77.4 all-reduce.10
  220.9 105.9 all-reduce.12
Sparse Core Ops, SparseCore 1:
  16.5 13.1 all-gather.2
  193.2 10.0 all-gather.4
where the time goes:
time: 339 us
  waiting for transfers between devices  255 us (75%)
  matrix products  42.3 us (12%)
  between operations  15.5 us (5%)
  other arithmetic  11.2 us (3%)
  local copies, waits for them, and re-layouts  9.27 us (3%)
  starting transfers between devices  5.03 us (1%)
    psum x1, waiting for transfers between devices, on_device(): lax.psum((spatial_terms, temporal_terms, cond_terms), ('space', 'tm'))  91.7 us
    psum x1, waiting for transfers between devices, on_device(): cot_sum = lax.psum(jnp.sum(cot, axis=1, dtype=jnp.float32), 'space')  79.6 us
    psum x1, waiting for transfers between devices, from_root(): return lax.psum(block, axis)  75.7 us
    dot_general x9, matrix products, on_device(): lax.dot_general(piece, dpre, dims, preferred_element_type=jnp.float32)  11.9 us
    dot_general x18, matrix products, spatial_sum(): total = total + jnp.dot(piece, kernel, preferred_element_type=jnp.float32)  11.7 us
    ppermute x2, waiting for transfers between devices, shifted(): return lax.ppermute(value, axis, pairs)  7.84 us
  transfers between devices with their start and end apart: 7, of which 4 were waited for; matrix products, arithmetic and copies ran while one was open for 12% of the time, Pallas kernels for 0%

commit v1 on v0

--- a/solution.py
+++ b/solution.py
@@ -4,15 +4,87 @@
 from jax.sharding import PartitionSpec as P
 
 
-def from_root(block, axis, source):
-    block = jnp.where(lax.axis_index(axis) == source, block, jnp.zeros_like(block))
-    return lax.psum(block, axis)
-
-
 def shifted(value, axis, by):
     count = lax.axis_size(axis)
     pairs = [(i, i + by) for i in range(count) if 0 <= i + by < count]
     return lax.ppermute(value, axis, pairs)
+
+
+def tree_broadcast(value, axis):
+    count = lax.axis_size(axis)
+    me = lax.axis_index(axis)
+    step = 1
+    while step * 2 < count:
+        step *= 2
+    while step >= 1 and count > 1:
+        pairs = [(i, i + step) for i in range(0, count, 2 * step) if i + step < count]
+        got = lax.ppermute(value, axis, pairs)
+        value = jnp.where(me % (2 * step) == step, got, value)
+        step //= 2
+    return value
+
+
+def tree_reduce(value, axis):
+    count = lax.axis_size(axis)
+    step = 1
+    while step < count:
+        pairs = [(i + step, i) for i in range(0, count, 2 * step) if i + step < count]
+        value = value + lax.ppermute(value, axis, pairs)
+        step *= 2
+    return value
+
+
+def halving_sum(flat, axis):
+    count = lax.axis_size(axis)
+    me = lax.axis_index(axis)
+    step = count // 2
+    while step >= 1:
+        half = flat.shape[0] // 2
+        upper = (me // step) % 2
+        keep = lax.dynamic_slice_in_dim(flat, upper * half, half, 0)
+        send = lax.dynamic_slice_in_dim(flat, (1 - upper) * half, half, 0)
+        pairs = [(i, i ^ step) for i in range(count)]
+        flat = keep + lax.ppermute(send, axis, pairs)
+        step //= 2
+    return flat
+
+
+def doubling_gather(piece, axis):
+    count = lax.axis_size(axis)
+    me = lax.axis_index(axis)
+    step = 1
+    while step < count:
+        got = lax.ppermute(piece, axis, [(i, i ^ step) for i in range(count)])
+        upper = (me // step) % 2 == 1
+        piece = jnp.where(
+            upper, jnp.concatenate([got, piece], 0), jnp.concatenate([piece, got], 0)
+        )
+        step *= 2
+    return piece
+
+
+def is_pow2(n):
+    return n >= 1 and (n & (n - 1)) == 0
+
+
+def all_sum_rounded(flat, axes, scale):
+    sizes = [lax.axis_size(a) for a in axes]
+    if not all(is_pow2(s) for s in sizes):
+        return (lax.psum(flat, tuple(axes)) * scale).astype(jnp.bfloat16)
+    parts = 1
+    for s in sizes:
+        parts *= s
+    rows = flat.shape[0]
+    unit = parts * 8
+    padded_rows = -(-rows // unit) * unit
+    if padded_rows != rows:
+        flat = jnp.pad(flat, ((0, padded_rows - rows), (0, 0)))
+    for a in axes:
+        flat = halving_sum(flat, a)
+    piece = (flat * scale).astype(jnp.bfloat16)
+    for a in reversed(axes):
+        piece = doubling_gather(piece, a)
+    return piece[:rows]
 
 
 def spatial_sum(padded, weights, flip):
@@ -68,10 +140,10 @@
     return jnp.stack(terms)
 
 
-def own_window(whole, rows):
-    padded_rows = jnp.pad(whole, ((0, 0), (0, 0), (1, 1), (0, 0), (0, 0)))
-    start = lax.axis_index("tm") * rows
-    return lax.dynamic_slice_in_dim(padded_rows, start, rows + 2, 2)
+def row_halo(x):
+    above = shifted(x[:, :, -1:], "tm", 1)
+    below = shifted(x[:, :, :1], "tm", -1)
+    return jnp.concatenate([above, x, below], axis=2)
 
 
 def on_device(latents, cotangent, valid_frames, spatial_weight, temporal_weight, cond_weight):
@@ -81,16 +153,18 @@
     mask = (frame_ids[None, :] < valid_frames[:, None]).astype(jnp.bfloat16)[:, :, None, None, None]
     mask_f = mask.astype(jnp.float32)
     masked = latents * mask
-    first = from_root(masked[:, 0], "space", 0)
-    rows_pad = own_window(lax.all_gather(masked, "tm", axis=2, tiled=True), rows)
+    cot = cotangent * mask
+    first = tree_broadcast(masked[:, 0], "space")
+    cot_local = jnp.sum(cot, axis=1, dtype=jnp.float32)
+    cot_sum = tree_reduce(cot_local, "space")
+    later = shifted(cot, "space", -1)
+    rows_pad = row_halo(masked)
     padded = jnp.pad(rows_pad, ((0, 0), (0, 0), (0, 0), (1, 1), (0, 0)))
     pre = spatial_sum(padded, spatial_weight, False)
     act = jax.nn.silu(pre).astype(jnp.bfloat16)
-    cot = cotangent * mask
     earlier = shifted(act, "space", 1)
     act_pad = jnp.concatenate([earlier, act], axis=1)
     mixed = lag_forward(act_pad, temporal_weight, frames)
-    later = shifted(cot, "space", -1)
     cot_pad = jnp.concatenate([cot, later], axis=1)
     dact = lag_backward(cot_pad, temporal_weight, frames)
     temporal_terms = lag_grads(act_pad, cot, frames)
@@ -98,9 +172,8 @@
     output = ((masked.astype(jnp.float32) + mixed + cond[:, None]) * mask_f).astype(jnp.bfloat16)
     sig = jax.nn.sigmoid(pre)
     dpre = (dact * sig * (1.0 + pre * (1.0 - sig))).astype(jnp.bfloat16)
-    cot_sum = lax.psum(jnp.sum(cot, axis=1, dtype=jnp.float32), "space")
     cond_back = jnp.dot(cot_sum, cond_weight.astype(jnp.float32).T, precision=lax.Precision.HIGHEST)
-    dpre_rows = own_window(lax.all_gather(dpre, "tm", axis=2, tiled=True), rows)
+    dpre_rows = row_halo(dpre)
     dpre_pad = jnp.pad(dpre_rows, ((0, 0), (0, 0), (0, 0), (1, 1), (0, 0)))
     dmasked = spatial_sum(dpre_pad, spatial_weight, True)
     is_first = (frame_ids == 0).astype(jnp.float32)[None, :, None, None, None]
@@ -116,18 +189,29 @@
                 lax.dot_general(piece, dpre, dims, preferred_element_type=jnp.float32)
             )
     spatial_terms = jnp.stack(spatial_terms)
-    is_owner = (slab == 0).astype(jnp.float32)
-    cond_terms = is_owner * lax.dot_general(
+    cond_terms = lax.dot_general(
         first.astype(jnp.float32),
-        cot_sum,
+        cot_local,
         (((0, 1, 2), (0, 1, 2)), ((), ())),
         precision=lax.Precision.HIGHEST,
     )
-    summed = lax.psum((spatial_terms, temporal_terms, cond_terms), ("space", "tm"))
+    taps_s = spatial_terms.shape[0]
+    taps_t = temporal_terms.shape[0]
+    flat = jnp.concatenate(
+        [
+            spatial_terms.reshape(-1, chans),
+            temporal_terms.reshape(-1, chans),
+            cond_terms.reshape(-1, chans),
+        ],
+        axis=0,
+    )
     scale = (clips * frames * rows * cols * lax.axis_size("space") * lax.axis_size("tm")) ** (-0.5)
-    grad_spatial = (summed[0] * scale).astype(jnp.bfloat16)
-    grad_temporal = (summed[1] * scale).astype(jnp.bfloat16)
-    grad_cond = (summed[2] * scale).astype(jnp.bfloat16)
+    summed = all_sum_rounded(flat, ("tm", "space"), scale)
+    n_s = taps_s * chans
+    n_t = taps_t * chans
+    grad_spatial = summed[:n_s].reshape(taps_s, chans, chans)
+    grad_temporal = summed[n_s : n_s + n_t].reshape(taps_t, chans, chans)
+    grad_cond = summed[n_s + n_t :]
     return (output, grad_latents, grad_spatial, grad_temporal, grad_cond)
 
 

time: 339 us -> 204 us (0.60)
  waiting for transfers between devices: 255 us -> 91.1 us
  starting transfers between devices: 5.03 us -> 66.4 us
  between operations: 15.5 us -> 1.37 us
  matrix products: 42.3 us -> 30.5 us
  local copies, waits for them, and re-layouts: 9.27 us -> 4.73 us
    psum x3 -> x0, waiting for transfers between devices: 247 us -> none  [the longest x1 91.7 us: on_device(): lax.psum((spatial_terms, temporal_terms, cond_terms), ('space', 'tm'))]
    ppermute x0 -> x14, waiting for transfers between devices: none -> 85.8 us  [the longest x4 43 us: doubling_gather(): got = lax.ppermute(piece, axis, [(i, i ^ step) for i in range(count)])]
    ppermute x0 -> x14, starting transfers between devices: none -> 50.8 us  [the longest x4 34.2 us: halving_sum(): flat = keep + lax.ppermute(send, axis, pairs)]
    ppermute x2 -> x6, starting transfers between devices: 4.83 us -> 15.5 us  [shifted(): return lax.ppermute(value, axis, pairs)]
    unnamed x54 -> x8, local copies, waits for them, and re-layouts: 5.67 us -> 0.03 us
    dot_general x9, matrix products: 11.9 us -> 6.44 us  [on_device(): lax.dot_general(piece, dpre, dims, preferred_element_type=jnp.float32)]
    convert_element_type x3 -> x1, other arithmetic: 4.53 us -> 0.03 us  [all_sum_rounded(): piece = (flat * scale).astype(jnp.bfloat16)]
    slice x0 -> x5, local copies, waits for them, and re-layouts: none -> 3.63 us  [the longest x1 1.09 us: on_device(): grad_spatial = summed[:n_s].reshape(taps_s, chans, chans)]
  transfers between devices with their start and end apart: 7 -> 20, of which waited for: 4 -> 9; matrix products, arithmetic and copies ran while one was open for 12% -> 19% of each run, Pallas kernels for 0% -> 0%
where the time goes in v1:
time: 204 us; the launch traced here: 203 us
  waiting for transfers between devices  91.1 us (45%)
  starting transfers between devices  66.4 us (33%)
  matrix products  30.5 us (15%)
  other arithmetic  8.84 us (4%)
  local copies, waits for them, and re-layouts  4.73 us (2%)
    ppermute x4, waiting for transfers between devices, doubling_gather(): got = lax.ppermute(piece, axis, [(i, i ^ step) for i in range(count)])  43 us
    ppermute x4, starting transfers between devices, halving_sum(): flat = keep + lax.ppermute(send, axis, pairs)  34.2 us
    ppermute x4, waiting for transfers between devices, halving_sum(): flat = keep + lax.ppermute(send, axis, pairs)  28.3 us
    ppermute x6, starting transfers between devices, shifted(): return lax.ppermute(value, axis, pairs)  15.5 us
    ppermute x3, waiting for transfers between devices, tree_broadcast(): got = lax.ppermute(value, axis, pairs)  14.6 us
    dot_general x18, matrix products, spatial_sum(): total = total + jnp.dot(piece, kernel, preferred_element_type=jnp.float32)  14 us
    ppermute x3, starting transfers between devices, tree_broadcast(): got = lax.ppermute(value, axis, pairs)  10.9 us
    dot_general x9, matrix products, on_device(): lax.dot_general(piece, dpre, dims, preferred_element_type=jnp.float32)  6.44 us
  transfers between devices with their start and end apart: 20, of which 9 were waited for; matrix products, arithmetic and copies ran while one was open for 19% of the time, Pallas kernels for 0%

profile of v1, /device:TPU:0, one launch (start us, length us, event | category | flops | bytes accessed | tf_op | source)
XLA Modules:
  0.0 202.9 jit_solution(12294039518381100214)
XLA Ops:
  1.4 1.5 broadcast_multiply_fusion.1
  3.9 3.2 %collective-permute-start = (bf16[2,2,1,256,256]{4,3,2,1,0:T(8,128)(2,1)}, bf16[2,2,1,256,256]{4,3,2,1,0:T(8,128)(2,1)}, u32[]{:S(2)}, u32[]{:S(2)}) collective-permute-start(bf16[2,2,1,256,256]{4,3,2,1,0:T(8,128)(2,1)} %get-tuple-element.11), channel_id=1, source_target_pairs={{0,1},{2,3},{4,5},{6,7},{8,9},{10,11},{12,13},{14,15},{16,17},{18,... | collective-permute-start | bytes 1572872 | tf_op jit(solution)/shard_map/ppermute | solution.py:10
  10.9 8.1 %collective-permute-start.3 = (bf16[2,2,256,256]{3,2,1,0:T(8,128)(2,1)}, bf16[2,2,256,256]{3,2,1,0:T(8,128)(2,1)}, u32[]{:S(2)}, u32[]{:S(2)}) collective-permute-start(bf16[2,2,256,256]{3,2,1,0:T(8,128)(2,1)} %slice_bitcast_fusion), channel_id=1, source_target_pairs={{0,8},{1,9},{16,24},{17,25}} | collective-permute-start | bytes 1572872 | tf_op jit(solution)/shard_map/ppermute | solution.py:21
  20.6 1.4 fusion.82
  22.4 2.1 %select_maximum_fusion.2 = bf16[2,2,4,258,256]{4,3,2,1,0:T(8,128)(2,1)S(1)} fusion(bf16[2,2,1,256,256]{4,3,2,1,0:T(8,128)(2,1)} %collective-permute-done.1, bf16[2,2,2,256,256]{4,3,2,1,0:T(8,128)(2,1)S(1)} %broadcast_multiply_fusion.1, bf16[2,2,1,256,256]{4,3,2,1,0:T(8,128)(2,1)} %collective-permute-done), kind=kLoop, calls=%fused_computation.8 | loop fusion | flops 12681216 | bytes 4210688 | tf_op jit(solution)/shard_map/concatenate | solution.py:146
  26.8 1.5 fusion.43
  28.2 1.5 fusion.44
  29.7 1.3 multiply_convert_fusion.2
  31.0 5.4 %collective-permute-start.2 = (bf16[2,2,2,256,256]{4,3,2,1,0:T(8,128)(2,1)S(1)}, bf16[2,2,2,256,256]{4,3,2,1,0:T(8,128)(2,1)S(1)}, u32[]{:S(2)}, u32[]{:S(2)}) collective-permute-start(bf16[2,2,2,256,256]{4,3,2,1,0:T(8,128)(2,1)S(1)} %get-tuple-element.13), channel_id=1, source_target_pairs={{0,2},{2,4},{4,6},{6,8},{8,10},{10,12},{12,14},{1,3},{3,5},{5,7},{... | collective-permute-start | bytes 3145736 | tf_op jit(solution)/shard_map/ppermute | solution.py:10
  36.5 1.3 collective-permute-start.4
  38.3 1.5 fusion.5
  39.9 2.3 %multiply_convert_fusion = bf16[2,2,2,256,256]{4,3,2,1,0:T(8,128)(2,1)S(1)} fusion(f32[2,2,2,256,256]{4,3,2,1,0:T(8,128)S(1)} %get-tuple-element.14, f32[2,2,2,256,256]{4,3,2,1,0:T(8,128)S(1)} %fusion.99, f32[2,2,2,256,256]{4,3,2,1,0:T(8,128)S(1)} %fusion.5, bf16[2,2,2,256,256]{4,3,2,1,0:T(8,128)(2,1)} %collective-permute-done.6, ...), kind=kOutput, calls=%fused_computation.19 | convolution fusion | flops 274202624 | bytes 8519680 | tf_op jit(solution)/shard_map/dot_general | solution.py:122
  42.6 1.5 fusion.21
  45.7 4.4 %collective-permute-done.4 = bf16[2,2,256,256]{3,2,1,0:T(8,128)(2,1)S(1)} collective-permute-done((bf16[2,2,256,256]{3,2,1,0:T(8,128)(2,1)S(1)}, bf16[2,2,256,256]{3,2,1,0:T(8,128)(2,1)S(1)}, u32[]{:S(2)}, u32[]{:S(2)}) %collective-permute-start.4) | collective-permute-done | bytes 524320 | tf_op jit(solution)/shard_map/ppermute | solution.py:21
  50.1 1.5 collective-permute-start.5
  52.6 1.5 fusion.20
  54.6 5.3 %collective-permute-done.2 = bf16[2,2,2,256,256]{4,3,2,1,0:T(8,128)(2,1)S(1)} collective-permute-done((bf16[2,2,2,256,256]{4,3,2,1,0:T(8,128)(2,1)S(1)}, bf16[2,2,2,256,256]{4,3,2,1,0:T(8,128)(2,1)S(1)}, u32[]{:S(2)}, u32[]{:S(2)}) %collective-permute-start.2) | collective-permute-done | bytes 1048608 | tf_op jit(solution)/shard_map/ppermute | solution.py:10
  60.9 10.2 %collective-permute-done.5 = bf16[2,2,256,256]{3,2,1,0:T(8,128)(2,1)S(1)} collective-permute-done((bf16[2,2,256,256]{3,2,1,0:T(8,128)(2,1)S(1)}, bf16[2,2,256,256]{3,2,1,0:T(8,128)(2,1)S(1)}, u32[]{:S(2)}, u32[]{:S(2)}) %collective-permute-start.5) | collective-permute-done | bytes 524320 | tf_op jit(solution)/shard_map/ppermute | solution.py:21
  74.4 3.1 %collective-permute-start.7 = (bf16[2,2,1,256,256]{4,3,2,1,0:T(8,128)(2,1)S(1)}, bf16[2,2,1,256,256]{4,3,2,1,0:T(8,128)(2,1)S(1)}, u32[]{:S(2)}, u32[]{:S(2)}) collective-permute-start(bf16[2,2,1,256,256]{4,3,2,1,0:T(8,128)(2,1)S(1)} %get-tuple-element.10), channel_id=1, source_target_pairs={{0,1},{2,3},{4,5},{6,7},{8,9},{10,11},{12,13},{14,15},{16,17},{18,... | collective-permute-start | bytes 1572872 | tf_op jit(solution)/shard_map/ppermute | solution.py:10
  77.5 1.4 add.207
  82.8 11.6 %collective-permute-start.13 = (f32[832,256]{1,0:T(8,128)S(1)}, f32[832,256]{1,0:T(8,128)S(1)}, u32[]{:S(2)}, u32[]{:S(2)}) collective-permute-start(f32[832,256]{1,0:T(8,128)S(1)} %constant_dynamic-slice_fusion.2), channel_id=1, source_target_pairs={{0,8},{2,10},{4,12},{6,14},{8,0},{10,2},{12,4},{14,6},{1,9},{3,11}... | collective-permute-start | bytes 2555912 | tf_op jit(solution)/shard_map/ppermute | solution.py:47
  95.7 17.3 %collective-permute-done.13 = f32[832,256]{1,0:T(8,128)S(1)} collective-permute-done((f32[832,256]{1,0:T(8,128)S(1)}, f32[832,256]{1,0:T(8,128)S(1)}, u32[]{:S(2)}, u32[]{:S(2)}) %collective-permute-start.13) | collective-permute-done | bytes 852000 | tf_op jit(solution)/shard_map/ppermute | solution.py:47
  113.1 22.1 %collective-permute-start.14 = (f32[416,256]{1,0:T(8,128)S(1)}, f32[416,256]{1,0:T(8,128)S(1)}, u32[]{:S(2)}, u32[]{:S(2)}) collective-permute-start(f32[416,256]{1,0:T(8,128)S(1)} %constant_dynamic-slice_fusion.1), channel_id=1, source_target_pairs={{0,4},{2,6},{4,0},{6,2},{8,12},{10,14},{12,8},{14,10},{1,5},{3,7},... | collective-permute-start | bytes 1277960 | tf_op jit(solution)/shard_map/ppermute | solution.py:47
  135.3 1.8 multiply_convert_fusion.1
  137.0 6.7 %collective-permute-done.14 = f32[416,256]{1,0:T(8,128)S(1)} collective-permute-done((f32[416,256]{1,0:T(8,128)S(1)}, f32[416,256]{1,0:T(8,128)S(1)}, u32[]{:S(2)}, u32[]{:S(2)}) %collective-permute-start.14) | collective-permute-done | bytes 426016 | tf_op jit(solution)/shard_map/ppermute | solution.py:47
  144.5 1.5 collective-permute-start.11
  146.0 4.3 %collective-permute-done.15 = f32[208,256]{1,0:T(8,128)S(1)} collective-permute-done((f32[208,256]{1,0:T(8,128)S(1)}, f32[208,256]{1,0:T(8,128)S(1)}, u32[]{:S(2)}, u32[]{:S(2)}) %collective-permute-start.15) | collective-permute-done | bytes 213024 | tf_op jit(solution)/shard_map/ppermute | solution.py:47
  150.9 4.2 %collective-permute-done.16 = bf16[208,256]{1,0:T(8,128)(2,1)S(1)} collective-permute-done((bf16[208,256]{1,0:T(8,128)(2,1)S(1)}, bf16[208,256]{1,0:T(8,128)(2,1)S(1)}, u32[]{:S(2)}, u32[]{:S(2)}) %collective-permute-start.16) | collective-permute-done | bytes 106528 | tf_op jit(solution)/shard_map/ppermute | solution.py:57
  155.2 1.4 collective-permute-start.17
  157.0 19.2 %collective-permute-done.17 = bf16[416,256]{1,0:T(8,128)(2,1)S(1)} collective-permute-done((bf16[416,256]{1,0:T(8,128)(2,1)S(1)}, bf16[416,256]{1,0:T(8,128)(2,1)S(1)}, u32[]{:S(2)}, u32[]{:S(2)}) %collective-permute-start.17) | collective-permute-done | bytes 213024 | tf_op jit(solution)/shard_map/ppermute | solution.py:57
  177.6 19.6 %collective-permute-done.18 = bf16[832,256]{1,0:T(8,128)(2,1)S(1)} collective-permute-done((bf16[832,256]{1,0:T(8,128)(2,1)S(1)}, bf16[832,256]{1,0:T(8,128)(2,1)S(1)}, u32[]{:S(2)}, u32[]{:S(2)}) %collective-permute-start.18) | collective-permute-done | bytes 426016 | tf_op jit(solution)/shard_map/ppermute | solution.py:57
  197.5 2.4 %fusion.4 = bf16[2,2,2,256,256]{4,3,2,1,0:T(8,128)(2,1)} fusion(bf16[2,2,2,256,256]{4,3,2,1,0:T(8,128)(2,1)S(1)} %get-tuple-element.6, f32[2,2,2,256,256]{4,3,2,1,0:T(8,128)S(1)} %fusion.13, f32[2,2,2,256,256]{4,3,2,1,0:T(8,128)S(1)} %fusion.31, f32[2,2,2,256,256]{4,3,2,1,0:T(8,128)S(1)} %fusion.33, f32[2,2,2,256,256]{4,3,2,1,0:T(8,128)S(1)} %fusion.80, ...), kind=kOutput, calls=%fused_computation.13 | convolution fusion | flops 275775488 | bytes 21104128 | tf_op jit(solution)/shard_map/dot_general | solution.py:104
  (86 shorter events, 29.6 us)
Async XLA Ops:
  0.6 93.8 %copy-start = (bf16[256,256]{1,0:T(8,128)(2,1)S(1)}, bf16[256,256]{1,0:T(8,128)(2,1)}, u32[]{:S(2)}) copy-start(bf16[256,256]{1,0:T(8,128)(2,1)} %param.11) | copy-start | bytes 393220
  1.4 6.9 %copy-start.3 = (bf16[2,2,2,256,256]{4,3,2,1,0:T(8,128)(2,1)S(1)}, bf16[2,2,2,256,256]{4,3,2,1,0:T(8,128)(2,1)}, u32[]{:S(2)}) copy-start(bf16[2,2,2,256,256]{4,3,2,1,0:T(8,128)(2,1)} %param.7) | copy-start | bytes 3145732
  3.9 18.5 %collective-permute-start = (bf16[2,2,1,256,256]{4,3,2,1,0:T(8,128)(2,1)}, bf16[2,2,1,256,256]{4,3,2,1,0:T(8,128)(2,1)}, u32[]{:S(2)}, u32[]{:S(2)}) collective-permute-start(bf16[2,2,1,256,256]{4,3,2,1,0:T(8,128)(2,1)} %get-tuple-element.11), channel_id=1, source_target_pairs={{0,1},{2,3},{4,5},{6,7},{8,9},{10,11},{12,13},{14,15},{16,17},{18,... | collective-permute-start | bytes 1572872 | tf_op jit(solution)/shard_map/ppermute | solution.py:10
  7.1 15.4 %collective-permute-start.1 = (bf16[2,2,1,256,256]{4,3,2,1,0:T(8,128)(2,1)}, bf16[2,2,1,256,256]{4,3,2,1,0:T(8,128)(2,1)}, u32[]{:S(2)}, u32[]{:S(2)}) collective-permute-start(bf16[2,2,1,256,256]{4,3,2,1,0:T(8,128)(2,1)} %get-tuple-element.12), channel_id=1, source_target_pairs={{1,0},{3,2},{5,4},{7,6},{9,8},{11,10},{13,12},{15,14},{17,16},{19,... | collective-permute-start | bytes 1572872 | tf_op jit(solution)/shard_map/ppermute | solution.py:10
  8.8 29.5 %collective-permute-start.6 = (bf16[2,2,2,256,256]{4,3,2,1,0:T(8,128)(2,1)S(1)}, bf16[2,2,2,256,256]{4,3,2,1,0:T(8,128)(2,1)}, u32[]{:S(2)}, u32[]{:S(2)}) collective-permute-start(bf16[2,2,2,256,256]{4,3,2,1,0:T(8,128)(2,1)S(1)} %get-tuple-element.6), channel_id=1, source_target_pairs={{2,0},{4,2},{6,4},{8,6},{10,8},{12,10},{14,12},{3,1},{5,3},{7,5},{... | collective-permute-start | bytes 3145736 | tf_op jit(solution)/shard_map/ppermute | solution.py:10
  10.9 25.5 %collective-permute-start.3 = (bf16[2,2,256,256]{3,2,1,0:T(8,128)(2,1)}, bf16[2,2,256,256]{3,2,1,0:T(8,128)(2,1)}, u32[]{:S(2)}, u32[]{:S(2)}) collective-permute-start(bf16[2,2,256,256]{3,2,1,0:T(8,128)(2,1)} %slice_bitcast_fusion), channel_id=1, source_target_pairs={{0,8},{1,9},{16,24},{17,25}} | collective-permute-start | bytes 1572872 | tf_op jit(solution)/shard_map/ppermute | solution.py:21
  19.0 58.5 %collective-permute-start.9 = (f32[2,2,256,256]{3,2,1,0:T(8,128)S(1)}, f32[2,2,256,256]{3,2,1,0:T(8,128)}, u32[]{:S(2)}, u32[]{:S(2)}) collective-permute-start(f32[2,2,256,256]{3,2,1,0:T(8,128)S(1)} %get-tuple-element.5), channel_id=1, source_target_pairs={{2,0},{6,4},{10,8},{14,12},{3,1},{7,5},{11,9},{15,13},{18,16},{22,... | collective-permute-start | bytes 3145736 | tf_op jit(solution)/shard_map/ppermute | solution.py:32
  20.5 1.4 copy-start.2
  22.4 2.1 %copy-start.1 = (bf16[9,256,256]{2,1,0:T(8,128)(2,1)S(1)}, bf16[9,256,256]{2,1,0:T(8,128)(2,1)}, u32[]{:S(2)}) copy-start(bf16[9,256,256]{2,1,0:T(8,128)(2,1)} %param.9) | copy-start | bytes 3538948
  31.0 28.9 %collective-permute-start.2 = (bf16[2,2,2,256,256]{4,3,2,1,0:T(8,128)(2,1)S(1)}, bf16[2,2,2,256,256]{4,3,2,1,0:T(8,128)(2,1)S(1)}, u32[]{:S(2)}, u32[]{:S(2)}) collective-permute-start(bf16[2,2,2,256,256]{4,3,2,1,0:T(8,128)(2,1)S(1)} %get-tuple-element.13), channel_id=1, source_target_pairs={{0,2},{2,4},{4,6},{6,8},{8,10},{10,12},{12,14},{1,3},{3,5},{5,7},{... | collective-permute-start | bytes 3145736 | tf_op jit(solution)/shard_map/ppermute | solution.py:10
  36.5 13.5 %collective-permute-start.4 = (bf16[2,2,256,256]{3,2,1,0:T(8,128)(2,1)S(1)}, bf16[2,2,256,256]{3,2,1,0:T(8,128)(2,1)S(1)}, u32[]{:S(2)}, u32[]{:S(2)}) collective-permute-start(bf16[2,2,256,256]{3,2,1,0:T(8,128)(2,1)S(1)} %broadcast_select_fusion), channel_id=1, source_target_pairs={{0,4},{8,12},{1,5},{9,13},{16,20},{24,28},{17,21},{25,29}} | collective-permute-start | bytes 1572872 | tf_op jit(solution)/shard_map/ppermute | solution.py:21
  50.1 21.0 %collective-permute-start.5 = (bf16[2,2,256,256]{3,2,1,0:T(8,128)(2,1)S(1)}, bf16[2,2,256,256]{3,2,1,0:T(8,128)(2,1)S(1)}, u32[]{:S(2)}, u32[]{:S(2)}) collective-permute-start(bf16[2,2,256,256]{3,2,1,0:T(8,128)(2,1)S(1)} %broadcast_select_fusion.1), channel_id=1, source_target_pairs={{0,2},{4,6},{8,10},{12,14},{1,3},{5,7},{9,11},{13,15},{16,18},{20,... | collective-permute-start | bytes 1572872 | tf_op jit(solution)/shard_map/ppermute | solution.py:21
  72.3 10.1 %collective-permute-start.12 = (f32[1664,256]{1,0:T(8,128)S(1)}, f32[1664,256]{1,0:T(8,128)S(1)}, u32[]{:S(2)}, u32[]{:S(2)}) collective-permute-start(f32[1664,256]{1,0:T(8,128)S(1)} %constant_dynamic-slice_fusion.3), channel_id=1, source_target_pairs={{0,1},{1,0},{2,3},{3,2},{4,5},{5,4},{6,7},{7,6},{8,9},{9,8},{10,11... | collective-permute-start | bytes 5111816 | tf_op jit(solution)/shard_map/ppermute | solution.py:47
  73.1 8.0 %collective-permute-start.8 = (bf16[2,2,1,256,256]{4,3,2,1,0:T(8,128)(2,1)S(1)}, bf16[2,2,1,256,256]{4,3,2,1,0:T(8,128)(2,1)S(1)}, u32[]{:S(2)}, u32[]{:S(2)}) collective-permute-start(bf16[2,2,1,256,256]{4,3,2,1,0:T(8,128)(2,1)S(1)} %get-tuple-element.9), channel_id=1, source_target_pairs={{1,0},{3,2},{5,4},{7,6},{9,8},{11,10},{13,12},{15,14},{17,16},{19,... | collective-permute-start | bytes 1572872 | tf_op jit(solution)/shard_map/ppermute | solution.py:10
  74.4 6.7 %collective-permute-start.7 = (bf16[2,2,1,256,256]{4,3,2,1,0:T(8,128)(2,1)S(1)}, bf16[2,2,1,256,256]{4,3,2,1,0:T(8,128)(2,1)S(1)}, u32[]{:S(2)}, u32[]{:S(2)}) collective-permute-start(bf16[2,2,1,256,256]{4,3,2,1,0:T(8,128)(2,1)S(1)} %get-tuple-element.10), channel_id=1, source_target_pairs={{0,1},{2,3},{4,5},{6,7},{8,9},{10,11},{12,13},{14,15},{16,17},{18,... | collective-permute-start | bytes 1572872 | tf_op jit(solution)/shard_map/ppermute | solution.py:10
  78.9 65.5 %collective-permute-start.10 = (f32[2,2,256,256]{3,2,1,0:T(8,128)S(1)}, f32[2,2,256,256]{3,2,1,0:T(8,128)S(1)}, u32[]{:S(2)}, u32[]{:S(2)}) collective-permute-start(f32[2,2,256,256]{3,2,1,0:T(8,128)S(1)} %add.207), channel_id=1, source_target_pairs={{4,0},{12,8},{5,1},{13,9},{20,16},{28,24},{21,17},{29,25}} | collective-permute-start | bytes 3145736 | tf_op jit(solution)/shard_map/ppermute | solution.py:32
  82.8 30.2 %collective-permute-start.13 = (f32[832,256]{1,0:T(8,128)S(1)}, f32[832,256]{1,0:T(8,128)S(1)}, u32[]{:S(2)}, u32[]{:S(2)}) collective-permute-start(f32[832,256]{1,0:T(8,128)S(1)} %constant_dynamic-slice_fusion.2), channel_id=1, source_target_pairs={{0,8},{2,10},{4,12},{6,14},{8,0},{10,2},{12,4},{14,6},{1,9},{3,11}... | collective-permute-start | bytes 2555912 | tf_op jit(solution)/shard_map/ppermute | solution.py:47
  113.1 30.5 %collective-permute-start.14 = (f32[416,256]{1,0:T(8,128)S(1)}, f32[416,256]{1,0:T(8,128)S(1)}, u32[]{:S(2)}, u32[]{:S(2)}) collective-permute-start(f32[416,256]{1,0:T(8,128)S(1)} %constant_dynamic-slice_fusion.1), channel_id=1, source_target_pairs={{0,4},{2,6},{4,0},{6,2},{8,12},{10,14},{12,8},{14,10},{1,5},{3,7},... | collective-permute-start | bytes 1277960 | tf_op jit(solution)/shard_map/ppermute | solution.py:47
  143.8 6.5 %collective-permute-start.15 = (f32[208,256]{1,0:T(8,128)S(1)}, f32[208,256]{1,0:T(8,128)S(1)}, u32[]{:S(2)}, u32[]{:S(2)}) collective-permute-start(f32[208,256]{1,0:T(8,128)S(1)} %constant_dynamic-slice_fusion), channel_id=1, source_target_pairs={{0,2},{2,0},{4,6},{6,4},{8,10},{10,8},{12,14},{14,12},{1,3},{3,1},... | collective-permute-start | bytes 638984 | tf_op jit(solution)/shard_map/ppermute | solution.py:47
  144.5 32.5 %collective-permute-start.11 = (f32[2,2,256,256]{3,2,1,0:T(8,128)S(1)}, f32[2,2,256,256]{3,2,1,0:T(8,128)S(1)}, u32[]{:S(2)}, u32[]{:S(2)}) collective-permute-start(f32[2,2,256,256]{3,2,1,0:T(8,128)S(1)} %add.208), channel_id=1, source_target_pairs={{8,0},{9,1},{24,16},{25,17}} | collective-permute-start | bytes 3145736 | tf_op jit(solution)/shard_map/ppermute | solution.py:32
  150.3 4.8 %collective-permute-start.16 = (bf16[208,256]{1,0:T(8,128)(2,1)S(1)}, bf16[208,256]{1,0:T(8,128)(2,1)S(1)}, u32[]{:S(2)}, u32[]{:S(2)}) collective-permute-start(bf16[208,256]{1,0:T(8,128)(2,1)S(1)} %multiply_convert_fusion.3), channel_id=1, source_target_pairs={{0,2},{2,0},{4,6},{6,4},{8,10},{10,8},{12,14},{14,12},{1,3},{3,1},... | collective-permute-start | bytes 319496 | tf_op jit(solution)/shard_map/ppermute | solution.py:57
  155.2 21.1 %collective-permute-start.17 = (bf16[416,256]{1,0:T(8,128)(2,1)S(1)}, bf16[416,256]{1,0:T(8,128)(2,1)S(1)}, u32[]{:S(2)}, u32[]{:S(2)}) collective-permute-start(bf16[416,256]{1,0:T(8,128)(2,1)S(1)} %maximum_select_fusion.3), channel_id=1, source_target_pairs={{0,4},{2,6},{4,0},{6,2},{8,12},{10,14},{12,8},{14,10},{1,5},{3,7},... | collective-permute-start | bytes 638984 | tf_op jit(solution)/shard_map/ppermute | solution.py:57
  176.4 20.8 %collective-permute-start.18 = (bf16[832,256]{1,0:T(8,128)(2,1)S(1)}, bf16[832,256]{1,0:T(8,128)(2,1)S(1)}, u32[]{:S(2)}, u32[]{:S(2)}) collective-permute-start(bf16[832,256]{1,0:T(8,128)(2,1)S(1)} %maximum_select_fusion.2), channel_id=1, source_target_pairs={{0,8},{2,10},{4,12},{6,14},{8,0},{10,2},{12,4},{14,6},{1,9},{3,11}... | collective-permute-start | bytes 1277960 | tf_op jit(solution)/shard_map/ppermute | solution.py:57
  197.4 2.5 %collective-permute-start.19 = (bf16[1664,256]{1,0:T(8,128)(2,1)S(1)}, bf16[1664,256]{1,0:T(8,128)(2,1)S(1)}, u32[]{:S(2)}, u32[]{:S(2)}) collective-permute-start(bf16[1664,256]{1,0:T(8,128)(2,1)S(1)} %maximum_select_fusion.1), channel_id=1, source_target_pairs={{0,1},{1,0},{2,3},{3,2},{4,5},{5,4},{6,7},{7,6},{8,9},{9,8},{10,11... | collective-permute-start | bytes 2555912 | tf_op jit(solution)/shard_map/ppermute | solution.py:57

commit v2 on v1

--- a/solution.py
+++ b/solution.py
@@ -34,56 +34,92 @@
     return value
 
 
-def halving_sum(flat, axis):
-    count = lax.axis_size(axis)
-    me = lax.axis_index(axis)
-    step = count // 2
-    while step >= 1:
+def xor_halving(flat, axis, steps):
+    me = lax.axis_index(axis)
+    count = lax.axis_size(axis)
+    for step in steps:
         half = flat.shape[0] // 2
         upper = (me // step) % 2
         keep = lax.dynamic_slice_in_dim(flat, upper * half, half, 0)
         send = lax.dynamic_slice_in_dim(flat, (1 - upper) * half, half, 0)
         pairs = [(i, i ^ step) for i in range(count)]
         flat = keep + lax.ppermute(send, axis, pairs)
-        step //= 2
     return flat
 
 
-def doubling_gather(piece, axis):
-    count = lax.axis_size(axis)
-    me = lax.axis_index(axis)
-    step = 1
-    while step < count:
+def xor_doubling(piece, axis, steps):
+    me = lax.axis_index(axis)
+    count = lax.axis_size(axis)
+    for step in reversed(steps):
         got = lax.ppermute(piece, axis, [(i, i ^ step) for i in range(count)])
         upper = (me // step) % 2 == 1
         piece = jnp.where(
             upper, jnp.concatenate([got, piece], 0), jnp.concatenate([piece, got], 0)
         )
-        step *= 2
     return piece
+
+
+def direct_scatter(flat, axis, low, high):
+    me = lax.axis_index(axis)
+    j = me // low
+    blk = flat.shape[0] // high
+    total = lax.dynamic_slice_in_dim(flat, j * blk, blk, 0)
+    for d in range(1, high):
+        send = lax.dynamic_slice_in_dim(flat, ((j + d) % high) * blk, blk, 0)
+        pairs = [
+            (a * low + b, ((a + d) % high) * low + b) for a in range(high) for b in range(low)
+        ]
+        total = total + lax.ppermute(send, axis, pairs)
+    return total
+
+
+def direct_gather(piece, axis, low, high):
+    me = lax.axis_index(axis)
+    j = me // low
+    out = jnp.zeros((high,) + piece.shape, piece.dtype)
+    out = lax.dynamic_update_index_in_dim(out, piece, j, 0)
+    for d in range(1, high):
+        pairs = [
+            (a * low + b, ((a + d) % high) * low + b) for a in range(high) for b in range(low)
+        ]
+        got = lax.ppermute(piece, axis, pairs)
+        out = lax.dynamic_update_index_in_dim(out, got, (j - d) % high, 0)
+    return out.reshape((-1,) + piece.shape[1:])
 
 
 def is_pow2(n):
     return n >= 1 and (n & (n - 1)) == 0
 
 
-def all_sum_rounded(flat, axes, scale):
-    sizes = [lax.axis_size(a) for a in axes]
-    if not all(is_pow2(s) for s in sizes):
-        return (lax.psum(flat, tuple(axes)) * scale).astype(jnp.bfloat16)
-    parts = 1
-    for s in sizes:
-        parts *= s
+def all_sum_rounded(flat, scale):
+    n_tm = lax.axis_size("tm")
+    n_sp = lax.axis_size("space")
+    if not (is_pow2(n_tm) and is_pow2(n_sp)):
+        return (lax.psum(flat, ("tm", "space")) * scale).astype(jnp.bfloat16)
+    high = min(4, n_sp)
+    low = n_sp // high
+    tm_steps = []
+    s = 1
+    while s < n_tm:
+        tm_steps.append(s)
+        s *= 2
+    sp_steps = []
+    s = 1
+    while s < low:
+        sp_steps.append(s)
+        s *= 2
     rows = flat.shape[0]
-    unit = parts * 8
+    unit = n_tm * n_sp * 8
     padded_rows = -(-rows // unit) * unit
     if padded_rows != rows:
         flat = jnp.pad(flat, ((0, padded_rows - rows), (0, 0)))
-    for a in axes:
-        flat = halving_sum(flat, a)
+    flat = xor_halving(flat, "tm", tm_steps)
+    flat = xor_halving(flat, "space", sp_steps)
+    flat = direct_scatter(flat, "space", low, high)
     piece = (flat * scale).astype(jnp.bfloat16)
-    for a in reversed(axes):
-        piece = doubling_gather(piece, a)
+    piece = direct_gather(piece, "space", low, high)
+    piece = xor_doubling(piece, "space", sp_steps)
+    piece = xor_doubling(piece, "tm", tm_steps)
     return piece[:rows]
 
 
@@ -206,7 +242,7 @@
         axis=0,
     )
     scale = (clips * frames * rows * cols * lax.axis_size("space") * lax.axis_size("tm")) ** (-0.5)
-    summed = all_sum_rounded(flat, ("tm", "space"), scale)
+    summed = all_sum_rounded(flat, scale)
     n_s = taps_s * chans
     n_t = taps_t * chans
     grad_spatial = summed[:n_s].reshape(taps_s, chans, chans)

time: 204 us -> 184 us (0.902)
  starting transfers between devices: 66.4 us -> 54.9 us
  waiting for transfers between devices: 91.1 us -> 82 us
    ppermute x8 -> x10, starting transfers between devices: 35.8 us -> 24.7 us  [the longest x3 14.8 us: direct_scatter(): total = total + lax.ppermute(send, axis, pairs)]
    ppermute x8 -> x10, waiting for transfers between devices: 71.3 us -> 63.1 us  [the longest x3 26 us: direct_gather(): got = lax.ppermute(piece, axis, pairs)]
  transfers between devices with their start and end apart: 20 -> 22, of which waited for: 9 -> 10; matrix products, arithmetic and copies ran while one was open for 19% -> 21% of each run, Pallas kernels for 0% -> 0%
where the time goes in v2:
time: 184 us; the launch traced here: 182 us
  waiting for transfers between devices  82 us (45%)
  starting transfers between devices  54.9 us (30%)
  matrix products  30.7 us (17%)
  other arithmetic  8.55 us (5%)
  local copies, waits for them, and re-layouts  4.78 us (3%)
    ppermute x3, waiting for transfers between devices, direct_gather(): got = lax.ppermute(piece, axis, pairs)  26 us
    ppermute x2, waiting for transfers between devices, xor_halving(): flat = keep + lax.ppermute(send, axis, pairs)  17.1 us
    ppermute x6, starting transfers between devices, shifted(): return lax.ppermute(value, axis, pairs)  15.4 us
    ppermute x3, starting transfers between devices, direct_scatter(): total = total + lax.ppermute(send, axis, pairs)  14.8 us
    dot_general x18, matrix products, spatial_sum(): total = total + jnp.dot(piece, kernel, preferred_element_type=jnp.float32)  14.2 us
    ppermute x3, waiting for transfers between devices, tree_broadcast(): got = lax.ppermute(value, axis, pairs)  13.6 us
    ppermute x3, starting transfers between devices, tree_broadcast(): got = lax.ppermute(value, axis, pairs)  11 us
    ppermute x2, waiting for transfers between devices, xor_doubling(): got = lax.ppermute(piece, axis, [(i, i ^ step) for i in range(count)])  10.2 us
  transfers between devices with their start and end apart: 22, of which 10 were waited for; matrix products, arithmetic and copies ran while one was open for 21% of the time, Pallas kernels for 0%

profile of v2, /device:TPU:0, one launch (start us, length us, event | category | flops | bytes accessed | tf_op | source)
XLA Modules:
  0.0 182.4 jit_solution(16189507838127194119)
XLA Ops:
  1.4 1.5 broadcast_multiply_fusion.1
  3.9 3.1 %collective-permute-start = (bf16[2,2,1,256,256]{4,3,2,1,0:T(8,128)(2,1)}, bf16[2,2,1,256,256]{4,3,2,1,0:T(8,128)(2,1)}, u32[]{:S(2)}, u32[]{:S(2)}) collective-permute-start(bf16[2,2,1,256,256]{4,3,2,1,0:T(8,128)(2,1)} %get-tuple-element.13), channel_id=1, source_target_pairs={{0,1},{2,3},{4,5},{6,7},{8,9},{10,11},{12,13},{14,15},{16,17},{18,... | collective-permute-start | bytes 1572872 | tf_op jit(solution)/shard_map/ppermute | solution.py:10
  10.9 8.1 %collective-permute-start.3 = (bf16[2,2,256,256]{3,2,1,0:T(8,128)(2,1)}, bf16[2,2,256,256]{3,2,1,0:T(8,128)(2,1)}, u32[]{:S(2)}, u32[]{:S(2)}) collective-permute-start(bf16[2,2,256,256]{3,2,1,0:T(8,128)(2,1)} %slice_bitcast_fusion), channel_id=1, source_target_pairs={{0,8},{1,9},{16,24},{17,25}} | collective-permute-start | bytes 1572872 | tf_op jit(solution)/shard_map/ppermute | solution.py:21
  20.7 1.4 fusion.82
  22.6 2.1 %select_maximum_fusion.2 = bf16[2,2,4,258,256]{4,3,2,1,0:T(8,128)(2,1)S(1)} fusion(bf16[2,2,1,256,256]{4,3,2,1,0:T(8,128)(2,1)} %collective-permute-done.1, bf16[2,2,2,256,256]{4,3,2,1,0:T(8,128)(2,1)S(1)} %broadcast_multiply_fusion.1, bf16[2,2,1,256,256]{4,3,2,1,0:T(8,128)(2,1)} %collective-permute-done), kind=kLoop, calls=%fused_computation.8 | loop fusion | flops 12681216 | bytes 4210688 | tf_op jit(solution)/shard_map/concatenate | solution.py:182
  26.9 1.5 fusion.43
  28.4 1.5 fusion.44
  29.8 1.5 multiply_convert_fusion.2
  31.4 5.3 %collective-permute-start.2 = (bf16[2,2,2,256,256]{4,3,2,1,0:T(8,128)(2,1)S(1)}, bf16[2,2,2,256,256]{4,3,2,1,0:T(8,128)(2,1)S(1)}, u32[]{:S(2)}, u32[]{:S(2)}) collective-permute-start(bf16[2,2,2,256,256]{4,3,2,1,0:T(8,128)(2,1)S(1)} %get-tuple-element.18), channel_id=1, source_target_pairs={{0,2},{2,4},{4,6},{6,8},{8,10},{10,12},{12,14},{1,3},{3,5},{5,7},{... | collective-permute-start | bytes 3145736 | tf_op jit(solution)/shard_map/ppermute | solution.py:10
  36.8 1.3 collective-permute-start.4
  39.0 1.5 fusion.5
  40.5 2.3 %multiply_convert_fusion = bf16[2,2,2,256,256]{4,3,2,1,0:T(8,128)(2,1)S(1)} fusion(f32[2,2,2,256,256]{4,3,2,1,0:T(8,128)S(1)} %get-tuple-element.19, f32[2,2,2,256,256]{4,3,2,1,0:T(8,128)S(1)} %fusion.99, f32[2,2,2,256,256]{4,3,2,1,0:T(8,128)S(1)} %fusion.5, bf16[2,2,2,256,256]{4,3,2,1,0:T(8,128)(2,1)} %collective-permute-done.6, ...), kind=kOutput, calls=%fused_computation.19 | convolution fusion | flops 274202624 | bytes 8519680 | tf_op jit(solution)/shard_map/dot_general | solution.py:158
  43.3 1.5 fusion.21
  46.8 3.4 %collective-permute-done.4 = bf16[2,2,256,256]{3,2,1,0:T(8,128)(2,1)S(1)} collective-permute-done((bf16[2,2,256,256]{3,2,1,0:T(8,128)(2,1)S(1)}, bf16[2,2,256,256]{3,2,1,0:T(8,128)(2,1)S(1)}, u32[]{:S(2)}, u32[]{:S(2)}) %collective-permute-start.4) | collective-permute-done | bytes 524320 | tf_op jit(solution)/shard_map/ppermute | solution.py:21
  50.3 1.5 collective-permute-start.5
  52.3 1.5 fusion.20
  54.8 5.2 %collective-permute-done.2 = bf16[2,2,2,256,256]{4,3,2,1,0:T(8,128)(2,1)S(1)} collective-permute-done((bf16[2,2,2,256,256]{4,3,2,1,0:T(8,128)(2,1)S(1)}, bf16[2,2,2,256,256]{4,3,2,1,0:T(8,128)(2,1)S(1)}, u32[]{:S(2)}, u32[]{:S(2)}) %collective-permute-start.2) | collective-permute-done | bytes 1048608 | tf_op jit(solution)/shard_map/ppermute | solution.py:10
  61.0 10.2 %collective-permute-done.5 = bf16[2,2,256,256]{3,2,1,0:T(8,128)(2,1)S(1)} collective-permute-done((bf16[2,2,256,256]{3,2,1,0:T(8,128)(2,1)S(1)}, bf16[2,2,256,256]{3,2,1,0:T(8,128)(2,1)S(1)}, u32[]{:S(2)}, u32[]{:S(2)}) %collective-permute-start.5) | collective-permute-done | bytes 524320 | tf_op jit(solution)/shard_map/ppermute | solution.py:21
  74.2 3.1 %collective-permute-start.7 = (bf16[2,2,1,256,256]{4,3,2,1,0:T(8,128)(2,1)S(1)}, bf16[2,2,1,256,256]{4,3,2,1,0:T(8,128)(2,1)S(1)}, u32[]{:S(2)}, u32[]{:S(2)}) collective-permute-start(bf16[2,2,1,256,256]{4,3,2,1,0:T(8,128)(2,1)S(1)} %get-tuple-element.12), channel_id=1, source_target_pairs={{0,1},{2,3},{4,5},{6,7},{8,9},{10,11},{12,13},{14,15},{16,17},{18,... | collective-permute-start | bytes 1572872 | tf_op jit(solution)/shard_map/ppermute | solution.py:10
  77.3 1.4 add.244
  82.1 1.7 multiply_convert_fusion.1
  84.1 1.8 collective-permute-start.13
  87.3 17.1 %collective-permute-done.13 = f32[832,256]{1,0:T(8,128)S(1)} collective-permute-done((f32[832,256]{1,0:T(8,128)S(1)}, f32[832,256]{1,0:T(8,128)S(1)}, u32[]{:S(2)}, u32[]{:S(2)}) %collective-permute-start.13) | collective-permute-done | bytes 852000 | tf_op jit(solution)/shard_map/ppermute | solution.py:46
  104.6 7.5 %collective-permute-start.14 = (f32[208,256]{1,0:T(8,128)S(1)}, f32[208,256]{1,0:T(8,128)S(1)}, u32[]{:S(2)}, u32[]{:S(2)}) collective-permute-start(f32[208,256]{1,0:T(8,128)S(1)} %get-tuple-element.15), channel_id=1, source_target_pairs={{0,4},{2,6},{4,8},{6,10},{8,12},{10,14},{12,0},{14,2},{1,5},{3,7},... | collective-permute-start | bytes 638984 | tf_op jit(solution)/shard_map/ppermute | solution.py:72
  112.0 6.8 %collective-permute-start.15 = (f32[208,256]{1,0:T(8,128)S(1)}, f32[208,256]{1,0:T(8,128)S(1)}, u32[]{:S(2)}, u32[]{:S(2)}) collective-permute-start(f32[208,256]{1,0:T(8,128)S(1)} %get-tuple-element.17), channel_id=1, source_target_pairs={{0,8},{2,10},{4,12},{6,14},{8,0},{10,2},{12,4},{14,6},{1,9},{3,11}... | collective-permute-start | bytes 638984 | tf_op jit(solution)/shard_map/ppermute | solution.py:72
  121.3 3.2 %collective-permute-done.14 = f32[208,256]{1,0:T(8,128)S(1)} collective-permute-done((f32[208,256]{1,0:T(8,128)S(1)}, f32[208,256]{1,0:T(8,128)S(1)}, u32[]{:S(2)}, u32[]{:S(2)}) %collective-permute-start.14) | collective-permute-done | bytes 213024 | tf_op jit(solution)/shard_map/ppermute | solution.py:72
  124.5 6.6 %collective-permute-done.15 = f32[208,256]{1,0:T(8,128)S(1)} collective-permute-done((f32[208,256]{1,0:T(8,128)S(1)}, f32[208,256]{1,0:T(8,128)S(1)}, u32[]{:S(2)}, u32[]{:S(2)}) %collective-permute-start.15) | collective-permute-done | bytes 213024 | tf_op jit(solution)/shard_map/ppermute | solution.py:72
  131.2 5.2 %collective-permute-start.17 = (bf16[208,256]{1,0:T(8,128)(2,1)S(1)}, bf16[208,256]{1,0:T(8,128)(2,1)S(1)}, u32[]{:S(2)}, u32[]{:S(2)}) collective-permute-start(bf16[208,256]{1,0:T(8,128)(2,1)S(1)} %get-tuple-element.6), channel_id=1, source_target_pairs={{0,4},{2,6},{4,8},{6,10},{8,12},{10,14},{12,0},{14,2},{1,5},{3,7},... | collective-permute-start | bytes 319496 | tf_op jit(solution)/shard_map/ppermute | solution.py:85
  137.9 1.4 collective-permute-start.19
  139.8 25.3 %collective-permute-done.18 = bf16[208,256]{1,0:T(8,128)(2,1)S(1)} collective-permute-done((bf16[208,256]{1,0:T(8,128)(2,1)S(1)}, bf16[208,256]{1,0:T(8,128)(2,1)S(1)}, u32[]{:S(2)}, u32[]{:S(2)}) %collective-permute-start.18) | collective-permute-done | bytes 106528 | tf_op jit(solution)/shard_map/ppermute | solution.py:85
  166.6 10.2 %collective-permute-done.20 = bf16[832,256]{1,0:T(8,128)(2,1)S(1)} collective-permute-done((bf16[832,256]{1,0:T(8,128)(2,1)S(1)}, bf16[832,256]{1,0:T(8,128)(2,1)S(1)}, u32[]{:S(2)}, u32[]{:S(2)}) %collective-permute-start.20) | collective-permute-done | bytes 426016 | tf_op jit(solution)/shard_map/ppermute | solution.py:54
  177.1 2.3 %fusion.4 = bf16[2,2,2,256,256]{4,3,2,1,0:T(8,128)(2,1)} fusion(bf16[2,2,2,256,256]{4,3,2,1,0:T(8,128)(2,1)S(1)} %get-tuple-element.8, f32[2,2,2,256,256]{4,3,2,1,0:T(8,128)S(1)} %fusion.13, f32[2,2,2,256,256]{4,3,2,1,0:T(8,128)S(1)} %fusion.31, f32[2,2,2,256,256]{4,3,2,1,0:T(8,128)S(1)} %fusion.33, f32[2,2,2,256,256]{4,3,2,1,0:T(8,128)S(1)} %fusion.80, ...), kind=kOutput, calls=%fused_computation.13 | convolution fusion | flops 275775488 | bytes 21104128 | tf_op jit(solution)/shard_map/dot_general | solution.py:140
  (90 shorter events, 33.0 us)
Async XLA Ops:
  0.6 79.8 %copy-start = (bf16[256,256]{1,0:T(8,128)(2,1)S(1)}, bf16[256,256]{1,0:T(8,128)(2,1)}, u32[]{:S(2)}) copy-start(bf16[256,256]{1,0:T(8,128)(2,1)} %param.11) | copy-start | bytes 393220
  1.4 6.9 %copy-start.3 = (bf16[2,2,2,256,256]{4,3,2,1,0:T(8,128)(2,1)S(1)}, bf16[2,2,2,256,256]{4,3,2,1,0:T(8,128)(2,1)}, u32[]{:S(2)}) copy-start(bf16[2,2,2,256,256]{4,3,2,1,0:T(8,128)(2,1)} %param.7) | copy-start | bytes 3145732
  3.9 18.6 %collective-permute-start = (bf16[2,2,1,256,256]{4,3,2,1,0:T(8,128)(2,1)}, bf16[2,2,1,256,256]{4,3,2,1,0:T(8,128)(2,1)}, u32[]{:S(2)}, u32[]{:S(2)}) collective-permute-start(bf16[2,2,1,256,256]{4,3,2,1,0:T(8,128)(2,1)} %get-tuple-element.13), channel_id=1, source_target_pairs={{0,1},{2,3},{4,5},{6,7},{8,9},{10,11},{12,13},{14,15},{16,17},{18,... | collective-permute-start | bytes 1572872 | tf_op jit(solution)/shard_map/ppermute | solution.py:10
  7.1 15.5 %collective-permute-start.1 = (bf16[2,2,1,256,256]{4,3,2,1,0:T(8,128)(2,1)}, bf16[2,2,1,256,256]{4,3,2,1,0:T(8,128)(2,1)}, u32[]{:S(2)}, u32[]{:S(2)}) collective-permute-start(bf16[2,2,1,256,256]{4,3,2,1,0:T(8,128)(2,1)} %get-tuple-element.14), channel_id=1, source_target_pairs={{1,0},{3,2},{5,4},{7,6},{9,8},{11,10},{13,12},{15,14},{17,16},{19,... | collective-permute-start | bytes 1572872 | tf_op jit(solution)/shard_map/ppermute | solution.py:10
  8.8 30.2 %collective-permute-start.6 = (bf16[2,2,2,256,256]{4,3,2,1,0:T(8,128)(2,1)S(1)}, bf16[2,2,2,256,256]{4,3,2,1,0:T(8,128)(2,1)}, u32[]{:S(2)}, u32[]{:S(2)}) collective-permute-start(bf16[2,2,2,256,256]{4,3,2,1,0:T(8,128)(2,1)S(1)} %get-tuple-element.8), channel_id=1, source_target_pairs={{2,0},{4,2},{6,4},{8,6},{10,8},{12,10},{14,12},{3,1},{5,3},{7,5},{... | collective-permute-start | bytes 3145736 | tf_op jit(solution)/shard_map/ppermute | solution.py:10
  10.9 25.7 %collective-permute-start.3 = (bf16[2,2,256,256]{3,2,1,0:T(8,128)(2,1)}, bf16[2,2,256,256]{3,2,1,0:T(8,128)(2,1)}, u32[]{:S(2)}, u32[]{:S(2)}) collective-permute-start(bf16[2,2,256,256]{3,2,1,0:T(8,128)(2,1)} %slice_bitcast_fusion), channel_id=1, source_target_pairs={{0,8},{1,9},{16,24},{17,25}} | collective-permute-start | bytes 1572872 | tf_op jit(solution)/shard_map/ppermute | solution.py:21
  19.1 58.3 %collective-permute-start.9 = (f32[2,2,256,256]{3,2,1,0:T(8,128)S(1)}, f32[2,2,256,256]{3,2,1,0:T(8,128)}, u32[]{:S(2)}, u32[]{:S(2)}) collective-permute-start(f32[2,2,256,256]{3,2,1,0:T(8,128)S(1)} %get-tuple-element.7), channel_id=1, source_target_pairs={{2,0},{6,4},{10,8},{14,12},{3,1},{7,5},{11,9},{15,13},{18,16},{22,... | collective-permute-start | bytes 3145736 | tf_op jit(solution)/shard_map/ppermute | solution.py:32
  20.6 1.4 copy-start.2
  22.5 2.1 %copy-start.1 = (bf16[9,256,256]{2,1,0:T(8,128)(2,1)S(1)}, bf16[9,256,256]{2,1,0:T(8,128)(2,1)}, u32[]{:S(2)}) copy-start(bf16[9,256,256]{2,1,0:T(8,128)(2,1)} %param.9) | copy-start | bytes 3538948
  31.4 28.6 %collective-permute-start.2 = (bf16[2,2,2,256,256]{4,3,2,1,0:T(8,128)(2,1)S(1)}, bf16[2,2,2,256,256]{4,3,2,1,0:T(8,128)(2,1)S(1)}, u32[]{:S(2)}, u32[]{:S(2)}) collective-permute-start(bf16[2,2,2,256,256]{4,3,2,1,0:T(8,128)(2,1)S(1)} %get-tuple-element.18), channel_id=1, source_target_pairs={{0,2},{2,4},{4,6},{6,8},{8,10},{10,12},{12,14},{1,3},{3,5},{5,7},{... | collective-permute-start | bytes 3145736 | tf_op jit(solution)/shard_map/ppermute | solution.py:10
  36.8 13.5 %collective-permute-start.4 = (bf16[2,2,256,256]{3,2,1,0:T(8,128)(2,1)S(1)}, bf16[2,2,256,256]{3,2,1,0:T(8,128)(2,1)S(1)}, u32[]{:S(2)}, u32[]{:S(2)}) collective-permute-start(bf16[2,2,256,256]{3,2,1,0:T(8,128)(2,1)S(1)} %broadcast_select_fusion), channel_id=1, source_target_pairs={{0,4},{8,12},{1,5},{9,13},{16,20},{24,28},{17,21},{25,29}} | collective-permute-start | bytes 1572872 | tf_op jit(solution)/shard_map/ppermute | solution.py:21
  50.3 21.0 %collective-permute-start.5 = (bf16[2,2,256,256]{3,2,1,0:T(8,128)(2,1)S(1)}, bf16[2,2,256,256]{3,2,1,0:T(8,128)(2,1)S(1)}, u32[]{:S(2)}, u32[]{:S(2)}) collective-permute-start(bf16[2,2,256,256]{3,2,1,0:T(8,128)(2,1)S(1)} %broadcast_select_fusion.1), channel_id=1, source_target_pairs={{0,2},{4,6},{8,10},{12,14},{1,3},{5,7},{9,11},{13,15},{16,18},{20,... | collective-permute-start | bytes 1572872 | tf_op jit(solution)/shard_map/ppermute | solution.py:21
  72.4 11.4 %collective-permute-start.12 = (f32[1664,256]{1,0:T(8,128)S(1)}, f32[1664,256]{1,0:T(8,128)S(1)}, u32[]{:S(2)}, u32[]{:S(2)}) collective-permute-start(f32[1664,256]{1,0:T(8,128)S(1)} %constant_dynamic-slice_fusion.4), channel_id=1, source_target_pairs={{0,1},{1,0},{2,3},{3,2},{4,5},{5,4},{6,7},{7,6},{8,9},{9,8},{10,11... | collective-permute-start | bytes 5111816 | tf_op jit(solution)/shard_map/ppermute | solution.py:46
  72.9 7.8 %collective-permute-start.8 = (bf16[2,2,1,256,256]{4,3,2,1,0:T(8,128)(2,1)S(1)}, bf16[2,2,1,256,256]{4,3,2,1,0:T(8,128)(2,1)S(1)}, u32[]{:S(2)}, u32[]{:S(2)}) collective-permute-start(bf16[2,2,1,256,256]{4,3,2,1,0:T(8,128)(2,1)S(1)} %get-tuple-element.11), channel_id=1, source_target_pairs={{1,0},{3,2},{5,4},{7,6},{9,8},{11,10},{13,12},{15,14},{17,16},{19,... | collective-permute-start | bytes 1572872 | tf_op jit(solution)/shard_map/ppermute | solution.py:10
  74.2 6.5 %collective-permute-start.7 = (bf16[2,2,1,256,256]{4,3,2,1,0:T(8,128)(2,1)S(1)}, bf16[2,2,1,256,256]{4,3,2,1,0:T(8,128)(2,1)S(1)}, u32[]{:S(2)}, u32[]{:S(2)}) collective-permute-start(bf16[2,2,1,256,256]{4,3,2,1,0:T(8,128)(2,1)S(1)} %get-tuple-element.12), channel_id=1, source_target_pairs={{0,1},{2,3},{4,5},{6,7},{8,9},{10,11},{12,13},{14,15},{16,17},{18,... | collective-permute-start | bytes 1572872 | tf_op jit(solution)/shard_map/ppermute | solution.py:10
  78.7 41.2 %collective-permute-start.10 = (f32[2,2,256,256]{3,2,1,0:T(8,128)S(1)}, f32[2,2,256,256]{3,2,1,0:T(8,128)S(1)}, u32[]{:S(2)}, u32[]{:S(2)}) collective-permute-start(f32[2,2,256,256]{3,2,1,0:T(8,128)S(1)} %add.244), channel_id=1, source_target_pairs={{4,0},{12,8},{5,1},{13,9},{20,16},{28,24},{21,17},{29,25}} | collective-permute-start | bytes 3145736 | tf_op jit(solution)/shard_map/ppermute | solution.py:32
  84.1 20.3 %collective-permute-start.13 = (f32[832,256]{1,0:T(8,128)S(1)}, f32[832,256]{1,0:T(8,128)S(1)}, u32[]{:S(2)}, u32[]{:S(2)}) collective-permute-start(f32[832,256]{1,0:T(8,128)S(1)} %constant_dynamic-slice_fusion.3), channel_id=1, source_target_pairs={{0,2},{2,0},{4,6},{6,4},{8,10},{10,8},{12,14},{14,12},{1,3},{3,1},... | collective-permute-start | bytes 2555912 | tf_op jit(solution)/shard_map/ppermute | solution.py:46
  104.6 20.0 %collective-permute-start.14 = (f32[208,256]{1,0:T(8,128)S(1)}, f32[208,256]{1,0:T(8,128)S(1)}, u32[]{:S(2)}, u32[]{:S(2)}) collective-permute-start(f32[208,256]{1,0:T(8,128)S(1)} %get-tuple-element.15), channel_id=1, source_target_pairs={{0,4},{2,6},{4,8},{6,10},{8,12},{10,14},{12,0},{14,2},{1,5},{3,7},... | collective-permute-start | bytes 638984 | tf_op jit(solution)/shard_map/ppermute | solution.py:72
  112.0 19.1 %collective-permute-start.15 = (f32[208,256]{1,0:T(8,128)S(1)}, f32[208,256]{1,0:T(8,128)S(1)}, u32[]{:S(2)}, u32[]{:S(2)}) collective-permute-start(f32[208,256]{1,0:T(8,128)S(1)} %get-tuple-element.17), channel_id=1, source_target_pairs={{0,8},{2,10},{4,12},{6,14},{8,0},{10,2},{12,4},{14,6},{1,9},{3,11}... | collective-permute-start | bytes 638984 | tf_op jit(solution)/shard_map/ppermute | solution.py:72
  118.9 12.2 %collective-permute-start.16 = (f32[208,256]{1,0:T(8,128)S(1)}, f32[208,256]{1,0:T(8,128)S(1)}, u32[]{:S(2)}, u32[]{:S(2)}) collective-permute-start(f32[208,256]{1,0:T(8,128)S(1)} %get-tuple-element.16), channel_id=1, source_target_pairs={{0,12},{2,14},{4,0},{6,2},{8,4},{10,6},{12,8},{14,10},{1,13},{3,15... | collective-permute-start | bytes 638984 | tf_op jit(solution)/shard_map/ppermute | solution.py:72
  120.0 45.9 %collective-permute-start.11 = (f32[2,2,256,256]{3,2,1,0:T(8,128)S(1)}, f32[2,2,256,256]{3,2,1,0:T(8,128)S(1)}, u32[]{:S(2)}, u32[]{:S(2)}) collective-permute-start(f32[2,2,256,256]{3,2,1,0:T(8,128)S(1)} %add.245), channel_id=1, source_target_pairs={{8,0},{9,1},{24,16},{25,17}} | collective-permute-start | bytes 3145736 | tf_op jit(solution)/shard_map/ppermute | solution.py:32
  131.2 8.6 %collective-permute-start.17 = (bf16[208,256]{1,0:T(8,128)(2,1)S(1)}, bf16[208,256]{1,0:T(8,128)(2,1)S(1)}, u32[]{:S(2)}, u32[]{:S(2)}) collective-permute-start(bf16[208,256]{1,0:T(8,128)(2,1)S(1)} %get-tuple-element.6), channel_id=1, source_target_pairs={{0,4},{2,6},{4,8},{6,10},{8,12},{10,14},{12,0},{14,2},{1,5},{3,7},... | collective-permute-start | bytes 319496 | tf_op jit(solution)/shard_map/ppermute | solution.py:85
  136.9 28.2 %collective-permute-start.18 = (bf16[208,256]{1,0:T(8,128)(2,1)S(1)}, bf16[208,256]{1,0:T(8,128)(2,1)S(1)}, u32[]{:S(2)}, u32[]{:S(2)}) collective-permute-start(bf16[208,256]{1,0:T(8,128)(2,1)S(1)} %get-tuple-element.6), channel_id=1, source_target_pairs={{0,8},{2,10},{4,12},{6,14},{8,0},{10,2},{12,4},{14,6},{1,9},{3,11}... | collective-permute-start | bytes 319496 | tf_op jit(solution)/shard_map/ppermute | solution.py:85
  137.9 27.4 %collective-permute-start.19 = (bf16[208,256]{1,0:T(8,128)(2,1)S(1)}, bf16[208,256]{1,0:T(8,128)(2,1)S(1)}, u32[]{:S(2)}, u32[]{:S(2)}) collective-permute-start(bf16[208,256]{1,0:T(8,128)(2,1)S(1)} %get-tuple-element.6), channel_id=1, source_target_pairs={{0,12},{2,14},{4,0},{6,2},{8,4},{10,6},{12,8},{14,10},{1,13},{3,15... | collective-permute-start | bytes 319496 | tf_op jit(solution)/shard_map/ppermute | solution.py:85
  165.3 11.4 %collective-permute-start.20 = (bf16[832,256]{1,0:T(8,128)(2,1)S(1)}, bf16[832,256]{1,0:T(8,128)(2,1)S(1)}, u32[]{:S(2)}, u32[]{:S(2)}) collective-permute-start(bf16[832,256]{1,0:T(8,128)(2,1)S(1)} %bitcast.256), channel_id=1, source_target_pairs={{0,2},{2,0},{4,6},{6,4},{8,10},{10,8},{12,14},{14,12},{1,3},{3,1},... | collective-permute-start | bytes 1277960 | tf_op jit(solution)/shard_map/ppermute | solution.py:54
  177.0 2.4 %collective-permute-start.21 = (bf16[1664,256]{1,0:T(8,128)(2,1)S(1)}, bf16[1664,256]{1,0:T(8,128)(2,1)S(1)}, u32[]{:S(2)}, u32[]{:S(2)}) collective-permute-start(bf16[1664,256]{1,0:T(8,128)(2,1)S(1)} %maximum_select_fusion.1), channel_id=1, source_target_pairs={{0,1},{1,0},{2,3},{3,2},{4,5},{5,4},{6,7},{7,6},{8,9},{9,8},{10,11... | collective-permute-start | bytes 2555912 | tf_op jit(solution)/shard_map/ppermute | solution.py:54

commit v3 on v2

--- a/solution.py
+++ b/solution.py
@@ -233,21 +233,16 @@
     )
     taps_s = spatial_terms.shape[0]
     taps_t = temporal_terms.shape[0]
-    flat = jnp.concatenate(
-        [
-            spatial_terms.reshape(-1, chans),
-            temporal_terms.reshape(-1, chans),
-            cond_terms.reshape(-1, chans),
-        ],
-        axis=0,
+    scale = (clips * frames * rows * cols * lax.axis_size("space") * lax.axis_size("tm")) ** (-0.5)
+    grad_spatial = all_sum_rounded(spatial_terms.reshape(-1, chans), scale)
+    grad_spatial = grad_spatial.reshape(taps_s, chans, chans)
+    late = jnp.concatenate(
+        [temporal_terms.reshape(-1, chans), cond_terms.reshape(-1, chans)], axis=0
     )
-    scale = (clips * frames * rows * cols * lax.axis_size("space") * lax.axis_size("tm")) ** (-0.5)
-    summed = all_sum_rounded(flat, scale)
-    n_s = taps_s * chans
+    late = all_sum_rounded(late, scale)
     n_t = taps_t * chans
-    grad_spatial = summed[:n_s].reshape(taps_s, chans, chans)
-    grad_temporal = summed[n_s : n_s + n_t].reshape(taps_t, chans, chans)
-    grad_cond = summed[n_s + n_t :]
+    grad_temporal = late[:n_t].reshape(taps_t, chans, chans)
+    grad_cond = late[n_t:]
     return (output, grad_latents, grad_spatial, grad_temporal, grad_cond)
 
 

time: 184 us -> 185 us (level)
  starting transfers between devices: 54.9 us -> 70.5 us
  waiting for transfers between devices: 82 us -> 68.4 us
    ppermute x3 -> x6, waiting for transfers between devices: 9.77 us -> 31.1 us  [direct_scatter(): total = total + lax.ppermute(send, axis, pairs)]
    ppermute x3 -> x6, waiting for transfers between devices: 26 us -> 4.69 us  [direct_gather(): got = lax.ppermute(piece, axis, pairs)]
    ppermute x3 -> x6, starting transfers between devices: 14.8 us -> 26.6 us  [direct_scatter(): total = total + lax.ppermute(send, axis, pairs)]
    ppermute x3, waiting for transfers between devices: 13.6 us -> 2.18 us  [tree_broadcast(): got = lax.ppermute(value, axis, pairs)]
    ppermute x2 -> x4, waiting for transfers between devices: 17.1 us -> 6.4 us  [xor_halving(): flat = keep + lax.ppermute(send, axis, pairs)]
    ppermute x3, waiting for transfers between devices: 0.01 us -> 5.18 us  [tree_reduce(): value = value + lax.ppermute(value, axis, pairs)]
    ppermute x2 -> x4, waiting for transfers between devices: 10.2 us -> 12.8 us  [xor_doubling(): got = lax.ppermute(piece, axis, [(i, i ^ step) for i in range(count)])]
    ppermute x3 -> x6, starting transfers between devices: 7.62 us -> 10 us  [direct_gather(): got = lax.ppermute(piece, axis, pairs)]
  transfers between devices with their start and end apart: 22 -> 32, of which waited for: 10 -> 14; matrix products, arithmetic and copies ran while one was open for 21% -> 21% of each run, Pallas kernels for 0% -> 0%
where the time goes in v3:
time: 185 us
  starting transfers between devices  70.5 us (38%)
  waiting for transfers between devices  68.4 us (37%)
  matrix products  30.6 us (17%)
  other arithmetic  9.77 us (5%)
  local copies, waits for them, and re-layouts  3.69 us (2%)
    ppermute x6, waiting for transfers between devices, direct_scatter(): total = total + lax.ppermute(send, axis, pairs)  31.1 us
    ppermute x6, starting transfers between devices, direct_scatter(): total = total + lax.ppermute(send, axis, pairs)  26.6 us
    ppermute x6, starting transfers between devices, shifted(): return lax.ppermute(value, axis, pairs)  15.5 us
    dot_general x18, matrix products, spatial_sum(): total = total + jnp.dot(piece, kernel, preferred_element_type=jnp.float32)  14 us
    ppermute x4, waiting for transfers between devices, xor_doubling(): got = lax.ppermute(piece, axis, [(i, i ^ step) for i in range(count)])  12.8 us
    ppermute x6, starting transfers between devices, direct_gather(): got = lax.ppermute(piece, axis, pairs)  10 us
    ppermute x3, starting transfers between devices, tree_broadcast(): got = lax.ppermute(value, axis, pairs)  9.05 us
    dot_general x9, matrix products, on_device(): lax.dot_general(piece, dpre, dims, preferred_element_type=jnp.float32)  6.48 us
  transfers between devices with their start and end apart: 32, of which 14 were waited for; matrix products, arithmetic and copies ran while one was open for 21% of the time, Pallas kernels for 0%

profile of v3, /device:TPU:0, one launch (start us, length us, event | category | flops | bytes accessed | tf_op | source)
XLA Modules:
  0.0 184.6 jit_solution(12735038026627513264)
XLA Ops:
  3.8 3.2 %collective-permute-start = (bf16[2,2,1,256,256]{4,3,2,1,0:T(8,128)(2,1)}, bf16[2,2,1,256,256]{4,3,2,1,0:T(8,128)(2,1)}, u32[]{:S(2)}, u32[]{:S(2)}) collective-permute-start(bf16[2,2,1,256,256]{4,3,2,1,0:T(8,128)(2,1)} %get-tuple-element.15), channel_id=1, source_target_pairs={{0,1},{2,3},{4,5},{6,7},{8,9},{10,11},{12,13},{14,15},{16,17},{18,... | collective-permute-start | bytes 1572872 | tf_op jit(solution)/shard_map/ppermute | solution.py:10
  9.1 6.1 %collective-permute-start.3 = (bf16[2,2,256,256]{3,2,1,0:T(8,128)(2,1)}, bf16[2,2,256,256]{3,2,1,0:T(8,128)(2,1)}, u32[]{:S(2)}, u32[]{:S(2)}) collective-permute-start(bf16[2,2,256,256]{3,2,1,0:T(8,128)(2,1)} %slice_bitcast_fusion), channel_id=1, source_target_pairs={{0,8},{1,9},{16,24},{17,25}} | collective-permute-start | bytes 1572872 | tf_op jit(solution)/shard_map/ppermute | solution.py:21
  20.5 2.1 %select_maximum_fusion.2 = bf16[2,2,4,258,256]{4,3,2,1,0:T(8,128)(2,1)S(1)} fusion(bf16[2,2,1,256,256]{4,3,2,1,0:T(8,128)(2,1)} %collective-permute-done.1, bf16[2,2,2,256,256]{4,3,2,1,0:T(8,128)(2,1)S(1)} %broadcast_multiply_fusion.1, bf16[2,2,1,256,256]{4,3,2,1,0:T(8,128)(2,1)} %collective-permute-done), kind=kLoop, calls=%fused_computation.7 | loop fusion | flops 12681216 | bytes 4210688 | tf_op jit(solution)/shard_map/concatenate | solution.py:182
  24.9 1.5 fusion.43
  29.1 5.2 %collective-permute-start.2 = (bf16[2,2,2,256,256]{4,3,2,1,0:T(8,128)(2,1)S(1)}, bf16[2,2,2,256,256]{4,3,2,1,0:T(8,128)(2,1)S(1)}, u32[]{:S(2)}, u32[]{:S(2)}) collective-permute-start(bf16[2,2,2,256,256]{4,3,2,1,0:T(8,128)(2,1)S(1)} %get-tuple-element.23), channel_id=1, source_target_pairs={{0,2},{2,4},{4,6},{6,8},{8,10},{10,12},{12,14},{1,3},{3,5},{5,7},{... | collective-permute-start | bytes 3145736 | tf_op jit(solution)/shard_map/ppermute | solution.py:10
  34.5 1.6 collective-permute-start.4
  37.0 6.1 %collective-permute-done.6 = bf16[2,2,2,256,256]{4,3,2,1,0:T(8,128)(2,1)} collective-permute-done((bf16[2,2,2,256,256]{4,3,2,1,0:T(8,128)(2,1)S(1)}, bf16[2,2,2,256,256]{4,3,2,1,0:T(8,128)(2,1)}, u32[]{:S(2)}, u32[]{:S(2)}) %collective-permute-start.6) | collective-permute-done | bytes 1048608 | tf_op jit(solution)/shard_map/ppermute | solution.py:10
  43.1 1.5 fusion.5
  44.6 2.3 %multiply_convert_fusion = bf16[2,2,2,256,256]{4,3,2,1,0:T(8,128)(2,1)S(1)} fusion(f32[2,2,2,256,256]{4,3,2,1,0:T(8,128)S(1)} %get-tuple-element.24, f32[2,2,2,256,256]{4,3,2,1,0:T(8,128)S(1)} %fusion.102, f32[2,2,2,256,256]{4,3,2,1,0:T(8,128)S(1)} %fusion.5, bf16[2,2,2,256,256]{4,3,2,1,0:T(8,128)(2,1)} %collective-permute-done.6, ...), kind=kOutput, calls=%fused_computation.18 | convolution fusion | flops 274202624 | bytes 8519680 | tf_op jit(solution)/shard_map/dot_general | solution.py:158
  49.6 1.5 fusion.21
  54.4 3.3 %collective-permute-start.7 = (bf16[2,2,1,256,256]{4,3,2,1,0:T(8,128)(2,1)S(1)}, bf16[2,2,1,256,256]{4,3,2,1,0:T(8,128)(2,1)S(1)}, u32[]{:S(2)}, u32[]{:S(2)}) collective-permute-start(bf16[2,2,1,256,256]{4,3,2,1,0:T(8,128)(2,1)S(1)} %get-tuple-element.14), channel_id=1, source_target_pairs={{0,1},{2,3},{4,5},{6,7},{8,9},{10,11},{12,13},{14,15},{16,17},{18,... | collective-permute-start | bytes 1572872 | tf_op jit(solution)/shard_map/ppermute | solution.py:10
  58.2 1.5 fusion.20
  60.4 5.2 %collective-permute-done.9 = f32[2,2,256,256]{3,2,1,0:T(8,128)} collective-permute-done((f32[2,2,256,256]{3,2,1,0:T(8,128)S(1)}, f32[2,2,256,256]{3,2,1,0:T(8,128)}, u32[]{:S(2)}, u32[]{:S(2)}) %collective-permute-start.9) | collective-permute-done | bytes 1048608 | tf_op jit(solution)/shard_map/ppermute | solution.py:32
  75.3 1.8 multiply_convert_fusion.1
  78.3 2.5 %collective-permute-start.23 = (f32[256,256]{1,0:T(8,128)S(1)}, f32[256,256]{1,0:T(8,128)S(1)}, u32[]{:S(2)}, u32[]{:S(2)}) collective-permute-start(f32[256,256]{1,0:T(8,128)S(1)} %constant_dynamic-slice_fusion.3), channel_id=1, source_target_pairs={{0,2},{2,0},{4,6},{6,4},{8,10},{10,8},{12,14},{14,12},{1,3},{3,1},... | collective-permute-start | bytes 786440 | tf_op jit(solution)/shard_map/ppermute | solution.py:46
  81.2 6.4 %collective-permute-done.23 = f32[256,256]{1,0:T(8,128)S(1)} collective-permute-done((f32[256,256]{1,0:T(8,128)S(1)}, f32[256,256]{1,0:T(8,128)S(1)}, u32[]{:S(2)}, u32[]{:S(2)}) %collective-permute-start.23) | collective-permute-done | bytes 262176 | tf_op jit(solution)/shard_map/ppermute | solution.py:46
  87.7 18.2 %collective-permute-start.24 = (f32[64,256]{1,0:T(8,128)S(1)}, f32[64,256]{1,0:T(8,128)S(1)}, u32[]{:S(2)}, u32[]{:S(2)}) collective-permute-start(f32[64,256]{1,0:T(8,128)S(1)} %get-tuple-element.20), channel_id=1, source_target_pairs={{0,4},{2,6},{4,8},{6,10},{8,12},{10,14},{12,0},{14,2},{1,5},{3,7},... | collective-permute-start | bytes 196616 | tf_op jit(solution)/shard_map/ppermute | solution.py:72
  105.9 3.5 %collective-permute-start.25 = (f32[64,256]{1,0:T(8,128)S(1)}, f32[64,256]{1,0:T(8,128)S(1)}, u32[]{:S(2)}, u32[]{:S(2)}) collective-permute-start(f32[64,256]{1,0:T(8,128)S(1)} %get-tuple-element.22), channel_id=1, source_target_pairs={{0,8},{2,10},{4,12},{6,14},{8,0},{10,2},{12,4},{14,6},{1,9},{3,11}... | collective-permute-start | bytes 196616 | tf_op jit(solution)/shard_map/ppermute | solution.py:72
  109.8 7.9 %collective-permute-done.24 = f32[64,256]{1,0:T(8,128)S(1)} collective-permute-done((f32[64,256]{1,0:T(8,128)S(1)}, f32[64,256]{1,0:T(8,128)S(1)}, u32[]{:S(2)}, u32[]{:S(2)}) %collective-permute-start.24) | collective-permute-done | bytes 65568 | tf_op jit(solution)/shard_map/ppermute | solution.py:72
  117.7 1.8 collective-permute-start.27
  120.4 2.9 %collective-permute-start.29 = (bf16[64,256]{1,0:T(8,128)(2,1)S(1)}, bf16[64,256]{1,0:T(8,128)(2,1)S(1)}, u32[]{:S(2)}, u32[]{:S(2)}) collective-permute-start(bf16[64,256]{1,0:T(8,128)(2,1)S(1)} %get-tuple-element.6), channel_id=1, source_target_pairs={{0,12},{2,14},{4,0},{6,2},{8,4},{10,6},{12,8},{14,10},{1,13},{3,15... | collective-permute-start | bytes 98312 | tf_op jit(solution)/shard_map/ppermute | solution.py:85
  124.9 1.9 %collective-permute-start.30 = (bf16[256,256]{1,0:T(8,128)(2,1)S(1)}, bf16[256,256]{1,0:T(8,128)(2,1)S(1)}, u32[]{:S(2)}, u32[]{:S(2)}) collective-permute-start(bf16[256,256]{1,0:T(8,128)(2,1)S(1)} %bitcast.270), channel_id=1, source_target_pairs={{0,2},{2,0},{4,6},{6,4},{8,10},{10,8},{12,14},{14,12},{1,3},{3,1},... | collective-permute-start | bytes 393224 | tf_op jit(solution)/shard_map/ppermute | solution.py:54
  128.8 6.7 %collective-permute-done.30 = bf16[256,256]{1,0:T(8,128)(2,1)S(1)} collective-permute-done((bf16[256,256]{1,0:T(8,128)(2,1)S(1)}, bf16[256,256]{1,0:T(8,128)(2,1)S(1)}, u32[]{:S(2)}, u32[]{:S(2)}) %collective-permute-start.30) | collective-permute-done | bytes 131104 | tf_op jit(solution)/shard_map/ppermute | solution.py:54
  135.9 2.0 %collective-permute-start.14 = (f32[144,256]{1,0:T(8,128)S(1)}, f32[144,256]{1,0:T(8,128)S(1)}, u32[]{:S(2)}, u32[]{:S(2)}) collective-permute-start(f32[144,256]{1,0:T(8,128)S(1)} %get-tuple-element.17), channel_id=1, source_target_pairs={{0,4},{2,6},{4,8},{6,10},{8,12},{10,14},{12,0},{14,2},{1,5},{3,7},... | collective-permute-start | bytes 442376 | tf_op jit(solution)/shard_map/ppermute | solution.py:72
  138.3 2.2 %collective-permute-start.16 = (f32[144,256]{1,0:T(8,128)S(1)}, f32[144,256]{1,0:T(8,128)S(1)}, u32[]{:S(2)}, u32[]{:S(2)}) collective-permute-start(f32[144,256]{1,0:T(8,128)S(1)} %get-tuple-element.18), channel_id=1, source_target_pairs={{0,12},{2,14},{4,0},{6,2},{8,4},{10,6},{12,8},{14,10},{1,13},{3,15... | collective-permute-start | bytes 442376 | tf_op jit(solution)/shard_map/ppermute | solution.py:72
  141.0 3.5 %collective-permute-done.14 = f32[144,256]{1,0:T(8,128)S(1)} collective-permute-done((f32[144,256]{1,0:T(8,128)S(1)}, f32[144,256]{1,0:T(8,128)S(1)}, u32[]{:S(2)}, u32[]{:S(2)}) %collective-permute-start.14) | collective-permute-done | bytes 147488 | tf_op jit(solution)/shard_map/ppermute | solution.py:72
  144.5 19.7 %collective-permute-done.15 = f32[144,256]{1,0:T(8,128)S(1)} collective-permute-done((f32[144,256]{1,0:T(8,128)S(1)}, f32[144,256]{1,0:T(8,128)S(1)}, u32[]{:S(2)}, u32[]{:S(2)}) %collective-permute-start.15) | collective-permute-done | bytes 147488 | tf_op jit(solution)/shard_map/ppermute | solution.py:72
  164.3 2.2 %collective-permute-start.17 = (bf16[144,256]{1,0:T(8,128)(2,1)S(1)}, bf16[144,256]{1,0:T(8,128)(2,1)S(1)}, u32[]{:S(2)}, u32[]{:S(2)}) collective-permute-start(bf16[144,256]{1,0:T(8,128)(2,1)S(1)} %get-tuple-element.8), channel_id=1, source_target_pairs={{0,4},{2,6},{4,8},{6,10},{8,12},{10,14},{12,0},{14,2},{1,5},{3,7},... | collective-permute-start | bytes 221192 | tf_op jit(solution)/shard_map/ppermute | solution.py:85
  168.2 2.4 %collective-permute-start.19 = (bf16[144,256]{1,0:T(8,128)(2,1)S(1)}, bf16[144,256]{1,0:T(8,128)(2,1)S(1)}, u32[]{:S(2)}, u32[]{:S(2)}) collective-permute-start(bf16[144,256]{1,0:T(8,128)(2,1)S(1)} %get-tuple-element.8), channel_id=1, source_target_pairs={{0,12},{2,14},{4,0},{6,2},{8,4},{10,6},{12,8},{14,10},{1,13},{3,15... | collective-permute-start | bytes 221192 | tf_op jit(solution)/shard_map/ppermute | solution.py:85
  170.6 3.1 %collective-permute-done.18 = bf16[144,256]{1,0:T(8,128)(2,1)S(1)} collective-permute-done((bf16[144,256]{1,0:T(8,128)(2,1)S(1)}, bf16[144,256]{1,0:T(8,128)(2,1)S(1)}, u32[]{:S(2)}, u32[]{:S(2)}) %collective-permute-start.18) | collective-permute-done | bytes 73760 | tf_op jit(solution)/shard_map/ppermute | solution.py:85
  174.5 6.0 %collective-permute-done.20 = bf16[576,256]{1,0:T(8,128)(2,1)S(1)} collective-permute-done((bf16[576,256]{1,0:T(8,128)(2,1)S(1)}, bf16[576,256]{1,0:T(8,128)(2,1)S(1)}, u32[]{:S(2)}, u32[]{:S(2)}) %collective-permute-start.20) | collective-permute-done | bytes 294944 | tf_op jit(solution)/shard_map/ppermute | solution.py:54
  180.9 2.4 %fusion.4 = bf16[2,2,2,256,256]{4,3,2,1,0:T(8,128)(2,1)} fusion(bf16[2,2,2,256,256]{4,3,2,1,0:T(8,128)(2,1)S(1)} %get-tuple-element.10, f32[2,2,2,256,256]{4,3,2,1,0:T(8,128)S(1)} %fusion.13, f32[2,2,2,256,256]{4,3,2,1,0:T(8,128)S(1)} %fusion.31, f32[2,2,2,256,256]{4,3,2,1,0:T(8,128)S(1)} %fusion.33, f32[2,2,2,256,256]{4,3,2,1,0:T(8,128)S(1)} %fusion.83, ...), kind=kOutput, calls=%fused_computation.12 | convolution fusion | flops 275775488 | bytes 21104128 | tf_op jit(solution)/shard_map/dot_general | solution.py:140
  (120 shorter events, 44.8 us)
Async XLA Ops:
  3.8 16.7 %collective-permute-start = (bf16[2,2,1,256,256]{4,3,2,1,0:T(8,128)(2,1)}, bf16[2,2,1,256,256]{4,3,2,1,0:T(8,128)(2,1)}, u32[]{:S(2)}, u32[]{:S(2)}) collective-permute-start(bf16[2,2,1,256,256]{4,3,2,1,0:T(8,128)(2,1)} %get-tuple-element.15), channel_id=1, source_target_pairs={{0,1},{2,3},{4,5},{6,7},{8,9},{10,11},{12,13},{14,15},{16,17},{18,... | collective-permute-start | bytes 1572872 | tf_op jit(solution)/shard_map/ppermute | solution.py:10
  7.0 13.5 %collective-permute-start.1 = (bf16[2,2,1,256,256]{4,3,2,1,0:T(8,128)(2,1)}, bf16[2,2,1,256,256]{4,3,2,1,0:T(8,128)(2,1)}, u32[]{:S(2)}, u32[]{:S(2)}) collective-permute-start(bf16[2,2,1,256,256]{4,3,2,1,0:T(8,128)(2,1)} %get-tuple-element.16), channel_id=1, source_target_pairs={{1,0},{3,2},{5,4},{7,6},{9,8},{11,10},{13,12},{15,14},{17,16},{19,... | collective-permute-start | bytes 1572872 | tf_op jit(solution)/shard_map/ppermute | solution.py:10
  9.1 25.3 %collective-permute-start.3 = (bf16[2,2,256,256]{3,2,1,0:T(8,128)(2,1)}, bf16[2,2,256,256]{3,2,1,0:T(8,128)(2,1)}, u32[]{:S(2)}, u32[]{:S(2)}) collective-permute-start(bf16[2,2,256,256]{3,2,1,0:T(8,128)(2,1)} %slice_bitcast_fusion), channel_id=1, source_target_pairs={{0,8},{1,9},{16,24},{17,25}} | collective-permute-start | bytes 1572872 | tf_op jit(solution)/shard_map/ppermute | solution.py:21
  15.7 27.4 %collective-permute-start.6 = (bf16[2,2,2,256,256]{4,3,2,1,0:T(8,128)(2,1)S(1)}, bf16[2,2,2,256,256]{4,3,2,1,0:T(8,128)(2,1)}, u32[]{:S(2)}, u32[]{:S(2)}) collective-permute-start(bf16[2,2,2,256,256]{4,3,2,1,0:T(8,128)(2,1)S(1)} %get-tuple-element.10), channel_id=1, source_target_pairs={{2,0},{4,2},{6,4},{8,6},{10,8},{12,10},{14,12},{3,1},{5,3},{7,5},{... | collective-permute-start | bytes 3145736 | tf_op jit(solution)/shard_map/ppermute | solution.py:10
  17.0 48.6 %collective-permute-start.9 = (f32[2,2,256,256]{3,2,1,0:T(8,128)S(1)}, f32[2,2,256,256]{3,2,1,0:T(8,128)}, u32[]{:S(2)}, u32[]{:S(2)}) collective-permute-start(f32[2,2,256,256]{3,2,1,0:T(8,128)S(1)} %get-tuple-element.9), channel_id=1, source_target_pairs={{2,0},{6,4},{10,8},{14,12},{3,1},{7,5},{11,9},{15,13},{18,16},{22,... | collective-permute-start | bytes 3145736 | tf_op jit(solution)/shard_map/ppermute | solution.py:32
  29.1 41.3 %collective-permute-start.2 = (bf16[2,2,2,256,256]{4,3,2,1,0:T(8,128)(2,1)S(1)}, bf16[2,2,2,256,256]{4,3,2,1,0:T(8,128)(2,1)S(1)}, u32[]{:S(2)}, u32[]{:S(2)}) collective-permute-start(bf16[2,2,2,256,256]{4,3,2,1,0:T(8,128)(2,1)S(1)} %get-tuple-element.23), channel_id=1, source_target_pairs={{0,2},{2,4},{4,6},{6,8},{8,10},{10,12},{12,14},{1,3},{3,5},{5,7},{... | collective-permute-start | bytes 3145736 | tf_op jit(solution)/shard_map/ppermute | solution.py:10
  34.5 13.8 %collective-permute-start.4 = (bf16[2,2,256,256]{3,2,1,0:T(8,128)(2,1)S(1)}, bf16[2,2,256,256]{3,2,1,0:T(8,128)(2,1)S(1)}, u32[]{:S(2)}, u32[]{:S(2)}) collective-permute-start(bf16[2,2,256,256]{3,2,1,0:T(8,128)(2,1)S(1)} %broadcast_select_fusion), channel_id=1, source_target_pairs={{0,4},{8,12},{1,5},{9,13},{16,20},{24,28},{17,21},{25,29}} | collective-permute-start | bytes 1572872 | tf_op jit(solution)/shard_map/ppermute | solution.py:21
  48.3 25.0 %collective-permute-start.5 = (bf16[2,2,256,256]{3,2,1,0:T(8,128)(2,1)S(1)}, bf16[2,2,256,256]{3,2,1,0:T(8,128)(2,1)S(1)}, u32[]{:S(2)}, u32[]{:S(2)}) collective-permute-start(bf16[2,2,256,256]{3,2,1,0:T(8,128)(2,1)S(1)} %broadcast_select_fusion.1), channel_id=1, source_target_pairs={{0,2},{4,6},{8,10},{12,14},{1,3},{5,7},{9,11},{13,15},{16,18},{20,... | collective-permute-start | bytes 1572872 | tf_op jit(solution)/shard_map/ppermute | solution.py:21
  53.1 14.7 %collective-permute-start.8 = (bf16[2,2,1,256,256]{4,3,2,1,0:T(8,128)(2,1)S(1)}, bf16[2,2,1,256,256]{4,3,2,1,0:T(8,128)(2,1)S(1)}, u32[]{:S(2)}, u32[]{:S(2)}) collective-permute-start(bf16[2,2,1,256,256]{4,3,2,1,0:T(8,128)(2,1)S(1)} %get-tuple-element.13), channel_id=1, source_target_pairs={{1,0},{3,2},{5,4},{7,6},{9,8},{11,10},{13,12},{15,14},{17,16},{19,... | collective-permute-start | bytes 1572872 | tf_op jit(solution)/shard_map/ppermute | solution.py:10
  54.4 14.7 %collective-permute-start.7 = (bf16[2,2,1,256,256]{4,3,2,1,0:T(8,128)(2,1)S(1)}, bf16[2,2,1,256,256]{4,3,2,1,0:T(8,128)(2,1)S(1)}, u32[]{:S(2)}, u32[]{:S(2)}) collective-permute-start(bf16[2,2,1,256,256]{4,3,2,1,0:T(8,128)(2,1)S(1)} %get-tuple-element.14), channel_id=1, source_target_pairs={{0,1},{2,3},{4,5},{6,7},{8,9},{10,11},{12,13},{14,15},{16,17},{18,... | collective-permute-start | bytes 1572872 | tf_op jit(solution)/shard_map/ppermute | solution.py:10
  65.5 44.1 %collective-permute-start.12 = (f32[1152,256]{1,0:T(8,128)S(1)}, f32[1152,256]{1,0:T(8,128)S(1)}, u32[]{:S(2)}, u32[]{:S(2)}) collective-permute-start(f32[1152,256]{1,0:T(8,128)S(1)} %constant_dynamic-slice_fusion.8), channel_id=1, source_target_pairs={{0,1},{1,0},{2,3},{3,2},{4,5},{5,4},{6,7},{7,6},{8,9},{9,8},{10,11... | collective-permute-start | bytes 3538952 | tf_op jit(solution)/shard_map/ppermute | solution.py:46
  67.8 59.5 %collective-permute-start.10 = (f32[2,2,256,256]{3,2,1,0:T(8,128)S(1)}, f32[2,2,256,256]{3,2,1,0:T(8,128)S(1)}, u32[]{:S(2)}, u32[]{:S(2)}) collective-permute-start(f32[2,2,256,256]{3,2,1,0:T(8,128)S(1)} %add.301), channel_id=1, source_target_pairs={{4,0},{12,8},{5,1},{13,9},{20,16},{28,24},{21,17},{29,25}} | collective-permute-start | bytes 3145736 | tf_op jit(solution)/shard_map/ppermute | solution.py:32
  74.3 3.7 %collective-permute-start.22 = (f32[512,256]{1,0:T(8,128)S(1)}, f32[512,256]{1,0:T(8,128)S(1)}, u32[]{:S(2)}, u32[]{:S(2)}) collective-permute-start(f32[512,256]{1,0:T(8,128)S(1)} %fusion.65), channel_id=1, source_target_pairs={{0,1},{1,0},{2,3},{3,2},{4,5},{5,4},{6,7},{7,6},{8,9},{9,8},{10,11... | collective-permute-start | bytes 1572872 | tf_op jit(solution)/shard_map/ppermute | solution.py:46
  78.3 9.3 %collective-permute-start.23 = (f32[256,256]{1,0:T(8,128)S(1)}, f32[256,256]{1,0:T(8,128)S(1)}, u32[]{:S(2)}, u32[]{:S(2)}) collective-permute-start(f32[256,256]{1,0:T(8,128)S(1)} %constant_dynamic-slice_fusion.3), channel_id=1, source_target_pairs={{0,2},{2,0},{4,6},{6,4},{8,10},{10,8},{12,14},{14,12},{1,3},{3,1},... | collective-permute-start | bytes 786440 | tf_op jit(solution)/shard_map/ppermute | solution.py:46
  87.7 30.0 %collective-permute-start.24 = (f32[64,256]{1,0:T(8,128)S(1)}, f32[64,256]{1,0:T(8,128)S(1)}, u32[]{:S(2)}, u32[]{:S(2)}) collective-permute-start(f32[64,256]{1,0:T(8,128)S(1)} %get-tuple-element.20), channel_id=1, source_target_pairs={{0,4},{2,6},{4,8},{6,10},{8,12},{10,14},{12,0},{14,2},{1,5},{3,7},... | collective-permute-start | bytes 196616 | tf_op jit(solution)/shard_map/ppermute | solution.py:72
  105.9 11.8 %collective-permute-start.25 = (f32[64,256]{1,0:T(8,128)S(1)}, f32[64,256]{1,0:T(8,128)S(1)}, u32[]{:S(2)}, u32[]{:S(2)}) collective-permute-start(f32[64,256]{1,0:T(8,128)S(1)} %get-tuple-element.22), channel_id=1, source_target_pairs={{0,8},{2,10},{4,12},{6,14},{8,0},{10,2},{12,4},{14,6},{1,9},{3,11}... | collective-permute-start | bytes 196616 | tf_op jit(solution)/shard_map/ppermute | solution.py:72
  109.4 8.3 %collective-permute-start.26 = (f32[64,256]{1,0:T(8,128)S(1)}, f32[64,256]{1,0:T(8,128)S(1)}, u32[]{:S(2)}, u32[]{:S(2)}) collective-permute-start(f32[64,256]{1,0:T(8,128)S(1)} %get-tuple-element.21), channel_id=1, source_target_pairs={{0,12},{2,14},{4,0},{6,2},{8,4},{10,6},{12,8},{14,10},{1,13},{3,15... | collective-permute-start | bytes 196616 | tf_op jit(solution)/shard_map/ppermute | solution.py:72
  117.7 5.8 %collective-permute-start.27 = (bf16[64,256]{1,0:T(8,128)(2,1)S(1)}, bf16[64,256]{1,0:T(8,128)(2,1)S(1)}, u32[]{:S(2)}, u32[]{:S(2)}) collective-permute-start(bf16[64,256]{1,0:T(8,128)(2,1)S(1)} %get-tuple-element.6), channel_id=1, source_target_pairs={{0,4},{2,6},{4,8},{6,10},{8,12},{10,14},{12,0},{14,2},{1,5},{3,7},... | collective-permute-start | bytes 98312 | tf_op jit(solution)/shard_map/ppermute | solution.py:85
  119.5 16.2 %collective-permute-start.13 = (f32[576,256]{1,0:T(8,128)S(1)}, f32[576,256]{1,0:T(8,128)S(1)}, u32[]{:S(2)}, u32[]{:S(2)}) collective-permute-start(f32[576,256]{1,0:T(8,128)S(1)} %constant_dynamic-slice_fusion.7), channel_id=1, source_target_pairs={{0,2},{2,0},{4,6},{6,4},{8,10},{10,8},{12,14},{14,12},{1,3},{3,1},... | collective-permute-start | bytes 1769480 | tf_op jit(solution)/shard_map/ppermute | solution.py:46
  119.6 5.0 %collective-permute-start.28 = (bf16[64,256]{1,0:T(8,128)(2,1)S(1)}, bf16[64,256]{1,0:T(8,128)(2,1)S(1)}, u32[]{:S(2)}, u32[]{:S(2)}) collective-permute-start(bf16[64,256]{1,0:T(8,128)(2,1)S(1)} %get-tuple-element.6), channel_id=1, source_target_pairs={{0,8},{2,10},{4,12},{6,14},{8,0},{10,2},{12,4},{14,6},{1,9},{3,11}... | collective-permute-start | bytes 98312 | tf_op jit(solution)/shard_map/ppermute | solution.py:85
  120.4 4.5 %collective-permute-start.29 = (bf16[64,256]{1,0:T(8,128)(2,1)S(1)}, bf16[64,256]{1,0:T(8,128)(2,1)S(1)}, u32[]{:S(2)}, u32[]{:S(2)}) collective-permute-start(bf16[64,256]{1,0:T(8,128)(2,1)S(1)} %get-tuple-element.6), channel_id=1, source_target_pairs={{0,12},{2,14},{4,0},{6,2},{8,4},{10,6},{12,8},{14,10},{1,13},{3,15... | collective-permute-start | bytes 98312 | tf_op jit(solution)/shard_map/ppermute | solution.py:85
  124.9 10.6 %collective-permute-start.30 = (bf16[256,256]{1,0:T(8,128)(2,1)S(1)}, bf16[256,256]{1,0:T(8,128)(2,1)S(1)}, u32[]{:S(2)}, u32[]{:S(2)}) collective-permute-start(bf16[256,256]{1,0:T(8,128)(2,1)S(1)} %bitcast.270), channel_id=1, source_target_pairs={{0,2},{2,0},{4,6},{6,4},{8,10},{10,8},{12,14},{14,12},{1,3},{3,1},... | collective-permute-start | bytes 393224 | tf_op jit(solution)/shard_map/ppermute | solution.py:54
  127.5 46.3 %collective-permute-start.11 = (f32[2,2,256,256]{3,2,1,0:T(8,128)S(1)}, f32[2,2,256,256]{3,2,1,0:T(8,128)S(1)}, u32[]{:S(2)}, u32[]{:S(2)}) collective-permute-start(f32[2,2,256,256]{3,2,1,0:T(8,128)S(1)} %add.302), channel_id=1, source_target_pairs={{8,0},{9,1},{24,16},{25,17}} | collective-permute-start | bytes 3145736 | tf_op jit(solution)/shard_map/ppermute | solution.py:32
  135.6 30.9 %collective-permute-start.31 = (bf16[512,256]{1,0:T(8,128)(2,1)S(1)}, bf16[512,256]{1,0:T(8,128)(2,1)S(1)}, u32[]{:S(2)}, u32[]{:S(2)}) collective-permute-start(bf16[512,256]{1,0:T(8,128)(2,1)S(1)} %maximum_select_fusion.3), channel_id=1, source_target_pairs={{0,1},{1,0},{2,3},{3,2},{4,5},{5,4},{6,7},{7,6},{8,9},{9,8},{10,11... | collective-permute-start | bytes 786440 | tf_op jit(solution)/shard_map/ppermute | solution.py:54
  135.9 8.6 %collective-permute-start.14 = (f32[144,256]{1,0:T(8,128)S(1)}, f32[144,256]{1,0:T(8,128)S(1)}, u32[]{:S(2)}, u32[]{:S(2)}) collective-permute-start(f32[144,256]{1,0:T(8,128)S(1)} %get-tuple-element.17), channel_id=1, source_target_pairs={{0,4},{2,6},{4,8},{6,10},{8,12},{10,14},{12,0},{14,2},{1,5},{3,7},... | collective-permute-start | bytes 442376 | tf_op jit(solution)/shard_map/ppermute | solution.py:72
  137.9 26.4 %collective-permute-start.15 = (f32[144,256]{1,0:T(8,128)S(1)}, f32[144,256]{1,0:T(8,128)S(1)}, u32[]{:S(2)}, u32[]{:S(2)}) collective-permute-start(f32[144,256]{1,0:T(8,128)S(1)} %get-tuple-element.19), channel_id=1, source_target_pairs={{0,8},{2,10},{4,12},{6,14},{8,0},{10,2},{12,4},{14,6},{1,9},{3,11}... | collective-permute-start | bytes 442376 | tf_op jit(solution)/shard_map/ppermute | solution.py:72
  138.3 25.9 %collective-permute-start.16 = (f32[144,256]{1,0:T(8,128)S(1)}, f32[144,256]{1,0:T(8,128)S(1)}, u32[]{:S(2)}, u32[]{:S(2)}) collective-permute-start(f32[144,256]{1,0:T(8,128)S(1)} %get-tuple-element.18), channel_id=1, source_target_pairs={{0,12},{2,14},{4,0},{6,2},{8,4},{10,6},{12,8},{14,10},{1,13},{3,15... | collective-permute-start | bytes 442376 | tf_op jit(solution)/shard_map/ppermute | solution.py:72
  164.3 6.3 %collective-permute-start.17 = (bf16[144,256]{1,0:T(8,128)(2,1)S(1)}, bf16[144,256]{1,0:T(8,128)(2,1)S(1)}, u32[]{:S(2)}, u32[]{:S(2)}) collective-permute-start(bf16[144,256]{1,0:T(8,128)(2,1)S(1)} %get-tuple-element.8), channel_id=1, source_target_pairs={{0,4},{2,6},{4,8},{6,10},{8,12},{10,14},{12,0},{14,2},{1,5},{3,7},... | collective-permute-start | bytes 221192 | tf_op jit(solution)/shard_map/ppermute | solution.py:85
  168.2 5.5 %collective-permute-start.18 = (bf16[144,256]{1,0:T(8,128)(2,1)S(1)}, bf16[144,256]{1,0:T(8,128)(2,1)S(1)}, u32[]{:S(2)}, u32[]{:S(2)}) collective-permute-start(bf16[144,256]{1,0:T(8,128)(2,1)S(1)} %get-tuple-element.8), channel_id=1, source_target_pairs={{0,8},{2,10},{4,12},{6,14},{8,0},{10,2},{12,4},{14,6},{1,9},{3,11}... | collective-permute-start | bytes 221192 | tf_op jit(solution)/shard_map/ppermute | solution.py:85
  168.2 5.5 %collective-permute-start.19 = (bf16[144,256]{1,0:T(8,128)(2,1)S(1)}, bf16[144,256]{1,0:T(8,128)(2,1)S(1)}, u32[]{:S(2)}, u32[]{:S(2)}) collective-permute-start(bf16[144,256]{1,0:T(8,128)(2,1)S(1)} %get-tuple-element.8), channel_id=1, source_target_pairs={{0,12},{2,14},{4,0},{6,2},{8,4},{10,6},{12,8},{14,10},{1,13},{3,15... | collective-permute-start | bytes 221192 | tf_op jit(solution)/shard_map/ppermute | solution.py:85
  173.7 6.8 %collective-permute-start.20 = (bf16[576,256]{1,0:T(8,128)(2,1)S(1)}, bf16[576,256]{1,0:T(8,128)(2,1)S(1)}, u32[]{:S(2)}, u32[]{:S(2)}) collective-permute-start(bf16[576,256]{1,0:T(8,128)(2,1)S(1)} %bitcast.268), channel_id=1, source_target_pairs={{0,2},{2,0},{4,6},{6,4},{8,10},{10,8},{12,14},{14,12},{1,3},{3,1},... | collective-permute-start | bytes 884744 | tf_op jit(solution)/shard_map/ppermute | solution.py:54
  180.8 2.5 %collective-permute-start.21 = (bf16[1152,256]{1,0:T(8,128)(2,1)S(1)}, bf16[1152,256]{1,0:T(8,128)(2,1)S(1)}, u32[]{:S(2)}, u32[]{:S(2)}) collective-permute-start(bf16[1152,256]{1,0:T(8,128)(2,1)S(1)} %maximum_select_fusion.1), channel_id=1, source_target_pairs={{0,1},{1,0},{2,3},{3,2},{4,5},{5,4},{6,7},{7,6},{8,9},{9,8},{10,11... | collective-permute-start | bytes 1769480 | tf_op jit(solution)/shard_map/ppermute | solution.py:54
  (4 other events, 90.3 us)

commit v4 on v2

--- a/solution.py
+++ b/solution.py
@@ -117,10 +117,11 @@
     flat = xor_halving(flat, "space", sp_steps)
     flat = direct_scatter(flat, "space", low, high)
     piece = (flat * scale).astype(jnp.bfloat16)
-    piece = direct_gather(piece, "space", low, high)
-    piece = xor_doubling(piece, "space", sp_steps)
-    piece = xor_doubling(piece, "tm", tm_steps)
-    return piece[:rows]
+    blk = piece.shape[0]
+    whole = lax.all_gather(piece, ("tm", "space"), axis=0, tiled=True)
+    whole = whole.reshape(n_tm, high, low, blk, flat.shape[1])
+    whole = jnp.transpose(whole, (0, 2, 1, 3, 4)).reshape(-1, flat.shape[1])
+    return whole[:rows]
 
 
 def spatial_sum(padded, weights, flip):
@@ -177,6 +178,14 @@
 
 
 def row_halo(x):
+    if lax.axis_size("tm") == 2:
+        me = lax.axis_index("tm")
+        edge = jnp.where(me == 0, x[:, :, -1:], x[:, :, :1])
+        got = lax.ppermute(edge, "tm", [(0, 1), (1, 0)])
+        zero = jnp.zeros_like(got)
+        above = jnp.where(me == 1, got, zero)
+        below = jnp.where(me == 0, got, zero)
+        return jnp.concatenate([above, x, below], axis=2)
     above = shifted(x[:, :, -1:], "tm", 1)
     below = shifted(x[:, :, :1], "tm", -1)
     return jnp.concatenate([above, x, below], axis=2)

time: 184 us -> 212 us (1.15)
  matrix products: 30.7 us -> 47.6 us
  starting transfers between devices: 54.9 us -> 39.9 us
  between operations: 1.47 us -> 14.6 us
  other arithmetic: 8.55 us -> 14.5 us
  local copies, waits for them, and re-layouts: 4.78 us -> 9.74 us
  waiting for transfers between devices: 82 us -> 84.5 us
    ppermute x5 -> x2, waiting for transfers between devices: 36.2 us -> 0.01 us  [row_halo(): got = lax.ppermute(edge, 'tm', [(0, 1), (1, 0)])]
    ppermute x3, waiting for transfers between devices: 0.01 us -> 24.6 us  [tree_reduce(): value = value + lax.ppermute(value, axis, pairs)]
    all_gather x0 -> x1, waiting for transfers between devices: none -> 13.5 us  [all_sum_rounded(): whole = lax.all_gather(piece, ('tm', 'space'), axis=0, tiled=True)]
    dot_general x18, matrix products: 14.2 us -> 25 us  [spatial_sum(): total = total + jnp.dot(piece, kernel, preferred_element_type=jnp.float32)]
    ppermute x6 -> x2, starting transfers between devices: 15.4 us -> 6.82 us  [shifted(): return lax.ppermute(value, axis, pairs)]
    ppermute x5 -> x2, starting transfers between devices: 7.76 us -> 1.01 us  [row_halo(): got = lax.ppermute(edge, 'tm', [(0, 1), (1, 0)])]
    ppermute x6 -> x2, waiting for transfers between devices: 5.23 us -> 10.8 us  [shifted(): return lax.ppermute(value, axis, pairs)]
    dot_general x3, matrix products: 2.6 us -> 8.14 us  [lag_forward(): jnp.dot(padded_act[:, 2 - lag:2 - lag + count], weights[lag], preferred_e...]
  transfers between devices with their start and end apart: 22 -> 16, of which waited for: 10 -> 9; matrix products, arithmetic and copies ran while one was open for 21% -> 29% of each run, Pallas kernels for 0% -> 0%
where the time goes in v4:
time: 212 us; the launch traced here: 211 us
  waiting for transfers between devices  84.5 us (40%)
  matrix products  47.6 us (22%)
  starting transfers between devices  39.9 us (19%)
  between operations  14.6 us (7%)
  other arithmetic  14.5 us (7%)
  local copies, waits for them, and re-layouts  9.74 us (5%)
    dot_general x18, matrix products, spatial_sum(): total = total + jnp.dot(piece, kernel, preferred_element_type=jnp.float32)  25 us
    ppermute x3, waiting for transfers between devices, tree_reduce(): value = value + lax.ppermute(value, axis, pairs)  24.6 us
    all_gather x1, waiting for transfers between devices, all_sum_rounded(): whole = lax.all_gather(piece, ('tm', 'space'), axis=0, tiled=True)  13.5 us
    ppermute x2, waiting for transfers between devices, xor_halving(): flat = keep + lax.ppermute(send, axis, pairs)  13.1 us
    ppermute x3, starting transfers between devices, direct_scatter(): total = total + lax.ppermute(send, axis, pairs)  12.9 us
    ppermute x3, waiting for transfers between devices, tree_broadcast(): got = lax.ppermute(value, axis, pairs)  12.3 us
    ppermute x3, starting transfers between devices, tree_broadcast(): got = lax.ppermute(value, axis, pairs)  12 us
    ppermute x2, waiting for transfers between devices, shifted(): return lax.ppermute(value, axis, pairs)  10.8 us
  transfers between devices with their start and end apart: 16, of which 9 were waited for; matrix products, arithmetic and copies ran while one was open for 29% of the time, Pallas kernels for 0%

profile of v4, /device:TPU:0, one launch (start us, length us, event | category | flops | bytes accessed | tf_op | source)
XLA Modules:
  0.0 210.8 jit_solution(6929756060617687034)
XLA Ops:
  14.3 8.7 %collective-permute-start.2 = (bf16[2,2,256,256]{3,2,1,0:T(8,128)(2,1)}, bf16[2,2,256,256]{3,2,1,0:T(8,128)(2,1)}, u32[]{:S(2)}, u32[]{:S(2)}) collective-permute-start(bf16[2,2,256,256]{3,2,1,0:T(8,128)(2,1)} %slice_bitcast_fusion), channel_id=1, source_target_pairs={{0,8},{1,9},{16,24},{17,25}} | collective-permute-start | bytes 1572872 | tf_op jit(solution)/shard_map/ppermute | solution.py:21
  32.2 5.5 %collective-permute-start.1 = (bf16[2,2,2,256,256]{4,3,2,1,0:T(8,128)(2,1)S(1)}, bf16[2,2,2,256,256]{4,3,2,1,0:T(8,128)(2,1)S(1)}, u32[]{:S(2)}, u32[]{:S(2)}) collective-permute-start(bf16[2,2,2,256,256]{4,3,2,1,0:T(8,128)(2,1)S(1)} %get-tuple-element.16), channel_id=1, source_target_pairs={{0,2},{2,4},{4,6},{6,8},{8,10},{10,12},{12,14},{1,3},{3,5},{5,7},{... | collective-permute-start | bytes 3145736 | tf_op jit(solution)/shard_map/ppermute | solution.py:10
  42.6 2.3 %multiply_convert_fusion = bf16[2,2,2,256,256]{4,3,2,1,0:T(8,128)(2,1)S(1)} fusion(f32[2,2,2,256,256]{4,3,2,1,0:T(8,128)S(1)} %get-tuple-element.17, f32[2,2,2,256,256]{4,3,2,1,0:T(8,128)S(1)} %fusion.99, f32[2,2,2,256,256]{4,3,2,1,0:T(8,128)S(1)} %fusion.5, bf16[2,2,2,256,256]{4,3,2,1,0:T(8,128)(2,1)} %collective-permute-done.5, ...), kind=kOutput, calls=%fused_computation.19 | convolution fusion | flops 274202624 | bytes 8519680 | tf_op jit(solution)/shard_map/dot_general | solution.py:159
  47.4 2.2 %collective-permute-done.3 = bf16[2,2,256,256]{3,2,1,0:T(8,128)(2,1)S(1)} collective-permute-done((bf16[2,2,256,256]{3,2,1,0:T(8,128)(2,1)S(1)}, bf16[2,2,256,256]{3,2,1,0:T(8,128)(2,1)S(1)}, u32[]{:S(2)}, u32[]{:S(2)}) %collective-permute-start.3) | collective-permute-done | bytes 524320 | tf_op jit(solution)/shard_map/ppermute | solution.py:21
  49.6 2.0 collective-permute-start.4
  53.6 9.4 %collective-permute-done.1 = bf16[2,2,2,256,256]{4,3,2,1,0:T(8,128)(2,1)S(1)} collective-permute-done((bf16[2,2,2,256,256]{4,3,2,1,0:T(8,128)(2,1)S(1)}, bf16[2,2,2,256,256]{4,3,2,1,0:T(8,128)(2,1)S(1)}, u32[]{:S(2)}, u32[]{:S(2)}) %collective-permute-start.1) | collective-permute-done | bytes 1048608 | tf_op jit(solution)/shard_map/ppermute | solution.py:10
  64.0 10.1 %collective-permute-done.4 = bf16[2,2,256,256]{3,2,1,0:T(8,128)(2,1)S(1)} collective-permute-done((bf16[2,2,256,256]{3,2,1,0:T(8,128)(2,1)S(1)}, bf16[2,2,256,256]{3,2,1,0:T(8,128)(2,1)S(1)}, u32[]{:S(2)}, u32[]{:S(2)}) %collective-permute-start.4) | collective-permute-done | bytes 524320 | tf_op jit(solution)/shard_map/ppermute | solution.py:21
  74.1 2.2 %convolution_bitcast_fusion.2 = f32[256,256]{1,0:T(8,128)S(1)} fusion(f32[2,2,256,256]{3,2,1,0:T(8,128)} %get-tuple-element.5, bf16[2,2,256,256]{3,2,1,0:T(8,128)(2,1)S(1)} %collective-permute-done.4, bf16[2,2,256,256]{3,2,1,0:T(8,128)(2,1)S(1)} %broadcast_select_fusion.1, pred[]{:T(512)S(6)} %eq.37), kind=kOutput, calls=%fused_computation.42 | convolution fusion | flops 805568512 | bytes 2359297 | tf_op jit(solution)/shard_map/dot_general | solution.py:237
  76.6 1.7 copy-done.7
  80.8 2.7 %fusion.101 = f32[2,2,2,256,256]{4,3,2,1,0:T(8,128)} fusion(bf16[2,2,2,256,256]{4,3,2,1,0:T(8,128)(2,1)S(1)} %copy-done.4, bf16[3,256,256]{2,1,0:T(8,128)(2,1)} %param.10), kind=kOutput, calls=%fused_computation.138 | convolution fusion | flops 268435456 | bytes 3276800 | tf_op jit(solution)/shard_map/dot_general | solution.py:148
  83.5 2.6 %add.217 = f32[2,2,256,256]{3,2,1,0:T(8,128)} add(f32[2,2,256,256]{3,2,1,0:T(8,128)} %get-tuple-element.5, f32[2,2,256,256]{3,2,1,0:T(8,128)} %collective-permute-done.7) | non-fusion elementwise | flops 262144 | bytes 3145728 | tf_op jit(solution)/shard_map/add | solution.py:32
  87.5 2.7 %fusion.80 = f32[2,2,2,256,256]{4,3,2,1,0:T(8,128)} fusion(bf16[2,2,2,256,256]{4,3,2,1,0:T(8,128)(2,1)S(1)} %multiply_convert_fusion, bf16[9,256,256]{2,1,0:T(8,128)(2,1)} %param.9), kind=kOutput, calls=%fused_computation.119 | convolution fusion | flops 268435456 | bytes 3276800 | tf_op jit(solution)/shard_map/dot_general | solution.py:141
  90.3 2.8 %fusion.9 = f32[2,2,2,256,256]{4,3,2,1,0:T(8,128)} fusion(bf16[2,2,1,256,256]{4,3,2,1,0:T(8,128)(2,1)S(1)} %get-tuple-element.12, bf16[2,2,2,256,256]{4,3,2,1,0:T(8,128)(2,1)S(1)} %multiply_convert_fusion, bf16[9,256,256]{2,1,0:T(8,128)(2,1)} %param.9), kind=kOutput, calls=%fused_computation.27 | convolution fusion | flops 271581184 | bytes 3801088 | tf_op jit(solution)/shard_map/dot_general | solution.py:141
  93.1 1.7 dynamic-slice_add_fusion
  94.9 3.0 %collective-permute-start.11 = (f32[832,256]{1,0:T(8,128)S(1)}, f32[832,256]{1,0:T(8,128)S(1)}, u32[]{:S(2)}, u32[]{:S(2)}) collective-permute-start(f32[832,256]{1,0:T(8,128)S(1)} %constant_dynamic-slice_fusion.3), channel_id=1, source_target_pairs={{0,2},{2,0},{4,6},{6,4},{8,10},{10,8},{12,14},{14,12},{1,3},{3,1},... | collective-permute-start | bytes 2555912 | tf_op jit(solution)/shard_map/ppermute | solution.py:46
  97.9 2.7 %fusion.13 = f32[2,2,2,256,256]{4,3,2,1,0:T(8,128)} fusion(bf16[2,2,2,256,256]{4,3,2,1,0:T(8,128)(2,1)S(1)} %multiply_convert_fusion, bf16[2,2,1,256,256]{4,3,2,1,0:T(8,128)(2,1)S(1)} %get-tuple-element.13, bf16[9,256,256]{2,1,0:T(8,128)(2,1)} %param.9), kind=kOutput, calls=%fused_computation.31 | convolution fusion | flops 271581184 | bytes 3801088 | tf_op jit(solution)/shard_map/dot_general | solution.py:141
  101.5 2.9 %fusion.31 = f32[2,2,2,256,256]{4,3,2,1,0:T(8,128)} fusion(bf16[2,2,4,258,256]{4,3,2,1,0:T(8,128)(2,1)S(1)} %select_maximum_fusion, bf16[9,256,256]{2,1,0:T(8,128)(2,1)} %param.9), kind=kOutput, calls=%fused_computation.61 | convolution fusion | flops 268435456 | bytes 3276800 | tf_op jit(solution)/shard_map/dot_general | solution.py:141
  104.3 13.1 %collective-permute-done.11 = f32[832,256]{1,0:T(8,128)S(1)} collective-permute-done((f32[832,256]{1,0:T(8,128)S(1)}, f32[832,256]{1,0:T(8,128)S(1)}, u32[]{:S(2)}, u32[]{:S(2)}) %collective-permute-start.11) | collective-permute-done | bytes 852000 | tf_op jit(solution)/shard_map/ppermute | solution.py:46
  117.7 9.0 %collective-permute-start.12 = (f32[208,256]{1,0:T(8,128)S(1)}, f32[208,256]{1,0:T(8,128)S(1)}, u32[]{:S(2)}, u32[]{:S(2)}) collective-permute-start(f32[208,256]{1,0:T(8,128)S(1)} %get-tuple-element.9), channel_id=1, source_target_pairs={{0,4},{2,6},{4,8},{6,10},{8,12},{10,14},{12,0},{14,2},{1,5},{3,7},... | collective-permute-start | bytes 638984 | tf_op jit(solution)/shard_map/ppermute | solution.py:72
  126.6 3.3 %collective-permute-start.13 = (f32[208,256]{1,0:T(8,128)S(1)}, f32[208,256]{1,0:T(8,128)S(1)}, u32[]{:S(2)}, u32[]{:S(2)}) collective-permute-start(f32[208,256]{1,0:T(8,128)S(1)} %get-tuple-element.11), channel_id=1, source_target_pairs={{0,8},{2,10},{4,12},{6,14},{8,0},{10,2},{12,4},{14,6},{1,9},{3,11}... | collective-permute-start | bytes 638984 | tf_op jit(solution)/shard_map/ppermute | solution.py:72
  130.6 2.7 %fusion.17 = f32[2,2,2,256,256]{4,3,2,1,0:T(8,128)} fusion(bf16[2,2,2,256,256]{4,3,2,1,0:T(8,128)(2,1)S(1)} %copy-done.4, bf16[2,2,2,256,256]{4,3,2,1,0:T(8,128)(2,1)S(1)} %copy-done.6, bf16[3,256,256]{2,1,0:T(8,128)(2,1)} %param.10), kind=kOutput, calls=%fused_computation.35 | convolution fusion | flops 272629760 | bytes 4325376 | tf_op jit(solution)/shard_map/dot_general | solution.py:148
  133.3 2.3 %collective-permute-done.12 = f32[208,256]{1,0:T(8,128)S(1)} collective-permute-done((f32[208,256]{1,0:T(8,128)S(1)}, f32[208,256]{1,0:T(8,128)S(1)}, u32[]{:S(2)}, u32[]{:S(2)}) %collective-permute-start.12) | collective-permute-done | bytes 213024 | tf_op jit(solution)/shard_map/ppermute | solution.py:72
  135.6 7.8 %collective-permute-done.13 = f32[208,256]{1,0:T(8,128)S(1)} collective-permute-done((f32[208,256]{1,0:T(8,128)S(1)}, f32[208,256]{1,0:T(8,128)S(1)}, u32[]{:S(2)}, u32[]{:S(2)}) %collective-permute-start.13) | collective-permute-done | bytes 213024 | tf_op jit(solution)/shard_map/ppermute | solution.py:72
  148.7 1.7 add.218
  150.4 1.5 collective-permute-start.9
  151.9 1.5 fusion.37
  153.4 1.5 fusion.39
  155.1 2.8 %multiply_convert_fusion.1 = bf16[2,2,2,256,256]{4,3,2,1,0:T(8,128)(2,1)} fusion(f32[2,2,2,256,256]{4,3,2,1,0:T(8,128)S(1)} %copy-done.9, f32[2,2,2,256,256]{4,3,2,1,0:T(8,128)S(1)} %copy-done.10, bf16[2,2,2,256,256]{4,3,2,1,0:T(8,128)(2,1)S(1)} %broadcast_multiply_fusion.1, f32[2,2]{1,0:T(2,128)S(1)} %get-tuple-element.7, ...), kind=kOutput, calls=%fused_computation.20 | convolution fusion | flops 272105472 | bytes 8519696 | tf_op jit(solution)/shard_map/dot_general | solution.py:148
  157.9 24.6 %collective-permute-done.9 = f32[2,2,256,256]{3,2,1,0:T(8,128)S(1)} collective-permute-done((f32[2,2,256,256]{3,2,1,0:T(8,128)S(1)}, f32[2,2,256,256]{3,2,1,0:T(8,128)S(1)}, u32[]{:S(2)}, u32[]{:S(2)}) %collective-permute-start.9) | collective-permute-done | bytes 1048608 | tf_op jit(solution)/shard_map/ppermute | solution.py:32
  183.2 3.1 %fusion.4 = bf16[2,2,2,256,256]{4,3,2,1,0:T(8,128)(2,1)} fusion(bf16[2,2,2,256,256]{4,3,2,1,0:T(8,128)(2,1)S(1)} %get-tuple-element.6, f32[2,2,2,256,256]{4,3,2,1,0:T(8,128)S(1)} %copy-done.12, f32[2,2,2,256,256]{4,3,2,1,0:T(8,128)S(1)} %copy-done.13, f32[2,2,2,256,256]{4,3,2,1,0:T(8,128)S(1)} %fusion.33, f32[2,2,2,256,256]{4,3,2,1,0:T(8,128)S(1)} %copy-done.11, ...), kind=kOutput, calls=%fused_computation.13 | convolution fusion | flops 275775488 | bytes 21104128 | tf_op jit(solution)/shard_map/dot_general | solution.py:141
  186.3 13.5 %all-gather.2.cloned.1.call-done = bf16[3328,256]{1,0:T(8,128)(2,1)} async-done(((bf16[208,256]{1,0:T(8,128)(2,1)}), bf16[3328,256]{1,0:T(8,128)(2,1)}) %all-gather.2.cloned.1.call-update) | async-done | bytes 1703952 | tf_op jit(solution)/shard_map/all_gather | solution.py:121
  199.9 1.6 copy.24
  (108 shorter events, 40.8 us)
Async XLA Ops:
  7.2 137.0 %copy-start = (bf16[256,256]{1,0:T(8,128)(2,1)S(1)}, bf16[256,256]{1,0:T(8,128)(2,1)}, u32[]{:S(2)}) copy-start(bf16[256,256]{1,0:T(8,128)(2,1)} %param.11) | copy-start | bytes 393220
  7.2 192.7 %all-gather.2.cloned.1.call-start = ((), (), s32[]{:S(2)}) async-start(), calls=%async_computation | async-start | bytes 1810432 | tf_op jit(solution)/shard_map/all_gather | solution.py:121
  10.2 14.1 %copy-start.15 = (bf16[9,256,256]{2,1,0:T(8,128)(2,1)S(1)}, bf16[9,256,256]{2,1,0:T(8,128)(2,1)}, u32[]{:S(2)}) copy-start(bf16[9,256,256]{2,1,0:T(8,128)(2,1)} %param.9) | copy-start | bytes 3538948
  10.2 15.6 %collective-permute-start = (bf16[2,2,1,256,256]{4,3,2,1,0:T(8,128)(2,1)}, bf16[2,2,1,256,256]{4,3,2,1,0:T(8,128)(2,1)}, u32[]{:S(2)}, u32[]{:S(2)}) collective-permute-start(bf16[2,2,1,256,256]{4,3,2,1,0:T(8,128)(2,1)} %slice_select_fusion.1), channel_id=1, source_target_pairs={{0,1},{1,0},{2,3},{3,2},{4,5},{5,4},{6,7},{7,6},{8,9},{9,8},{10,11... | collective-permute-start | bytes 1572872 | tf_op jit(solution)/shard_map/ppermute | solution.py:184
  12.2 28.9 %collective-permute-start.5 = (bf16[2,2,2,256,256]{4,3,2,1,0:T(8,128)(2,1)S(1)}, bf16[2,2,2,256,256]{4,3,2,1,0:T(8,128)(2,1)}, u32[]{:S(2)}, u32[]{:S(2)}) collective-permute-start(bf16[2,2,2,256,256]{4,3,2,1,0:T(8,128)(2,1)S(1)} %get-tuple-element.6), channel_id=1, source_target_pairs={{2,0},{4,2},{6,4},{8,6},{10,8},{12,10},{14,12},{3,1},{5,3},{7,5},{... | collective-permute-start | bytes 3145736 | tf_op jit(solution)/shard_map/ppermute | solution.py:10
  14.3 23.5 %collective-permute-start.2 = (bf16[2,2,256,256]{3,2,1,0:T(8,128)(2,1)}, bf16[2,2,256,256]{3,2,1,0:T(8,128)(2,1)}, u32[]{:S(2)}, u32[]{:S(2)}) collective-permute-start(bf16[2,2,256,256]{3,2,1,0:T(8,128)(2,1)} %slice_bitcast_fusion), channel_id=1, source_target_pairs={{0,8},{1,9},{16,24},{17,25}} | collective-permute-start | bytes 1572872 | tf_op jit(solution)/shard_map/ppermute | solution.py:21
  23.0 60.5 %collective-permute-start.7 = (f32[2,2,256,256]{3,2,1,0:T(8,128)}, f32[2,2,256,256]{3,2,1,0:T(8,128)}, u32[]{:S(2)}, u32[]{:S(2)}) collective-permute-start(f32[2,2,256,256]{3,2,1,0:T(8,128)} %get-tuple-element.5), channel_id=1, source_target_pairs={{2,0},{6,4},{10,8},{14,12},{3,1},{7,5},{11,9},{15,13},{18,16},{22,... | collective-permute-start | bytes 3145736 | tf_op jit(solution)/shard_map/ppermute | solution.py:32
  32.2 31.3 %copy-start.3 = (bf16[2,2,2,256,256]{4,3,2,1,0:T(8,128)(2,1)}, bf16[2,2,2,256,256]{4,3,2,1,0:T(8,128)(2,1)S(1)}, u32[]{:S(2)}) copy-start(bf16[2,2,2,256,256]{4,3,2,1,0:T(8,128)(2,1)S(1)} %get-tuple-element.16) | copy-start | bytes 3145732
  32.2 30.8 %collective-permute-start.1 = (bf16[2,2,2,256,256]{4,3,2,1,0:T(8,128)(2,1)S(1)}, bf16[2,2,2,256,256]{4,3,2,1,0:T(8,128)(2,1)S(1)}, u32[]{:S(2)}, u32[]{:S(2)}) collective-permute-start(bf16[2,2,2,256,256]{4,3,2,1,0:T(8,128)(2,1)S(1)} %get-tuple-element.16), channel_id=1, source_target_pairs={{0,2},{2,4},{4,6},{6,8},{8,10},{10,12},{12,14},{1,3},{3,5},{5,7},{... | collective-permute-start | bytes 3145736 | tf_op jit(solution)/shard_map/ppermute | solution.py:10
  37.8 11.8 %collective-permute-start.3 = (bf16[2,2,256,256]{3,2,1,0:T(8,128)(2,1)S(1)}, bf16[2,2,256,256]{3,2,1,0:T(8,128)(2,1)S(1)}, u32[]{:S(2)}, u32[]{:S(2)}) collective-permute-start(bf16[2,2,256,256]{3,2,1,0:T(8,128)(2,1)S(1)} %broadcast_select_fusion), channel_id=1, source_target_pairs={{0,4},{8,12},{1,5},{9,13},{16,20},{24,28},{17,21},{25,29}} | collective-permute-start | bytes 1572872 | tf_op jit(solution)/shard_map/ppermute | solution.py:21
  49.6 24.5 %copy-start.14 = (bf16[2,2,256,256]{3,2,1,0:T(8,128)(2,1)}, bf16[2,2,256,256]{3,2,1,0:T(8,128)(2,1)S(1)}, u32[]{:S(2)}) copy-start(bf16[2,2,256,256]{3,2,1,0:T(8,128)(2,1)S(1)} %broadcast_select_fusion.1) | copy-start | bytes 1572868
  49.6 24.5 %collective-permute-start.4 = (bf16[2,2,256,256]{3,2,1,0:T(8,128)(2,1)S(1)}, bf16[2,2,256,256]{3,2,1,0:T(8,128)(2,1)S(1)}, u32[]{:S(2)}, u32[]{:S(2)}) collective-permute-start(bf16[2,2,256,256]{3,2,1,0:T(8,128)(2,1)S(1)} %broadcast_select_fusion.1), channel_id=1, source_target_pairs={{0,2},{4,6},{8,10},{12,14},{1,3},{5,7},{9,11},{13,15},{16,18},{20,... | collective-permute-start | bytes 1572872 | tf_op jit(solution)/shard_map/ppermute | solution.py:21
  74.1 2.2 %copy-start.16 = (bf16[2,2,256,256]{3,2,1,0:T(8,128)(2,1)}, bf16[2,2,256,256]{3,2,1,0:T(8,128)(2,1)S(1)}, u32[]{:S(2)}) copy-start(bf16[2,2,256,256]{3,2,1,0:T(8,128)(2,1)S(1)} %collective-permute-done.4) | copy-start | bytes 1572868
  76.6 1.7 copy-start.7
  79.6 13.5 %collective-permute-start.10 = (f32[1664,256]{1,0:T(8,128)}, f32[1664,256]{1,0:T(8,128)}, u32[]{:S(2)}, u32[]{:S(2)}) collective-permute-start(f32[1664,256]{1,0:T(8,128)} %constant_dynamic-slice_fusion.4), channel_id=1, source_target_pairs={{0,1},{1,0},{2,3},{3,2},{4,5},{5,4},{6,7},{7,6},{8,9},{9,8},{10,11... | collective-permute-start | bytes 5111816 | tf_op jit(solution)/shard_map/ppermute | solution.py:46
  79.7 10.5 %collective-permute-start.6 = (bf16[2,2,1,256,256]{4,3,2,1,0:T(8,128)(2,1)S(1)}, bf16[2,2,1,256,256]{4,3,2,1,0:T(8,128)(2,1)S(1)}, u32[]{:S(2)}, u32[]{:S(2)}) collective-permute-start(bf16[2,2,1,256,256]{4,3,2,1,0:T(8,128)(2,1)S(1)} %slice_select_fusion), channel_id=1, source_target_pairs={{0,1},{1,0},{2,3},{3,2},{4,5},{5,4},{6,7},{7,6},{8,9},{9,8},{10,11... | collective-permute-start | bytes 1572872 | tf_op jit(solution)/shard_map/ppermute | solution.py:184
  86.2 62.5 %collective-permute-start.8 = (f32[2,2,256,256]{3,2,1,0:T(8,128)}, f32[2,2,256,256]{3,2,1,0:T(8,128)}, u32[]{:S(2)}, u32[]{:S(2)}) collective-permute-start(f32[2,2,256,256]{3,2,1,0:T(8,128)} %add.217), channel_id=1, source_target_pairs={{4,0},{12,8},{5,1},{13,9},{20,16},{28,24},{21,17},{29,25}} | collective-permute-start | bytes 3145736 | tf_op jit(solution)/shard_map/ppermute | solution.py:32
  90.3 2.9 %copy-start.8 = (f32[3328,256]{1,0:T(8,128)S(1)}, f32[3328,256]{1,0:T(8,128)}, u32[]{:S(2)}) copy-start(f32[3328,256]{1,0:T(8,128)} %copy-done.7) | copy-start | bytes 10223620
  94.9 22.6 %collective-permute-start.11 = (f32[832,256]{1,0:T(8,128)S(1)}, f32[832,256]{1,0:T(8,128)S(1)}, u32[]{:S(2)}, u32[]{:S(2)}) collective-permute-start(f32[832,256]{1,0:T(8,128)S(1)} %constant_dynamic-slice_fusion.3), channel_id=1, source_target_pairs={{0,2},{2,0},{4,6},{6,4},{8,10},{10,8},{12,14},{14,12},{1,3},{3,1},... | collective-permute-start | bytes 2555912 | tf_op jit(solution)/shard_map/ppermute | solution.py:46
  101.5 16.1 %copy-start.1 = (bf16[2,2,4,258,256]{4,3,2,1,0:T(8,128)(2,1)}, bf16[2,2,4,258,256]{4,3,2,1,0:T(8,128)(2,1)S(1)}, u32[]{:S(2)}) copy-start(bf16[2,2,4,258,256]{4,3,2,1,0:T(8,128)(2,1)S(1)} %select_maximum_fusion) | copy-start | bytes 6340612
  104.3 26.2 %copy-start.6 = (bf16[2,2,2,256,256]{4,3,2,1,0:T(8,128)(2,1)S(1)}, bf16[2,2,2,256,256]{4,3,2,1,0:T(8,128)(2,1)}, u32[]{:S(2)}) copy-start(bf16[2,2,2,256,256]{4,3,2,1,0:T(8,128)(2,1)} %copy-done.5) | copy-start | bytes 3145732
  117.7 17.9 %collective-permute-start.12 = (f32[208,256]{1,0:T(8,128)S(1)}, f32[208,256]{1,0:T(8,128)S(1)}, u32[]{:S(2)}, u32[]{:S(2)}) collective-permute-start(f32[208,256]{1,0:T(8,128)S(1)} %get-tuple-element.9), channel_id=1, source_target_pairs={{0,4},{2,6},{4,8},{6,10},{8,12},{10,14},{12,0},{14,2},{1,5},{3,7},... | collective-permute-start | bytes 638984 | tf_op jit(solution)/shard_map/ppermute | solution.py:72
  126.6 16.7 %collective-permute-start.13 = (f32[208,256]{1,0:T(8,128)S(1)}, f32[208,256]{1,0:T(8,128)S(1)}, u32[]{:S(2)}, u32[]{:S(2)}) collective-permute-start(f32[208,256]{1,0:T(8,128)S(1)} %get-tuple-element.11), channel_id=1, source_target_pairs={{0,8},{2,10},{4,12},{6,14},{8,0},{10,2},{12,4},{14,6},{1,9},{3,11}... | collective-permute-start | bytes 638984 | tf_op jit(solution)/shard_map/ppermute | solution.py:72
  129.9 13.5 %collective-permute-start.14 = (f32[208,256]{1,0:T(8,128)S(1)}, f32[208,256]{1,0:T(8,128)S(1)}, u32[]{:S(2)}, u32[]{:S(2)}) collective-permute-start(f32[208,256]{1,0:T(8,128)S(1)} %get-tuple-element.10), channel_id=1, source_target_pairs={{0,12},{2,14},{4,0},{6,2},{8,4},{10,6},{12,8},{14,10},{1,13},{3,15... | collective-permute-start | bytes 638984 | tf_op jit(solution)/shard_map/ppermute | solution.py:72
  144.1 1.8 copy-start.2
  150.4 32.1 %collective-permute-start.9 = (f32[2,2,256,256]{3,2,1,0:T(8,128)S(1)}, f32[2,2,256,256]{3,2,1,0:T(8,128)S(1)}, u32[]{:S(2)}, u32[]{:S(2)}) collective-permute-start(f32[2,2,256,256]{3,2,1,0:T(8,128)S(1)} %add.218), channel_id=1, source_target_pairs={{8,0},{9,1},{24,16},{25,17}} | collective-permute-start | bytes 3145736 | tf_op jit(solution)/shard_map/ppermute | solution.py:32
  151.9 3.1 %copy-start.10 = (f32[2,2,2,256,256]{4,3,2,1,0:T(8,128)S(1)}, f32[2,2,2,256,256]{4,3,2,1,0:T(8,128)}, u32[]{:S(2)}) copy-start(f32[2,2,2,256,256]{4,3,2,1,0:T(8,128)} %fusion.17) | copy-start | bytes 6291460
  153.4 1.7 copy-start.9
  155.1 28.1 %copy-start.12 = (f32[2,2,2,256,256]{4,3,2,1,0:T(8,128)S(1)}, f32[2,2,2,256,256]{4,3,2,1,0:T(8,128)}, u32[]{:S(2)}) copy-start(f32[2,2,2,256,256]{4,3,2,1,0:T(8,128)} %fusion.13) | copy-start | bytes 6291460
  155.1 28.1 %copy-start.13 = (f32[2,2,2,256,256]{4,3,2,1,0:T(8,128)S(1)}, f32[2,2,2,256,256]{4,3,2,1,0:T(8,128)}, u32[]{:S(2)}) copy-start(f32[2,2,2,256,256]{4,3,2,1,0:T(8,128)} %fusion.31) | copy-start | bytes 6291460
  155.1 28.1 %copy-start.17 = (f32[2,2,2,256,256]{4,3,2,1,0:T(8,128)S(1)}, f32[2,2,2,256,256]{4,3,2,1,0:T(8,128)}, u32[]{:S(2)}) copy-start(f32[2,2,2,256,256]{4,3,2,1,0:T(8,128)} %fusion.9) | copy-start | bytes 6291460
  157.9 25.3 %copy-start.11 = (f32[2,2,2,256,256]{4,3,2,1,0:T(8,128)S(1)}, f32[2,2,2,256,256]{4,3,2,1,0:T(8,128)}, u32[]{:S(2)}) copy-start(f32[2,2,2,256,256]{4,3,2,1,0:T(8,128)} %fusion.80) | copy-start | bytes 6291460
  (4 other events, 4.6 us)
Sparse Core Ops, SparseCore 0:
  144.2 55.5 all-gather.1

commit v5 on v2

--- a/solution.py
+++ b/solution.py
@@ -161,14 +161,14 @@
     return total
 
 
-def lag_grads(padded_act, cot, count):
+def lag_grads(act, padded_cot, count):
     dims = (((0, 1, 2, 3), (0, 1, 2, 3)), ((), ()))
     terms = []
     for lag in range(3):
         terms.append(
             lax.dot_general(
-                padded_act[:, 2 - lag : 2 - lag + count],
-                cot,
+                act,
+                padded_cot[:, lag : lag + count],
                 dims,
                 preferred_element_type=jnp.float32,
             )
@@ -177,6 +177,14 @@
 
 
 def row_halo(x):
+    if lax.axis_size("tm") == 2:
+        me = lax.axis_index("tm")
+        edge = jnp.where(me == 0, x[:, :, -1:], x[:, :, :1])
+        got = lax.ppermute(edge, "tm", [(0, 1), (1, 0)])
+        zero = jnp.zeros_like(got)
+        above = jnp.where(me == 1, got, zero)
+        below = jnp.where(me == 0, got, zero)
+        return jnp.concatenate([above, x, below], axis=2)
     above = shifted(x[:, :, -1:], "tm", 1)
     below = shifted(x[:, :, :1], "tm", -1)
     return jnp.concatenate([above, x, below], axis=2)
@@ -203,7 +211,7 @@
     mixed = lag_forward(act_pad, temporal_weight, frames)
     cot_pad = jnp.concatenate([cot, later], axis=1)
     dact = lag_backward(cot_pad, temporal_weight, frames)
-    temporal_terms = lag_grads(act_pad, cot, frames)
+    temporal_terms = lag_grads(act, cot_pad, frames)
     cond = jnp.dot(first, cond_weight, preferred_element_type=jnp.float32)
     output = ((masked.astype(jnp.float32) + mixed + cond[:, None]) * mask_f).astype(jnp.bfloat16)
     sig = jax.nn.sigmoid(pre)

time: 184 us -> 184 us (level)
  matrix products: 30.7 us -> 28.7 us
    ppermute x6 -> x2, starting transfers between devices: 15.4 us -> 4.38 us  [shifted(): return lax.ppermute(value, axis, pairs)]
    ppermute x3, waiting for transfers between devices: 0.01 us -> 9.66 us  [tree_reduce(): value = value + lax.ppermute(value, axis, pairs)]
    ppermute x3, starting transfers between devices: 14.8 us -> 23.2 us  [direct_scatter(): total = total + lax.ppermute(send, axis, pairs)]
    ppermute x3, waiting for transfers between devices: 13.6 us -> 5.92 us  [tree_broadcast(): got = lax.ppermute(value, axis, pairs)]
    ppermute x6 -> x2, waiting for transfers between devices: 5.23 us -> 0.69 us  [shifted(): return lax.ppermute(value, axis, pairs)]
    ppermute x3, starting transfers between devices: 11 us -> 14.2 us  [tree_broadcast(): got = lax.ppermute(value, axis, pairs)]
    dot_general x3, matrix products: 1.42 us -> 3.71 us  [lag_grads(): lax.dot_general(act, padded_cot[:, lag:lag + count], dims, preferred_elem...]
    dot_general x18, matrix products: 14.2 us -> 12 us  [spatial_sum(): total = total + jnp.dot(piece, kernel, preferred_element_type=jnp.float32)]
  transfers between devices with their start and end apart: 22 -> 20, of which waited for: 10 -> 10; matrix products, arithmetic and copies ran while one was open for 21% -> 19% of each run, Pallas kernels for 0% -> 0%
where the time goes in v5:
time: 184 us; the launch traced here: 183 us
  waiting for transfers between devices  82.3 us (45%)
  starting transfers between devices  56.6 us (31%)
  matrix products  28.7 us (16%)
  other arithmetic  9.29 us (5%)
  local copies, waits for them, and re-layouts  4.2 us (2%)
    ppermute x3, waiting for transfers between devices, direct_gather(): got = lax.ppermute(piece, axis, pairs)  25.7 us
    ppermute x3, starting transfers between devices, direct_scatter(): total = total + lax.ppermute(send, axis, pairs)  23.2 us
    ppermute x2, waiting for transfers between devices, xor_halving(): flat = keep + lax.ppermute(send, axis, pairs)  18.2 us
    ppermute x3, starting transfers between devices, tree_broadcast(): got = lax.ppermute(value, axis, pairs)  14.2 us
    dot_general x18, matrix products, spatial_sum(): total = total + jnp.dot(piece, kernel, preferred_element_type=jnp.float32)  12 us
    ppermute x3, waiting for transfers between devices, direct_scatter(): total = total + lax.ppermute(send, axis, pairs)  11.7 us
    ppermute x2, waiting for transfers between devices, xor_doubling(): got = lax.ppermute(piece, axis, [(i, i ^ step) for i in range(count)])  10.5 us
    ppermute x3, waiting for transfers between devices, tree_reduce(): value = value + lax.ppermute(value, axis, pairs)  9.66 us
  transfers between devices with their start and end apart: 20, of which 10 were waited for; matrix products, arithmetic and copies ran while one was open for 19% of the time, Pallas kernels for 0%

profile of v5, /device:TPU:0, one launch (start us, length us, event | category | flops | bytes accessed | tf_op | source)
XLA Modules:
  0.0 182.5 jit_solution(3453113742417126245)
XLA Ops:
  1.4 1.4 broadcast_multiply_fusion.1
  4.6 1.3 collective-permute-start.5
  6.8 8.7 %collective-permute-start.2 = (bf16[2,2,256,256]{3,2,1,0:T(8,128)(2,1)}, bf16[2,2,256,256]{3,2,1,0:T(8,128)(2,1)}, u32[]{:S(2)}, u32[]{:S(2)}) collective-permute-start(bf16[2,2,256,256]{3,2,1,0:T(8,128)(2,1)} %slice_bitcast_fusion), channel_id=1, source_target_pairs={{0,8},{1,9},{16,24},{17,25}} | collective-permute-start | bytes 1572872 | tf_op jit(solution)/shard_map/ppermute | solution.py:21
  15.5 1.3 collective-permute-start.7
  17.1 1.4 fusion.86
  19.0 1.1 broadcast_select_fusion.6
  24.5 1.6 collective-permute-done.2
  26.1 1.3 collective-permute-start.3
  27.4 1.4 multiply_convert_fusion.2
  28.9 3.1 %collective-permute-start.1 = (bf16[2,2,2,256,256]{4,3,2,1,0:T(8,128)(2,1)S(1)}, bf16[2,2,2,256,256]{4,3,2,1,0:T(8,128)(2,1)S(1)}, u32[]{:S(2)}, u32[]{:S(2)}) collective-permute-start(bf16[2,2,2,256,256]{4,3,2,1,0:T(8,128)(2,1)S(1)} %get-tuple-element.18), channel_id=1, source_target_pairs={{0,2},{2,4},{4,6},{6,8},{8,10},{10,12},{12,14},{1,3},{3,5},{5,7},{... | collective-permute-start | bytes 3145736 | tf_op jit(solution)/shard_map/ppermute | solution.py:10
  33.6 1.5 fusion.9
  35.1 2.3 %multiply_convert_fusion = bf16[2,2,2,256,256]{4,3,2,1,0:T(8,128)(2,1)S(1)} fusion(f32[2,2,2,256,256]{4,3,2,1,0:T(8,128)S(1)} %get-tuple-element.19, f32[2,2,2,256,256]{4,3,2,1,0:T(8,128)S(1)} %fusion.103, f32[2,2,2,256,256]{4,3,2,1,0:T(8,128)S(1)} %fusion.9, bf16[2,2,2,256,256]{4,3,2,1,0:T(8,128)(2,1)} %collective-permute-done.5, ...), kind=kOutput, calls=%fused_computation.22 | convolution fusion | flops 274202624 | bytes 8519680 | tf_op jit(solution)/shard_map/dot_general | solution.py:158
  39.5 4.2 %collective-permute-start.4 = (bf16[2,2,256,256]{3,2,1,0:T(8,128)(2,1)S(1)}, bf16[2,2,256,256]{3,2,1,0:T(8,128)(2,1)S(1)}, u32[]{:S(2)}, u32[]{:S(2)}) collective-permute-start(bf16[2,2,256,256]{3,2,1,0:T(8,128)(2,1)S(1)} %broadcast_select_fusion.1), channel_id=1, source_target_pairs={{0,2},{4,6},{8,10},{12,14},{1,3},{5,7},{9,11},{13,15},{16,18},{20,... | collective-permute-start | bytes 1572872 | tf_op jit(solution)/shard_map/ppermute | solution.py:21
  45.7 9.7 %collective-permute-done.7 = f32[2,2,256,256]{3,2,1,0:T(8,128)} collective-permute-done((f32[2,2,256,256]{3,2,1,0:T(8,128)S(1)}, f32[2,2,256,256]{3,2,1,0:T(8,128)}, u32[]{:S(2)}, u32[]{:S(2)}) %collective-permute-start.7) | collective-permute-done | bytes 1048608 | tf_op jit(solution)/shard_map/ppermute | solution.py:32
  55.3 1.4 add.244
  56.7 1.3 collective-permute-start.8
  58.0 1.5 convolution_bitcast_fusion.4
  59.5 1.7 convolution_bitcast_fusion.3
  62.3 4.4 %collective-permute-done.4 = bf16[2,2,256,256]{3,2,1,0:T(8,128)(2,1)S(1)} collective-permute-done((bf16[2,2,256,256]{3,2,1,0:T(8,128)(2,1)S(1)}, bf16[2,2,256,256]{3,2,1,0:T(8,128)(2,1)S(1)}, u32[]{:S(2)}, u32[]{:S(2)}) %collective-permute-start.4) | collective-permute-done | bytes 524320 | tf_op jit(solution)/shard_map/ppermute | solution.py:21
  70.1 1.7 multiply_convert_fusion.1
  72.1 2.5 %collective-permute-start.11 = (f32[832,256]{1,0:T(8,128)S(1)}, f32[832,256]{1,0:T(8,128)S(1)}, u32[]{:S(2)}, u32[]{:S(2)}) collective-permute-start(f32[832,256]{1,0:T(8,128)S(1)} %constant_dynamic-slice_fusion.3), channel_id=1, source_target_pairs={{0,2},{2,0},{4,6},{6,4},{8,10},{10,8},{12,14},{14,12},{1,3},{3,1},... | collective-permute-start | bytes 2555912 | tf_op jit(solution)/shard_map/ppermute | solution.py:46
  76.1 18.2 %collective-permute-done.11 = f32[832,256]{1,0:T(8,128)S(1)} collective-permute-done((f32[832,256]{1,0:T(8,128)S(1)}, f32[832,256]{1,0:T(8,128)S(1)}, u32[]{:S(2)}, u32[]{:S(2)}) %collective-permute-start.11) | collective-permute-done | bytes 852000 | tf_op jit(solution)/shard_map/ppermute | solution.py:46
  94.4 19.3 %collective-permute-start.12 = (f32[208,256]{1,0:T(8,128)S(1)}, f32[208,256]{1,0:T(8,128)S(1)}, u32[]{:S(2)}, u32[]{:S(2)}) collective-permute-start(f32[208,256]{1,0:T(8,128)S(1)} %get-tuple-element.11), channel_id=1, source_target_pairs={{0,4},{2,6},{4,8},{6,10},{8,12},{10,14},{12,0},{14,2},{1,5},{3,7},... | collective-permute-start | bytes 638984 | tf_op jit(solution)/shard_map/ppermute | solution.py:72
  113.8 3.7 %collective-permute-start.13 = (f32[208,256]{1,0:T(8,128)S(1)}, f32[208,256]{1,0:T(8,128)S(1)}, u32[]{:S(2)}, u32[]{:S(2)}) collective-permute-start(f32[208,256]{1,0:T(8,128)S(1)} %get-tuple-element.13), channel_id=1, source_target_pairs={{0,8},{2,10},{4,12},{6,14},{8,0},{10,2},{12,4},{14,6},{1,9},{3,11}... | collective-permute-start | bytes 638984 | tf_op jit(solution)/shard_map/ppermute | solution.py:72
  118.3 1.3 collective-permute-start.9
  119.6 3.5 %collective-permute-done.12 = f32[208,256]{1,0:T(8,128)S(1)} collective-permute-done((f32[208,256]{1,0:T(8,128)S(1)}, f32[208,256]{1,0:T(8,128)S(1)}, u32[]{:S(2)}, u32[]{:S(2)}) %collective-permute-start.12) | collective-permute-done | bytes 213024 | tf_op jit(solution)/shard_map/ppermute | solution.py:72
  123.1 8.2 %collective-permute-done.13 = f32[208,256]{1,0:T(8,128)S(1)} collective-permute-done((f32[208,256]{1,0:T(8,128)S(1)}, f32[208,256]{1,0:T(8,128)S(1)}, u32[]{:S(2)}, u32[]{:S(2)}) %collective-permute-start.13) | collective-permute-done | bytes 213024 | tf_op jit(solution)/shard_map/ppermute | solution.py:72
  131.4 5.2 %collective-permute-start.15 = (bf16[208,256]{1,0:T(8,128)(2,1)S(1)}, bf16[208,256]{1,0:T(8,128)(2,1)S(1)}, u32[]{:S(2)}, u32[]{:S(2)}) collective-permute-start(bf16[208,256]{1,0:T(8,128)(2,1)S(1)} %get-tuple-element.6), channel_id=1, source_target_pairs={{0,4},{2,6},{4,8},{6,10},{8,12},{10,14},{12,0},{14,2},{1,5},{3,7},... | collective-permute-start | bytes 319496 | tf_op jit(solution)/shard_map/ppermute | solution.py:85
  137.4 2.0 %collective-permute-start.17 = (bf16[208,256]{1,0:T(8,128)(2,1)S(1)}, bf16[208,256]{1,0:T(8,128)(2,1)S(1)}, u32[]{:S(2)}, u32[]{:S(2)}) collective-permute-start(bf16[208,256]{1,0:T(8,128)(2,1)S(1)} %get-tuple-element.6), channel_id=1, source_target_pairs={{0,12},{2,14},{4,0},{6,2},{8,4},{10,6},{12,8},{14,10},{1,13},{3,15... | collective-permute-start | bytes 319496 | tf_op jit(solution)/shard_map/ppermute | solution.py:85
  139.9 25.2 %collective-permute-done.16 = bf16[208,256]{1,0:T(8,128)(2,1)S(1)} collective-permute-done((bf16[208,256]{1,0:T(8,128)(2,1)S(1)}, bf16[208,256]{1,0:T(8,128)(2,1)S(1)}, u32[]{:S(2)}, u32[]{:S(2)}) %collective-permute-start.16) | collective-permute-done | bytes 106528 | tf_op jit(solution)/shard_map/ppermute | solution.py:85
  166.4 10.5 %collective-permute-done.18 = bf16[832,256]{1,0:T(8,128)(2,1)S(1)} collective-permute-done((bf16[832,256]{1,0:T(8,128)(2,1)S(1)}, bf16[832,256]{1,0:T(8,128)(2,1)S(1)}, u32[]{:S(2)}, u32[]{:S(2)}) %collective-permute-start.18) | collective-permute-done | bytes 426016 | tf_op jit(solution)/shard_map/ppermute | solution.py:54
  177.2 2.3 %fusion.4 = bf16[2,2,2,256,256]{4,3,2,1,0:T(8,128)(2,1)} fusion(bf16[2,2,2,256,256]{4,3,2,1,0:T(8,128)(2,1)S(1)} %get-tuple-element.8, f32[2,2,2,256,256]{4,3,2,1,0:T(8,128)S(1)} %fusion.17, f32[2,2,2,256,256]{4,3,2,1,0:T(8,128)S(1)} %fusion.35, f32[2,2,2,256,256]{4,3,2,1,0:T(8,128)S(1)} %fusion.37, f32[2,2,2,256,256]{4,3,2,1,0:T(8,128)S(1)} %fusion.84, ...), kind=kOutput, calls=%fused_computation.13 | convolution fusion | flops 275775488 | bytes 21104128 | tf_op jit(solution)/shard_map/dot_general | solution.py:140
  (88 shorter events, 27.0 us)
Async XLA Ops:
  0.6 67.8 %copy-start = (bf16[256,256]{1,0:T(8,128)(2,1)S(1)}, bf16[256,256]{1,0:T(8,128)(2,1)}, u32[]{:S(2)}) copy-start(bf16[256,256]{1,0:T(8,128)(2,1)} %param.11) | copy-start | bytes 393220
  2.8 1.4 copy-start.3
  3.7 15.3 %collective-permute-start = (bf16[2,2,1,256,256]{4,3,2,1,0:T(8,128)(2,1)}, bf16[2,2,1,256,256]{4,3,2,1,0:T(8,128)(2,1)}, u32[]{:S(2)}, u32[]{:S(2)}) collective-permute-start(bf16[2,2,1,256,256]{4,3,2,1,0:T(8,128)(2,1)} %slice_select_fusion.1), channel_id=1, source_target_pairs={{0,1},{1,0},{2,3},{3,2},{4,5},{5,4},{6,7},{7,6},{8,9},{9,8},{10,11... | collective-permute-start | bytes 1572872 | tf_op jit(solution)/shard_map/ppermute | solution.py:183
  4.6 28.9 %collective-permute-start.5 = (bf16[2,2,2,256,256]{4,3,2,1,0:T(8,128)(2,1)S(1)}, bf16[2,2,2,256,256]{4,3,2,1,0:T(8,128)(2,1)}, u32[]{:S(2)}, u32[]{:S(2)}) collective-permute-start(bf16[2,2,2,256,256]{4,3,2,1,0:T(8,128)(2,1)S(1)} %get-tuple-element.8), channel_id=1, source_target_pairs={{2,0},{4,2},{6,4},{8,6},{10,8},{12,10},{14,12},{3,1},{5,3},{7,5},{... | collective-permute-start | bytes 3145736 | tf_op jit(solution)/shard_map/ppermute | solution.py:10
  6.8 19.3 %collective-permute-start.2 = (bf16[2,2,256,256]{3,2,1,0:T(8,128)(2,1)}, bf16[2,2,256,256]{3,2,1,0:T(8,128)(2,1)}, u32[]{:S(2)}, u32[]{:S(2)}) collective-permute-start(bf16[2,2,256,256]{3,2,1,0:T(8,128)(2,1)} %slice_bitcast_fusion), channel_id=1, source_target_pairs={{0,8},{1,9},{16,24},{17,25}} | collective-permute-start | bytes 1572872 | tf_op jit(solution)/shard_map/ppermute | solution.py:21
  15.5 39.8 %collective-permute-start.7 = (f32[2,2,256,256]{3,2,1,0:T(8,128)S(1)}, f32[2,2,256,256]{3,2,1,0:T(8,128)}, u32[]{:S(2)}, u32[]{:S(2)}) collective-permute-start(f32[2,2,256,256]{3,2,1,0:T(8,128)S(1)} %get-tuple-element.7), channel_id=1, source_target_pairs={{2,0},{6,4},{10,8},{14,12},{3,1},{7,5},{11,9},{15,13},{18,16},{22,... | collective-permute-start | bytes 3145736 | tf_op jit(solution)/shard_map/ppermute | solution.py:32
  17.1 1.4 copy-start.2
  20.1 1.3 copy-start.1
  26.1 13.3 %collective-permute-start.3 = (bf16[2,2,256,256]{3,2,1,0:T(8,128)(2,1)S(1)}, bf16[2,2,256,256]{3,2,1,0:T(8,128)(2,1)S(1)}, u32[]{:S(2)}, u32[]{:S(2)}) collective-permute-start(bf16[2,2,256,256]{3,2,1,0:T(8,128)(2,1)S(1)} %broadcast_select_fusion), channel_id=1, source_target_pairs={{0,4},{8,12},{1,5},{9,13},{16,20},{24,28},{17,21},{25,29}} | collective-permute-start | bytes 1572872 | tf_op jit(solution)/shard_map/ppermute | solution.py:21
  28.9 39.1 %collective-permute-start.1 = (bf16[2,2,2,256,256]{4,3,2,1,0:T(8,128)(2,1)S(1)}, bf16[2,2,2,256,256]{4,3,2,1,0:T(8,128)(2,1)S(1)}, u32[]{:S(2)}, u32[]{:S(2)}) collective-permute-start(bf16[2,2,2,256,256]{4,3,2,1,0:T(8,128)(2,1)S(1)} %get-tuple-element.18), channel_id=1, source_target_pairs={{0,2},{2,4},{4,6},{6,8},{8,10},{10,12},{12,14},{1,3},{3,5},{5,7},{... | collective-permute-start | bytes 3145736 | tf_op jit(solution)/shard_map/ppermute | solution.py:10
  39.5 27.2 %collective-permute-start.4 = (bf16[2,2,256,256]{3,2,1,0:T(8,128)(2,1)S(1)}, bf16[2,2,256,256]{3,2,1,0:T(8,128)(2,1)S(1)}, u32[]{:S(2)}, u32[]{:S(2)}) collective-permute-start(bf16[2,2,256,256]{3,2,1,0:T(8,128)(2,1)S(1)} %broadcast_select_fusion.1), channel_id=1, source_target_pairs={{0,2},{4,6},{8,10},{12,14},{1,3},{5,7},{9,11},{13,15},{16,18},{20,... | collective-permute-start | bytes 1572872 | tf_op jit(solution)/shard_map/ppermute | solution.py:21
  43.6 24.3 %collective-permute-start.6 = (bf16[2,2,1,256,256]{4,3,2,1,0:T(8,128)(2,1)S(1)}, bf16[2,2,1,256,256]{4,3,2,1,0:T(8,128)(2,1)S(1)}, u32[]{:S(2)}, u32[]{:S(2)}) collective-permute-start(bf16[2,2,1,256,256]{4,3,2,1,0:T(8,128)(2,1)S(1)} %slice_select_fusion), channel_id=1, source_target_pairs={{0,1},{1,0},{2,3},{3,2},{4,5},{5,4},{6,7},{7,6},{8,9},{9,8},{10,11... | collective-permute-start | bytes 1572872 | tf_op jit(solution)/shard_map/ppermute | solution.py:183
  56.7 61.4 %collective-permute-start.8 = (f32[2,2,256,256]{3,2,1,0:T(8,128)S(1)}, f32[2,2,256,256]{3,2,1,0:T(8,128)S(1)}, u32[]{:S(2)}, u32[]{:S(2)}) collective-permute-start(f32[2,2,256,256]{3,2,1,0:T(8,128)S(1)} %add.244), channel_id=1, source_target_pairs={{4,0},{12,8},{5,1},{13,9},{20,16},{28,24},{21,17},{29,25}} | collective-permute-start | bytes 3145736 | tf_op jit(solution)/shard_map/ppermute | solution.py:32
  67.8 4.0 %collective-permute-start.10 = (f32[1664,256]{1,0:T(8,128)S(1)}, f32[1664,256]{1,0:T(8,128)S(1)}, u32[]{:S(2)}, u32[]{:S(2)}) collective-permute-start(f32[1664,256]{1,0:T(8,128)S(1)} %constant_dynamic-slice_fusion.4), channel_id=1, source_target_pairs={{0,1},{1,0},{2,3},{3,2},{4,5},{5,4},{6,7},{7,6},{8,9},{9,8},{10,11... | collective-permute-start | bytes 5111816 | tf_op jit(solution)/shard_map/ppermute | solution.py:46
  72.1 22.1 %collective-permute-start.11 = (f32[832,256]{1,0:T(8,128)S(1)}, f32[832,256]{1,0:T(8,128)S(1)}, u32[]{:S(2)}, u32[]{:S(2)}) collective-permute-start(f32[832,256]{1,0:T(8,128)S(1)} %constant_dynamic-slice_fusion.3), channel_id=1, source_target_pairs={{0,2},{2,0},{4,6},{6,4},{8,10},{10,8},{12,14},{14,12},{1,3},{3,1},... | collective-permute-start | bytes 2555912 | tf_op jit(solution)/shard_map/ppermute | solution.py:46
  94.4 28.7 %collective-permute-start.12 = (f32[208,256]{1,0:T(8,128)S(1)}, f32[208,256]{1,0:T(8,128)S(1)}, u32[]{:S(2)}, u32[]{:S(2)}) collective-permute-start(f32[208,256]{1,0:T(8,128)S(1)} %get-tuple-element.11), channel_id=1, source_target_pairs={{0,4},{2,6},{4,8},{6,10},{8,12},{10,14},{12,0},{14,2},{1,5},{3,7},... | collective-permute-start | bytes 638984 | tf_op jit(solution)/shard_map/ppermute | solution.py:72
  113.8 17.5 %collective-permute-start.13 = (f32[208,256]{1,0:T(8,128)S(1)}, f32[208,256]{1,0:T(8,128)S(1)}, u32[]{:S(2)}, u32[]{:S(2)}) collective-permute-start(f32[208,256]{1,0:T(8,128)S(1)} %get-tuple-element.13), channel_id=1, source_target_pairs={{0,8},{2,10},{4,12},{6,14},{8,0},{10,2},{12,4},{14,6},{1,9},{3,11}... | collective-permute-start | bytes 638984 | tf_op jit(solution)/shard_map/ppermute | solution.py:72
  117.4 13.8 %collective-permute-start.14 = (f32[208,256]{1,0:T(8,128)S(1)}, f32[208,256]{1,0:T(8,128)S(1)}, u32[]{:S(2)}, u32[]{:S(2)}) collective-permute-start(f32[208,256]{1,0:T(8,128)S(1)} %get-tuple-element.12), channel_id=1, source_target_pairs={{0,12},{2,14},{4,0},{6,2},{8,4},{10,6},{12,8},{14,10},{1,13},{3,15... | collective-permute-start | bytes 638984 | tf_op jit(solution)/shard_map/ppermute | solution.py:72
  118.3 47.5 %collective-permute-start.9 = (f32[2,2,256,256]{3,2,1,0:T(8,128)S(1)}, f32[2,2,256,256]{3,2,1,0:T(8,128)S(1)}, u32[]{:S(2)}, u32[]{:S(2)}) collective-permute-start(f32[2,2,256,256]{3,2,1,0:T(8,128)S(1)} %add.245), channel_id=1, source_target_pairs={{8,0},{9,1},{24,16},{25,17}} | collective-permute-start | bytes 3145736 | tf_op jit(solution)/shard_map/ppermute | solution.py:32
  131.4 8.5 %collective-permute-start.15 = (bf16[208,256]{1,0:T(8,128)(2,1)S(1)}, bf16[208,256]{1,0:T(8,128)(2,1)S(1)}, u32[]{:S(2)}, u32[]{:S(2)}) collective-permute-start(bf16[208,256]{1,0:T(8,128)(2,1)S(1)} %get-tuple-element.6), channel_id=1, source_target_pairs={{0,4},{2,6},{4,8},{6,10},{8,12},{10,14},{12,0},{14,2},{1,5},{3,7},... | collective-permute-start | bytes 319496 | tf_op jit(solution)/shard_map/ppermute | solution.py:85
  137.0 28.1 %collective-permute-start.16 = (bf16[208,256]{1,0:T(8,128)(2,1)S(1)}, bf16[208,256]{1,0:T(8,128)(2,1)S(1)}, u32[]{:S(2)}, u32[]{:S(2)}) collective-permute-start(bf16[208,256]{1,0:T(8,128)(2,1)S(1)} %get-tuple-element.6), channel_id=1, source_target_pairs={{0,8},{2,10},{4,12},{6,14},{8,0},{10,2},{12,4},{14,6},{1,9},{3,11}... | collective-permute-start | bytes 319496 | tf_op jit(solution)/shard_map/ppermute | solution.py:85
  137.4 27.7 %collective-permute-start.17 = (bf16[208,256]{1,0:T(8,128)(2,1)S(1)}, bf16[208,256]{1,0:T(8,128)(2,1)S(1)}, u32[]{:S(2)}, u32[]{:S(2)}) collective-permute-start(bf16[208,256]{1,0:T(8,128)(2,1)S(1)} %get-tuple-element.6), channel_id=1, source_target_pairs={{0,12},{2,14},{4,0},{6,2},{8,4},{10,6},{12,8},{14,10},{1,13},{3,15... | collective-permute-start | bytes 319496 | tf_op jit(solution)/shard_map/ppermute | solution.py:85
  165.2 11.7 %collective-permute-start.18 = (bf16[832,256]{1,0:T(8,128)(2,1)S(1)}, bf16[832,256]{1,0:T(8,128)(2,1)S(1)}, u32[]{:S(2)}, u32[]{:S(2)}) collective-permute-start(bf16[832,256]{1,0:T(8,128)(2,1)S(1)} %bitcast.256), channel_id=1, source_target_pairs={{0,2},{2,0},{4,6},{6,4},{8,10},{10,8},{12,14},{14,12},{1,3},{3,1},... | collective-permute-start | bytes 1277960 | tf_op jit(solution)/shard_map/ppermute | solution.py:54
  177.1 2.4 %collective-permute-start.19 = (bf16[1664,256]{1,0:T(8,128)(2,1)S(1)}, bf16[1664,256]{1,0:T(8,128)(2,1)S(1)}, u32[]{:S(2)}, u32[]{:S(2)}) collective-permute-start(bf16[1664,256]{1,0:T(8,128)(2,1)S(1)} %maximum_select_fusion.1), channel_id=1, source_target_pairs={{0,1},{1,0},{2,3},{3,2},{4,5},{5,4},{6,7},{7,6},{8,9},{9,8},{10,11... | collective-permute-start | bytes 2555912 | tf_op jit(solution)/shard_map/ppermute | solution.py:54

commit v6 on v5

--- a/solution.py
+++ b/solution.py
@@ -216,14 +216,6 @@
     output = ((masked.astype(jnp.float32) + mixed + cond[:, None]) * mask_f).astype(jnp.bfloat16)
     sig = jax.nn.sigmoid(pre)
     dpre = (dact * sig * (1.0 + pre * (1.0 - sig))).astype(jnp.bfloat16)
-    cond_back = jnp.dot(cot_sum, cond_weight.astype(jnp.float32).T, precision=lax.Precision.HIGHEST)
-    dpre_rows = row_halo(dpre)
-    dpre_pad = jnp.pad(dpre_rows, ((0, 0), (0, 0), (0, 0), (1, 1), (0, 0)))
-    dmasked = spatial_sum(dpre_pad, spatial_weight, True)
-    is_first = (frame_ids == 0).astype(jnp.float32)[None, :, None, None, None]
-    grad_latents = (
-        (cot.astype(jnp.float32) + dmasked + is_first * cond_back[:, None]) * mask_f
-    ).astype(jnp.bfloat16)
     dims = (((0, 1, 2, 3), (0, 1, 2, 3)), ((), ()))
     spatial_terms = []
     for row_off in range(3):
@@ -250,7 +242,16 @@
         axis=0,
     )
     scale = (clips * frames * rows * cols * lax.axis_size("space") * lax.axis_size("tm")) ** (-0.5)
+    flat, cot_sum = lax.optimization_barrier((flat, cot_sum))
     summed = all_sum_rounded(flat, scale)
+    cond_back = jnp.dot(cot_sum, cond_weight.astype(jnp.float32).T, precision=lax.Precision.HIGHEST)
+    dpre_rows = row_halo(dpre)
+    dpre_pad = jnp.pad(dpre_rows, ((0, 0), (0, 0), (0, 0), (1, 1), (0, 0)))
+    dmasked = spatial_sum(dpre_pad, spatial_weight, True)
+    is_first = (frame_ids == 0).astype(jnp.float32)[None, :, None, None, None]
+    grad_latents = (
+        (cot.astype(jnp.float32) + dmasked + is_first * cond_back[:, None]) * mask_f
+    ).astype(jnp.bfloat16)
     n_s = taps_s * chans
     n_t = taps_t * chans
     grad_spatial = summed[:n_s].reshape(taps_s, chans, chans)

time: 184 us -> 202 us (1.098)
  waiting for transfers between devices: 82.3 us -> 124 us
  starting transfers between devices: 56.6 us -> 32.8 us
    ppermute x3, waiting for transfers between devices: 9.66 us -> 78.6 us  [tree_reduce(): value = value + lax.ppermute(value, axis, pairs)]
    ppermute x3, waiting for transfers between devices: 25.7 us -> 4.26 us  [direct_gather(): got = lax.ppermute(piece, axis, pairs)]
    ppermute x3, starting transfers between devices: 23.2 us -> 3.86 us  [direct_scatter(): total = total + lax.ppermute(send, axis, pairs)]
    ppermute x3, waiting for transfers between devices: 5.92 us -> 1.58 us  [tree_broadcast(): got = lax.ppermute(value, axis, pairs)]
    ppermute x2, waiting for transfers between devices: 10.5 us -> 6.53 us  [xor_doubling(): got = lax.ppermute(piece, axis, [(i, i ^ step) for i in range(count)])]
    ppermute x3, starting transfers between devices: 14.2 us -> 11.6 us  [tree_broadcast(): got = lax.ppermute(value, axis, pairs)]
    ppermute x2, starting transfers between devices: 2.63 us -> 0.14 us  [xor_halving(): flat = keep + lax.ppermute(send, axis, pairs)]
  transfers between devices with their start and end apart: 20 -> 20, of which waited for: 10 -> 13; matrix products, arithmetic and copies ran while one was open for 19% -> 18% of each run, Pallas kernels for 0% -> 0%
where the time goes in v6:
time: 202 us; the launch traced here: 201 us
  waiting for transfers between devices  124 us (61%)
  starting transfers between devices  32.8 us (16%)
  matrix products  28.8 us (14%)
  other arithmetic  9.45 us (5%)
  local copies, waits for them, and re-layouts  4.2 us (2%)
    ppermute x3, waiting for transfers between devices, tree_reduce(): value = value + lax.ppermute(value, axis, pairs)  78.6 us
    ppermute x2, waiting for transfers between devices, xor_halving(): flat = keep + lax.ppermute(send, axis, pairs)  19.2 us
    ppermute x3, waiting for transfers between devices, direct_scatter(): total = total + lax.ppermute(send, axis, pairs)  13.3 us
    dot_general x18, matrix products, spatial_sum(): total = total + jnp.dot(piece, kernel, preferred_element_type=jnp.float32)  12.1 us
    ppermute x3, starting transfers between devices, tree_broadcast(): got = lax.ppermute(value, axis, pairs)  11.6 us
    ppermute x3, starting transfers between devices, direct_gather(): got = lax.ppermute(piece, axis, pairs)  7.76 us
    ppermute x2, waiting for transfers between devices, xor_doubling(): got = lax.ppermute(piece, axis, [(i, i ^ step) for i in range(count)])  6.53 us
    dot_general x9, matrix products, on_device(): lax.dot_general(piece, dpre, dims, preferred_element_type=jnp.float32)  4.41 us
  transfers between devices with their start and end apart: 20, of which 13 were waited for; matrix products, arithmetic and copies ran while one was open for 18% of the time, Pallas kernels for 0%

profile of v6, /device:TPU:0, one launch (start us, length us, event | category | flops | bytes accessed | tf_op | source)
XLA Modules:
  0.0 200.8 jit_solution(13008008294508604702)
XLA Ops:
  1.4 1.4 broadcast_multiply_fusion.1
  4.6 1.3 collective-permute-start.5
  6.8 8.7 %collective-permute-start.2 = (bf16[2,2,256,256]{3,2,1,0:T(8,128)(2,1)}, bf16[2,2,256,256]{3,2,1,0:T(8,128)(2,1)}, u32[]{:S(2)}, u32[]{:S(2)}) collective-permute-start(bf16[2,2,256,256]{3,2,1,0:T(8,128)(2,1)} %slice_bitcast_fusion), channel_id=1, source_target_pairs={{0,8},{1,9},{16,24},{17,25}} | collective-permute-start | bytes 1572872 | tf_op jit(solution)/shard_map/ppermute | solution.py:21
  15.5 1.3 collective-permute-start.7
  17.1 1.4 fusion.83
  19.0 1.1 broadcast_select_fusion.6
  24.5 1.6 collective-permute-done.2
  26.1 1.3 collective-permute-start.3
  27.4 1.6 multiply_convert_fusion.2
  29.0 3.1 %collective-permute-start.1 = (bf16[2,2,2,256,256]{4,3,2,1,0:T(8,128)(2,1)S(1)}, bf16[2,2,2,256,256]{4,3,2,1,0:T(8,128)(2,1)S(1)}, u32[]{:S(2)}, u32[]{:S(2)}) collective-permute-start(bf16[2,2,2,256,256]{4,3,2,1,0:T(8,128)(2,1)S(1)} %get-tuple-element.22), channel_id=1, source_target_pairs={{0,2},{2,4},{4,6},{6,8},{8,10},{10,12},{12,14},{1,3},{3,5},{5,7},{... | collective-permute-start | bytes 3145736 | tf_op jit(solution)/shard_map/ppermute | solution.py:10
  33.6 1.5 fusion.9
  35.1 2.3 %multiply_convert_fusion = bf16[2,2,2,256,256]{4,3,2,1,0:T(8,128)(2,1)S(1)} fusion(f32[2,2,2,256,256]{4,3,2,1,0:T(8,128)S(1)} %get-tuple-element.23, f32[2,2,2,256,256]{4,3,2,1,0:T(8,128)S(1)} %fusion.100, f32[2,2,2,256,256]{4,3,2,1,0:T(8,128)S(1)} %fusion.9, bf16[2,2,2,256,256]{4,3,2,1,0:T(8,128)(2,1)} %collective-permute-done.5, ...), kind=kOutput, calls=%fused_computation.22 | convolution fusion | flops 274202624 | bytes 8519680 | tf_op jit(solution)/shard_map/dot_general | solution.py:158
  39.8 15.5 %collective-permute-done.7 = f32[2,2,256,256]{3,2,1,0:T(8,128)} collective-permute-done((f32[2,2,256,256]{3,2,1,0:T(8,128)S(1)}, f32[2,2,256,256]{3,2,1,0:T(8,128)}, u32[]{:S(2)}, u32[]{:S(2)}) %collective-permute-start.7) | collective-permute-done | bytes 1048608 | tf_op jit(solution)/shard_map/ppermute | solution.py:32
  55.3 1.4 add.244
  56.7 1.3 collective-permute-start.8
  59.2 1.5 collective-permute-start.4
  60.7 1.7 convolution_bitcast_fusion.3
  63.4 1.5 convolution_bitcast_fusion.4
  64.9 39.7 %collective-permute-done.8 = f32[2,2,256,256]{3,2,1,0:T(8,128)S(1)} collective-permute-done((f32[2,2,256,256]{3,2,1,0:T(8,128)S(1)}, f32[2,2,256,256]{3,2,1,0:T(8,128)S(1)}, u32[]{:S(2)}, u32[]{:S(2)}) %collective-permute-start.8) | collective-permute-done | bytes 1048608 | tf_op jit(solution)/shard_map/ppermute | solution.py:32
  104.8 1.3 collective-permute-start.9
  107.8 23.4 %collective-permute-done.9 = f32[2,2,256,256]{3,2,1,0:T(8,128)S(1)} collective-permute-done((f32[2,2,256,256]{3,2,1,0:T(8,128)S(1)}, f32[2,2,256,256]{3,2,1,0:T(8,128)S(1)}, u32[]{:S(2)}, u32[]{:S(2)}) %collective-permute-start.9) | collective-permute-done | bytes 1048608 | tf_op jit(solution)/shard_map/ppermute | solution.py:32
  136.2 1.8 multiply_convert_fusion.1
  138.0 18.4 %collective-permute-done.11 = f32[832,256]{1,0:T(8,128)S(1)} collective-permute-done((f32[832,256]{1,0:T(8,128)S(1)}, f32[832,256]{1,0:T(8,128)S(1)}, u32[]{:S(2)}, u32[]{:S(2)}) %collective-permute-start.11) | collective-permute-done | bytes 852000 | tf_op jit(solution)/shard_map/ppermute | solution.py:46
  156.7 3.7 %collective-permute-start.14 = (f32[208,256]{1,0:T(8,128)S(1)}, f32[208,256]{1,0:T(8,128)S(1)}, u32[]{:S(2)}, u32[]{:S(2)}) collective-permute-start(f32[208,256]{1,0:T(8,128)S(1)} %get-tuple-element.16), channel_id=1, source_target_pairs={{0,12},{2,14},{4,0},{6,2},{8,4},{10,6},{12,8},{14,10},{1,13},{3,15... | collective-permute-start | bytes 638984 | tf_op jit(solution)/shard_map/ppermute | solution.py:72
  161.0 5.8 %collective-permute-done.12 = f32[208,256]{1,0:T(8,128)S(1)} collective-permute-done((f32[208,256]{1,0:T(8,128)S(1)}, f32[208,256]{1,0:T(8,128)S(1)}, u32[]{:S(2)}, u32[]{:S(2)}) %collective-permute-start.12) | collective-permute-done | bytes 213024 | tf_op jit(solution)/shard_map/ppermute | solution.py:72
  166.7 7.5 %collective-permute-done.13 = f32[208,256]{1,0:T(8,128)S(1)} collective-permute-done((f32[208,256]{1,0:T(8,128)S(1)}, f32[208,256]{1,0:T(8,128)S(1)}, u32[]{:S(2)}, u32[]{:S(2)}) %collective-permute-start.13) | collective-permute-done | bytes 213024 | tf_op jit(solution)/shard_map/ppermute | solution.py:72
  174.4 5.3 %collective-permute-start.15 = (bf16[208,256]{1,0:T(8,128)(2,1)S(1)}, bf16[208,256]{1,0:T(8,128)(2,1)S(1)}, u32[]{:S(2)}, u32[]{:S(2)}) collective-permute-start(bf16[208,256]{1,0:T(8,128)(2,1)S(1)} %get-tuple-element.10), channel_id=1, source_target_pairs={{0,4},{2,6},{4,8},{6,10},{8,12},{10,14},{12,0},{14,2},{1,5},{3,7},... | collective-permute-start | bytes 319496 | tf_op jit(solution)/shard_map/ppermute | solution.py:85
  180.2 2.4 %collective-permute-start.17 = (bf16[208,256]{1,0:T(8,128)(2,1)S(1)}, bf16[208,256]{1,0:T(8,128)(2,1)S(1)}, u32[]{:S(2)}, u32[]{:S(2)}) collective-permute-start(bf16[208,256]{1,0:T(8,128)(2,1)S(1)} %get-tuple-element.10), channel_id=1, source_target_pairs={{0,12},{2,14},{4,0},{6,2},{8,4},{10,6},{12,8},{14,10},{1,13},{3,15... | collective-permute-start | bytes 319496 | tf_op jit(solution)/shard_map/ppermute | solution.py:85
  182.7 4.1 %collective-permute-done.16 = bf16[208,256]{1,0:T(8,128)(2,1)S(1)} collective-permute-done((bf16[208,256]{1,0:T(8,128)(2,1)S(1)}, bf16[208,256]{1,0:T(8,128)(2,1)S(1)}, u32[]{:S(2)}, u32[]{:S(2)}) %collective-permute-start.16) | collective-permute-done | bytes 106528 | tf_op jit(solution)/shard_map/ppermute | solution.py:85
  188.7 6.4 %collective-permute-done.18 = bf16[832,256]{1,0:T(8,128)(2,1)S(1)} collective-permute-done((bf16[832,256]{1,0:T(8,128)(2,1)S(1)}, bf16[832,256]{1,0:T(8,128)(2,1)S(1)}, u32[]{:S(2)}, u32[]{:S(2)}) %collective-permute-start.18) | collective-permute-done | bytes 426016 | tf_op jit(solution)/shard_map/ppermute | solution.py:54
  195.4 2.2 %fusion.4 = bf16[2,2,2,256,256]{4,3,2,1,0:T(8,128)(2,1)} fusion(bf16[2,2,2,256,256]{4,3,2,1,0:T(8,128)(2,1)S(1)} %get-tuple-element.12, f32[2,2,2,256,256]{4,3,2,1,0:T(8,128)S(1)} %fusion.17, f32[2,2,2,256,256]{4,3,2,1,0:T(8,128)S(1)} %fusion.37, f32[2,2,2,256,256]{4,3,2,1,0:T(8,128)S(1)} %fusion.39, f32[2,2,2,256,256]{4,3,2,1,0:T(8,128)S(1)} %fusion.81, ...), kind=kOutput, calls=%fused_computation.13 | convolution fusion | flops 275775488 | bytes 21104128 | tf_op jit(solution)/shard_map/dot_general | solution.py:140
  198.2 1.1 slice.203
  (89 shorter events, 26.7 us)
Async XLA Ops:
  0.6 134.8 %copy-start = (bf16[256,256]{1,0:T(8,128)(2,1)S(1)}, bf16[256,256]{1,0:T(8,128)(2,1)}, u32[]{:S(2)}) copy-start(bf16[256,256]{1,0:T(8,128)(2,1)} %param.11) | copy-start | bytes 393220
  2.8 1.4 copy-start.3
  3.7 15.3 %collective-permute-start = (bf16[2,2,1,256,256]{4,3,2,1,0:T(8,128)(2,1)}, bf16[2,2,1,256,256]{4,3,2,1,0:T(8,128)(2,1)}, u32[]{:S(2)}, u32[]{:S(2)}) collective-permute-start(bf16[2,2,1,256,256]{4,3,2,1,0:T(8,128)(2,1)} %slice_select_fusion.1), channel_id=1, source_target_pairs={{0,1},{1,0},{2,3},{3,2},{4,5},{5,4},{6,7},{7,6},{8,9},{9,8},{10,11... | collective-permute-start | bytes 1572872 | tf_op jit(solution)/shard_map/ppermute | solution.py:183
  4.6 28.9 %collective-permute-start.5 = (bf16[2,2,2,256,256]{4,3,2,1,0:T(8,128)(2,1)S(1)}, bf16[2,2,2,256,256]{4,3,2,1,0:T(8,128)(2,1)}, u32[]{:S(2)}, u32[]{:S(2)}) collective-permute-start(bf16[2,2,2,256,256]{4,3,2,1,0:T(8,128)(2,1)S(1)} %get-tuple-element.12), channel_id=1, source_target_pairs={{2,0},{4,2},{6,4},{8,6},{10,8},{12,10},{14,12},{3,1},{5,3},{7,5},{... | collective-permute-start | bytes 3145736 | tf_op jit(solution)/shard_map/ppermute | solution.py:10
  6.8 19.3 %collective-permute-start.2 = (bf16[2,2,256,256]{3,2,1,0:T(8,128)(2,1)}, bf16[2,2,256,256]{3,2,1,0:T(8,128)(2,1)}, u32[]{:S(2)}, u32[]{:S(2)}) collective-permute-start(bf16[2,2,256,256]{3,2,1,0:T(8,128)(2,1)} %slice_bitcast_fusion), channel_id=1, source_target_pairs={{0,8},{1,9},{16,24},{17,25}} | collective-permute-start | bytes 1572872 | tf_op jit(solution)/shard_map/ppermute | solution.py:21
  15.5 39.8 %collective-permute-start.7 = (f32[2,2,256,256]{3,2,1,0:T(8,128)S(1)}, f32[2,2,256,256]{3,2,1,0:T(8,128)}, u32[]{:S(2)}, u32[]{:S(2)}) collective-permute-start(f32[2,2,256,256]{3,2,1,0:T(8,128)S(1)} %get-tuple-element.11), channel_id=1, source_target_pairs={{2,0},{6,4},{10,8},{14,12},{3,1},{7,5},{11,9},{15,13},{18,16},{22,... | collective-permute-start | bytes 3145736 | tf_op jit(solution)/shard_map/ppermute | solution.py:32
  17.1 1.4 copy-start.2
  20.1 1.3 copy-start.1
  26.1 32.9 %collective-permute-start.3 = (bf16[2,2,256,256]{3,2,1,0:T(8,128)(2,1)S(1)}, bf16[2,2,256,256]{3,2,1,0:T(8,128)(2,1)S(1)}, u32[]{:S(2)}, u32[]{:S(2)}) collective-permute-start(bf16[2,2,256,256]{3,2,1,0:T(8,128)(2,1)S(1)} %broadcast_select_fusion), channel_id=1, source_target_pairs={{0,4},{8,12},{1,5},{9,13},{16,20},{24,28},{17,21},{25,29}} | collective-permute-start | bytes 1572872 | tf_op jit(solution)/shard_map/ppermute | solution.py:21
  29.0 102.6 %collective-permute-start.1 = (bf16[2,2,2,256,256]{4,3,2,1,0:T(8,128)(2,1)S(1)}, bf16[2,2,2,256,256]{4,3,2,1,0:T(8,128)(2,1)S(1)}, u32[]{:S(2)}, u32[]{:S(2)}) collective-permute-start(bf16[2,2,2,256,256]{4,3,2,1,0:T(8,128)(2,1)S(1)} %get-tuple-element.22), channel_id=1, source_target_pairs={{0,2},{2,4},{4,6},{6,8},{8,10},{10,12},{12,14},{1,3},{3,5},{5,7},{... | collective-permute-start | bytes 3145736 | tf_op jit(solution)/shard_map/ppermute | solution.py:10
  56.7 48.0 %collective-permute-start.8 = (f32[2,2,256,256]{3,2,1,0:T(8,128)S(1)}, f32[2,2,256,256]{3,2,1,0:T(8,128)S(1)}, u32[]{:S(2)}, u32[]{:S(2)}) collective-permute-start(f32[2,2,256,256]{3,2,1,0:T(8,128)S(1)} %add.244), channel_id=1, source_target_pairs={{4,0},{12,8},{5,1},{13,9},{20,16},{28,24},{21,17},{29,25}} | collective-permute-start | bytes 3145736 | tf_op jit(solution)/shard_map/ppermute | solution.py:32
  59.2 47.6 %collective-permute-start.4 = (bf16[2,2,256,256]{3,2,1,0:T(8,128)(2,1)S(1)}, bf16[2,2,256,256]{3,2,1,0:T(8,128)(2,1)S(1)}, u32[]{:S(2)}, u32[]{:S(2)}) collective-permute-start(bf16[2,2,256,256]{3,2,1,0:T(8,128)(2,1)S(1)} %broadcast_select_fusion.1), channel_id=1, source_target_pairs={{0,2},{4,6},{8,10},{12,14},{1,3},{5,7},{9,11},{13,15},{16,18},{20,... | collective-permute-start | bytes 1572872 | tf_op jit(solution)/shard_map/ppermute | solution.py:21
  60.7 70.8 %collective-permute-start.6 = (bf16[2,2,1,256,256]{4,3,2,1,0:T(8,128)(2,1)S(1)}, bf16[2,2,1,256,256]{4,3,2,1,0:T(8,128)(2,1)S(1)}, u32[]{:S(2)}, u32[]{:S(2)}) collective-permute-start(bf16[2,2,1,256,256]{4,3,2,1,0:T(8,128)(2,1)S(1)} %slice_select_fusion), channel_id=1, source_target_pairs={{0,1},{1,0},{2,3},{3,2},{4,5},{5,4},{6,7},{7,6},{8,9},{9,8},{10,11... | collective-permute-start | bytes 1572872 | tf_op jit(solution)/shard_map/ppermute | solution.py:183
  104.8 26.3 %collective-permute-start.9 = (f32[2,2,256,256]{3,2,1,0:T(8,128)S(1)}, f32[2,2,256,256]{3,2,1,0:T(8,128)S(1)}, u32[]{:S(2)}, u32[]{:S(2)}) collective-permute-start(f32[2,2,256,256]{3,2,1,0:T(8,128)S(1)} %add.245), channel_id=1, source_target_pairs={{8,0},{9,1},{24,16},{25,17}} | collective-permute-start | bytes 3145736 | tf_op jit(solution)/shard_map/ppermute | solution.py:32
  131.4 3.7 %collective-permute-start.10 = (f32[1664,256]{1,0:T(8,128)S(1)}, f32[1664,256]{1,0:T(8,128)S(1)}, u32[]{:S(2)}, u32[]{:S(2)}) collective-permute-start(f32[1664,256]{1,0:T(8,128)S(1)} %constant_dynamic-slice_fusion.4), channel_id=1, source_target_pairs={{0,1},{1,0},{2,3},{3,2},{4,5},{5,4},{6,7},{7,6},{8,9},{9,8},{10,11... | collective-permute-start | bytes 5111816 | tf_op jit(solution)/shard_map/ppermute | solution.py:46
  135.4 21.1 %collective-permute-start.11 = (f32[832,256]{1,0:T(8,128)S(1)}, f32[832,256]{1,0:T(8,128)S(1)}, u32[]{:S(2)}, u32[]{:S(2)}) collective-permute-start(f32[832,256]{1,0:T(8,128)S(1)} %constant_dynamic-slice_fusion.3), channel_id=1, source_target_pairs={{0,2},{2,0},{4,6},{6,4},{8,10},{10,8},{12,14},{14,12},{1,3},{3,1},... | collective-permute-start | bytes 2555912 | tf_op jit(solution)/shard_map/ppermute | solution.py:46
  156.6 10.1 %collective-permute-start.12 = (f32[208,256]{1,0:T(8,128)S(1)}, f32[208,256]{1,0:T(8,128)S(1)}, u32[]{:S(2)}, u32[]{:S(2)}) collective-permute-start(f32[208,256]{1,0:T(8,128)S(1)} %get-tuple-element.15), channel_id=1, source_target_pairs={{0,4},{2,6},{4,8},{6,10},{8,12},{10,14},{12,0},{14,2},{1,5},{3,7},... | collective-permute-start | bytes 638984 | tf_op jit(solution)/shard_map/ppermute | solution.py:72
  156.7 17.6 %collective-permute-start.13 = (f32[208,256]{1,0:T(8,128)S(1)}, f32[208,256]{1,0:T(8,128)S(1)}, u32[]{:S(2)}, u32[]{:S(2)}) collective-permute-start(f32[208,256]{1,0:T(8,128)S(1)} %get-tuple-element.17), channel_id=1, source_target_pairs={{0,8},{2,10},{4,12},{6,14},{8,0},{10,2},{12,4},{14,6},{1,9},{3,11}... | collective-permute-start | bytes 638984 | tf_op jit(solution)/shard_map/ppermute | solution.py:72
  156.7 17.5 %collective-permute-start.14 = (f32[208,256]{1,0:T(8,128)S(1)}, f32[208,256]{1,0:T(8,128)S(1)}, u32[]{:S(2)}, u32[]{:S(2)}) collective-permute-start(f32[208,256]{1,0:T(8,128)S(1)} %get-tuple-element.16), channel_id=1, source_target_pairs={{0,12},{2,14},{4,0},{6,2},{8,4},{10,6},{12,8},{14,10},{1,13},{3,15... | collective-permute-start | bytes 638984 | tf_op jit(solution)/shard_map/ppermute | solution.py:72
  174.4 8.4 %collective-permute-start.15 = (bf16[208,256]{1,0:T(8,128)(2,1)S(1)}, bf16[208,256]{1,0:T(8,128)(2,1)S(1)}, u32[]{:S(2)}, u32[]{:S(2)}) collective-permute-start(bf16[208,256]{1,0:T(8,128)(2,1)S(1)} %get-tuple-element.10), channel_id=1, source_target_pairs={{0,4},{2,6},{4,8},{6,10},{8,12},{10,14},{12,0},{14,2},{1,5},{3,7},... | collective-permute-start | bytes 319496 | tf_op jit(solution)/shard_map/ppermute | solution.py:85
  180.2 6.7 %collective-permute-start.16 = (bf16[208,256]{1,0:T(8,128)(2,1)S(1)}, bf16[208,256]{1,0:T(8,128)(2,1)S(1)}, u32[]{:S(2)}, u32[]{:S(2)}) collective-permute-start(bf16[208,256]{1,0:T(8,128)(2,1)S(1)} %get-tuple-element.10), channel_id=1, source_target_pairs={{0,8},{2,10},{4,12},{6,14},{8,0},{10,2},{12,4},{14,6},{1,9},{3,11}... | collective-permute-start | bytes 319496 | tf_op jit(solution)/shard_map/ppermute | solution.py:85
  180.2 6.6 %collective-permute-start.17 = (bf16[208,256]{1,0:T(8,128)(2,1)S(1)}, bf16[208,256]{1,0:T(8,128)(2,1)S(1)}, u32[]{:S(2)}, u32[]{:S(2)}) collective-permute-start(bf16[208,256]{1,0:T(8,128)(2,1)S(1)} %get-tuple-element.10), channel_id=1, source_target_pairs={{0,12},{2,14},{4,0},{6,2},{8,4},{10,6},{12,8},{14,10},{1,13},{3,15... | collective-permute-start | bytes 319496 | tf_op jit(solution)/shard_map/ppermute | solution.py:85
  186.9 8.2 %collective-permute-start.18 = (bf16[832,256]{1,0:T(8,128)(2,1)S(1)}, bf16[832,256]{1,0:T(8,128)(2,1)S(1)}, u32[]{:S(2)}, u32[]{:S(2)}) collective-permute-start(bf16[832,256]{1,0:T(8,128)(2,1)S(1)} %bitcast.255), channel_id=1, source_target_pairs={{0,2},{2,0},{4,6},{6,4},{8,10},{10,8},{12,14},{14,12},{1,3},{3,1},... | collective-permute-start | bytes 1277960 | tf_op jit(solution)/shard_map/ppermute | solution.py:54
  195.3 2.4 %collective-permute-start.19 = (bf16[1664,256]{1,0:T(8,128)(2,1)S(1)}, bf16[1664,256]{1,0:T(8,128)(2,1)S(1)}, u32[]{:S(2)}, u32[]{:S(2)}) collective-permute-start(bf16[1664,256]{1,0:T(8,128)(2,1)S(1)} %maximum_select_fusion.1), channel_id=1, source_target_pairs={{0,1},{1,0},{2,3},{3,2},{4,5},{5,4},{6,7},{7,6},{8,9},{9,8},{10,11... | collective-permute-start | bytes 2555912 | tf_op jit(solution)/shard_map/ppermute | solution.py:54

commit v7 on v5

--- a/solution.py
+++ b/solution.py
@@ -24,9 +24,8 @@
     return value
 
 
-def tree_reduce(value, axis):
-    count = lax.axis_size(axis)
-    step = 1
+def tree_reduce(value, axis, step=1):
+    count = lax.axis_size(axis)
     while step < count:
         pairs = [(i + step, i) for i in range(0, count, 2 * step) if i + step < count]
         value = value + lax.ppermute(value, axis, pairs)
@@ -200,8 +199,12 @@
     cot = cotangent * mask
     first = tree_broadcast(masked[:, 0], "space")
     cot_local = jnp.sum(cot, axis=1, dtype=jnp.float32)
-    cot_sum = tree_reduce(cot_local, "space")
     later = shifted(cot, "space", -1)
+    if lax.axis_size("space") % 2 == 0:
+        cot_pair = cot_local + jnp.sum(later, axis=1, dtype=jnp.float32)
+        cot_sum = tree_reduce(cot_pair, "space", 2)
+    else:
+        cot_sum = tree_reduce(cot_local, "space")
     rows_pad = row_halo(masked)
     padded = jnp.pad(rows_pad, ((0, 0), (0, 0), (0, 0), (1, 1), (0, 0)))
     pre = spatial_sum(padded, spatial_weight, False)

time: 184 us -> 173 us (0.940)
  starting transfers between devices: 56.6 us -> 42.3 us
  waiting for transfers between devices: 82.3 us -> 91.2 us
  matrix products: 28.7 us -> 24.2 us
    ppermute x3, waiting for transfers between devices: 5.92 us -> 23.3 us  [tree_broadcast(): got = lax.ppermute(value, axis, pairs)]
    ppermute x3, starting transfers between devices: 23.2 us -> 11.5 us  [direct_scatter(): total = total + lax.ppermute(send, axis, pairs)]
    ppermute x3 -> x2, waiting for transfers between devices: 9.66 us -> 0.01 us  [tree_reduce(): value = value + lax.ppermute(value, axis, pairs)]
    dot_general x3, matrix products: 3.71 us -> 1.43 us  [lag_grads(): lax.dot_general(act, padded_cot[:, lag:lag + count], dims, preferred_elem...]
    dot_general x3, matrix products: 4.24 us -> 2.01 us  [lag_backward(): jnp.dot(padded_cot[:, lag:lag + count], weights[lag].T, preferred_element...]
    ppermute x3 -> x2, starting transfers between devices: 3.86 us -> 2.8 us  [tree_reduce(): value = value + lax.ppermute(value, axis, pairs)]
  transfers between devices with their start and end apart: 20 -> 19, of which waited for: 10 -> 10; matrix products, arithmetic and copies ran while one was open for 19% -> 18% of each run, Pallas kernels for 0% -> 0%
where the time goes in v7:
time: 173 us; the launch traced here: 172 us
  waiting for transfers between devices  91.2 us (53%)
  starting transfers between devices  42.3 us (24%)
  matrix products  24.2 us (14%)
  other arithmetic  9.24 us (5%)
  local copies, waits for them, and re-layouts  4.1 us (2%)
    ppermute x3, waiting for transfers between devices, direct_gather(): got = lax.ppermute(piece, axis, pairs)  25.7 us
    ppermute x3, waiting for transfers between devices, tree_broadcast(): got = lax.ppermute(value, axis, pairs)  23.3 us
    ppermute x2, waiting for transfers between devices, xor_halving(): flat = keep + lax.ppermute(send, axis, pairs)  18.2 us
    ppermute x3, starting transfers between devices, tree_broadcast(): got = lax.ppermute(value, axis, pairs)  14.3 us
    ppermute x3, waiting for transfers between devices, direct_scatter(): total = total + lax.ppermute(send, axis, pairs)  12.1 us
    dot_general x18, matrix products, spatial_sum(): total = total + jnp.dot(piece, kernel, preferred_element_type=jnp.float32)  12 us
    ppermute x3, starting transfers between devices, direct_scatter(): total = total + lax.ppermute(send, axis, pairs)  11.5 us
    ppermute x2, waiting for transfers between devices, xor_doubling(): got = lax.ppermute(piece, axis, [(i, i ^ step) for i in range(count)])  10.5 us
  transfers between devices with their start and end apart: 19, of which 10 were waited for; matrix products, arithmetic and copies ran while one was open for 18% of the time, Pallas kernels for 0%

profile of v7, /device:TPU:0, one launch (start us, length us, event | category | flops | bytes accessed | tf_op | source)
XLA Modules:
  0.0 172.2 jit_solution(3040833817475502972)
XLA Ops:
  1.5 1.4 broadcast_multiply_fusion.1
  2.9 0.9 slice_select_fusion.1
  4.2 1.4 convert_reduce_fusion
  5.6 1.3 collective-permute-start.5
  7.7 8.3 %collective-permute-start.2 = (bf16[2,2,256,256]{3,2,1,0:T(8,128)(2,1)}, bf16[2,2,256,256]{3,2,1,0:T(8,128)(2,1)}, u32[]{:S(2)}, u32[]{:S(2)}) collective-permute-start(bf16[2,2,256,256]{3,2,1,0:T(8,128)(2,1)} %slice_bitcast_fusion), channel_id=1, source_target_pairs={{0,8},{1,9},{16,24},{17,25}} | collective-permute-start | bytes 1572872 | tf_op jit(solution)/shard_map/ppermute | solution.py:21
  16.0 1.4 fusion.86
  17.8 1.1 broadcast_select_fusion.6
  19.0 0.8 select_maximum_fusion.2
  23.3 3.7 %collective-permute-done.2 = bf16[2,2,256,256]{3,2,1,0:T(8,128)(2,1)} collective-permute-done((bf16[2,2,256,256]{3,2,1,0:T(8,128)(2,1)}, bf16[2,2,256,256]{3,2,1,0:T(8,128)(2,1)}, u32[]{:S(2)}, u32[]{:S(2)}) %collective-permute-start.2) | collective-permute-done | bytes 524320 | tf_op jit(solution)/shard_map/ppermute | solution.py:21
  27.1 1.3 collective-permute-start.3
  28.4 1.4 multiply_convert_fusion.2
  29.9 1.5 collective-permute-start.1
  32.3 1.4 collective-permute-done.5
  34.2 1.1 multiply_convert_fusion
  39.5 4.7 %collective-permute-start.4 = (bf16[2,2,256,256]{3,2,1,0:T(8,128)(2,1)S(1)}, bf16[2,2,256,256]{3,2,1,0:T(8,128)(2,1)S(1)}, u32[]{:S(2)}, u32[]{:S(2)}) collective-permute-start(bf16[2,2,256,256]{3,2,1,0:T(8,128)(2,1)S(1)} %broadcast_select_fusion.1), channel_id=1, source_target_pairs={{0,2},{4,6},{8,10},{12,14},{1,3},{5,7},{9,11},{13,15},{16,18},{20,... | collective-permute-start | bytes 1572872 | tf_op jit(solution)/shard_map/ppermute | solution.py:21
  44.6 1.5 collective-permute-start.7
  48.1 19.5 %collective-permute-done.4 = bf16[2,2,256,256]{3,2,1,0:T(8,128)(2,1)S(1)} collective-permute-done((bf16[2,2,256,256]{3,2,1,0:T(8,128)(2,1)S(1)}, bf16[2,2,256,256]{3,2,1,0:T(8,128)(2,1)S(1)}, u32[]{:S(2)}, u32[]{:S(2)}) %collective-permute-start.4) | collective-permute-done | bytes 524320 | tf_op jit(solution)/shard_map/ppermute | solution.py:21
  69.7 0.9 select_maximum_fusion
  71.1 1.7 %multiply_convert_fusion.1 = bf16[2,2,2,256,256]{4,3,2,1,0:T(8,128)(2,1)} fusion(f32[2,2,2,256,256]{4,3,2,1,0:T(8,128)S(1)} %fusion.105, f32[2,2,2,256,256]{4,3,2,1,0:T(8,128)S(1)} %fusion.5, bf16[2,2,2,256,256]{4,3,2,1,0:T(8,128)(2,1)S(1)} %broadcast_multiply_fusion.1, f32[2,2]{1,0:T(2,128)S(1)} %get-tuple-element.9, f32[2,2,256,256]{3,2,1,0:T(8,128)S(1)} %fusion.69, ...), kind=kOutput, calls=%fused_computation.24 | convolution fusion | flops 272105472 | bytes 8520704 | tf_op jit(solution)/shard_map/dot_general | solution.py:146
  73.1 2.6 %collective-permute-start.10 = (f32[832,256]{1,0:T(8,128)S(1)}, f32[832,256]{1,0:T(8,128)S(1)}, u32[]{:S(2)}, u32[]{:S(2)}) collective-permute-start(f32[832,256]{1,0:T(8,128)S(1)} %constant_dynamic-slice_fusion.3), channel_id=1, source_target_pairs={{0,2},{2,0},{4,6},{6,4},{8,10},{10,8},{12,14},{14,12},{1,3},{3,1},... | collective-permute-start | bytes 2555912 | tf_op jit(solution)/shard_map/ppermute | solution.py:45
  77.1 18.1 %collective-permute-done.10 = f32[832,256]{1,0:T(8,128)S(1)} collective-permute-done((f32[832,256]{1,0:T(8,128)S(1)}, f32[832,256]{1,0:T(8,128)S(1)}, u32[]{:S(2)}, u32[]{:S(2)}) %collective-permute-start.10) | collective-permute-done | bytes 852000 | tf_op jit(solution)/shard_map/ppermute | solution.py:45
  95.4 8.9 %collective-permute-start.11 = (f32[208,256]{1,0:T(8,128)S(1)}, f32[208,256]{1,0:T(8,128)S(1)}, u32[]{:S(2)}, u32[]{:S(2)}) collective-permute-start(f32[208,256]{1,0:T(8,128)S(1)} %get-tuple-element.11), channel_id=1, source_target_pairs={{0,4},{2,6},{4,8},{6,10},{8,12},{10,14},{12,0},{14,2},{1,5},{3,7},... | collective-permute-start | bytes 638984 | tf_op jit(solution)/shard_map/ppermute | solution.py:71
  104.3 2.6 %collective-permute-start.12 = (f32[208,256]{1,0:T(8,128)S(1)}, f32[208,256]{1,0:T(8,128)S(1)}, u32[]{:S(2)}, u32[]{:S(2)}) collective-permute-start(f32[208,256]{1,0:T(8,128)S(1)} %get-tuple-element.13), channel_id=1, source_target_pairs={{0,8},{2,10},{4,12},{6,14},{8,0},{10,2},{12,4},{14,6},{1,9},{3,11}... | collective-permute-start | bytes 638984 | tf_op jit(solution)/shard_map/ppermute | solution.py:71
  107.5 1.3 collective-permute-start.8
  108.8 3.7 %collective-permute-done.11 = f32[208,256]{1,0:T(8,128)S(1)} collective-permute-done((f32[208,256]{1,0:T(8,128)S(1)}, f32[208,256]{1,0:T(8,128)S(1)}, u32[]{:S(2)}, u32[]{:S(2)}) %collective-permute-start.11) | collective-permute-done | bytes 213024 | tf_op jit(solution)/shard_map/ppermute | solution.py:71
  112.5 8.4 %collective-permute-done.12 = f32[208,256]{1,0:T(8,128)S(1)} collective-permute-done((f32[208,256]{1,0:T(8,128)S(1)}, f32[208,256]{1,0:T(8,128)S(1)}, u32[]{:S(2)}, u32[]{:S(2)}) %collective-permute-start.12) | collective-permute-done | bytes 213024 | tf_op jit(solution)/shard_map/ppermute | solution.py:71
  121.0 5.2 %collective-permute-start.14 = (bf16[208,256]{1,0:T(8,128)(2,1)S(1)}, bf16[208,256]{1,0:T(8,128)(2,1)S(1)}, u32[]{:S(2)}, u32[]{:S(2)}) collective-permute-start(bf16[208,256]{1,0:T(8,128)(2,1)S(1)} %get-tuple-element.6), channel_id=1, source_target_pairs={{0,4},{2,6},{4,8},{6,10},{8,12},{10,14},{12,0},{14,2},{1,5},{3,7},... | collective-permute-start | bytes 319496 | tf_op jit(solution)/shard_map/ppermute | solution.py:84
  126.9 2.2 %collective-permute-start.16 = (bf16[208,256]{1,0:T(8,128)(2,1)S(1)}, bf16[208,256]{1,0:T(8,128)(2,1)S(1)}, u32[]{:S(2)}, u32[]{:S(2)}) collective-permute-start(bf16[208,256]{1,0:T(8,128)(2,1)S(1)} %get-tuple-element.6), channel_id=1, source_target_pairs={{0,12},{2,14},{4,0},{6,2},{8,4},{10,6},{12,8},{14,10},{1,13},{3,15... | collective-permute-start | bytes 319496 | tf_op jit(solution)/shard_map/ppermute | solution.py:84
  129.6 25.2 %collective-permute-done.15 = bf16[208,256]{1,0:T(8,128)(2,1)S(1)} collective-permute-done((bf16[208,256]{1,0:T(8,128)(2,1)S(1)}, bf16[208,256]{1,0:T(8,128)(2,1)S(1)}, u32[]{:S(2)}, u32[]{:S(2)}) %collective-permute-start.15) | collective-permute-done | bytes 106528 | tf_op jit(solution)/shard_map/ppermute | solution.py:84
  156.0 10.5 %collective-permute-done.17 = bf16[832,256]{1,0:T(8,128)(2,1)S(1)} collective-permute-done((bf16[832,256]{1,0:T(8,128)(2,1)S(1)}, bf16[832,256]{1,0:T(8,128)(2,1)S(1)}, u32[]{:S(2)}, u32[]{:S(2)}) %collective-permute-start.17) | collective-permute-done | bytes 426016 | tf_op jit(solution)/shard_map/ppermute | solution.py:53
  166.8 2.3 %fusion.4 = bf16[2,2,2,256,256]{4,3,2,1,0:T(8,128)(2,1)} fusion(bf16[2,2,2,256,256]{4,3,2,1,0:T(8,128)(2,1)S(1)} %get-tuple-element.8, f32[2,2,2,256,256]{4,3,2,1,0:T(8,128)S(1)} %fusion.17, f32[2,2,2,256,256]{4,3,2,1,0:T(8,128)S(1)} %fusion.35, f32[2,2,2,256,256]{4,3,2,1,0:T(8,128)S(1)} %fusion.37, f32[2,2,2,256,256]{4,3,2,1,0:T(8,128)S(1)} %fusion.84, ...), kind=kOutput, calls=%fused_computation.13 | convolution fusion | flops 275775488 | bytes 21104128 | tf_op jit(solution)/shard_map/dot_general | solution.py:139
  169.6 1.1 slice.203
  (89 shorter events, 23.7 us)
Async XLA Ops:
  0.6 68.8 %copy-start = (bf16[256,256]{1,0:T(8,128)(2,1)S(1)}, bf16[256,256]{1,0:T(8,128)(2,1)}, u32[]{:S(2)}) copy-start(bf16[256,256]{1,0:T(8,128)(2,1)} %param.11) | copy-start | bytes 393220
  0.6 3.5 %copy-start.4 = (bf16[2,2,2,256,256]{4,3,2,1,0:T(8,128)(2,1)S(1)}, bf16[2,2,2,256,256]{4,3,2,1,0:T(8,128)(2,1)}, u32[]{:S(2)}) copy-start(bf16[2,2,2,256,256]{4,3,2,1,0:T(8,128)(2,1)} %param.7) | copy-start | bytes 3145732
  3.7 14.1 %collective-permute-start = (bf16[2,2,1,256,256]{4,3,2,1,0:T(8,128)(2,1)}, bf16[2,2,1,256,256]{4,3,2,1,0:T(8,128)(2,1)}, u32[]{:S(2)}, u32[]{:S(2)}) collective-permute-start(bf16[2,2,1,256,256]{4,3,2,1,0:T(8,128)(2,1)} %slice_select_fusion.1), channel_id=1, source_target_pairs={{0,1},{1,0},{2,3},{3,2},{4,5},{5,4},{6,7},{7,6},{8,9},{9,8},{10,11... | collective-permute-start | bytes 1572872 | tf_op jit(solution)/shard_map/ppermute | solution.py:182
  5.6 28.2 %collective-permute-start.5 = (bf16[2,2,2,256,256]{4,3,2,1,0:T(8,128)(2,1)S(1)}, bf16[2,2,2,256,256]{4,3,2,1,0:T(8,128)(2,1)S(1)}, u32[]{:S(2)}, u32[]{:S(2)}) collective-permute-start(bf16[2,2,2,256,256]{4,3,2,1,0:T(8,128)(2,1)S(1)} %get-tuple-element.8), channel_id=1, source_target_pairs={{2,0},{4,2},{6,4},{8,6},{10,8},{12,10},{14,12},{3,1},{5,3},{7,5},{... | collective-permute-start | bytes 3145736 | tf_op jit(solution)/shard_map/ppermute | solution.py:10
  7.7 19.4 %collective-permute-start.2 = (bf16[2,2,256,256]{3,2,1,0:T(8,128)(2,1)}, bf16[2,2,256,256]{3,2,1,0:T(8,128)(2,1)}, u32[]{:S(2)}, u32[]{:S(2)}) collective-permute-start(bf16[2,2,256,256]{3,2,1,0:T(8,128)(2,1)} %slice_bitcast_fusion), channel_id=1, source_target_pairs={{0,8},{1,9},{16,24},{17,25}} | collective-permute-start | bytes 1572872 | tf_op jit(solution)/shard_map/ppermute | solution.py:21
  16.0 1.4 copy-start.3
  19.0 1.3 copy-start.2
  27.1 12.3 %collective-permute-start.3 = (bf16[2,2,256,256]{3,2,1,0:T(8,128)(2,1)S(1)}, bf16[2,2,256,256]{3,2,1,0:T(8,128)(2,1)S(1)}, u32[]{:S(2)}, u32[]{:S(2)}) collective-permute-start(bf16[2,2,256,256]{3,2,1,0:T(8,128)(2,1)S(1)} %broadcast_select_fusion), channel_id=1, source_target_pairs={{0,4},{8,12},{1,5},{9,13},{16,20},{24,28},{17,21},{25,29}} | collective-permute-start | bytes 1572872 | tf_op jit(solution)/shard_map/ppermute | solution.py:21
  29.9 39.1 %collective-permute-start.1 = (bf16[2,2,2,256,256]{4,3,2,1,0:T(8,128)(2,1)S(1)}, bf16[2,2,2,256,256]{4,3,2,1,0:T(8,128)(2,1)S(1)}, u32[]{:S(2)}, u32[]{:S(2)}) collective-permute-start(bf16[2,2,2,256,256]{4,3,2,1,0:T(8,128)(2,1)S(1)} %get-tuple-element.18), channel_id=1, source_target_pairs={{0,2},{2,4},{4,6},{6,8},{8,10},{10,12},{12,14},{1,3},{3,5},{5,7},{... | collective-permute-start | bytes 3145736 | tf_op jit(solution)/shard_map/ppermute | solution.py:10
  39.3 5.1 %copy-start.1 = (f32[2,2,256,256]{3,2,1,0:T(8,128)S(1)}, f32[2,2,256,256]{3,2,1,0:T(8,128)}, u32[]{:S(2)}) copy-start(f32[2,2,256,256]{3,2,1,0:T(8,128)} %get-tuple-element.7) | copy-start | bytes 3145732
  39.5 28.2 %collective-permute-start.4 = (bf16[2,2,256,256]{3,2,1,0:T(8,128)(2,1)S(1)}, bf16[2,2,256,256]{3,2,1,0:T(8,128)(2,1)S(1)}, u32[]{:S(2)}, u32[]{:S(2)}) collective-permute-start(bf16[2,2,256,256]{3,2,1,0:T(8,128)(2,1)S(1)} %broadcast_select_fusion.1), channel_id=1, source_target_pairs={{0,2},{4,6},{8,10},{12,14},{1,3},{5,7},{9,11},{13,15},{16,18},{20,... | collective-permute-start | bytes 1572872 | tf_op jit(solution)/shard_map/ppermute | solution.py:21
  44.2 24.7 %collective-permute-start.6 = (bf16[2,2,1,256,256]{4,3,2,1,0:T(8,128)(2,1)S(1)}, bf16[2,2,1,256,256]{4,3,2,1,0:T(8,128)(2,1)S(1)}, u32[]{:S(2)}, u32[]{:S(2)}) collective-permute-start(bf16[2,2,1,256,256]{4,3,2,1,0:T(8,128)(2,1)S(1)} %slice_select_fusion), channel_id=1, source_target_pairs={{0,1},{1,0},{2,3},{3,2},{4,5},{5,4},{6,7},{7,6},{8,9},{9,8},{10,11... | collective-permute-start | bytes 1572872 | tf_op jit(solution)/shard_map/ppermute | solution.py:182
  44.6 62.8 %collective-permute-start.7 = (f32[2,2,256,256]{3,2,1,0:T(8,128)S(1)}, f32[2,2,256,256]{3,2,1,0:T(8,128)S(1)}, u32[]{:S(2)}, u32[]{:S(2)}) collective-permute-start(f32[2,2,256,256]{3,2,1,0:T(8,128)S(1)} %add.244), channel_id=1, source_target_pairs={{4,0},{12,8},{5,1},{13,9},{20,16},{28,24},{21,17},{29,25}} | collective-permute-start | bytes 3145736 | tf_op jit(solution)/shard_map/ppermute | solution.py:31
  68.8 4.0 %collective-permute-start.9 = (f32[1664,256]{1,0:T(8,128)S(1)}, f32[1664,256]{1,0:T(8,128)S(1)}, u32[]{:S(2)}, u32[]{:S(2)}) collective-permute-start(f32[1664,256]{1,0:T(8,128)S(1)} %constant_dynamic-slice_fusion.4), channel_id=1, source_target_pairs={{0,1},{1,0},{2,3},{3,2},{4,5},{5,4},{6,7},{7,6},{8,9},{9,8},{10,11... | collective-permute-start | bytes 5111816 | tf_op jit(solution)/shard_map/ppermute | solution.py:45
  73.1 22.1 %collective-permute-start.10 = (f32[832,256]{1,0:T(8,128)S(1)}, f32[832,256]{1,0:T(8,128)S(1)}, u32[]{:S(2)}, u32[]{:S(2)}) collective-permute-start(f32[832,256]{1,0:T(8,128)S(1)} %constant_dynamic-slice_fusion.3), channel_id=1, source_target_pairs={{0,2},{2,0},{4,6},{6,4},{8,10},{10,8},{12,14},{14,12},{1,3},{3,1},... | collective-permute-start | bytes 2555912 | tf_op jit(solution)/shard_map/ppermute | solution.py:45
  95.4 17.1 %collective-permute-start.11 = (f32[208,256]{1,0:T(8,128)S(1)}, f32[208,256]{1,0:T(8,128)S(1)}, u32[]{:S(2)}, u32[]{:S(2)}) collective-permute-start(f32[208,256]{1,0:T(8,128)S(1)} %get-tuple-element.11), channel_id=1, source_target_pairs={{0,4},{2,6},{4,8},{6,10},{8,12},{10,14},{12,0},{14,2},{1,5},{3,7},... | collective-permute-start | bytes 638984 | tf_op jit(solution)/shard_map/ppermute | solution.py:71
  104.3 16.6 %collective-permute-start.12 = (f32[208,256]{1,0:T(8,128)S(1)}, f32[208,256]{1,0:T(8,128)S(1)}, u32[]{:S(2)}, u32[]{:S(2)}) collective-permute-start(f32[208,256]{1,0:T(8,128)S(1)} %get-tuple-element.13), channel_id=1, source_target_pairs={{0,8},{2,10},{4,12},{6,14},{8,0},{10,2},{12,4},{14,6},{1,9},{3,11}... | collective-permute-start | bytes 638984 | tf_op jit(solution)/shard_map/ppermute | solution.py:71
  106.9 14.0 %collective-permute-start.13 = (f32[208,256]{1,0:T(8,128)S(1)}, f32[208,256]{1,0:T(8,128)S(1)}, u32[]{:S(2)}, u32[]{:S(2)}) collective-permute-start(f32[208,256]{1,0:T(8,128)S(1)} %get-tuple-element.12), channel_id=1, source_target_pairs={{0,12},{2,14},{4,0},{6,2},{8,4},{10,6},{12,8},{14,10},{1,13},{3,15... | collective-permute-start | bytes 638984 | tf_op jit(solution)/shard_map/ppermute | solution.py:71
  107.5 47.8 %collective-permute-start.8 = (f32[2,2,256,256]{3,2,1,0:T(8,128)S(1)}, f32[2,2,256,256]{3,2,1,0:T(8,128)S(1)}, u32[]{:S(2)}, u32[]{:S(2)}) collective-permute-start(f32[2,2,256,256]{3,2,1,0:T(8,128)S(1)} %add.245), channel_id=1, source_target_pairs={{8,0},{9,1},{24,16},{25,17}} | collective-permute-start | bytes 3145736 | tf_op jit(solution)/shard_map/ppermute | solution.py:31
  121.0 8.5 %collective-permute-start.14 = (bf16[208,256]{1,0:T(8,128)(2,1)S(1)}, bf16[208,256]{1,0:T(8,128)(2,1)S(1)}, u32[]{:S(2)}, u32[]{:S(2)}) collective-permute-start(bf16[208,256]{1,0:T(8,128)(2,1)S(1)} %get-tuple-element.6), channel_id=1, source_target_pairs={{0,4},{2,6},{4,8},{6,10},{8,12},{10,14},{12,0},{14,2},{1,5},{3,7},... | collective-permute-start | bytes 319496 | tf_op jit(solution)/shard_map/ppermute | solution.py:84
  126.6 28.1 %collective-permute-start.15 = (bf16[208,256]{1,0:T(8,128)(2,1)S(1)}, bf16[208,256]{1,0:T(8,128)(2,1)S(1)}, u32[]{:S(2)}, u32[]{:S(2)}) collective-permute-start(bf16[208,256]{1,0:T(8,128)(2,1)S(1)} %get-tuple-element.6), channel_id=1, source_target_pairs={{0,8},{2,10},{4,12},{6,14},{8,0},{10,2},{12,4},{14,6},{1,9},{3,11}... | collective-permute-start | bytes 319496 | tf_op jit(solution)/shard_map/ppermute | solution.py:84
  126.9 27.9 %collective-permute-start.16 = (bf16[208,256]{1,0:T(8,128)(2,1)S(1)}, bf16[208,256]{1,0:T(8,128)(2,1)S(1)}, u32[]{:S(2)}, u32[]{:S(2)}) collective-permute-start(bf16[208,256]{1,0:T(8,128)(2,1)S(1)} %get-tuple-element.6), channel_id=1, source_target_pairs={{0,12},{2,14},{4,0},{6,2},{8,4},{10,6},{12,8},{14,10},{1,13},{3,15... | collective-permute-start | bytes 319496 | tf_op jit(solution)/shard_map/ppermute | solution.py:84
  154.8 11.7 %collective-permute-start.17 = (bf16[832,256]{1,0:T(8,128)(2,1)S(1)}, bf16[832,256]{1,0:T(8,128)(2,1)S(1)}, u32[]{:S(2)}, u32[]{:S(2)}) collective-permute-start(bf16[832,256]{1,0:T(8,128)(2,1)S(1)} %bitcast.256), channel_id=1, source_target_pairs={{0,2},{2,0},{4,6},{6,4},{8,10},{10,8},{12,14},{14,12},{1,3},{3,1},... | collective-permute-start | bytes 1277960 | tf_op jit(solution)/shard_map/ppermute | solution.py:53
  166.7 2.4 %collective-permute-start.18 = (bf16[1664,256]{1,0:T(8,128)(2,1)S(1)}, bf16[1664,256]{1,0:T(8,128)(2,1)S(1)}, u32[]{:S(2)}, u32[]{:S(2)}) collective-permute-start(bf16[1664,256]{1,0:T(8,128)(2,1)S(1)} %maximum_select_fusion.1), channel_id=1, source_target_pairs={{0,1},{1,0},{2,3},{3,2},{4,5},{5,4},{6,7},{7,6},{8,9},{9,8},{10,11... | collective-permute-start | bytes 2555912 | tf_op jit(solution)/shard_map/ppermute | solution.py:53

commit v8 on v7

--- a/solution.py
+++ b/solution.py
@@ -14,13 +14,11 @@
     count = lax.axis_size(axis)
     me = lax.axis_index(axis)
     step = 1
-    while step * 2 < count:
+    while step < count:
+        pairs = [(i, i + step) for i in range(step) if i + step < count]
+        got = lax.ppermute(value, axis, pairs)
+        value = jnp.where((me >= step) & (me < 2 * step), got, value)
         step *= 2
-    while step >= 1 and count > 1:
-        pairs = [(i, i + step) for i in range(0, count, 2 * step) if i + step < count]
-        got = lax.ppermute(value, axis, pairs)
-        value = jnp.where(me % (2 * step) == step, got, value)
-        step //= 2
     return value
 
 

time: 173 us -> 191 us (1.10)
  starting transfers between devices: 42.3 us -> 55.8 us
  waiting for transfers between devices: 91.2 us -> 95.6 us
    ppermute x2, starting transfers between devices: 2.64 us -> 17.8 us  [xor_halving(): flat = keep + lax.ppermute(send, axis, pairs)]
    ppermute x3, waiting for transfers between devices: 23.3 us -> 31.6 us  [tree_broadcast(): got = lax.ppermute(value, axis, pairs)]
    ppermute x3, starting transfers between devices: 11.5 us -> 6.34 us  [direct_scatter(): total = total + lax.ppermute(send, axis, pairs)]
    ppermute x2, starting transfers between devices: 2.82 us -> 6.95 us  [shifted(): return lax.ppermute(value, axis, pairs)]
    ppermute x3, waiting for transfers between devices: 12.1 us -> 9.89 us  [direct_scatter(): total = total + lax.ppermute(send, axis, pairs)]
  transfers between devices with their start and end apart: 19 -> 19, of which waited for: 10 -> 9; matrix products, arithmetic and copies ran while one was open for 18% -> 16% of each run, Pallas kernels for 0% -> 0%
where the time goes in v8:
time: 191 us; the launch traced here: 190 us
  waiting for transfers between devices  95.6 us (50%)
  starting transfers between devices  55.8 us (29%)
  matrix products  24.2 us (13%)
  other arithmetic  9.24 us (5%)
  local copies, waits for them, and re-layouts  4.1 us (2%)
    ppermute x3, waiting for transfers between devices, tree_broadcast(): got = lax.ppermute(value, axis, pairs)  31.6 us
    ppermute x3, waiting for transfers between devices, direct_gather(): got = lax.ppermute(piece, axis, pairs)  25.9 us
    ppermute x2, waiting for transfers between devices, xor_halving(): flat = keep + lax.ppermute(send, axis, pairs)  18.2 us
    ppermute x2, starting transfers between devices, xor_halving(): flat = keep + lax.ppermute(send, axis, pairs)  17.8 us
    ppermute x3, starting transfers between devices, tree_broadcast(): got = lax.ppermute(value, axis, pairs)  13.6 us
    dot_general x18, matrix products, spatial_sum(): total = total + jnp.dot(piece, kernel, preferred_element_type=jnp.float32)  12 us
    ppermute x2, waiting for transfers between devices, xor_doubling(): got = lax.ppermute(piece, axis, [(i, i ^ step) for i in range(count)])  10.1 us
    ppermute x3, waiting for transfers between devices, direct_scatter(): total = total + lax.ppermute(send, axis, pairs)  9.89 us
  transfers between devices with their start and end apart: 19, of which 9 were waited for; matrix products, arithmetic and copies ran while one was open for 16% of the time, Pallas kernels for 0%

profile of v8, /device:TPU:0, one launch (start us, length us, event | category | flops | bytes accessed | tf_op | source)
XLA Modules:
  0.0 190.1 jit_solution(1576407578929586795)
XLA Ops:
  1.5 1.4 broadcast_multiply_fusion.1
  2.9 0.9 slice_select_fusion.1
  4.2 1.4 convert_reduce_fusion
  5.6 1.3 collective-permute-start.5
  7.7 5.8 %collective-permute-start.2 = (bf16[2,2,256,256]{3,2,1,0:T(8,128)(2,1)}, bf16[2,2,256,256]{3,2,1,0:T(8,128)(2,1)}, u32[]{:S(2)}, u32[]{:S(2)}) collective-permute-start(bf16[2,2,256,256]{3,2,1,0:T(8,128)(2,1)} %slice_bitcast_fusion), channel_id=1, source_target_pairs={{0,2},{1,3},{16,18},{17,19}} | collective-permute-start | bytes 1572872 | tf_op jit(solution)/shard_map/ppermute | solution.py:19
  13.5 1.4 fusion.86
  15.4 1.1 broadcast_select_fusion.6
  16.5 0.8 select_maximum_fusion.2
  20.8 24.4 %collective-permute-done.2 = bf16[2,2,256,256]{3,2,1,0:T(8,128)(2,1)} collective-permute-done((bf16[2,2,256,256]{3,2,1,0:T(8,128)(2,1)}, bf16[2,2,256,256]{3,2,1,0:T(8,128)(2,1)}, u32[]{:S(2)}, u32[]{:S(2)}) %collective-permute-start.2) | collective-permute-done | bytes 524320 | tf_op jit(solution)/shard_map/ppermute | solution.py:19
  45.3 1.3 collective-permute-start.3
  46.7 1.4 multiply_convert_fusion.2
  48.1 5.7 %collective-permute-start.1 = (bf16[2,2,2,256,256]{4,3,2,1,0:T(8,128)(2,1)S(1)}, bf16[2,2,2,256,256]{4,3,2,1,0:T(8,128)(2,1)S(1)}, u32[]{:S(2)}, u32[]{:S(2)}) collective-permute-start(bf16[2,2,2,256,256]{4,3,2,1,0:T(8,128)(2,1)S(1)} %get-tuple-element.18), channel_id=1, source_target_pairs={{0,2},{2,4},{4,6},{6,8},{8,10},{10,12},{12,14},{1,3},{3,5},{5,7},{... | collective-permute-start | bytes 3145736 | tf_op jit(solution)/shard_map/ppermute | solution.py:10
  55.2 1.1 multiply_convert_fusion
  60.3 6.4 %collective-permute-start.4 = (bf16[2,2,256,256]{3,2,1,0:T(8,128)(2,1)S(1)}, bf16[2,2,256,256]{3,2,1,0:T(8,128)(2,1)S(1)}, u32[]{:S(2)}, u32[]{:S(2)}) collective-permute-start(bf16[2,2,256,256]{3,2,1,0:T(8,128)(2,1)S(1)} %broadcast_select_fusion.1), channel_id=1, source_target_pairs={{0,8},{2,10},{4,12},{6,14},{1,9},{3,11},{5,13},{7,15},{16,24},{18,... | collective-permute-start | bytes 1572872 | tf_op jit(solution)/shard_map/ppermute | solution.py:19
  67.2 1.5 collective-permute-start.7
  70.7 7.1 %collective-permute-done.4 = bf16[2,2,256,256]{3,2,1,0:T(8,128)(2,1)S(1)} collective-permute-done((bf16[2,2,256,256]{3,2,1,0:T(8,128)(2,1)S(1)}, bf16[2,2,256,256]{3,2,1,0:T(8,128)(2,1)S(1)}, u32[]{:S(2)}, u32[]{:S(2)}) %collective-permute-start.4) | collective-permute-done | bytes 524320 | tf_op jit(solution)/shard_map/ppermute | solution.py:19
  79.9 0.9 select_maximum_fusion
  81.3 1.7 multiply_convert_fusion.1
  83.3 17.8 %collective-permute-start.10 = (f32[832,256]{1,0:T(8,128)S(1)}, f32[832,256]{1,0:T(8,128)S(1)}, u32[]{:S(2)}, u32[]{:S(2)}) collective-permute-start(f32[832,256]{1,0:T(8,128)S(1)} %constant_dynamic-slice_fusion.3), channel_id=1, source_target_pairs={{0,2},{2,0},{4,6},{6,4},{8,10},{10,8},{12,14},{14,12},{1,3},{3,1},... | collective-permute-start | bytes 2555912 | tf_op jit(solution)/shard_map/ppermute | solution.py:43
  102.5 18.2 %collective-permute-done.10 = f32[832,256]{1,0:T(8,128)S(1)} collective-permute-done((f32[832,256]{1,0:T(8,128)S(1)}, f32[832,256]{1,0:T(8,128)S(1)}, u32[]{:S(2)}, u32[]{:S(2)}) %collective-permute-start.10) | collective-permute-done | bytes 852000 | tf_op jit(solution)/shard_map/ppermute | solution.py:43
  120.9 3.4 %collective-permute-start.12 = (f32[208,256]{1,0:T(8,128)S(1)}, f32[208,256]{1,0:T(8,128)S(1)}, u32[]{:S(2)}, u32[]{:S(2)}) collective-permute-start(f32[208,256]{1,0:T(8,128)S(1)} %get-tuple-element.13), channel_id=1, source_target_pairs={{0,8},{2,10},{4,12},{6,14},{8,0},{10,2},{12,4},{14,6},{1,9},{3,11}... | collective-permute-start | bytes 638984 | tf_op jit(solution)/shard_map/ppermute | solution.py:69
  124.4 2.8 %collective-permute-start.13 = (f32[208,256]{1,0:T(8,128)S(1)}, f32[208,256]{1,0:T(8,128)S(1)}, u32[]{:S(2)}, u32[]{:S(2)}) collective-permute-start(f32[208,256]{1,0:T(8,128)S(1)} %get-tuple-element.12), channel_id=1, source_target_pairs={{0,12},{2,14},{4,0},{6,2},{8,4},{10,6},{12,8},{14,10},{1,13},{3,15... | collective-permute-start | bytes 638984 | tf_op jit(solution)/shard_map/ppermute | solution.py:69
  127.8 1.3 collective-permute-start.8
  129.1 1.8 collective-permute-done.11
  130.9 8.1 %collective-permute-done.12 = f32[208,256]{1,0:T(8,128)S(1)} collective-permute-done((f32[208,256]{1,0:T(8,128)S(1)}, f32[208,256]{1,0:T(8,128)S(1)}, u32[]{:S(2)}, u32[]{:S(2)}) %collective-permute-start.12) | collective-permute-done | bytes 213024 | tf_op jit(solution)/shard_map/ppermute | solution.py:69
  139.1 5.2 %collective-permute-start.14 = (bf16[208,256]{1,0:T(8,128)(2,1)S(1)}, bf16[208,256]{1,0:T(8,128)(2,1)S(1)}, u32[]{:S(2)}, u32[]{:S(2)}) collective-permute-start(bf16[208,256]{1,0:T(8,128)(2,1)S(1)} %get-tuple-element.6), channel_id=1, source_target_pairs={{0,4},{2,6},{4,8},{6,10},{8,12},{10,14},{12,0},{14,2},{1,5},{3,7},... | collective-permute-start | bytes 319496 | tf_op jit(solution)/shard_map/ppermute | solution.py:82
  144.8 2.4 %collective-permute-start.15 = (bf16[208,256]{1,0:T(8,128)(2,1)S(1)}, bf16[208,256]{1,0:T(8,128)(2,1)S(1)}, u32[]{:S(2)}, u32[]{:S(2)}) collective-permute-start(bf16[208,256]{1,0:T(8,128)(2,1)S(1)} %get-tuple-element.6), channel_id=1, source_target_pairs={{0,8},{2,10},{4,12},{6,14},{8,0},{10,2},{12,4},{14,6},{1,9},{3,11}... | collective-permute-start | bytes 319496 | tf_op jit(solution)/shard_map/ppermute | solution.py:82
  147.2 2.8 %collective-permute-done.14 = bf16[208,256]{1,0:T(8,128)(2,1)S(1)} collective-permute-done((bf16[208,256]{1,0:T(8,128)(2,1)S(1)}, bf16[208,256]{1,0:T(8,128)(2,1)S(1)}, u32[]{:S(2)}, u32[]{:S(2)}) %collective-permute-start.14) | collective-permute-done | bytes 106528 | tf_op jit(solution)/shard_map/ppermute | solution.py:82
  150.0 22.9 %collective-permute-done.15 = bf16[208,256]{1,0:T(8,128)(2,1)S(1)} collective-permute-done((bf16[208,256]{1,0:T(8,128)(2,1)S(1)}, bf16[208,256]{1,0:T(8,128)(2,1)S(1)}, u32[]{:S(2)}, u32[]{:S(2)}) %collective-permute-start.15) | collective-permute-done | bytes 106528 | tf_op jit(solution)/shard_map/ppermute | solution.py:82
  174.4 10.1 %collective-permute-done.17 = bf16[832,256]{1,0:T(8,128)(2,1)S(1)} collective-permute-done((bf16[832,256]{1,0:T(8,128)(2,1)S(1)}, bf16[832,256]{1,0:T(8,128)(2,1)S(1)}, u32[]{:S(2)}, u32[]{:S(2)}) %collective-permute-start.17) | collective-permute-done | bytes 426016 | tf_op jit(solution)/shard_map/ppermute | solution.py:51
  184.8 2.3 %fusion.4 = bf16[2,2,2,256,256]{4,3,2,1,0:T(8,128)(2,1)} fusion(bf16[2,2,2,256,256]{4,3,2,1,0:T(8,128)(2,1)S(1)} %get-tuple-element.8, f32[2,2,2,256,256]{4,3,2,1,0:T(8,128)S(1)} %fusion.17, f32[2,2,2,256,256]{4,3,2,1,0:T(8,128)S(1)} %fusion.35, f32[2,2,2,256,256]{4,3,2,1,0:T(8,128)S(1)} %fusion.37, f32[2,2,2,256,256]{4,3,2,1,0:T(8,128)S(1)} %fusion.84, ...), kind=kOutput, calls=%fused_computation.13 | convolution fusion | flops 275775488 | bytes 21104128 | tf_op jit(solution)/shard_map/dot_general | solution.py:137
  187.6 1.1 slice.203
  (89 shorter events, 23.1 us)
Async XLA Ops:
  0.6 79.0 %copy-start = (bf16[256,256]{1,0:T(8,128)(2,1)S(1)}, bf16[256,256]{1,0:T(8,128)(2,1)}, u32[]{:S(2)}) copy-start(bf16[256,256]{1,0:T(8,128)(2,1)} %param.11) | copy-start | bytes 393220
  0.6 3.5 %copy-start.4 = (bf16[2,2,2,256,256]{4,3,2,1,0:T(8,128)(2,1)S(1)}, bf16[2,2,2,256,256]{4,3,2,1,0:T(8,128)(2,1)}, u32[]{:S(2)}) copy-start(bf16[2,2,2,256,256]{4,3,2,1,0:T(8,128)(2,1)} %param.7) | copy-start | bytes 3145732
  3.7 11.6 %collective-permute-start = (bf16[2,2,1,256,256]{4,3,2,1,0:T(8,128)(2,1)}, bf16[2,2,1,256,256]{4,3,2,1,0:T(8,128)(2,1)}, u32[]{:S(2)}, u32[]{:S(2)}) collective-permute-start(bf16[2,2,1,256,256]{4,3,2,1,0:T(8,128)(2,1)} %slice_select_fusion.1), channel_id=1, source_target_pairs={{0,1},{1,0},{2,3},{3,2},{4,5},{5,4},{6,7},{7,6},{8,9},{9,8},{10,11... | collective-permute-start | bytes 1572872 | tf_op jit(solution)/shard_map/ppermute | solution.py:180
  5.6 49.1 %collective-permute-start.5 = (bf16[2,2,2,256,256]{4,3,2,1,0:T(8,128)(2,1)S(1)}, bf16[2,2,2,256,256]{4,3,2,1,0:T(8,128)(2,1)S(1)}, u32[]{:S(2)}, u32[]{:S(2)}) collective-permute-start(bf16[2,2,2,256,256]{4,3,2,1,0:T(8,128)(2,1)S(1)} %get-tuple-element.8), channel_id=1, source_target_pairs={{2,0},{4,2},{6,4},{8,6},{10,8},{12,10},{14,12},{3,1},{5,3},{7,5},{... | collective-permute-start | bytes 3145736 | tf_op jit(solution)/shard_map/ppermute | solution.py:10
  7.7 37.6 %collective-permute-start.2 = (bf16[2,2,256,256]{3,2,1,0:T(8,128)(2,1)}, bf16[2,2,256,256]{3,2,1,0:T(8,128)(2,1)}, u32[]{:S(2)}, u32[]{:S(2)}) collective-permute-start(bf16[2,2,256,256]{3,2,1,0:T(8,128)(2,1)} %slice_bitcast_fusion), channel_id=1, source_target_pairs={{0,2},{1,3},{16,18},{17,19}} | collective-permute-start | bytes 1572872 | tf_op jit(solution)/shard_map/ppermute | solution.py:19
  13.5 1.4 copy-start.3
  16.5 1.3 copy-start.2
  45.3 14.9 %collective-permute-start.3 = (bf16[2,2,256,256]{3,2,1,0:T(8,128)(2,1)S(1)}, bf16[2,2,256,256]{3,2,1,0:T(8,128)(2,1)S(1)}, u32[]{:S(2)}, u32[]{:S(2)}) collective-permute-start(bf16[2,2,256,256]{3,2,1,0:T(8,128)(2,1)S(1)} %broadcast_select_fusion), channel_id=1, source_target_pairs={{0,4},{2,6},{1,5},{3,7},{16,20},{18,22},{17,21},{19,23}} | collective-permute-start | bytes 1572872 | tf_op jit(solution)/shard_map/ppermute | solution.py:19
  48.1 31.1 %collective-permute-start.1 = (bf16[2,2,2,256,256]{4,3,2,1,0:T(8,128)(2,1)S(1)}, bf16[2,2,2,256,256]{4,3,2,1,0:T(8,128)(2,1)S(1)}, u32[]{:S(2)}, u32[]{:S(2)}) collective-permute-start(bf16[2,2,2,256,256]{4,3,2,1,0:T(8,128)(2,1)S(1)} %get-tuple-element.18), channel_id=1, source_target_pairs={{0,2},{2,4},{4,6},{6,8},{8,10},{10,12},{12,14},{1,3},{3,5},{5,7},{... | collective-permute-start | bytes 3145736 | tf_op jit(solution)/shard_map/ppermute | solution.py:10
  60.2 6.8 %copy-start.1 = (f32[2,2,256,256]{3,2,1,0:T(8,128)S(1)}, f32[2,2,256,256]{3,2,1,0:T(8,128)}, u32[]{:S(2)}) copy-start(f32[2,2,256,256]{3,2,1,0:T(8,128)} %get-tuple-element.7) | copy-start | bytes 3145732
  60.3 17.5 %collective-permute-start.4 = (bf16[2,2,256,256]{3,2,1,0:T(8,128)(2,1)S(1)}, bf16[2,2,256,256]{3,2,1,0:T(8,128)(2,1)S(1)}, u32[]{:S(2)}, u32[]{:S(2)}) collective-permute-start(bf16[2,2,256,256]{3,2,1,0:T(8,128)(2,1)S(1)} %broadcast_select_fusion.1), channel_id=1, source_target_pairs={{0,8},{2,10},{4,12},{6,14},{1,9},{3,11},{5,13},{7,15},{16,24},{18,... | collective-permute-start | bytes 1572872 | tf_op jit(solution)/shard_map/ppermute | solution.py:19
  66.8 12.3 %collective-permute-start.6 = (bf16[2,2,1,256,256]{4,3,2,1,0:T(8,128)(2,1)S(1)}, bf16[2,2,1,256,256]{4,3,2,1,0:T(8,128)(2,1)S(1)}, u32[]{:S(2)}, u32[]{:S(2)}) collective-permute-start(bf16[2,2,1,256,256]{4,3,2,1,0:T(8,128)(2,1)S(1)} %slice_select_fusion), channel_id=1, source_target_pairs={{0,1},{1,0},{2,3},{3,2},{4,5},{5,4},{6,7},{7,6},{8,9},{9,8},{10,11... | collective-permute-start | bytes 1572872 | tf_op jit(solution)/shard_map/ppermute | solution.py:180
  67.2 60.5 %collective-permute-start.7 = (f32[2,2,256,256]{3,2,1,0:T(8,128)S(1)}, f32[2,2,256,256]{3,2,1,0:T(8,128)S(1)}, u32[]{:S(2)}, u32[]{:S(2)}) collective-permute-start(f32[2,2,256,256]{3,2,1,0:T(8,128)S(1)} %add.234), channel_id=1, source_target_pairs={{4,0},{12,8},{5,1},{13,9},{20,16},{28,24},{21,17},{29,25}} | collective-permute-start | bytes 3145736 | tf_op jit(solution)/shard_map/ppermute | solution.py:29
  79.0 4.0 %collective-permute-start.9 = (f32[1664,256]{1,0:T(8,128)S(1)}, f32[1664,256]{1,0:T(8,128)S(1)}, u32[]{:S(2)}, u32[]{:S(2)}) collective-permute-start(f32[1664,256]{1,0:T(8,128)S(1)} %constant_dynamic-slice_fusion.4), channel_id=1, source_target_pairs={{0,1},{1,0},{2,3},{3,2},{4,5},{5,4},{6,7},{7,6},{8,9},{9,8},{10,11... | collective-permute-start | bytes 5111816 | tf_op jit(solution)/shard_map/ppermute | solution.py:43
  83.3 37.4 %collective-permute-start.10 = (f32[832,256]{1,0:T(8,128)S(1)}, f32[832,256]{1,0:T(8,128)S(1)}, u32[]{:S(2)}, u32[]{:S(2)}) collective-permute-start(f32[832,256]{1,0:T(8,128)S(1)} %constant_dynamic-slice_fusion.3), channel_id=1, source_target_pairs={{0,2},{2,0},{4,6},{6,4},{8,10},{10,8},{12,14},{14,12},{1,3},{3,1},... | collective-permute-start | bytes 2555912 | tf_op jit(solution)/shard_map/ppermute | solution.py:43
  120.8 10.1 %collective-permute-start.11 = (f32[208,256]{1,0:T(8,128)S(1)}, f32[208,256]{1,0:T(8,128)S(1)}, u32[]{:S(2)}, u32[]{:S(2)}) collective-permute-start(f32[208,256]{1,0:T(8,128)S(1)} %get-tuple-element.11), channel_id=1, source_target_pairs={{0,4},{2,6},{4,8},{6,10},{8,12},{10,14},{12,0},{14,2},{1,5},{3,7},... | collective-permute-start | bytes 638984 | tf_op jit(solution)/shard_map/ppermute | solution.py:69
  120.9 18.1 %collective-permute-start.12 = (f32[208,256]{1,0:T(8,128)S(1)}, f32[208,256]{1,0:T(8,128)S(1)}, u32[]{:S(2)}, u32[]{:S(2)}) collective-permute-start(f32[208,256]{1,0:T(8,128)S(1)} %get-tuple-element.13), channel_id=1, source_target_pairs={{0,8},{2,10},{4,12},{6,14},{8,0},{10,2},{12,4},{14,6},{1,9},{3,11}... | collective-permute-start | bytes 638984 | tf_op jit(solution)/shard_map/ppermute | solution.py:69
  124.4 14.7 %collective-permute-start.13 = (f32[208,256]{1,0:T(8,128)S(1)}, f32[208,256]{1,0:T(8,128)S(1)}, u32[]{:S(2)}, u32[]{:S(2)}) collective-permute-start(f32[208,256]{1,0:T(8,128)S(1)} %get-tuple-element.12), channel_id=1, source_target_pairs={{0,12},{2,14},{4,0},{6,2},{8,4},{10,6},{12,8},{14,10},{1,13},{3,15... | collective-permute-start | bytes 638984 | tf_op jit(solution)/shard_map/ppermute | solution.py:69
  127.8 45.9 %collective-permute-start.8 = (f32[2,2,256,256]{3,2,1,0:T(8,128)S(1)}, f32[2,2,256,256]{3,2,1,0:T(8,128)S(1)}, u32[]{:S(2)}, u32[]{:S(2)}) collective-permute-start(f32[2,2,256,256]{3,2,1,0:T(8,128)S(1)} %add.235), channel_id=1, source_target_pairs={{8,0},{9,1},{24,16},{25,17}} | collective-permute-start | bytes 3145736 | tf_op jit(solution)/shard_map/ppermute | solution.py:29
  139.1 10.9 %collective-permute-start.14 = (bf16[208,256]{1,0:T(8,128)(2,1)S(1)}, bf16[208,256]{1,0:T(8,128)(2,1)S(1)}, u32[]{:S(2)}, u32[]{:S(2)}) collective-permute-start(bf16[208,256]{1,0:T(8,128)(2,1)S(1)} %get-tuple-element.6), channel_id=1, source_target_pairs={{0,4},{2,6},{4,8},{6,10},{8,12},{10,14},{12,0},{14,2},{1,5},{3,7},... | collective-permute-start | bytes 319496 | tf_op jit(solution)/shard_map/ppermute | solution.py:82
  144.8 28.1 %collective-permute-start.15 = (bf16[208,256]{1,0:T(8,128)(2,1)S(1)}, bf16[208,256]{1,0:T(8,128)(2,1)S(1)}, u32[]{:S(2)}, u32[]{:S(2)}) collective-permute-start(bf16[208,256]{1,0:T(8,128)(2,1)S(1)} %get-tuple-element.6), channel_id=1, source_target_pairs={{0,8},{2,10},{4,12},{6,14},{8,0},{10,2},{12,4},{14,6},{1,9},{3,11}... | collective-permute-start | bytes 319496 | tf_op jit(solution)/shard_map/ppermute | solution.py:82
  147.2 26.0 %collective-permute-start.16 = (bf16[208,256]{1,0:T(8,128)(2,1)S(1)}, bf16[208,256]{1,0:T(8,128)(2,1)S(1)}, u32[]{:S(2)}, u32[]{:S(2)}) collective-permute-start(bf16[208,256]{1,0:T(8,128)(2,1)S(1)} %get-tuple-element.6), channel_id=1, source_target_pairs={{0,12},{2,14},{4,0},{6,2},{8,4},{10,6},{12,8},{14,10},{1,13},{3,15... | collective-permute-start | bytes 319496 | tf_op jit(solution)/shard_map/ppermute | solution.py:82
  173.2 11.3 %collective-permute-start.17 = (bf16[832,256]{1,0:T(8,128)(2,1)S(1)}, bf16[832,256]{1,0:T(8,128)(2,1)S(1)}, u32[]{:S(2)}, u32[]{:S(2)}) collective-permute-start(bf16[832,256]{1,0:T(8,128)(2,1)S(1)} %bitcast.256), channel_id=1, source_target_pairs={{0,2},{2,0},{4,6},{6,4},{8,10},{10,8},{12,14},{14,12},{1,3},{3,1},... | collective-permute-start | bytes 1277960 | tf_op jit(solution)/shard_map/ppermute | solution.py:51
  184.7 2.4 %collective-permute-start.18 = (bf16[1664,256]{1,0:T(8,128)(2,1)S(1)}, bf16[1664,256]{1,0:T(8,128)(2,1)S(1)}, u32[]{:S(2)}, u32[]{:S(2)}) collective-permute-start(bf16[1664,256]{1,0:T(8,128)(2,1)S(1)} %maximum_select_fusion.1), channel_id=1, source_target_pairs={{0,1},{1,0},{2,3},{3,2},{4,5},{5,4},{6,7},{7,6},{8,9},{9,8},{10,11... | collective-permute-start | bytes 2555912 | tf_op jit(solution)/shard_map/ppermute | solution.py:51

commit v9 on v7

--- a/solution.py
+++ b/solution.py
@@ -209,7 +209,8 @@
     padded = jnp.pad(rows_pad, ((0, 0), (0, 0), (0, 0), (1, 1), (0, 0)))
     pre = spatial_sum(padded, spatial_weight, False)
     act = jax.nn.silu(pre).astype(jnp.bfloat16)
-    earlier = shifted(act, "space", 1)
+    act_out, first = lax.optimization_barrier((act, first))
+    earlier = shifted(act_out, "space", 1)
     act_pad = jnp.concatenate([earlier, act], axis=1)
     mixed = lag_forward(act_pad, temporal_weight, frames)
     cot_pad = jnp.concatenate([cot, later], axis=1)

time: 173 us -> 174 us (level)
  waiting for transfers between devices: 91.2 us -> 72.5 us
  starting transfers between devices: 42.3 us -> 59.5 us
  other arithmetic: 9.24 us -> 11.6 us
    ppermute x3, starting transfers between devices: 11.5 us -> 28 us  [direct_scatter(): total = total + lax.ppermute(send, axis, pairs)]
    ppermute x3, waiting for transfers between devices: 23.3 us -> 9.96 us  [tree_broadcast(): got = lax.ppermute(value, axis, pairs)]
    ppermute x3, waiting for transfers between devices: 12.1 us -> 8.11 us  [direct_scatter(): total = total + lax.ppermute(send, axis, pairs)]
  transfers between devices with their start and end apart: 19 -> 19, of which waited for: 10 -> 13; matrix products, arithmetic and copies ran while one was open for 18% -> 19% of each run, Pallas kernels for 0% -> 0%
where the time goes in v9:
time: 174 us; the launch traced here: 173 us
  waiting for transfers between devices  72.5 us (42%)
  starting transfers between devices  59.5 us (34%)
  matrix products  24 us (14%)
  other arithmetic  11.6 us (7%)
  local copies, waits for them, and re-layouts  4.09 us (2%)
    ppermute x3, starting transfers between devices, direct_scatter(): total = total + lax.ppermute(send, axis, pairs)  28 us
    ppermute x3, waiting for transfers between devices, direct_gather(): got = lax.ppermute(piece, axis, pairs)  25.7 us
    ppermute x2, waiting for transfers between devices, xor_halving(): flat = keep + lax.ppermute(send, axis, pairs)  16.6 us
    ppermute x3, starting transfers between devices, tree_broadcast(): got = lax.ppermute(value, axis, pairs)  14.4 us
    dot_general x18, matrix products, spatial_sum(): total = total + jnp.dot(piece, kernel, preferred_element_type=jnp.float32)  11.8 us
    ppermute x3, waiting for transfers between devices, tree_broadcast(): got = lax.ppermute(value, axis, pairs)  9.96 us
    ppermute x2, waiting for transfers between devices, xor_doubling(): got = lax.ppermute(piece, axis, [(i, i ^ step) for i in range(count)])  9 us
    ppermute x3, waiting for transfers between devices, direct_scatter(): total = total + lax.ppermute(send, axis, pairs)  8.11 us
  transfers between devices with their start and end apart: 19, of which 13 were waited for; matrix products, arithmetic and copies ran while one was open for 19% of the time, Pallas kernels for 0%

profile of v9, /device:TPU:0, one launch (start us, length us, event | category | flops | bytes accessed | tf_op | source)
XLA Modules:
  0.0 172.8 jit_solution(8653421596679237363)
XLA Ops:
  1.5 1.4 broadcast_multiply_fusion.1
  4.2 1.4 convert_reduce_fusion
  5.6 1.3 collective-permute-start.5
  7.7 8.3 %collective-permute-start.1 = (bf16[2,2,256,256]{3,2,1,0:T(8,128)(2,1)}, bf16[2,2,256,256]{3,2,1,0:T(8,128)(2,1)}, u32[]{:S(2)}, u32[]{:S(2)}) collective-permute-start(bf16[2,2,256,256]{3,2,1,0:T(8,128)(2,1)} %slice_bitcast_fusion), channel_id=1, source_target_pairs={{0,8},{1,9},{16,24},{17,25}} | collective-permute-start | bytes 1572872 | tf_op jit(solution)/shard_map/ppermute | solution.py:21
  16.0 1.4 fusion.86
  17.8 1.1 broadcast_select_fusion.6
  23.3 3.7 %collective-permute-done.1 = bf16[2,2,256,256]{3,2,1,0:T(8,128)(2,1)} collective-permute-done((bf16[2,2,256,256]{3,2,1,0:T(8,128)(2,1)}, bf16[2,2,256,256]{3,2,1,0:T(8,128)(2,1)}, u32[]{:S(2)}, u32[]{:S(2)}) %collective-permute-start.1) | collective-permute-done | bytes 524320 | tf_op jit(solution)/shard_map/ppermute | solution.py:21
  27.1 1.3 collective-permute-start.2
  28.4 1.3 multiply_convert_fusion.2
  30.6 3.1 %collective-permute-done.5 = bf16[2,2,2,256,256]{4,3,2,1,0:T(8,128)(2,1)S(1)} collective-permute-done((bf16[2,2,2,256,256]{4,3,2,1,0:T(8,128)(2,1)S(1)}, bf16[2,2,2,256,256]{4,3,2,1,0:T(8,128)(2,1)S(1)}, u32[]{:S(2)}, u32[]{:S(2)}) %collective-permute-start.5) | collective-permute-done | bytes 1048608 | tf_op jit(solution)/shard_map/ppermute | solution.py:10
  34.2 1.1 multiply_convert_fusion
  39.5 4.8 %collective-permute-start.3 = (bf16[2,2,256,256]{3,2,1,0:T(8,128)(2,1)S(1)}, bf16[2,2,256,256]{3,2,1,0:T(8,128)(2,1)S(1)}, u32[]{:S(2)}, u32[]{:S(2)}) collective-permute-start(bf16[2,2,256,256]{3,2,1,0:T(8,128)(2,1)S(1)} %broadcast_select_fusion.1), channel_id=1, source_target_pairs={{0,2},{4,6},{8,10},{12,14},{1,3},{5,7},{9,11},{13,15},{16,18},{20,... | collective-permute-start | bytes 1572872 | tf_op jit(solution)/shard_map/ppermute | solution.py:21
  44.6 1.1 add.244
  45.7 1.3 collective-permute-start.7
  49.0 6.2 %collective-permute-done.3 = bf16[2,2,256,256]{3,2,1,0:T(8,128)(2,1)S(1)} collective-permute-done((bf16[2,2,256,256]{3,2,1,0:T(8,128)(2,1)S(1)}, bf16[2,2,256,256]{3,2,1,0:T(8,128)(2,1)S(1)}, u32[]{:S(2)}, u32[]{:S(2)}) %collective-permute-start.3) | collective-permute-done | bytes 524320 | tf_op jit(solution)/shard_map/ppermute | solution.py:21
  60.3 2.5 %collective-permute-start.10 = (f32[832,256]{1,0:T(8,128)S(1)}, f32[832,256]{1,0:T(8,128)S(1)}, u32[]{:S(2)}, u32[]{:S(2)}) collective-permute-start(f32[832,256]{1,0:T(8,128)S(1)} %constant_dynamic-slice_fusion.3), channel_id=1, source_target_pairs={{0,2},{2,0},{4,6},{6,4},{8,10},{10,8},{12,14},{14,12},{1,3},{3,1},... | collective-permute-start | bytes 2555912 | tf_op jit(solution)/shard_map/ppermute | solution.py:45
  63.8 2.0 %collective-permute-start.4 = (bf16[2,2,2,256,256]{4,3,2,1,0:T(8,128)(2,1)S(1)}, bf16[2,2,2,256,256]{4,3,2,1,0:T(8,128)(2,1)S(1)}, u32[]{:S(2)}, u32[]{:S(2)}) collective-permute-start(bf16[2,2,2,256,256]{4,3,2,1,0:T(8,128)(2,1)S(1)} %get-tuple-element.7), channel_id=1, source_target_pairs={{0,2},{2,4},{4,6},{6,8},{8,10},{10,12},{12,14},{1,3},{3,5},{5,7},{... | collective-permute-start | bytes 3145736 | tf_op jit(solution)/shard_map/ppermute | solution.py:10
  66.3 15.9 %collective-permute-done.10 = f32[832,256]{1,0:T(8,128)S(1)} collective-permute-done((f32[832,256]{1,0:T(8,128)S(1)}, f32[832,256]{1,0:T(8,128)S(1)}, u32[]{:S(2)}, u32[]{:S(2)}) %collective-permute-start.10) | collective-permute-done | bytes 852000 | tf_op jit(solution)/shard_map/ppermute | solution.py:45
  82.3 24.0 %collective-permute-start.11 = (f32[208,256]{1,0:T(8,128)S(1)}, f32[208,256]{1,0:T(8,128)S(1)}, u32[]{:S(2)}, u32[]{:S(2)}) collective-permute-start(f32[208,256]{1,0:T(8,128)S(1)} %get-tuple-element.15), channel_id=1, source_target_pairs={{0,4},{2,6},{4,8},{6,10},{8,12},{10,14},{12,0},{14,2},{1,5},{3,7},... | collective-permute-start | bytes 638984 | tf_op jit(solution)/shard_map/ppermute | solution.py:71
  106.4 1.3 collective-permute-start.12
  107.7 2.6 %collective-permute-start.13 = (f32[208,256]{1,0:T(8,128)S(1)}, f32[208,256]{1,0:T(8,128)S(1)}, u32[]{:S(2)}, u32[]{:S(2)}) collective-permute-start(f32[208,256]{1,0:T(8,128)S(1)} %get-tuple-element.16), channel_id=1, source_target_pairs={{0,12},{2,14},{4,0},{6,2},{8,4},{10,6},{12,8},{14,10},{1,13},{3,15... | collective-permute-start | bytes 638984 | tf_op jit(solution)/shard_map/ppermute | solution.py:71
  110.6 1.4 add.245
  112.1 1.3 collective-permute-start.8
  113.4 8.1 %collective-permute-done.12 = f32[208,256]{1,0:T(8,128)S(1)} collective-permute-done((f32[208,256]{1,0:T(8,128)S(1)}, f32[208,256]{1,0:T(8,128)S(1)}, u32[]{:S(2)}, u32[]{:S(2)}) %collective-permute-start.12) | collective-permute-done | bytes 213024 | tf_op jit(solution)/shard_map/ppermute | solution.py:71
  121.6 5.2 %collective-permute-start.14 = (bf16[208,256]{1,0:T(8,128)(2,1)S(1)}, bf16[208,256]{1,0:T(8,128)(2,1)S(1)}, u32[]{:S(2)}, u32[]{:S(2)}) collective-permute-start(bf16[208,256]{1,0:T(8,128)(2,1)S(1)} %get-tuple-element.10), channel_id=1, source_target_pairs={{0,4},{2,6},{4,8},{6,10},{8,12},{10,14},{12,0},{14,2},{1,5},{3,7},... | collective-permute-start | bytes 319496 | tf_op jit(solution)/shard_map/ppermute | solution.py:84
  127.2 2.8 %collective-permute-start.15 = (bf16[208,256]{1,0:T(8,128)(2,1)S(1)}, bf16[208,256]{1,0:T(8,128)(2,1)S(1)}, u32[]{:S(2)}, u32[]{:S(2)}) collective-permute-start(bf16[208,256]{1,0:T(8,128)(2,1)S(1)} %get-tuple-element.10), channel_id=1, source_target_pairs={{0,8},{2,10},{4,12},{6,14},{8,0},{10,2},{12,4},{14,6},{1,9},{3,11}... | collective-permute-start | bytes 319496 | tf_op jit(solution)/shard_map/ppermute | solution.py:84
  130.0 2.8 %collective-permute-done.14 = bf16[208,256]{1,0:T(8,128)(2,1)S(1)} collective-permute-done((bf16[208,256]{1,0:T(8,128)(2,1)S(1)}, bf16[208,256]{1,0:T(8,128)(2,1)S(1)}, u32[]{:S(2)}, u32[]{:S(2)}) %collective-permute-start.14) | collective-permute-done | bytes 106528 | tf_op jit(solution)/shard_map/ppermute | solution.py:84
  132.8 22.6 %collective-permute-done.15 = bf16[208,256]{1,0:T(8,128)(2,1)S(1)} collective-permute-done((bf16[208,256]{1,0:T(8,128)(2,1)S(1)}, bf16[208,256]{1,0:T(8,128)(2,1)S(1)}, u32[]{:S(2)}, u32[]{:S(2)}) %collective-permute-start.15) | collective-permute-done | bytes 106528 | tf_op jit(solution)/shard_map/ppermute | solution.py:84
  155.8 1.7 %multiply_convert_fusion.1 = bf16[2,2,2,256,256]{4,3,2,1,0:T(8,128)(2,1)} fusion(f32[2,2,2,256,256]{4,3,2,1,0:T(8,128)S(1)} %fusion.102, f32[2,2,2,256,256]{4,3,2,1,0:T(8,128)S(1)} %fusion.5, bf16[2,2,2,256,256]{4,3,2,1,0:T(8,128)(2,1)S(1)} %broadcast_multiply_fusion.1, bf16[2,2,2,256,256]{4,3,2,1,0:T(8,128)(2,1)S(1)} %collective-permute-done.4, ...), kind=kOutput, calls=%fused_computation.24 | convolution fusion | flops 272105472 | bytes 8520704 | tf_op jit(solution)/shard_map/dot_general | solution.py:146
  158.2 8.9 %collective-permute-done.17 = bf16[832,256]{1,0:T(8,128)(2,1)S(1)} collective-permute-done((bf16[832,256]{1,0:T(8,128)(2,1)S(1)}, bf16[832,256]{1,0:T(8,128)(2,1)S(1)}, u32[]{:S(2)}, u32[]{:S(2)}) %collective-permute-start.17) | collective-permute-done | bytes 426016 | tf_op jit(solution)/shard_map/ppermute | solution.py:53
  167.4 2.3 %fusion.4 = bf16[2,2,2,256,256]{4,3,2,1,0:T(8,128)(2,1)} fusion(bf16[2,2,2,256,256]{4,3,2,1,0:T(8,128)(2,1)S(1)} %get-tuple-element.12, f32[2,2,2,256,256]{4,3,2,1,0:T(8,128)S(1)} %fusion.17, f32[2,2,2,256,256]{4,3,2,1,0:T(8,128)S(1)} %fusion.35, f32[2,2,2,256,256]{4,3,2,1,0:T(8,128)S(1)} %fusion.37, f32[2,2,2,256,256]{4,3,2,1,0:T(8,128)S(1)} %fusion.84, ...), kind=kOutput, calls=%fused_computation.13 | convolution fusion | flops 275775488 | bytes 21104128 | tf_op jit(solution)/shard_map/dot_general | solution.py:139
  170.3 1.1 slice.203
  (90 shorter events, 26.4 us)
Async XLA Ops:
  0.6 109.7 %copy-start = (bf16[256,256]{1,0:T(8,128)(2,1)S(1)}, bf16[256,256]{1,0:T(8,128)(2,1)}, u32[]{:S(2)}) copy-start(bf16[256,256]{1,0:T(8,128)(2,1)} %param.11) | copy-start | bytes 393220
  0.6 3.5 %copy-start.4 = (bf16[2,2,2,256,256]{4,3,2,1,0:T(8,128)(2,1)S(1)}, bf16[2,2,2,256,256]{4,3,2,1,0:T(8,128)(2,1)}, u32[]{:S(2)}) copy-start(bf16[2,2,2,256,256]{4,3,2,1,0:T(8,128)(2,1)} %param.7) | copy-start | bytes 3145732
  3.7 14.1 %collective-permute-start = (bf16[2,2,1,256,256]{4,3,2,1,0:T(8,128)(2,1)}, bf16[2,2,1,256,256]{4,3,2,1,0:T(8,128)(2,1)}, u32[]{:S(2)}, u32[]{:S(2)}) collective-permute-start(bf16[2,2,1,256,256]{4,3,2,1,0:T(8,128)(2,1)} %slice_select_fusion.1), channel_id=1, source_target_pairs={{0,1},{1,0},{2,3},{3,2},{4,5},{5,4},{6,7},{7,6},{8,9},{9,8},{10,11... | collective-permute-start | bytes 1572872 | tf_op jit(solution)/shard_map/ppermute | solution.py:182
  5.6 28.2 %collective-permute-start.5 = (bf16[2,2,2,256,256]{4,3,2,1,0:T(8,128)(2,1)S(1)}, bf16[2,2,2,256,256]{4,3,2,1,0:T(8,128)(2,1)S(1)}, u32[]{:S(2)}, u32[]{:S(2)}) collective-permute-start(bf16[2,2,2,256,256]{4,3,2,1,0:T(8,128)(2,1)S(1)} %get-tuple-element.12), channel_id=1, source_target_pairs={{2,0},{4,2},{6,4},{8,6},{10,8},{12,10},{14,12},{3,1},{5,3},{7,5},{... | collective-permute-start | bytes 3145736 | tf_op jit(solution)/shard_map/ppermute | solution.py:10
  7.7 19.4 %collective-permute-start.1 = (bf16[2,2,256,256]{3,2,1,0:T(8,128)(2,1)}, bf16[2,2,256,256]{3,2,1,0:T(8,128)(2,1)}, u32[]{:S(2)}, u32[]{:S(2)}) collective-permute-start(bf16[2,2,256,256]{3,2,1,0:T(8,128)(2,1)} %slice_bitcast_fusion), channel_id=1, source_target_pairs={{0,8},{1,9},{16,24},{17,25}} | collective-permute-start | bytes 1572872 | tf_op jit(solution)/shard_map/ppermute | solution.py:21
  16.0 1.4 copy-start.3
  19.0 1.3 copy-start.2
  27.1 12.3 %collective-permute-start.2 = (bf16[2,2,256,256]{3,2,1,0:T(8,128)(2,1)S(1)}, bf16[2,2,256,256]{3,2,1,0:T(8,128)(2,1)S(1)}, u32[]{:S(2)}, u32[]{:S(2)}) collective-permute-start(bf16[2,2,256,256]{3,2,1,0:T(8,128)(2,1)S(1)} %broadcast_select_fusion), channel_id=1, source_target_pairs={{0,4},{8,12},{1,5},{9,13},{16,20},{24,28},{17,21},{25,29}} | collective-permute-start | bytes 1572872 | tf_op jit(solution)/shard_map/ppermute | solution.py:21
  39.3 5.2 %copy-start.1 = (f32[2,2,256,256]{3,2,1,0:T(8,128)S(1)}, f32[2,2,256,256]{3,2,1,0:T(8,128)}, u32[]{:S(2)}) copy-start(f32[2,2,256,256]{3,2,1,0:T(8,128)} %get-tuple-element.11) | copy-start | bytes 3145732
  39.5 15.7 %collective-permute-start.3 = (bf16[2,2,256,256]{3,2,1,0:T(8,128)(2,1)S(1)}, bf16[2,2,256,256]{3,2,1,0:T(8,128)(2,1)S(1)}, u32[]{:S(2)}, u32[]{:S(2)}) collective-permute-start(bf16[2,2,256,256]{3,2,1,0:T(8,128)(2,1)S(1)} %broadcast_select_fusion.1), channel_id=1, source_target_pairs={{0,2},{4,6},{8,10},{12,14},{1,3},{5,7},{9,11},{13,15},{16,18},{20,... | collective-permute-start | bytes 1572872 | tf_op jit(solution)/shard_map/ppermute | solution.py:21
  44.3 12.1 %collective-permute-start.6 = (bf16[2,2,1,256,256]{4,3,2,1,0:T(8,128)(2,1)S(1)}, bf16[2,2,1,256,256]{4,3,2,1,0:T(8,128)(2,1)S(1)}, u32[]{:S(2)}, u32[]{:S(2)}) collective-permute-start(bf16[2,2,1,256,256]{4,3,2,1,0:T(8,128)(2,1)S(1)} %slice_select_fusion), channel_id=1, source_target_pairs={{0,1},{1,0},{2,3},{3,2},{4,5},{5,4},{6,7},{7,6},{8,9},{9,8},{10,11... | collective-permute-start | bytes 1572872 | tf_op jit(solution)/shard_map/ppermute | solution.py:182
  45.7 65.0 %collective-permute-start.7 = (f32[2,2,256,256]{3,2,1,0:T(8,128)}, f32[2,2,256,256]{3,2,1,0:T(8,128)S(1)}, u32[]{:S(2)}, u32[]{:S(2)}) collective-permute-start(f32[2,2,256,256]{3,2,1,0:T(8,128)} %add.244), channel_id=1, source_target_pairs={{4,0},{12,8},{5,1},{13,9},{20,16},{28,24},{21,17},{29,25}} | collective-permute-start | bytes 3145736 | tf_op jit(solution)/shard_map/ppermute | solution.py:31
  56.3 3.7 %collective-permute-start.9 = (f32[1664,256]{1,0:T(8,128)S(1)}, f32[1664,256]{1,0:T(8,128)S(1)}, u32[]{:S(2)}, u32[]{:S(2)}) collective-permute-start(f32[1664,256]{1,0:T(8,128)S(1)} %constant_dynamic-slice_fusion.4), channel_id=1, source_target_pairs={{0,1},{1,0},{2,3},{3,2},{4,5},{5,4},{6,7},{7,6},{8,9},{9,8},{10,11... | collective-permute-start | bytes 5111816 | tf_op jit(solution)/shard_map/ppermute | solution.py:45
  60.3 21.9 %collective-permute-start.10 = (f32[832,256]{1,0:T(8,128)S(1)}, f32[832,256]{1,0:T(8,128)S(1)}, u32[]{:S(2)}, u32[]{:S(2)}) collective-permute-start(f32[832,256]{1,0:T(8,128)S(1)} %constant_dynamic-slice_fusion.3), channel_id=1, source_target_pairs={{0,2},{2,0},{4,6},{6,4},{8,10},{10,8},{12,14},{14,12},{1,3},{3,1},... | collective-permute-start | bytes 2555912 | tf_op jit(solution)/shard_map/ppermute | solution.py:45
  63.8 63.0 %collective-permute-start.4 = (bf16[2,2,2,256,256]{4,3,2,1,0:T(8,128)(2,1)S(1)}, bf16[2,2,2,256,256]{4,3,2,1,0:T(8,128)(2,1)S(1)}, u32[]{:S(2)}, u32[]{:S(2)}) collective-permute-start(bf16[2,2,2,256,256]{4,3,2,1,0:T(8,128)(2,1)S(1)} %get-tuple-element.7), channel_id=1, source_target_pairs={{0,2},{2,4},{4,6},{6,8},{8,10},{10,12},{12,14},{1,3},{3,5},{5,7},{... | collective-permute-start | bytes 3145736 | tf_op jit(solution)/shard_map/ppermute | solution.py:10
  82.3 31.1 %collective-permute-start.11 = (f32[208,256]{1,0:T(8,128)S(1)}, f32[208,256]{1,0:T(8,128)S(1)}, u32[]{:S(2)}, u32[]{:S(2)}) collective-permute-start(f32[208,256]{1,0:T(8,128)S(1)} %get-tuple-element.15), channel_id=1, source_target_pairs={{0,4},{2,6},{4,8},{6,10},{8,12},{10,14},{12,0},{14,2},{1,5},{3,7},... | collective-permute-start | bytes 638984 | tf_op jit(solution)/shard_map/ppermute | solution.py:71
  106.4 15.1 %collective-permute-start.12 = (f32[208,256]{1,0:T(8,128)S(1)}, f32[208,256]{1,0:T(8,128)S(1)}, u32[]{:S(2)}, u32[]{:S(2)}) collective-permute-start(f32[208,256]{1,0:T(8,128)S(1)} %get-tuple-element.17), channel_id=1, source_target_pairs={{0,8},{2,10},{4,12},{6,14},{8,0},{10,2},{12,4},{14,6},{1,9},{3,11}... | collective-permute-start | bytes 638984 | tf_op jit(solution)/shard_map/ppermute | solution.py:71
  107.7 13.7 %collective-permute-start.13 = (f32[208,256]{1,0:T(8,128)S(1)}, f32[208,256]{1,0:T(8,128)S(1)}, u32[]{:S(2)}, u32[]{:S(2)}) collective-permute-start(f32[208,256]{1,0:T(8,128)S(1)} %get-tuple-element.16), channel_id=1, source_target_pairs={{0,12},{2,14},{4,0},{6,2},{8,4},{10,6},{12,8},{14,10},{1,13},{3,15... | collective-permute-start | bytes 638984 | tf_op jit(solution)/shard_map/ppermute | solution.py:71
  112.1 45.5 %collective-permute-start.8 = (f32[2,2,256,256]{3,2,1,0:T(8,128)S(1)}, f32[2,2,256,256]{3,2,1,0:T(8,128)S(1)}, u32[]{:S(2)}, u32[]{:S(2)}) collective-permute-start(f32[2,2,256,256]{3,2,1,0:T(8,128)S(1)} %add.245), channel_id=1, source_target_pairs={{8,0},{9,1},{24,16},{25,17}} | collective-permute-start | bytes 3145736 | tf_op jit(solution)/shard_map/ppermute | solution.py:31
  121.6 11.2 %collective-permute-start.14 = (bf16[208,256]{1,0:T(8,128)(2,1)S(1)}, bf16[208,256]{1,0:T(8,128)(2,1)S(1)}, u32[]{:S(2)}, u32[]{:S(2)}) collective-permute-start(bf16[208,256]{1,0:T(8,128)(2,1)S(1)} %get-tuple-element.10), channel_id=1, source_target_pairs={{0,4},{2,6},{4,8},{6,10},{8,12},{10,14},{12,0},{14,2},{1,5},{3,7},... | collective-permute-start | bytes 319496 | tf_op jit(solution)/shard_map/ppermute | solution.py:84
  127.2 28.1 %collective-permute-start.15 = (bf16[208,256]{1,0:T(8,128)(2,1)S(1)}, bf16[208,256]{1,0:T(8,128)(2,1)S(1)}, u32[]{:S(2)}, u32[]{:S(2)}) collective-permute-start(bf16[208,256]{1,0:T(8,128)(2,1)S(1)} %get-tuple-element.10), channel_id=1, source_target_pairs={{0,8},{2,10},{4,12},{6,14},{8,0},{10,2},{12,4},{14,6},{1,9},{3,11}... | collective-permute-start | bytes 319496 | tf_op jit(solution)/shard_map/ppermute | solution.py:84
  130.0 25.7 %collective-permute-start.16 = (bf16[208,256]{1,0:T(8,128)(2,1)S(1)}, bf16[208,256]{1,0:T(8,128)(2,1)S(1)}, u32[]{:S(2)}, u32[]{:S(2)}) collective-permute-start(bf16[208,256]{1,0:T(8,128)(2,1)S(1)} %get-tuple-element.10), channel_id=1, source_target_pairs={{0,12},{2,14},{4,0},{6,2},{8,4},{10,6},{12,8},{14,10},{1,13},{3,15... | collective-permute-start | bytes 319496 | tf_op jit(solution)/shard_map/ppermute | solution.py:84
  155.7 11.4 %collective-permute-start.17 = (bf16[832,256]{1,0:T(8,128)(2,1)S(1)}, bf16[832,256]{1,0:T(8,128)(2,1)S(1)}, u32[]{:S(2)}, u32[]{:S(2)}) collective-permute-start(bf16[832,256]{1,0:T(8,128)(2,1)S(1)} %bitcast.256), channel_id=1, source_target_pairs={{0,2},{2,0},{4,6},{6,4},{8,10},{10,8},{12,14},{14,12},{1,3},{3,1},... | collective-permute-start | bytes 1277960 | tf_op jit(solution)/shard_map/ppermute | solution.py:53
  167.4 2.4 %collective-permute-start.18 = (bf16[1664,256]{1,0:T(8,128)(2,1)S(1)}, bf16[1664,256]{1,0:T(8,128)(2,1)S(1)}, u32[]{:S(2)}, u32[]{:S(2)}) collective-permute-start(bf16[1664,256]{1,0:T(8,128)(2,1)S(1)} %maximum_select_fusion.1), channel_id=1, source_target_pairs={{0,1},{1,0},{2,3},{3,2},{4,5},{5,4},{6,7},{7,6},{8,9},{9,8},{10,11... | collective-permute-start | bytes 2555912 | tf_op jit(solution)/shard_map/ppermute | solution.py:53

commit v10 on v7

--- a/solution.py
+++ b/solution.py
@@ -24,9 +24,10 @@
     return value
 
 
-def tree_reduce(value, axis, step=1):
-    count = lax.axis_size(axis)
-    while step < count:
+def tree_reduce(value, axis, step=1, stop=None):
+    count = lax.axis_size(axis)
+    stop = count if stop is None else stop
+    while step < min(count, stop):
         pairs = [(i + step, i) for i in range(0, count, 2 * step) if i + step < count]
         value = value + lax.ppermute(value, axis, pairs)
         step *= 2
@@ -202,9 +203,9 @@
     later = shifted(cot, "space", -1)
     if lax.axis_size("space") % 2 == 0:
         cot_pair = cot_local + jnp.sum(later, axis=1, dtype=jnp.float32)
-        cot_sum = tree_reduce(cot_pair, "space", 2)
+        cot_part = tree_reduce(cot_pair, "space", 2, 4)
     else:
-        cot_sum = tree_reduce(cot_local, "space")
+        cot_part = tree_reduce(cot_local, "space", 1, 2)
     rows_pad = row_halo(masked)
     padded = jnp.pad(rows_pad, ((0, 0), (0, 0), (0, 0), (1, 1), (0, 0)))
     pre = spatial_sum(padded, spatial_weight, False)
@@ -219,14 +220,9 @@
     output = ((masked.astype(jnp.float32) + mixed + cond[:, None]) * mask_f).astype(jnp.bfloat16)
     sig = jax.nn.sigmoid(pre)
     dpre = (dact * sig * (1.0 + pre * (1.0 - sig))).astype(jnp.bfloat16)
-    cond_back = jnp.dot(cot_sum, cond_weight.astype(jnp.float32).T, precision=lax.Precision.HIGHEST)
     dpre_rows = row_halo(dpre)
     dpre_pad = jnp.pad(dpre_rows, ((0, 0), (0, 0), (0, 0), (1, 1), (0, 0)))
     dmasked = spatial_sum(dpre_pad, spatial_weight, True)
-    is_first = (frame_ids == 0).astype(jnp.float32)[None, :, None, None, None]
-    grad_latents = (
-        (cot.astype(jnp.float32) + dmasked + is_first * cond_back[:, None]) * mask_f
-    ).astype(jnp.bfloat16)
     dims = (((0, 1, 2, 3), (0, 1, 2, 3)), ((), ()))
     spatial_terms = []
     for row_off in range(3):
@@ -253,7 +249,17 @@
         axis=0,
     )
     scale = (clips * frames * rows * cols * lax.axis_size("space") * lax.axis_size("tm")) ** (-0.5)
+    flat, cot_part = lax.optimization_barrier((flat, cot_part))
+    if lax.axis_size("space") % 2 == 0:
+        cot_sum = tree_reduce(cot_part, "space", 4)
+    else:
+        cot_sum = tree_reduce(cot_part, "space", 2)
     summed = all_sum_rounded(flat, scale)
+    cond_back = jnp.dot(cot_sum, cond_weight.astype(jnp.float32).T, precision=lax.Precision.HIGHEST)
+    is_first = (frame_ids == 0).astype(jnp.float32)[None, :, None, None, None]
+    grad_latents = (
+        (cot.astype(jnp.float32) + dmasked + is_first * cond_back[:, None]) * mask_f
+    ).astype(jnp.bfloat16)
     n_s = taps_s * chans
     n_t = taps_t * chans
     grad_spatial = summed[:n_s].reshape(taps_s, chans, chans)

time: 173 us -> 184 us (1.064)
  waiting for transfers between devices: 91.2 us -> 110 us
  starting transfers between devices: 42.3 us -> 34 us
    ppermute x2, waiting for transfers between devices: 0.01 us -> 21.6 us  [tree_reduce(): value = value + lax.ppermute(value, axis, pairs)]
    ppermute x3, starting transfers between devices: 11.5 us -> 5.56 us  [direct_scatter(): total = total + lax.ppermute(send, axis, pairs)]
    ppermute x2, starting transfers between devices: 2.64 us -> 0.14 us  [xor_halving(): flat = keep + lax.ppermute(send, axis, pairs)]
  transfers between devices with their start and end apart: 19 -> 19, of which waited for: 10 -> 12; matrix products, arithmetic and copies ran while one was open for 18% -> 17% of each run, Pallas kernels for 0% -> 0%
where the time goes in v10:
time: 184 us; the launch traced here: 183 us
  waiting for transfers between devices  110 us (60%)
  starting transfers between devices  34 us (18%)
  matrix products  24.3 us (13%)
  other arithmetic  9.26 us (5%)
  local copies, waits for them, and re-layouts  4.1 us (2%)
    ppermute x3, waiting for transfers between devices, direct_gather(): got = lax.ppermute(piece, axis, pairs)  25.7 us
    ppermute x3, waiting for transfers between devices, tree_broadcast(): got = lax.ppermute(value, axis, pairs)  23.2 us
    ppermute x2, waiting for transfers between devices, tree_reduce(): value = value + lax.ppermute(value, axis, pairs)  21.6 us
    ppermute x2, waiting for transfers between devices, xor_halving(): flat = keep + lax.ppermute(send, axis, pairs)  19.2 us
    ppermute x3, starting transfers between devices, tree_broadcast(): got = lax.ppermute(value, axis, pairs)  14.4 us
    dot_general x18, matrix products, spatial_sum(): total = total + jnp.dot(piece, kernel, preferred_element_type=jnp.float32)  12.1 us
    ppermute x3, waiting for transfers between devices, direct_scatter(): total = total + lax.ppermute(send, axis, pairs)  10.3 us
    ppermute x2, waiting for transfers between devices, xor_doubling(): got = lax.ppermute(piece, axis, [(i, i ^ step) for i in range(count)])  8.86 us
  transfers between devices with their start and end apart: 19, of which 12 were waited for; matrix products, arithmetic and copies ran while one was open for 17% of the time, Pallas kernels for 0%

profile of v10, /device:TPU:0, one launch (start us, length us, event | category | flops | bytes accessed | tf_op | source)
XLA Modules:
  0.0 182.9 jit_solution(8150190102452156902)
XLA Ops:
  1.5 1.4 broadcast_multiply_fusion.1
  4.2 1.4 convert_reduce_fusion
  5.6 1.3 collective-permute-start.5
  7.7 8.3 %collective-permute-start.2 = (bf16[2,2,256,256]{3,2,1,0:T(8,128)(2,1)}, bf16[2,2,256,256]{3,2,1,0:T(8,128)(2,1)}, u32[]{:S(2)}, u32[]{:S(2)}) collective-permute-start(bf16[2,2,256,256]{3,2,1,0:T(8,128)(2,1)} %slice_bitcast_fusion), channel_id=1, source_target_pairs={{0,8},{1,9},{16,24},{17,25}} | collective-permute-start | bytes 1572872 | tf_op jit(solution)/shard_map/ppermute | solution.py:21
  16.0 1.4 fusion.86
  17.8 1.1 broadcast_select_fusion.6
  23.3 3.7 %collective-permute-done.2 = bf16[2,2,256,256]{3,2,1,0:T(8,128)(2,1)} collective-permute-done((bf16[2,2,256,256]{3,2,1,0:T(8,128)(2,1)}, bf16[2,2,256,256]{3,2,1,0:T(8,128)(2,1)}, u32[]{:S(2)}, u32[]{:S(2)}) %collective-permute-start.2) | collective-permute-done | bytes 524320 | tf_op jit(solution)/shard_map/ppermute | solution.py:21
  27.1 1.3 collective-permute-start.3
  28.4 1.6 multiply_convert_fusion.2
  30.0 1.5 collective-permute-start.1
  32.5 1.3 collective-permute-done.5
  34.2 1.1 multiply_convert_fusion
  39.9 4.8 %collective-permute-start.4 = (bf16[2,2,256,256]{3,2,1,0:T(8,128)(2,1)S(1)}, bf16[2,2,256,256]{3,2,1,0:T(8,128)(2,1)S(1)}, u32[]{:S(2)}, u32[]{:S(2)}) collective-permute-start(bf16[2,2,256,256]{3,2,1,0:T(8,128)(2,1)S(1)} %broadcast_select_fusion.1), channel_id=1, source_target_pairs={{0,2},{4,6},{8,10},{12,14},{1,3},{5,7},{9,11},{13,15},{16,18},{20,... | collective-permute-start | bytes 1572872 | tf_op jit(solution)/shard_map/ppermute | solution.py:21
  45.0 1.5 collective-permute-start.7
  48.2 19.4 %collective-permute-done.4 = bf16[2,2,256,256]{3,2,1,0:T(8,128)(2,1)S(1)} collective-permute-done((bf16[2,2,256,256]{3,2,1,0:T(8,128)(2,1)S(1)}, bf16[2,2,256,256]{3,2,1,0:T(8,128)(2,1)S(1)}, u32[]{:S(2)}, u32[]{:S(2)}) %collective-permute-start.4) | collective-permute-done | bytes 524320 | tf_op jit(solution)/shard_map/ppermute | solution.py:21
  68.7 21.6 %collective-permute-done.7 = f32[2,2,256,256]{3,2,1,0:T(8,128)S(1)} collective-permute-done((f32[2,2,256,256]{3,2,1,0:T(8,128)S(1)}, f32[2,2,256,256]{3,2,1,0:T(8,128)S(1)}, u32[]{:S(2)}, u32[]{:S(2)}) %collective-permute-start.7) | collective-permute-done | bytes 1048608 | tf_op jit(solution)/shard_map/ppermute | solution.py:32
  91.2 0.9 select_maximum_fusion
  95.4 1.8 multiply_convert_fusion.1
  97.1 18.4 %collective-permute-done.10 = f32[832,256]{1,0:T(8,128)S(1)} collective-permute-done((f32[832,256]{1,0:T(8,128)S(1)}, f32[832,256]{1,0:T(8,128)S(1)}, u32[]{:S(2)}, u32[]{:S(2)}) %collective-permute-start.10) | collective-permute-done | bytes 852000 | tf_op jit(solution)/shard_map/ppermute | solution.py:46
  115.8 2.7 %collective-permute-start.12 = (f32[208,256]{1,0:T(8,128)S(1)}, f32[208,256]{1,0:T(8,128)S(1)}, u32[]{:S(2)}, u32[]{:S(2)}) collective-permute-start(f32[208,256]{1,0:T(8,128)S(1)} %get-tuple-element.17), channel_id=1, source_target_pairs={{0,8},{2,10},{4,12},{6,14},{8,0},{10,2},{12,4},{14,6},{1,9},{3,11}... | collective-permute-start | bytes 638984 | tf_op jit(solution)/shard_map/ppermute | solution.py:72
  118.5 2.8 %collective-permute-start.13 = (f32[208,256]{1,0:T(8,128)S(1)}, f32[208,256]{1,0:T(8,128)S(1)}, u32[]{:S(2)}, u32[]{:S(2)}) collective-permute-start(f32[208,256]{1,0:T(8,128)S(1)} %get-tuple-element.16), channel_id=1, source_target_pairs={{0,12},{2,14},{4,0},{6,2},{8,4},{10,6},{12,8},{14,10},{1,13},{3,15... | collective-permute-start | bytes 638984 | tf_op jit(solution)/shard_map/ppermute | solution.py:72
  121.8 1.3 collective-permute-start.8
  123.1 2.8 %collective-permute-done.11 = f32[208,256]{1,0:T(8,128)S(1)} collective-permute-done((f32[208,256]{1,0:T(8,128)S(1)}, f32[208,256]{1,0:T(8,128)S(1)}, u32[]{:S(2)}, u32[]{:S(2)}) %collective-permute-start.11) | collective-permute-done | bytes 213024 | tf_op jit(solution)/shard_map/ppermute | solution.py:72
  125.9 7.5 %collective-permute-done.12 = f32[208,256]{1,0:T(8,128)S(1)} collective-permute-done((f32[208,256]{1,0:T(8,128)S(1)}, f32[208,256]{1,0:T(8,128)S(1)}, u32[]{:S(2)}, u32[]{:S(2)}) %collective-permute-start.12) | collective-permute-done | bytes 213024 | tf_op jit(solution)/shard_map/ppermute | solution.py:72
  133.5 5.2 %collective-permute-start.14 = (bf16[208,256]{1,0:T(8,128)(2,1)S(1)}, bf16[208,256]{1,0:T(8,128)(2,1)S(1)}, u32[]{:S(2)}, u32[]{:S(2)}) collective-permute-start(bf16[208,256]{1,0:T(8,128)(2,1)S(1)} %get-tuple-element.10), channel_id=1, source_target_pairs={{0,4},{2,6},{4,8},{6,10},{8,12},{10,14},{12,0},{14,2},{1,5},{3,7},... | collective-permute-start | bytes 319496 | tf_op jit(solution)/shard_map/ppermute | solution.py:85
  139.1 1.6 collective-permute-start.15
  140.7 0.9 collective-permute-start.16
  141.6 1.9 %collective-permute-done.14 = bf16[208,256]{1,0:T(8,128)(2,1)S(1)} collective-permute-done((bf16[208,256]{1,0:T(8,128)(2,1)S(1)}, bf16[208,256]{1,0:T(8,128)(2,1)S(1)}, u32[]{:S(2)}, u32[]{:S(2)}) %collective-permute-start.14) | collective-permute-done | bytes 106528 | tf_op jit(solution)/shard_map/ppermute | solution.py:85
  143.5 23.8 %collective-permute-done.15 = bf16[208,256]{1,0:T(8,128)(2,1)S(1)} collective-permute-done((bf16[208,256]{1,0:T(8,128)(2,1)S(1)}, bf16[208,256]{1,0:T(8,128)(2,1)S(1)}, u32[]{:S(2)}, u32[]{:S(2)}) %collective-permute-start.15) | collective-permute-done | bytes 106528 | tf_op jit(solution)/shard_map/ppermute | solution.py:85
  168.6 8.7 %collective-permute-done.17 = bf16[832,256]{1,0:T(8,128)(2,1)S(1)} collective-permute-done((bf16[832,256]{1,0:T(8,128)(2,1)S(1)}, bf16[832,256]{1,0:T(8,128)(2,1)S(1)}, u32[]{:S(2)}, u32[]{:S(2)}) %collective-permute-start.17) | collective-permute-done | bytes 426016 | tf_op jit(solution)/shard_map/ppermute | solution.py:54
  177.6 2.2 %fusion.4 = bf16[2,2,2,256,256]{4,3,2,1,0:T(8,128)(2,1)} fusion(bf16[2,2,2,256,256]{4,3,2,1,0:T(8,128)(2,1)S(1)} %get-tuple-element.12, f32[2,2,2,256,256]{4,3,2,1,0:T(8,128)S(1)} %fusion.17, f32[2,2,2,256,256]{4,3,2,1,0:T(8,128)S(1)} %fusion.35, f32[2,2,2,256,256]{4,3,2,1,0:T(8,128)S(1)} %fusion.37, f32[2,2,2,256,256]{4,3,2,1,0:T(8,128)S(1)} %fusion.84, ...), kind=kOutput, calls=%fused_computation.13 | convolution fusion | flops 275775488 | bytes 21104128 | tf_op jit(solution)/shard_map/dot_general | solution.py:140
  180.4 1.1 slice.203
  (89 shorter events, 25.5 us)
Async XLA Ops:
  0.6 94.0 %copy-start = (bf16[256,256]{1,0:T(8,128)(2,1)S(1)}, bf16[256,256]{1,0:T(8,128)(2,1)}, u32[]{:S(2)}) copy-start(bf16[256,256]{1,0:T(8,128)(2,1)} %param.11) | copy-start | bytes 393220
  0.6 3.5 %copy-start.4 = (bf16[2,2,2,256,256]{4,3,2,1,0:T(8,128)(2,1)S(1)}, bf16[2,2,2,256,256]{4,3,2,1,0:T(8,128)(2,1)}, u32[]{:S(2)}) copy-start(bf16[2,2,2,256,256]{4,3,2,1,0:T(8,128)(2,1)} %param.7) | copy-start | bytes 3145732
  3.7 14.1 %collective-permute-start = (bf16[2,2,1,256,256]{4,3,2,1,0:T(8,128)(2,1)}, bf16[2,2,1,256,256]{4,3,2,1,0:T(8,128)(2,1)}, u32[]{:S(2)}, u32[]{:S(2)}) collective-permute-start(bf16[2,2,1,256,256]{4,3,2,1,0:T(8,128)(2,1)} %slice_select_fusion.1), channel_id=1, source_target_pairs={{0,1},{1,0},{2,3},{3,2},{4,5},{5,4},{6,7},{7,6},{8,9},{9,8},{10,11... | collective-permute-start | bytes 1572872 | tf_op jit(solution)/shard_map/ppermute | solution.py:183
  5.6 28.2 %collective-permute-start.5 = (bf16[2,2,2,256,256]{4,3,2,1,0:T(8,128)(2,1)S(1)}, bf16[2,2,2,256,256]{4,3,2,1,0:T(8,128)(2,1)S(1)}, u32[]{:S(2)}, u32[]{:S(2)}) collective-permute-start(bf16[2,2,2,256,256]{4,3,2,1,0:T(8,128)(2,1)S(1)} %get-tuple-element.12), channel_id=1, source_target_pairs={{2,0},{4,2},{6,4},{8,6},{10,8},{12,10},{14,12},{3,1},{5,3},{7,5},{... | collective-permute-start | bytes 3145736 | tf_op jit(solution)/shard_map/ppermute | solution.py:10
  7.7 19.4 %collective-permute-start.2 = (bf16[2,2,256,256]{3,2,1,0:T(8,128)(2,1)}, bf16[2,2,256,256]{3,2,1,0:T(8,128)(2,1)}, u32[]{:S(2)}, u32[]{:S(2)}) collective-permute-start(bf16[2,2,256,256]{3,2,1,0:T(8,128)(2,1)} %slice_bitcast_fusion), channel_id=1, source_target_pairs={{0,8},{1,9},{16,24},{17,25}} | collective-permute-start | bytes 1572872 | tf_op jit(solution)/shard_map/ppermute | solution.py:21
  16.0 1.4 copy-start.3
  19.0 1.3 copy-start.2
  27.1 12.7 %collective-permute-start.3 = (bf16[2,2,256,256]{3,2,1,0:T(8,128)(2,1)S(1)}, bf16[2,2,256,256]{3,2,1,0:T(8,128)(2,1)S(1)}, u32[]{:S(2)}, u32[]{:S(2)}) collective-permute-start(bf16[2,2,256,256]{3,2,1,0:T(8,128)(2,1)S(1)} %broadcast_select_fusion), channel_id=1, source_target_pairs={{0,4},{8,12},{1,5},{9,13},{16,20},{24,28},{17,21},{25,29}} | collective-permute-start | bytes 1572872 | tf_op jit(solution)/shard_map/ppermute | solution.py:21
  30.0 60.7 %collective-permute-start.1 = (bf16[2,2,2,256,256]{4,3,2,1,0:T(8,128)(2,1)S(1)}, bf16[2,2,2,256,256]{4,3,2,1,0:T(8,128)(2,1)S(1)}, u32[]{:S(2)}, u32[]{:S(2)}) collective-permute-start(bf16[2,2,2,256,256]{4,3,2,1,0:T(8,128)(2,1)S(1)} %get-tuple-element.22), channel_id=1, source_target_pairs={{0,2},{2,4},{4,6},{6,8},{8,10},{10,12},{12,14},{1,3},{3,5},{5,7},{... | collective-permute-start | bytes 3145736 | tf_op jit(solution)/shard_map/ppermute | solution.py:10
  39.8 5.1 %copy-start.1 = (f32[2,2,256,256]{3,2,1,0:T(8,128)S(1)}, f32[2,2,256,256]{3,2,1,0:T(8,128)}, u32[]{:S(2)}) copy-start(f32[2,2,256,256]{3,2,1,0:T(8,128)} %get-tuple-element.11) | copy-start | bytes 3145732
  39.9 27.7 %collective-permute-start.4 = (bf16[2,2,256,256]{3,2,1,0:T(8,128)(2,1)S(1)}, bf16[2,2,256,256]{3,2,1,0:T(8,128)(2,1)S(1)}, u32[]{:S(2)}, u32[]{:S(2)}) collective-permute-start(bf16[2,2,256,256]{3,2,1,0:T(8,128)(2,1)S(1)} %broadcast_select_fusion.1), channel_id=1, source_target_pairs={{0,2},{4,6},{8,10},{12,14},{1,3},{5,7},{9,11},{13,15},{16,18},{20,... | collective-permute-start | bytes 1572872 | tf_op jit(solution)/shard_map/ppermute | solution.py:21
  45.0 45.2 %collective-permute-start.7 = (f32[2,2,256,256]{3,2,1,0:T(8,128)S(1)}, f32[2,2,256,256]{3,2,1,0:T(8,128)S(1)}, u32[]{:S(2)}, u32[]{:S(2)}) collective-permute-start(f32[2,2,256,256]{3,2,1,0:T(8,128)S(1)} %add.244), channel_id=1, source_target_pairs={{4,0},{12,8},{5,1},{13,9},{20,16},{28,24},{21,17},{29,25}} | collective-permute-start | bytes 3145736 | tf_op jit(solution)/shard_map/ppermute | solution.py:32
  46.6 44.1 %collective-permute-start.6 = (bf16[2,2,1,256,256]{4,3,2,1,0:T(8,128)(2,1)S(1)}, bf16[2,2,1,256,256]{4,3,2,1,0:T(8,128)(2,1)S(1)}, u32[]{:S(2)}, u32[]{:S(2)}) collective-permute-start(bf16[2,2,1,256,256]{4,3,2,1,0:T(8,128)(2,1)S(1)} %slice_select_fusion), channel_id=1, source_target_pairs={{0,1},{1,0},{2,3},{3,2},{4,5},{5,4},{6,7},{7,6},{8,9},{9,8},{10,11... | collective-permute-start | bytes 1572872 | tf_op jit(solution)/shard_map/ppermute | solution.py:183
  90.5 3.7 %collective-permute-start.9 = (f32[1664,256]{1,0:T(8,128)S(1)}, f32[1664,256]{1,0:T(8,128)S(1)}, u32[]{:S(2)}, u32[]{:S(2)}) collective-permute-start(f32[1664,256]{1,0:T(8,128)S(1)} %constant_dynamic-slice_fusion.4), channel_id=1, source_target_pairs={{0,1},{1,0},{2,3},{3,2},{4,5},{5,4},{6,7},{7,6},{8,9},{9,8},{10,11... | collective-permute-start | bytes 5111816 | tf_op jit(solution)/shard_map/ppermute | solution.py:46
  94.5 21.1 %collective-permute-start.10 = (f32[832,256]{1,0:T(8,128)S(1)}, f32[832,256]{1,0:T(8,128)S(1)}, u32[]{:S(2)}, u32[]{:S(2)}) collective-permute-start(f32[832,256]{1,0:T(8,128)S(1)} %constant_dynamic-slice_fusion.3), channel_id=1, source_target_pairs={{0,2},{2,0},{4,6},{6,4},{8,10},{10,8},{12,14},{14,12},{1,3},{3,1},... | collective-permute-start | bytes 2555912 | tf_op jit(solution)/shard_map/ppermute | solution.py:46
  115.7 10.1 %collective-permute-start.11 = (f32[208,256]{1,0:T(8,128)S(1)}, f32[208,256]{1,0:T(8,128)S(1)}, u32[]{:S(2)}, u32[]{:S(2)}) collective-permute-start(f32[208,256]{1,0:T(8,128)S(1)} %get-tuple-element.15), channel_id=1, source_target_pairs={{0,4},{2,6},{4,8},{6,10},{8,12},{10,14},{12,0},{14,2},{1,5},{3,7},... | collective-permute-start | bytes 638984 | tf_op jit(solution)/shard_map/ppermute | solution.py:72
  115.8 17.6 %collective-permute-start.12 = (f32[208,256]{1,0:T(8,128)S(1)}, f32[208,256]{1,0:T(8,128)S(1)}, u32[]{:S(2)}, u32[]{:S(2)}) collective-permute-start(f32[208,256]{1,0:T(8,128)S(1)} %get-tuple-element.17), channel_id=1, source_target_pairs={{0,8},{2,10},{4,12},{6,14},{8,0},{10,2},{12,4},{14,6},{1,9},{3,11}... | collective-permute-start | bytes 638984 | tf_op jit(solution)/shard_map/ppermute | solution.py:72
  118.5 14.9 %collective-permute-start.13 = (f32[208,256]{1,0:T(8,128)S(1)}, f32[208,256]{1,0:T(8,128)S(1)}, u32[]{:S(2)}, u32[]{:S(2)}) collective-permute-start(f32[208,256]{1,0:T(8,128)S(1)} %get-tuple-element.16), channel_id=1, source_target_pairs={{0,12},{2,14},{4,0},{6,2},{8,4},{10,6},{12,8},{14,10},{1,13},{3,15... | collective-permute-start | bytes 638984 | tf_op jit(solution)/shard_map/ppermute | solution.py:72
  121.8 46.1 %collective-permute-start.8 = (f32[2,2,256,256]{3,2,1,0:T(8,128)S(1)}, f32[2,2,256,256]{3,2,1,0:T(8,128)S(1)}, u32[]{:S(2)}, u32[]{:S(2)}) collective-permute-start(f32[2,2,256,256]{3,2,1,0:T(8,128)S(1)} %add.245), channel_id=1, source_target_pairs={{8,0},{9,1},{24,16},{25,17}} | collective-permute-start | bytes 3145736 | tf_op jit(solution)/shard_map/ppermute | solution.py:32
  133.5 10.0 %collective-permute-start.14 = (bf16[208,256]{1,0:T(8,128)(2,1)S(1)}, bf16[208,256]{1,0:T(8,128)(2,1)S(1)}, u32[]{:S(2)}, u32[]{:S(2)}) collective-permute-start(bf16[208,256]{1,0:T(8,128)(2,1)S(1)} %get-tuple-element.10), channel_id=1, source_target_pairs={{0,4},{2,6},{4,8},{6,10},{8,12},{10,14},{12,0},{14,2},{1,5},{3,7},... | collective-permute-start | bytes 319496 | tf_op jit(solution)/shard_map/ppermute | solution.py:85
  139.1 28.2 %collective-permute-start.15 = (bf16[208,256]{1,0:T(8,128)(2,1)S(1)}, bf16[208,256]{1,0:T(8,128)(2,1)S(1)}, u32[]{:S(2)}, u32[]{:S(2)}) collective-permute-start(bf16[208,256]{1,0:T(8,128)(2,1)S(1)} %get-tuple-element.10), channel_id=1, source_target_pairs={{0,8},{2,10},{4,12},{6,14},{8,0},{10,2},{12,4},{14,6},{1,9},{3,11}... | collective-permute-start | bytes 319496 | tf_op jit(solution)/shard_map/ppermute | solution.py:85
  140.7 26.6 %collective-permute-start.16 = (bf16[208,256]{1,0:T(8,128)(2,1)S(1)}, bf16[208,256]{1,0:T(8,128)(2,1)S(1)}, u32[]{:S(2)}, u32[]{:S(2)}) collective-permute-start(bf16[208,256]{1,0:T(8,128)(2,1)S(1)} %get-tuple-element.10), channel_id=1, source_target_pairs={{0,12},{2,14},{4,0},{6,2},{8,4},{10,6},{12,8},{14,10},{1,13},{3,15... | collective-permute-start | bytes 319496 | tf_op jit(solution)/shard_map/ppermute | solution.py:85
  167.4 9.9 %collective-permute-start.17 = (bf16[832,256]{1,0:T(8,128)(2,1)S(1)}, bf16[832,256]{1,0:T(8,128)(2,1)S(1)}, u32[]{:S(2)}, u32[]{:S(2)}) collective-permute-start(bf16[832,256]{1,0:T(8,128)(2,1)S(1)} %bitcast.256), channel_id=1, source_target_pairs={{0,2},{2,0},{4,6},{6,4},{8,10},{10,8},{12,14},{14,12},{1,3},{3,1},... | collective-permute-start | bytes 1277960 | tf_op jit(solution)/shard_map/ppermute | solution.py:54
  177.5 2.4 %collective-permute-start.18 = (bf16[1664,256]{1,0:T(8,128)(2,1)S(1)}, bf16[1664,256]{1,0:T(8,128)(2,1)S(1)}, u32[]{:S(2)}, u32[]{:S(2)}) collective-permute-start(bf16[1664,256]{1,0:T(8,128)(2,1)S(1)} %maximum_select_fusion.1), channel_id=1, source_target_pairs={{0,1},{1,0},{2,3},{3,2},{4,5},{5,4},{6,7},{7,6},{8,9},{9,8},{10,11... | collective-permute-start | bytes 2555912 | tf_op jit(solution)/shard_map/ppermute | solution.py:54

commit v11 on v7

--- a/solution.py
+++ b/solution.py
@@ -113,11 +113,11 @@
     if padded_rows != rows:
         flat = jnp.pad(flat, ((0, padded_rows - rows), (0, 0)))
     flat = xor_halving(flat, "tm", tm_steps)
+    flat = direct_scatter(flat, "space", low, high)
     flat = xor_halving(flat, "space", sp_steps)
-    flat = direct_scatter(flat, "space", low, high)
     piece = (flat * scale).astype(jnp.bfloat16)
+    piece = xor_doubling(piece, "space", sp_steps)
     piece = direct_gather(piece, "space", low, high)
-    piece = xor_doubling(piece, "space", sp_steps)
     piece = xor_doubling(piece, "tm", tm_steps)
     return piece[:rows]
 

time: 173 us -> 172 us (level)
  starting transfers between devices: 42.3 us -> 38.8 us
  waiting for transfers between devices: 91.2 us -> 93.8 us
    ppermute x2, waiting for transfers between devices: 0.01 us -> 37.7 us  [tree_reduce(): value = value + lax.ppermute(value, axis, pairs)]
    ppermute x3, waiting for transfers between devices: 25.7 us -> 10.9 us  [direct_gather(): got = lax.ppermute(piece, axis, pairs)]
    ppermute x2, waiting for transfers between devices: 18.2 us -> 6.6 us  [xor_halving(): flat = keep + lax.ppermute(send, axis, pairs)]
    ppermute x2, waiting for transfers between devices: 10.5 us -> 4.07 us  [xor_doubling(): got = lax.ppermute(piece, axis, [(i, i ^ step) for i in range(count)])]
    ppermute x2, starting transfers between devices: 2.64 us -> 0.15 us  [xor_halving(): flat = keep + lax.ppermute(send, axis, pairs)]
    ppermute x3, waiting for transfers between devices: 12.1 us -> 10.2 us  [direct_scatter(): total = total + lax.ppermute(send, axis, pairs)]
  transfers between devices with their start and end apart: 19 -> 19, of which waited for: 10 -> 12; matrix products, arithmetic and copies ran while one was open for 18% -> 18% of each run, Pallas kernels for 0% -> 0%
where the time goes in v11:
time: 172 us
  waiting for transfers between devices  93.8 us (55%)
  starting transfers between devices  38.8 us (23%)
  matrix products  24.4 us (14%)
  other arithmetic  9.16 us (5%)
  local copies, waits for them, and re-layouts  4.68 us (3%)
    ppermute x2, waiting for transfers between devices, tree_reduce(): value = value + lax.ppermute(value, axis, pairs)  37.7 us
    ppermute x3, waiting for transfers between devices, tree_broadcast(): got = lax.ppermute(value, axis, pairs)  23.1 us
    ppermute x3, starting transfers between devices, tree_broadcast(): got = lax.ppermute(value, axis, pairs)  14.4 us
    dot_general x18, matrix products, spatial_sum(): total = total + jnp.dot(piece, kernel, preferred_element_type=jnp.float32)  12.1 us
    ppermute x3, starting transfers between devices, direct_scatter(): total = total + lax.ppermute(send, axis, pairs)  11.6 us
    ppermute x3, waiting for transfers between devices, direct_gather(): got = lax.ppermute(piece, axis, pairs)  10.9 us
    ppermute x3, waiting for transfers between devices, direct_scatter(): total = total + lax.ppermute(send, axis, pairs)  10.2 us
    ppermute x2, waiting for transfers between devices, xor_halving(): flat = keep + lax.ppermute(send, axis, pairs)  6.6 us
  transfers between devices with their start and end apart: 19, of which 12 were waited for; matrix products, arithmetic and copies ran while one was open for 18% of the time, Pallas kernels for 0%

profile of v11, /device:TPU:0, one launch (start us, length us, event | category | flops | bytes accessed | tf_op | source)
XLA Modules:
  0.0 172.1 jit_solution(14275347751783947696)
XLA Ops:
  1.5 1.4 broadcast_multiply_fusion.1
  2.9 0.9 slice_select_fusion.1
  4.2 1.4 convert_reduce_fusion
  5.6 1.3 collective-permute-start.5
  7.7 8.3 %collective-permute-start.2 = (bf16[2,2,256,256]{3,2,1,0:T(8,128)(2,1)}, bf16[2,2,256,256]{3,2,1,0:T(8,128)(2,1)}, u32[]{:S(2)}, u32[]{:S(2)}) collective-permute-start(bf16[2,2,256,256]{3,2,1,0:T(8,128)(2,1)} %slice_bitcast_fusion), channel_id=1, source_target_pairs={{0,8},{1,9},{16,24},{17,25}} | collective-permute-start | bytes 1572872 | tf_op jit(solution)/shard_map/ppermute | solution.py:21
  16.0 1.4 fusion.87
  17.8 1.1 broadcast_select_fusion.6
  23.3 3.7 %collective-permute-done.2 = bf16[2,2,256,256]{3,2,1,0:T(8,128)(2,1)} collective-permute-done((bf16[2,2,256,256]{3,2,1,0:T(8,128)(2,1)}, bf16[2,2,256,256]{3,2,1,0:T(8,128)(2,1)}, u32[]{:S(2)}, u32[]{:S(2)}) %collective-permute-start.2) | collective-permute-done | bytes 524320 | tf_op jit(solution)/shard_map/ppermute | solution.py:21
  27.1 1.3 collective-permute-start.3
  28.4 1.6 multiply_convert_fusion.2
  30.0 1.5 collective-permute-start.1
  32.5 1.3 collective-permute-done.5
  34.2 1.1 multiply_convert_fusion
  39.5 4.8 %collective-permute-start.4 = (bf16[2,2,256,256]{3,2,1,0:T(8,128)(2,1)S(1)}, bf16[2,2,256,256]{3,2,1,0:T(8,128)(2,1)S(1)}, u32[]{:S(2)}, u32[]{:S(2)}) collective-permute-start(bf16[2,2,256,256]{3,2,1,0:T(8,128)(2,1)S(1)} %broadcast_select_fusion.1), channel_id=1, source_target_pairs={{0,2},{4,6},{8,10},{12,14},{1,3},{5,7},{9,11},{13,15},{16,18},{20,... | collective-permute-start | bytes 1572872 | tf_op jit(solution)/shard_map/ppermute | solution.py:21
  44.7 1.5 collective-permute-start.7
  48.2 19.4 %collective-permute-done.4 = bf16[2,2,256,256]{3,2,1,0:T(8,128)(2,1)S(1)} collective-permute-done((bf16[2,2,256,256]{3,2,1,0:T(8,128)(2,1)S(1)}, bf16[2,2,256,256]{3,2,1,0:T(8,128)(2,1)S(1)}, u32[]{:S(2)}, u32[]{:S(2)}) %collective-permute-start.4) | collective-permute-done | bytes 524320 | tf_op jit(solution)/shard_map/ppermute | solution.py:21
  69.0 0.9 select_maximum_fusion
  73.9 9.0 %collective-permute-start.10 = (f32[416,256]{1,0:T(8,128)S(1)}, f32[416,256]{1,0:T(8,128)S(1)}, u32[]{:S(2)}, u32[]{:S(2)}) collective-permute-start(f32[416,256]{1,0:T(8,128)S(1)} %get-tuple-element.9), channel_id=1, source_target_pairs={{0,4},{2,6},{4,8},{6,10},{8,12},{10,14},{12,0},{14,2},{1,5},{3,7},... | collective-permute-start | bytes 1277960 | tf_op jit(solution)/shard_map/ppermute | solution.py:71
  82.9 2.6 %collective-permute-start.11 = (f32[416,256]{1,0:T(8,128)S(1)}, f32[416,256]{1,0:T(8,128)S(1)}, u32[]{:S(2)}, u32[]{:S(2)}) collective-permute-start(f32[416,256]{1,0:T(8,128)S(1)} %get-tuple-element.11), channel_id=1, source_target_pairs={{0,8},{2,10},{4,12},{6,14},{8,0},{10,2},{12,4},{14,6},{1,9},{3,11}... | collective-permute-start | bytes 1277960 | tf_op jit(solution)/shard_map/ppermute | solution.py:71
  85.5 1.8 %multiply_convert_fusion.1 = bf16[2,2,2,256,256]{4,3,2,1,0:T(8,128)(2,1)} fusion(f32[2,2,2,256,256]{4,3,2,1,0:T(8,128)S(1)} %fusion.106, f32[2,2,2,256,256]{4,3,2,1,0:T(8,128)S(1)} %fusion.5, bf16[2,2,2,256,256]{4,3,2,1,0:T(8,128)(2,1)S(1)} %broadcast_multiply_fusion.1, f32[2,2]{1,0:T(2,128)S(1)} %get-tuple-element.7, f32[2,2,256,256]{3,2,1,0:T(8,128)S(1)} %fusion.70, ...), kind=kOutput, calls=%fused_computation.24 | convolution fusion | flops 272105472 | bytes 8520704 | tf_op jit(solution)/shard_map/dot_general | solution.py:146
  87.3 19.4 %collective-permute-done.7 = f32[2,2,256,256]{3,2,1,0:T(8,128)S(1)} collective-permute-done((f32[2,2,256,256]{3,2,1,0:T(8,128)S(1)}, f32[2,2,256,256]{3,2,1,0:T(8,128)S(1)}, u32[]{:S(2)}, u32[]{:S(2)}) %collective-permute-start.7) | collective-permute-done | bytes 1048608 | tf_op jit(solution)/shard_map/ppermute | solution.py:31
  106.8 1.3 collective-permute-start.8
  108.1 6.7 %collective-permute-done.11 = f32[416,256]{1,0:T(8,128)S(1)} collective-permute-done((f32[416,256]{1,0:T(8,128)S(1)}, f32[416,256]{1,0:T(8,128)S(1)}, u32[]{:S(2)}, u32[]{:S(2)}) %collective-permute-start.11) | collective-permute-done | bytes 426016 | tf_op jit(solution)/shard_map/ppermute | solution.py:71
  114.8 3.5 %collective-permute-done.12 = f32[416,256]{1,0:T(8,128)S(1)} collective-permute-done((f32[416,256]{1,0:T(8,128)S(1)}, f32[416,256]{1,0:T(8,128)S(1)}, u32[]{:S(2)}, u32[]{:S(2)}) %collective-permute-start.12) | collective-permute-done | bytes 426016 | tf_op jit(solution)/shard_map/ppermute | solution.py:71
  119.0 6.6 %collective-permute-done.13 = f32[208,256]{1,0:T(8,128)S(1)} collective-permute-done((f32[208,256]{1,0:T(8,128)S(1)}, f32[208,256]{1,0:T(8,128)S(1)}, u32[]{:S(2)}, u32[]{:S(2)}) %collective-permute-start.13) | collective-permute-done | bytes 213024 | tf_op jit(solution)/shard_map/ppermute | solution.py:45
  126.4 3.9 %collective-permute-done.14 = bf16[208,256]{1,0:T(8,128)(2,1)S(1)} collective-permute-done((bf16[208,256]{1,0:T(8,128)(2,1)S(1)}, bf16[208,256]{1,0:T(8,128)(2,1)S(1)}, u32[]{:S(2)}, u32[]{:S(2)}) %collective-permute-start.14) | collective-permute-done | bytes 106528 | tf_op jit(solution)/shard_map/ppermute | solution.py:53
  130.5 6.0 %collective-permute-start.15 = (bf16[416,256]{1,0:T(8,128)(2,1)S(1)}, bf16[416,256]{1,0:T(8,128)(2,1)S(1)}, u32[]{:S(2)}, u32[]{:S(2)}) collective-permute-start(bf16[416,256]{1,0:T(8,128)(2,1)S(1)} %maximum_select_fusion.2), channel_id=1, source_target_pairs={{0,4},{2,6},{4,8},{6,10},{8,12},{10,14},{12,0},{14,2},{1,5},{3,7},... | collective-permute-start | bytes 638984 | tf_op jit(solution)/shard_map/ppermute | solution.py:84
  136.4 18.3 %collective-permute-done.8 = f32[2,2,256,256]{3,2,1,0:T(8,128)S(1)} collective-permute-done((f32[2,2,256,256]{3,2,1,0:T(8,128)S(1)}, f32[2,2,256,256]{3,2,1,0:T(8,128)S(1)}, u32[]{:S(2)}, u32[]{:S(2)}) %collective-permute-start.8) | collective-permute-done | bytes 1048608 | tf_op jit(solution)/shard_map/ppermute | solution.py:31
  155.7 8.8 %collective-permute-done.16 = bf16[416,256]{1,0:T(8,128)(2,1)S(1)} collective-permute-done((bf16[416,256]{1,0:T(8,128)(2,1)S(1)}, bf16[416,256]{1,0:T(8,128)(2,1)S(1)}, u32[]{:S(2)}, u32[]{:S(2)}) %collective-permute-start.16) | collective-permute-done | bytes 213024 | tf_op jit(solution)/shard_map/ppermute | solution.py:84
  164.6 2.0 %collective-permute-done.17 = bf16[416,256]{1,0:T(8,128)(2,1)S(1)} collective-permute-done((bf16[416,256]{1,0:T(8,128)(2,1)S(1)}, bf16[416,256]{1,0:T(8,128)(2,1)S(1)}, u32[]{:S(2)}, u32[]{:S(2)}) %collective-permute-start.17) | collective-permute-done | bytes 213024 | tf_op jit(solution)/shard_map/ppermute | solution.py:84
  166.7 2.2 %fusion.4 = bf16[2,2,2,256,256]{4,3,2,1,0:T(8,128)(2,1)} fusion(bf16[2,2,2,256,256]{4,3,2,1,0:T(8,128)(2,1)S(1)} %get-tuple-element.6, f32[2,2,2,256,256]{4,3,2,1,0:T(8,128)S(1)} %fusion.17, f32[2,2,2,256,256]{4,3,2,1,0:T(8,128)S(1)} %fusion.35, f32[2,2,2,256,256]{4,3,2,1,0:T(8,128)S(1)} %fusion.37, f32[2,2,2,256,256]{4,3,2,1,0:T(8,128)S(1)} %fusion.85, ...), kind=kOutput, calls=%fused_computation.13 | convolution fusion | flops 275775488 | bytes 21104128 | tf_op jit(solution)/shard_map/dot_general | solution.py:139
  169.5 1.1 slice.203
  (94 shorter events, 24.8 us)
Async XLA Ops:
  0.6 70.2 %copy-start = (bf16[256,256]{1,0:T(8,128)(2,1)S(1)}, bf16[256,256]{1,0:T(8,128)(2,1)}, u32[]{:S(2)}) copy-start(bf16[256,256]{1,0:T(8,128)(2,1)} %param.11) | copy-start | bytes 393220
  0.6 3.5 %copy-start.6 = (bf16[2,2,2,256,256]{4,3,2,1,0:T(8,128)(2,1)S(1)}, bf16[2,2,2,256,256]{4,3,2,1,0:T(8,128)(2,1)}, u32[]{:S(2)}) copy-start(bf16[2,2,2,256,256]{4,3,2,1,0:T(8,128)(2,1)} %param.7) | copy-start | bytes 3145732
  3.7 14.1 %collective-permute-start = (bf16[2,2,1,256,256]{4,3,2,1,0:T(8,128)(2,1)}, bf16[2,2,1,256,256]{4,3,2,1,0:T(8,128)(2,1)}, u32[]{:S(2)}, u32[]{:S(2)}) collective-permute-start(bf16[2,2,1,256,256]{4,3,2,1,0:T(8,128)(2,1)} %slice_select_fusion.1), channel_id=1, source_target_pairs={{0,1},{1,0},{2,3},{3,2},{4,5},{5,4},{6,7},{7,6},{8,9},{9,8},{10,11... | collective-permute-start | bytes 1572872 | tf_op jit(solution)/shard_map/ppermute | solution.py:182
  5.6 28.2 %collective-permute-start.5 = (bf16[2,2,2,256,256]{4,3,2,1,0:T(8,128)(2,1)S(1)}, bf16[2,2,2,256,256]{4,3,2,1,0:T(8,128)(2,1)S(1)}, u32[]{:S(2)}, u32[]{:S(2)}) collective-permute-start(bf16[2,2,2,256,256]{4,3,2,1,0:T(8,128)(2,1)S(1)} %get-tuple-element.6), channel_id=1, source_target_pairs={{2,0},{4,2},{6,4},{8,6},{10,8},{12,10},{14,12},{3,1},{5,3},{7,5},{... | collective-permute-start | bytes 3145736 | tf_op jit(solution)/shard_map/ppermute | solution.py:10
  7.7 19.4 %collective-permute-start.2 = (bf16[2,2,256,256]{3,2,1,0:T(8,128)(2,1)}, bf16[2,2,256,256]{3,2,1,0:T(8,128)(2,1)}, u32[]{:S(2)}, u32[]{:S(2)}) collective-permute-start(bf16[2,2,256,256]{3,2,1,0:T(8,128)(2,1)} %slice_bitcast_fusion), channel_id=1, source_target_pairs={{0,8},{1,9},{16,24},{17,25}} | collective-permute-start | bytes 1572872 | tf_op jit(solution)/shard_map/ppermute | solution.py:21
  16.0 1.4 copy-start.5
  19.0 1.3 copy-start.4
  27.1 12.3 %collective-permute-start.3 = (bf16[2,2,256,256]{3,2,1,0:T(8,128)(2,1)S(1)}, bf16[2,2,256,256]{3,2,1,0:T(8,128)(2,1)S(1)}, u32[]{:S(2)}, u32[]{:S(2)}) collective-permute-start(bf16[2,2,256,256]{3,2,1,0:T(8,128)(2,1)S(1)} %broadcast_select_fusion), channel_id=1, source_target_pairs={{0,4},{8,12},{1,5},{9,13},{16,20},{24,28},{17,21},{25,29}} | collective-permute-start | bytes 1572872 | tf_op jit(solution)/shard_map/ppermute | solution.py:21
  30.0 39.8 %collective-permute-start.1 = (bf16[2,2,2,256,256]{4,3,2,1,0:T(8,128)(2,1)S(1)}, bf16[2,2,2,256,256]{4,3,2,1,0:T(8,128)(2,1)S(1)}, u32[]{:S(2)}, u32[]{:S(2)}) collective-permute-start(bf16[2,2,2,256,256]{4,3,2,1,0:T(8,128)(2,1)S(1)} %get-tuple-element.16), channel_id=1, source_target_pairs={{0,2},{2,4},{4,6},{6,8},{8,10},{10,12},{12,14},{1,3},{3,5},{5,7},{... | collective-permute-start | bytes 3145736 | tf_op jit(solution)/shard_map/ppermute | solution.py:10
  39.4 5.2 %copy-start.1 = (f32[2,2,256,256]{3,2,1,0:T(8,128)S(1)}, f32[2,2,256,256]{3,2,1,0:T(8,128)}, u32[]{:S(2)}) copy-start(f32[2,2,256,256]{3,2,1,0:T(8,128)} %get-tuple-element.5) | copy-start | bytes 3145732
  39.5 28.1 %collective-permute-start.4 = (bf16[2,2,256,256]{3,2,1,0:T(8,128)(2,1)S(1)}, bf16[2,2,256,256]{3,2,1,0:T(8,128)(2,1)S(1)}, u32[]{:S(2)}, u32[]{:S(2)}) collective-permute-start(bf16[2,2,256,256]{3,2,1,0:T(8,128)(2,1)S(1)} %broadcast_select_fusion.1), channel_id=1, source_target_pairs={{0,2},{4,6},{8,10},{12,14},{1,3},{5,7},{9,11},{13,15},{16,18},{20,... | collective-permute-start | bytes 1572872 | tf_op jit(solution)/shard_map/ppermute | solution.py:21
  44.3 24.6 %collective-permute-start.6 = (bf16[2,2,1,256,256]{4,3,2,1,0:T(8,128)(2,1)S(1)}, bf16[2,2,1,256,256]{4,3,2,1,0:T(8,128)(2,1)S(1)}, u32[]{:S(2)}, u32[]{:S(2)}) collective-permute-start(bf16[2,2,1,256,256]{4,3,2,1,0:T(8,128)(2,1)S(1)} %slice_select_fusion), channel_id=1, source_target_pairs={{0,1},{1,0},{2,3},{3,2},{4,5},{5,4},{6,7},{7,6},{8,9},{9,8},{10,11... | collective-permute-start | bytes 1572872 | tf_op jit(solution)/shard_map/ppermute | solution.py:182
  44.7 61.9 %collective-permute-start.7 = (f32[2,2,256,256]{3,2,1,0:T(8,128)S(1)}, f32[2,2,256,256]{3,2,1,0:T(8,128)S(1)}, u32[]{:S(2)}, u32[]{:S(2)}) collective-permute-start(f32[2,2,256,256]{3,2,1,0:T(8,128)S(1)} %add.244), channel_id=1, source_target_pairs={{4,0},{12,8},{5,1},{13,9},{20,16},{28,24},{21,17},{29,25}} | collective-permute-start | bytes 3145736 | tf_op jit(solution)/shard_map/ppermute | solution.py:31
  68.8 4.7 %collective-permute-start.9 = (f32[1664,256]{1,0:T(8,128)S(1)}, f32[1664,256]{1,0:T(8,128)S(1)}, u32[]{:S(2)}, u32[]{:S(2)}) collective-permute-start(f32[1664,256]{1,0:T(8,128)S(1)} %constant_dynamic-slice_fusion.4), channel_id=1, source_target_pairs={{0,1},{1,0},{2,3},{3,2},{4,5},{5,4},{6,7},{7,6},{8,9},{9,8},{10,11... | collective-permute-start | bytes 5111816 | tf_op jit(solution)/shard_map/ppermute | solution.py:45
  69.8 1.0 copy-start.2
  73.8 11.7 %copy-start.3 = (bf16[2,2,2,256,256]{4,3,2,1,0:T(8,128)(2,1)S(1)}, bf16[2,2,2,256,256]{4,3,2,1,0:T(8,128)(2,1)}, u32[]{:S(2)}) copy-start(bf16[2,2,2,256,256]{4,3,2,1,0:T(8,128)(2,1)} %copy-done.2) | copy-start | bytes 3145732
  73.9 34.2 %collective-permute-start.10 = (f32[416,256]{1,0:T(8,128)S(1)}, f32[416,256]{1,0:T(8,128)S(1)}, u32[]{:S(2)}, u32[]{:S(2)}) collective-permute-start(f32[416,256]{1,0:T(8,128)S(1)} %get-tuple-element.9), channel_id=1, source_target_pairs={{0,4},{2,6},{4,8},{6,10},{8,12},{10,14},{12,0},{14,2},{1,5},{3,7},... | collective-permute-start | bytes 1277960 | tf_op jit(solution)/shard_map/ppermute | solution.py:71
  82.9 31.9 %collective-permute-start.11 = (f32[416,256]{1,0:T(8,128)S(1)}, f32[416,256]{1,0:T(8,128)S(1)}, u32[]{:S(2)}, u32[]{:S(2)}) collective-permute-start(f32[416,256]{1,0:T(8,128)S(1)} %get-tuple-element.11), channel_id=1, source_target_pairs={{0,8},{2,10},{4,12},{6,14},{8,0},{10,2},{12,4},{14,6},{1,9},{3,11}... | collective-permute-start | bytes 1277960 | tf_op jit(solution)/shard_map/ppermute | solution.py:71
  85.5 32.8 %collective-permute-start.12 = (f32[416,256]{1,0:T(8,128)S(1)}, f32[416,256]{1,0:T(8,128)S(1)}, u32[]{:S(2)}, u32[]{:S(2)}) collective-permute-start(f32[416,256]{1,0:T(8,128)S(1)} %get-tuple-element.10), channel_id=1, source_target_pairs={{0,12},{2,14},{4,0},{6,2},{8,4},{10,6},{12,8},{14,10},{1,13},{3,15... | collective-permute-start | bytes 1277960 | tf_op jit(solution)/shard_map/ppermute | solution.py:71
  106.8 48.0 %collective-permute-start.8 = (f32[2,2,256,256]{3,2,1,0:T(8,128)S(1)}, f32[2,2,256,256]{3,2,1,0:T(8,128)S(1)}, u32[]{:S(2)}, u32[]{:S(2)}) collective-permute-start(f32[2,2,256,256]{3,2,1,0:T(8,128)S(1)} %add.245), channel_id=1, source_target_pairs={{8,0},{9,1},{24,16},{25,17}} | collective-permute-start | bytes 3145736 | tf_op jit(solution)/shard_map/ppermute | solution.py:31
  118.4 7.1 %collective-permute-start.13 = (f32[208,256]{1,0:T(8,128)S(1)}, f32[208,256]{1,0:T(8,128)S(1)}, u32[]{:S(2)}, u32[]{:S(2)}) collective-permute-start(f32[208,256]{1,0:T(8,128)S(1)} %constant_dynamic-slice_fusion), channel_id=1, source_target_pairs={{0,2},{2,0},{4,6},{6,4},{8,10},{10,8},{12,14},{14,12},{1,3},{3,1},... | collective-permute-start | bytes 638984 | tf_op jit(solution)/shard_map/ppermute | solution.py:45
  125.6 4.8 %collective-permute-start.14 = (bf16[208,256]{1,0:T(8,128)(2,1)S(1)}, bf16[208,256]{1,0:T(8,128)(2,1)S(1)}, u32[]{:S(2)}, u32[]{:S(2)}) collective-permute-start(bf16[208,256]{1,0:T(8,128)(2,1)S(1)} %multiply_convert_fusion.3), channel_id=1, source_target_pairs={{0,2},{2,0},{4,6},{6,4},{8,10},{10,8},{12,14},{14,12},{1,3},{3,1},... | collective-permute-start | bytes 319496 | tf_op jit(solution)/shard_map/ppermute | solution.py:53
  130.5 25.2 %collective-permute-start.15 = (bf16[416,256]{1,0:T(8,128)(2,1)S(1)}, bf16[416,256]{1,0:T(8,128)(2,1)S(1)}, u32[]{:S(2)}, u32[]{:S(2)}) collective-permute-start(bf16[416,256]{1,0:T(8,128)(2,1)S(1)} %maximum_select_fusion.2), channel_id=1, source_target_pairs={{0,4},{2,6},{4,8},{6,10},{8,12},{10,14},{12,0},{14,2},{1,5},{3,7},... | collective-permute-start | bytes 638984 | tf_op jit(solution)/shard_map/ppermute | solution.py:84
  155.4 9.2 %collective-permute-start.16 = (bf16[416,256]{1,0:T(8,128)(2,1)S(1)}, bf16[416,256]{1,0:T(8,128)(2,1)S(1)}, u32[]{:S(2)}, u32[]{:S(2)}) collective-permute-start(bf16[416,256]{1,0:T(8,128)(2,1)S(1)} %maximum_select_fusion.2), channel_id=1, source_target_pairs={{0,8},{2,10},{4,12},{6,14},{8,0},{10,2},{12,4},{14,6},{1,9},{3,11}... | collective-permute-start | bytes 638984 | tf_op jit(solution)/shard_map/ppermute | solution.py:84
  155.5 11.1 %collective-permute-start.17 = (bf16[416,256]{1,0:T(8,128)(2,1)S(1)}, bf16[416,256]{1,0:T(8,128)(2,1)S(1)}, u32[]{:S(2)}, u32[]{:S(2)}) collective-permute-start(bf16[416,256]{1,0:T(8,128)(2,1)S(1)} %maximum_select_fusion.2), channel_id=1, source_target_pairs={{0,12},{2,14},{4,0},{6,2},{8,4},{10,6},{12,8},{14,10},{1,13},{3,15... | collective-permute-start | bytes 638984 | tf_op jit(solution)/shard_map/ppermute | solution.py:84
  166.7 2.4 %collective-permute-start.18 = (bf16[1664,256]{1,0:T(8,128)(2,1)S(1)}, bf16[1664,256]{1,0:T(8,128)(2,1)S(1)}, u32[]{:S(2)}, u32[]{:S(2)}) collective-permute-start(bf16[1664,256]{1,0:T(8,128)(2,1)S(1)} %bitcast.254), channel_id=1, source_target_pairs={{0,1},{1,0},{2,3},{3,2},{4,5},{5,4},{6,7},{7,6},{8,9},{9,8},{10,11... | collective-permute-start | bytes 2555912 | tf_op jit(solution)/shard_map/ppermute | solution.py:53

commit v12 on v11

--- a/solution.py
+++ b/solution.py
@@ -245,20 +245,15 @@
     taps_s = spatial_terms.shape[0]
     taps_t = temporal_terms.shape[0]
     flat = jnp.concatenate(
-        [
-            spatial_terms.reshape(-1, chans),
-            temporal_terms.reshape(-1, chans),
-            cond_terms.reshape(-1, chans),
-        ],
-        axis=0,
+        [spatial_terms.reshape(-1, chans), temporal_terms.reshape(-1, chans)], axis=0
     )
     scale = (clips * frames * rows * cols * lax.axis_size("space") * lax.axis_size("tm")) ** (-0.5)
     summed = all_sum_rounded(flat, scale)
+    grad_cond = all_sum_rounded(cond_terms, scale)
     n_s = taps_s * chans
     n_t = taps_t * chans
     grad_spatial = summed[:n_s].reshape(taps_s, chans, chans)
     grad_temporal = summed[n_s : n_s + n_t].reshape(taps_t, chans, chans)
-    grad_cond = summed[n_s + n_t :]
     return (output, grad_latents, grad_spatial, grad_temporal, grad_cond)
 
 

time: 172 us -> 191 us (1.11)
  waiting for transfers between devices: 93.8 us -> 110 us
    ppermute x2, waiting for transfers between devices: 37.7 us -> 19 us  [tree_reduce(): value = value + lax.ppermute(value, axis, pairs)]
    ppermute x3 -> x6, waiting for transfers between devices: 10.2 us -> 26.4 us  [direct_scatter(): total = total + lax.ppermute(send, axis, pairs)]
    ppermute x3 -> x6, waiting for transfers between devices: 10.9 us -> 19.9 us  [direct_gather(): got = lax.ppermute(piece, axis, pairs)]
    ppermute x3, starting transfers between devices: 14.4 us -> 9.9 us  [tree_broadcast(): got = lax.ppermute(value, axis, pairs)]
    ppermute x3 -> x6, starting transfers between devices: 6.09 us -> 10.5 us  [direct_gather(): got = lax.ppermute(piece, axis, pairs)]
    ppermute x2 -> x4, waiting for transfers between devices: 4.07 us -> 6.82 us  [xor_doubling(): got = lax.ppermute(piece, axis, [(i, i ^ step) for i in range(count)])]
    ppermute x2 -> x4, waiting for transfers between devices: 6.6 us -> 9.34 us  [xor_halving(): flat = keep + lax.ppermute(send, axis, pairs)]
    ppermute x2, starting transfers between devices: 2.82 us -> 4.92 us  [shifted(): return lax.ppermute(value, axis, pairs)]
  transfers between devices with their start and end apart: 19 -> 29, of which waited for: 12 -> 14; matrix products, arithmetic and copies ran while one was open for 18% -> 17% of each run, Pallas kernels for 0% -> 0%
where the time goes in v12:
time: 191 us; the launch traced here: 190 us
  waiting for transfers between devices  110 us (58%)
  starting transfers between devices  40.2 us (21%)
  matrix products  24.3 us (13%)
  other arithmetic  10.7 us (6%)
  local copies, waits for them, and re-layouts  3.83 us (2%)
    ppermute x6, waiting for transfers between devices, direct_scatter(): total = total + lax.ppermute(send, axis, pairs)  26.4 us
    ppermute x3, waiting for transfers between devices, tree_broadcast(): got = lax.ppermute(value, axis, pairs)  24.8 us
    ppermute x6, waiting for transfers between devices, direct_gather(): got = lax.ppermute(piece, axis, pairs)  19.9 us
    ppermute x2, waiting for transfers between devices, tree_reduce(): value = value + lax.ppermute(value, axis, pairs)  19 us
    dot_general x18, matrix products, spatial_sum(): total = total + jnp.dot(piece, kernel, preferred_element_type=jnp.float32)  12 us
    ppermute x6, starting transfers between devices, direct_scatter(): total = total + lax.ppermute(send, axis, pairs)  10.7 us
    ppermute x6, starting transfers between devices, direct_gather(): got = lax.ppermute(piece, axis, pairs)  10.5 us
    ppermute x3, starting transfers between devices, tree_broadcast(): got = lax.ppermute(value, axis, pairs)  9.9 us
  transfers between devices with their start and end apart: 29, of which 14 were waited for; matrix products, arithmetic and copies ran while one was open for 17% of the time, Pallas kernels for 0%

profile of v12, /device:TPU:0, one launch (start us, length us, event | category | flops | bytes accessed | tf_op | source)
XLA Modules:
  0.0 190.1 jit_solution(745800897320132077)
XLA Ops:
  1.4 1.5 broadcast_multiply_fusion.1
  3.7 6.7 %collective-permute-start.2 = (bf16[2,2,256,256]{3,2,1,0:T(8,128)(2,1)}, bf16[2,2,256,256]{3,2,1,0:T(8,128)(2,1)}, u32[]{:S(2)}, u32[]{:S(2)}) collective-permute-start(bf16[2,2,256,256]{3,2,1,0:T(8,128)(2,1)} %slice_bitcast_fusion), channel_id=1, source_target_pairs={{0,8},{1,9},{16,24},{17,25}} | collective-permute-start | bytes 1572872 | tf_op jit(solution)/shard_map/ppermute | solution.py:21
  11.3 1.4 convert_reduce_fusion
  12.7 1.3 collective-permute-start.5
  14.4 1.4 fusion.90
  16.2 1.1 broadcast_select_fusion.6
  21.8 1.7 collective-permute-start.3
  23.5 1.3 multiply_convert_fusion.2
  24.8 3.6 %collective-permute-start.1 = (bf16[2,2,2,256,256]{4,3,2,1,0:T(8,128)(2,1)S(1)}, bf16[2,2,2,256,256]{4,3,2,1,0:T(8,128)(2,1)S(1)}, u32[]{:S(2)}, u32[]{:S(2)}) collective-permute-start(bf16[2,2,2,256,256]{4,3,2,1,0:T(8,128)(2,1)S(1)} %get-tuple-element.19), channel_id=1, source_target_pairs={{0,2},{2,4},{4,6},{6,8},{8,10},{10,12},{12,14},{1,3},{3,5},{5,7},{... | collective-permute-start | bytes 3145736 | tf_op jit(solution)/shard_map/ppermute | solution.py:10
  29.3 5.9 %collective-permute-done.3 = bf16[2,2,256,256]{3,2,1,0:T(8,128)(2,1)S(1)} collective-permute-done((bf16[2,2,256,256]{3,2,1,0:T(8,128)(2,1)S(1)}, bf16[2,2,256,256]{3,2,1,0:T(8,128)(2,1)S(1)}, u32[]{:S(2)}, u32[]{:S(2)}) %collective-permute-start.3) | collective-permute-done | bytes 524320 | tf_op jit(solution)/shard_map/ppermute | solution.py:21
  35.3 1.5 collective-permute-start.4
  36.8 3.3 %collective-permute-done.5 = bf16[2,2,2,256,256]{4,3,2,1,0:T(8,128)(2,1)S(1)} collective-permute-done((bf16[2,2,2,256,256]{4,3,2,1,0:T(8,128)(2,1)S(1)}, bf16[2,2,2,256,256]{4,3,2,1,0:T(8,128)(2,1)S(1)}, u32[]{:S(2)}, u32[]{:S(2)}) %collective-permute-start.5) | collective-permute-done | bytes 1048608 | tf_op jit(solution)/shard_map/ppermute | solution.py:10
  49.2 1.3 collective-permute-start.7
  50.9 19.0 %collective-permute-done.4 = bf16[2,2,256,256]{3,2,1,0:T(8,128)(2,1)S(1)} collective-permute-done((bf16[2,2,256,256]{3,2,1,0:T(8,128)(2,1)S(1)}, bf16[2,2,256,256]{3,2,1,0:T(8,128)(2,1)S(1)}, u32[]{:S(2)}, u32[]{:S(2)}) %collective-permute-start.4) | collective-permute-done | bytes 524320 | tf_op jit(solution)/shard_map/ppermute | solution.py:21
  74.0 1.8 multiply_convert_fusion.1
  76.3 1.7 collective-permute-start.20
  78.0 3.2 %collective-permute-start.21 = (f32[32,256]{1,0:T(8,128)S(1)}, f32[32,256]{1,0:T(8,128)S(1)}, u32[]{:S(2)}, u32[]{:S(2)}) collective-permute-start(f32[32,256]{1,0:T(8,128)S(1)} %get-tuple-element.18), channel_id=1, source_target_pairs={{0,8},{2,10},{4,12},{6,14},{8,0},{10,2},{12,4},{14,6},{1,9},{3,11}... | collective-permute-start | bytes 98312 | tf_op jit(solution)/shard_map/ppermute | solution.py:71
  82.3 15.4 %collective-permute-done.20 = f32[32,256]{1,0:T(8,128)S(1)} collective-permute-done((f32[32,256]{1,0:T(8,128)S(1)}, f32[32,256]{1,0:T(8,128)S(1)}, u32[]{:S(2)}, u32[]{:S(2)}) %collective-permute-start.20) | collective-permute-done | bytes 32800 | tf_op jit(solution)/shard_map/ppermute | solution.py:71
  98.4 3.3 %collective-permute-done.23 = f32[16,256]{1,0:T(8,128)S(1)} collective-permute-done((f32[16,256]{1,0:T(8,128)S(1)}, f32[16,256]{1,0:T(8,128)S(1)}, u32[]{:S(2)}, u32[]{:S(2)}) %collective-permute-start.23) | collective-permute-done | bytes 16416 | tf_op jit(solution)/shard_map/ppermute | solution.py:45
  102.1 3.2 %collective-permute-done.24 = bf16[16,256]{1,0:T(8,128)(2,1)S(1)} collective-permute-done((bf16[16,256]{1,0:T(8,128)(2,1)S(1)}, bf16[16,256]{1,0:T(8,128)(2,1)S(1)}, u32[]{:S(2)}, u32[]{:S(2)}) %collective-permute-start.24) | collective-permute-done | bytes 8224 | tf_op jit(solution)/shard_map/ppermute | solution.py:53
  107.4 3.1 %collective-permute-start.10 = (f32[384,256]{1,0:T(8,128)S(1)}, f32[384,256]{1,0:T(8,128)S(1)}, u32[]{:S(2)}, u32[]{:S(2)}) collective-permute-start(f32[384,256]{1,0:T(8,128)S(1)} %get-tuple-element.9), channel_id=1, source_target_pairs={{0,4},{2,6},{4,8},{6,10},{8,12},{10,14},{12,0},{14,2},{1,5},{3,7},... | collective-permute-start | bytes 1179656 | tf_op jit(solution)/shard_map/ppermute | solution.py:71
  111.2 1.7 collective-permute-start.12
  112.9 8.9 %collective-permute-done.26 = bf16[32,256]{1,0:T(8,128)(2,1)S(1)} collective-permute-done((bf16[32,256]{1,0:T(8,128)(2,1)S(1)}, bf16[32,256]{1,0:T(8,128)(2,1)S(1)}, u32[]{:S(2)}, u32[]{:S(2)}) %collective-permute-start.26) | collective-permute-done | bytes 16416 | tf_op jit(solution)/shard_map/ppermute | solution.py:84
  122.0 1.3 collective-permute-start.8
  123.3 10.9 %collective-permute-done.11 = f32[384,256]{1,0:T(8,128)S(1)} collective-permute-done((f32[384,256]{1,0:T(8,128)S(1)}, f32[384,256]{1,0:T(8,128)S(1)}, u32[]{:S(2)}, u32[]{:S(2)}) %collective-permute-start.11) | collective-permute-done | bytes 393248 | tf_op jit(solution)/shard_map/ppermute | solution.py:71
  134.7 6.1 %collective-permute-done.13 = f32[192,256]{1,0:T(8,128)S(1)} collective-permute-done((f32[192,256]{1,0:T(8,128)S(1)}, f32[192,256]{1,0:T(8,128)S(1)}, u32[]{:S(2)}, u32[]{:S(2)}) %collective-permute-start.13) | collective-permute-done | bytes 196640 | tf_op jit(solution)/shard_map/ppermute | solution.py:45
  141.9 3.6 %collective-permute-done.14 = bf16[192,256]{1,0:T(8,128)(2,1)S(1)} collective-permute-done((bf16[192,256]{1,0:T(8,128)(2,1)S(1)}, bf16[192,256]{1,0:T(8,128)(2,1)S(1)}, u32[]{:S(2)}, u32[]{:S(2)}) %collective-permute-start.14) | collective-permute-done | bytes 98336 | tf_op jit(solution)/shard_map/ppermute | solution.py:53
  145.6 9.0 %collective-permute-start.15 = (bf16[384,256]{1,0:T(8,128)(2,1)S(1)}, bf16[384,256]{1,0:T(8,128)(2,1)S(1)}, u32[]{:S(2)}, u32[]{:S(2)}) collective-permute-start(bf16[384,256]{1,0:T(8,128)(2,1)S(1)} %maximum_select_fusion.2), channel_id=1, source_target_pairs={{0,4},{2,6},{4,8},{6,10},{8,12},{10,14},{12,0},{14,2},{1,5},{3,7},... | collective-permute-start | bytes 589832 | tf_op jit(solution)/shard_map/ppermute | solution.py:84
  154.6 19.0 %collective-permute-done.8 = f32[2,2,256,256]{3,2,1,0:T(8,128)S(1)} collective-permute-done((f32[2,2,256,256]{3,2,1,0:T(8,128)S(1)}, f32[2,2,256,256]{3,2,1,0:T(8,128)S(1)}, u32[]{:S(2)}, u32[]{:S(2)}) %collective-permute-start.8) | collective-permute-done | bytes 1048608 | tf_op jit(solution)/shard_map/ppermute | solution.py:31
  174.6 8.4 %collective-permute-done.16 = bf16[384,256]{1,0:T(8,128)(2,1)S(1)} collective-permute-done((bf16[384,256]{1,0:T(8,128)(2,1)S(1)}, bf16[384,256]{1,0:T(8,128)(2,1)S(1)}, u32[]{:S(2)}, u32[]{:S(2)}) %collective-permute-start.16) | collective-permute-done | bytes 196640 | tf_op jit(solution)/shard_map/ppermute | solution.py:84
  183.1 2.2 %collective-permute-done.17 = bf16[384,256]{1,0:T(8,128)(2,1)S(1)} collective-permute-done((bf16[384,256]{1,0:T(8,128)(2,1)S(1)}, bf16[384,256]{1,0:T(8,128)(2,1)S(1)}, u32[]{:S(2)}, u32[]{:S(2)}) %collective-permute-start.17) | collective-permute-done | bytes 196640 | tf_op jit(solution)/shard_map/ppermute | solution.py:84
  185.4 2.4 %fusion.4 = bf16[2,2,2,256,256]{4,3,2,1,0:T(8,128)(2,1)} fusion(bf16[2,2,2,256,256]{4,3,2,1,0:T(8,128)(2,1)S(1)} %get-tuple-element.6, f32[2,2,2,256,256]{4,3,2,1,0:T(8,128)S(1)} %fusion.20, f32[2,2,2,256,256]{4,3,2,1,0:T(8,128)S(1)} %fusion.38, f32[2,2,2,256,256]{4,3,2,1,0:T(8,128)S(1)} %fusion.40, f32[2,2,2,256,256]{4,3,2,1,0:T(8,128)S(1)} %fusion.88, ...), kind=kOutput, calls=%fused_computation.16 | convolution fusion | flops 275775488 | bytes 21104128 | tf_op jit(solution)/shard_map/dot_general | solution.py:139
  (121 shorter events, 32.3 us)
Async XLA Ops:
  0.6 73.1 %copy-start = (bf16[256,256]{1,0:T(8,128)(2,1)S(1)}, bf16[256,256]{1,0:T(8,128)(2,1)}, u32[]{:S(2)}) copy-start(bf16[256,256]{1,0:T(8,128)(2,1)} %param.11) | copy-start | bytes 393220
  1.4 9.9 %copy-start.4 = (bf16[2,2,2,256,256]{4,3,2,1,0:T(8,128)(2,1)S(1)}, bf16[2,2,2,256,256]{4,3,2,1,0:T(8,128)(2,1)}, u32[]{:S(2)}) copy-start(bf16[2,2,2,256,256]{4,3,2,1,0:T(8,128)(2,1)} %param.7) | copy-start | bytes 3145732
  3.7 18.0 %collective-permute-start.2 = (bf16[2,2,256,256]{3,2,1,0:T(8,128)(2,1)}, bf16[2,2,256,256]{3,2,1,0:T(8,128)(2,1)}, u32[]{:S(2)}, u32[]{:S(2)}) collective-permute-start(bf16[2,2,256,256]{3,2,1,0:T(8,128)(2,1)} %slice_bitcast_fusion), channel_id=1, source_target_pairs={{0,8},{1,9},{16,24},{17,25}} | collective-permute-start | bytes 1572872 | tf_op jit(solution)/shard_map/ppermute | solution.py:21
  11.3 4.9 %collective-permute-start = (bf16[2,2,1,256,256]{4,3,2,1,0:T(8,128)(2,1)}, bf16[2,2,1,256,256]{4,3,2,1,0:T(8,128)(2,1)}, u32[]{:S(2)}, u32[]{:S(2)}) collective-permute-start(bf16[2,2,1,256,256]{4,3,2,1,0:T(8,128)(2,1)} %slice_select_fusion.1), channel_id=1, source_target_pairs={{0,1},{1,0},{2,3},{3,2},{4,5},{5,4},{6,7},{7,6},{8,9},{9,8},{10,11... | collective-permute-start | bytes 1572872 | tf_op jit(solution)/shard_map/ppermute | solution.py:182
  12.7 27.5 %collective-permute-start.5 = (bf16[2,2,2,256,256]{4,3,2,1,0:T(8,128)(2,1)S(1)}, bf16[2,2,2,256,256]{4,3,2,1,0:T(8,128)(2,1)S(1)}, u32[]{:S(2)}, u32[]{:S(2)}) collective-permute-start(bf16[2,2,2,256,256]{4,3,2,1,0:T(8,128)(2,1)S(1)} %get-tuple-element.6), channel_id=1, source_target_pairs={{2,0},{4,2},{6,4},{8,6},{10,8},{12,10},{14,12},{3,1},{5,3},{7,5},{... | collective-permute-start | bytes 3145736 | tf_op jit(solution)/shard_map/ppermute | solution.py:10
  14.3 1.4 copy-start.3
  21.8 13.4 %collective-permute-start.3 = (bf16[2,2,256,256]{3,2,1,0:T(8,128)(2,1)S(1)}, bf16[2,2,256,256]{3,2,1,0:T(8,128)(2,1)S(1)}, u32[]{:S(2)}, u32[]{:S(2)}) collective-permute-start(bf16[2,2,256,256]{3,2,1,0:T(8,128)(2,1)S(1)} %broadcast_select_fusion), channel_id=1, source_target_pairs={{0,4},{8,12},{1,5},{9,13},{16,20},{24,28},{17,21},{25,29}} | collective-permute-start | bytes 1572872 | tf_op jit(solution)/shard_map/ppermute | solution.py:21
  24.8 48.5 %collective-permute-start.1 = (bf16[2,2,2,256,256]{4,3,2,1,0:T(8,128)(2,1)S(1)}, bf16[2,2,2,256,256]{4,3,2,1,0:T(8,128)(2,1)S(1)}, u32[]{:S(2)}, u32[]{:S(2)}) collective-permute-start(bf16[2,2,2,256,256]{4,3,2,1,0:T(8,128)(2,1)S(1)} %get-tuple-element.19), channel_id=1, source_target_pairs={{0,2},{2,4},{4,6},{6,8},{8,10},{10,12},{12,14},{1,3},{3,5},{5,7},{... | collective-permute-start | bytes 3145736 | tf_op jit(solution)/shard_map/ppermute | solution.py:10
  35.3 34.6 %collective-permute-start.4 = (bf16[2,2,256,256]{3,2,1,0:T(8,128)(2,1)S(1)}, bf16[2,2,256,256]{3,2,1,0:T(8,128)(2,1)S(1)}, u32[]{:S(2)}, u32[]{:S(2)}) collective-permute-start(bf16[2,2,256,256]{3,2,1,0:T(8,128)(2,1)S(1)} %broadcast_select_fusion.1), channel_id=1, source_target_pairs={{0,2},{4,6},{8,10},{12,14},{1,3},{5,7},{9,11},{13,15},{16,18},{20,... | collective-permute-start | bytes 1572872 | tf_op jit(solution)/shard_map/ppermute | solution.py:21
  47.9 58.8 %collective-permute-start.9 = (f32[1536,256]{1,0:T(8,128)S(1)}, f32[1536,256]{1,0:T(8,128)S(1)}, u32[]{:S(2)}, u32[]{:S(2)}) collective-permute-start(f32[1536,256]{1,0:T(8,128)S(1)} %fusion.13), channel_id=1, source_target_pairs={{0,1},{1,0},{2,3},{3,2},{4,5},{5,4},{6,7},{7,6},{8,9},{9,8},{10,11... | collective-permute-start | bytes 4718600 | tf_op jit(solution)/shard_map/ppermute | solution.py:45
  48.0 22.9 %collective-permute-start.6 = (bf16[2,2,1,256,256]{4,3,2,1,0:T(8,128)(2,1)S(1)}, bf16[2,2,1,256,256]{4,3,2,1,0:T(8,128)(2,1)S(1)}, u32[]{:S(2)}, u32[]{:S(2)}) collective-permute-start(bf16[2,2,1,256,256]{4,3,2,1,0:T(8,128)(2,1)S(1)} %slice_select_fusion), channel_id=1, source_target_pairs={{0,1},{1,0},{2,3},{3,2},{4,5},{5,4},{6,7},{7,6},{8,9},{9,8},{10,11... | collective-permute-start | bytes 1572872 | tf_op jit(solution)/shard_map/ppermute | solution.py:182
  49.2 72.7 %collective-permute-start.7 = (f32[2,2,256,256]{3,2,1,0:T(8,128)S(1)}, f32[2,2,256,256]{3,2,1,0:T(8,128)S(1)}, u32[]{:S(2)}, u32[]{:S(2)}) collective-permute-start(f32[2,2,256,256]{3,2,1,0:T(8,128)S(1)} %add.301), channel_id=1, source_target_pairs={{4,0},{12,8},{5,1},{13,9},{20,16},{28,24},{21,17},{29,25}} | collective-permute-start | bytes 3145736 | tf_op jit(solution)/shard_map/ppermute | solution.py:31
  70.8 5.5 %collective-permute-start.19 = (f32[128,256]{1,0:T(8,128)S(1)}, f32[128,256]{1,0:T(8,128)S(1)}, u32[]{:S(2)}, u32[]{:S(2)}) collective-permute-start(f32[128,256]{1,0:T(8,128)S(1)} %constant_dynamic-slice_fusion.4), channel_id=1, source_target_pairs={{0,1},{1,0},{2,3},{3,2},{4,5},{5,4},{6,7},{7,6},{8,9},{9,8},{10,11... | collective-permute-start | bytes 393224 | tf_op jit(solution)/shard_map/ppermute | solution.py:45
  76.3 21.5 %collective-permute-start.20 = (f32[32,256]{1,0:T(8,128)S(1)}, f32[32,256]{1,0:T(8,128)S(1)}, u32[]{:S(2)}, u32[]{:S(2)}) collective-permute-start(f32[32,256]{1,0:T(8,128)S(1)} %get-tuple-element.16), channel_id=1, source_target_pairs={{0,4},{2,6},{4,8},{6,10},{8,12},{10,14},{12,0},{14,2},{1,5},{3,7},... | collective-permute-start | bytes 98312 | tf_op jit(solution)/shard_map/ppermute | solution.py:71
  78.0 19.8 %collective-permute-start.21 = (f32[32,256]{1,0:T(8,128)S(1)}, f32[32,256]{1,0:T(8,128)S(1)}, u32[]{:S(2)}, u32[]{:S(2)}) collective-permute-start(f32[32,256]{1,0:T(8,128)S(1)} %get-tuple-element.18), channel_id=1, source_target_pairs={{0,8},{2,10},{4,12},{6,14},{8,0},{10,2},{12,4},{14,6},{1,9},{3,11}... | collective-permute-start | bytes 98312 | tf_op jit(solution)/shard_map/ppermute | solution.py:71
  81.2 16.6 %collective-permute-start.22 = (f32[32,256]{1,0:T(8,128)S(1)}, f32[32,256]{1,0:T(8,128)S(1)}, u32[]{:S(2)}, u32[]{:S(2)}) collective-permute-start(f32[32,256]{1,0:T(8,128)S(1)} %get-tuple-element.17), channel_id=1, source_target_pairs={{0,12},{2,14},{4,0},{6,2},{8,4},{10,6},{12,8},{14,10},{1,13},{3,15... | collective-permute-start | bytes 98312 | tf_op jit(solution)/shard_map/ppermute | solution.py:71
  97.8 3.8 %collective-permute-start.23 = (f32[16,256]{1,0:T(8,128)S(1)}, f32[16,256]{1,0:T(8,128)S(1)}, u32[]{:S(2)}, u32[]{:S(2)}) collective-permute-start(f32[16,256]{1,0:T(8,128)S(1)} %constant_dynamic-slice_fusion), channel_id=1, source_target_pairs={{0,2},{2,0},{4,6},{6,4},{8,10},{10,8},{12,14},{14,12},{1,3},{3,1},... | collective-permute-start | bytes 49160 | tf_op jit(solution)/shard_map/ppermute | solution.py:45
  101.6 3.7 %collective-permute-start.24 = (bf16[16,256]{1,0:T(8,128)(2,1)S(1)}, bf16[16,256]{1,0:T(8,128)(2,1)S(1)}, u32[]{:S(2)}, u32[]{:S(2)}) collective-permute-start(bf16[16,256]{1,0:T(8,128)(2,1)S(1)} %multiply_convert_fusion.4), channel_id=1, source_target_pairs={{0,2},{2,0},{4,6},{6,4},{8,10},{10,8},{12,14},{14,12},{1,3},{3,1},... | collective-permute-start | bytes 24584 | tf_op jit(solution)/shard_map/ppermute | solution.py:53
  105.3 5.9 %collective-permute-start.25 = (bf16[32,256]{1,0:T(8,128)(2,1)S(1)}, bf16[32,256]{1,0:T(8,128)(2,1)S(1)}, u32[]{:S(2)}, u32[]{:S(2)}) collective-permute-start(bf16[32,256]{1,0:T(8,128)(2,1)S(1)} %maximum_select_fusion.5), channel_id=1, source_target_pairs={{0,4},{2,6},{4,8},{6,10},{8,12},{10,14},{12,0},{14,2},{1,5},{3,7},... | collective-permute-start | bytes 49160 | tf_op jit(solution)/shard_map/ppermute | solution.py:84
  106.2 15.6 %collective-permute-start.26 = (bf16[32,256]{1,0:T(8,128)(2,1)S(1)}, bf16[32,256]{1,0:T(8,128)(2,1)S(1)}, u32[]{:S(2)}, u32[]{:S(2)}) collective-permute-start(bf16[32,256]{1,0:T(8,128)(2,1)S(1)} %maximum_select_fusion.5), channel_id=1, source_target_pairs={{0,8},{2,10},{4,12},{6,14},{8,0},{10,2},{12,4},{14,6},{1,9},{3,11}... | collective-permute-start | bytes 49160 | tf_op jit(solution)/shard_map/ppermute | solution.py:84
  107.4 15.9 %collective-permute-start.10 = (f32[384,256]{1,0:T(8,128)S(1)}, f32[384,256]{1,0:T(8,128)S(1)}, u32[]{:S(2)}, u32[]{:S(2)}) collective-permute-start(f32[384,256]{1,0:T(8,128)S(1)} %get-tuple-element.9), channel_id=1, source_target_pairs={{0,4},{2,6},{4,8},{6,10},{8,12},{10,14},{12,0},{14,2},{1,5},{3,7},... | collective-permute-start | bytes 1179656 | tf_op jit(solution)/shard_map/ppermute | solution.py:71
  110.5 23.7 %collective-permute-start.11 = (f32[384,256]{1,0:T(8,128)S(1)}, f32[384,256]{1,0:T(8,128)S(1)}, u32[]{:S(2)}, u32[]{:S(2)}) collective-permute-start(f32[384,256]{1,0:T(8,128)S(1)} %get-tuple-element.11), channel_id=1, source_target_pairs={{0,8},{2,10},{4,12},{6,14},{8,0},{10,2},{12,4},{14,6},{1,9},{3,11}... | collective-permute-start | bytes 1179656 | tf_op jit(solution)/shard_map/ppermute | solution.py:71
  111.2 23.0 %collective-permute-start.12 = (f32[384,256]{1,0:T(8,128)S(1)}, f32[384,256]{1,0:T(8,128)S(1)}, u32[]{:S(2)}, u32[]{:S(2)}) collective-permute-start(f32[384,256]{1,0:T(8,128)S(1)} %get-tuple-element.10), channel_id=1, source_target_pairs={{0,12},{2,14},{4,0},{6,2},{8,4},{10,6},{12,8},{14,10},{1,13},{3,15... | collective-permute-start | bytes 1179656 | tf_op jit(solution)/shard_map/ppermute | solution.py:71
  121.8 12.9 %collective-permute-start.27 = (bf16[32,256]{1,0:T(8,128)(2,1)S(1)}, bf16[32,256]{1,0:T(8,128)(2,1)S(1)}, u32[]{:S(2)}, u32[]{:S(2)}) collective-permute-start(bf16[32,256]{1,0:T(8,128)(2,1)S(1)} %maximum_select_fusion.5), channel_id=1, source_target_pairs={{0,12},{2,14},{4,0},{6,2},{8,4},{10,6},{12,8},{14,10},{1,13},{3,15... | collective-permute-start | bytes 49160 | tf_op jit(solution)/shard_map/ppermute | solution.py:84
  122.0 51.6 %collective-permute-start.8 = (f32[2,2,256,256]{3,2,1,0:T(8,128)S(1)}, f32[2,2,256,256]{3,2,1,0:T(8,128)S(1)}, u32[]{:S(2)}, u32[]{:S(2)}) collective-permute-start(f32[2,2,256,256]{3,2,1,0:T(8,128)S(1)} %add.302), channel_id=1, source_target_pairs={{8,0},{9,1},{24,16},{25,17}} | collective-permute-start | bytes 3145736 | tf_op jit(solution)/shard_map/ppermute | solution.py:31
  134.3 6.4 %collective-permute-start.13 = (f32[192,256]{1,0:T(8,128)S(1)}, f32[192,256]{1,0:T(8,128)S(1)}, u32[]{:S(2)}, u32[]{:S(2)}) collective-permute-start(f32[192,256]{1,0:T(8,128)S(1)} %constant_dynamic-slice_fusion.5), channel_id=1, source_target_pairs={{0,2},{2,0},{4,6},{6,4},{8,10},{10,8},{12,14},{14,12},{1,3},{3,1},... | collective-permute-start | bytes 589832 | tf_op jit(solution)/shard_map/ppermute | solution.py:45
  134.7 6.5 %collective-permute-start.28 = (bf16[128,256]{1,0:T(8,128)(2,1)S(1)}, bf16[128,256]{1,0:T(8,128)(2,1)S(1)}, u32[]{:S(2)}, u32[]{:S(2)}) collective-permute-start(bf16[128,256]{1,0:T(8,128)(2,1)S(1)} %bitcast.273), channel_id=1, source_target_pairs={{0,1},{1,0},{2,3},{3,2},{4,5},{5,4},{6,7},{7,6},{8,9},{9,8},{10,11... | collective-permute-start | bytes 196616 | tf_op jit(solution)/shard_map/ppermute | solution.py:53
  140.8 4.7 %collective-permute-start.14 = (bf16[192,256]{1,0:T(8,128)(2,1)S(1)}, bf16[192,256]{1,0:T(8,128)(2,1)S(1)}, u32[]{:S(2)}, u32[]{:S(2)}) collective-permute-start(bf16[192,256]{1,0:T(8,128)(2,1)S(1)} %multiply_convert_fusion.3), channel_id=1, source_target_pairs={{0,2},{2,0},{4,6},{6,4},{8,10},{10,8},{12,14},{14,12},{1,3},{3,1},... | collective-permute-start | bytes 294920 | tf_op jit(solution)/shard_map/ppermute | solution.py:53
  145.6 29.0 %collective-permute-start.15 = (bf16[384,256]{1,0:T(8,128)(2,1)S(1)}, bf16[384,256]{1,0:T(8,128)(2,1)S(1)}, u32[]{:S(2)}, u32[]{:S(2)}) collective-permute-start(bf16[384,256]{1,0:T(8,128)(2,1)S(1)} %maximum_select_fusion.2), channel_id=1, source_target_pairs={{0,4},{2,6},{4,8},{6,10},{8,12},{10,14},{12,0},{14,2},{1,5},{3,7},... | collective-permute-start | bytes 589832 | tf_op jit(solution)/shard_map/ppermute | solution.py:84
  174.3 8.8 %collective-permute-start.16 = (bf16[384,256]{1,0:T(8,128)(2,1)S(1)}, bf16[384,256]{1,0:T(8,128)(2,1)S(1)}, u32[]{:S(2)}, u32[]{:S(2)}) collective-permute-start(bf16[384,256]{1,0:T(8,128)(2,1)S(1)} %maximum_select_fusion.2), channel_id=1, source_target_pairs={{0,8},{2,10},{4,12},{6,14},{8,0},{10,2},{12,4},{14,6},{1,9},{3,11}... | collective-permute-start | bytes 589832 | tf_op jit(solution)/shard_map/ppermute | solution.py:84
  174.4 10.9 %collective-permute-start.17 = (bf16[384,256]{1,0:T(8,128)(2,1)S(1)}, bf16[384,256]{1,0:T(8,128)(2,1)S(1)}, u32[]{:S(2)}, u32[]{:S(2)}) collective-permute-start(bf16[384,256]{1,0:T(8,128)(2,1)S(1)} %maximum_select_fusion.2), channel_id=1, source_target_pairs={{0,12},{2,14},{4,0},{6,2},{8,4},{10,6},{12,8},{14,10},{1,13},{3,15... | collective-permute-start | bytes 589832 | tf_op jit(solution)/shard_map/ppermute | solution.py:84
  185.3 2.5 %collective-permute-start.18 = (bf16[1536,256]{1,0:T(8,128)(2,1)S(1)}, bf16[1536,256]{1,0:T(8,128)(2,1)S(1)}, u32[]{:S(2)}, u32[]{:S(2)}) collective-permute-start(bf16[1536,256]{1,0:T(8,128)(2,1)S(1)} %bitcast.267), channel_id=1, source_target_pairs={{0,1},{1,0},{2,3},{3,2},{4,5},{5,4},{6,7},{7,6},{8,9},{9,8},{10,11... | collective-permute-start | bytes 2359304 | tf_op jit(solution)/shard_map/ppermute | solution.py:53
  (2 other events, 2.5 us)

commit v13 on v11

--- a/solution.py
+++ b/solution.py
@@ -94,7 +94,7 @@
     n_tm = lax.axis_size("tm")
     n_sp = lax.axis_size("space")
     if not (is_pow2(n_tm) and is_pow2(n_sp)):
-        return (lax.psum(flat, ("tm", "space")) * scale).astype(jnp.bfloat16)
+        return (lax.psum(flat, ("tm", "space")) * scale).astype(jnp.bfloat16), [], flat.shape[0]
     high = min(4, n_sp)
     low = n_sp // high
     tm_steps = []
@@ -118,8 +118,28 @@
     piece = (flat * scale).astype(jnp.bfloat16)
     piece = xor_doubling(piece, "space", sp_steps)
     piece = direct_gather(piece, "space", low, high)
-    piece = xor_doubling(piece, "tm", tm_steps)
-    return piece[:rows]
+    return piece, tm_steps, rows
+
+
+def split_rows(gathered, cuts):
+    piece, tm_steps, rows = gathered
+    if len(tm_steps) != 1:
+        whole = xor_doubling(piece, "tm", tm_steps)
+        return [whole[a:b] for a, b in cuts]
+    me = lax.axis_index("tm")
+    got = lax.ppermute(piece, "tm", [(0, 1), (1, 0)])
+    lower = jnp.where(me == 0, piece, got)
+    upper = jnp.where(me == 0, got, piece)
+    half = piece.shape[0]
+    outs = []
+    for a, b in cuts:
+        parts = []
+        if a < half:
+            parts.append(lower[a : min(b, half)])
+        if b > half:
+            parts.append(upper[max(a, half) - half : b - half])
+        outs.append(parts[0] if len(parts) == 1 else jnp.concatenate(parts, 0))
+    return outs
 
 
 def spatial_sum(padded, weights, flip):
@@ -256,9 +276,11 @@
     summed = all_sum_rounded(flat, scale)
     n_s = taps_s * chans
     n_t = taps_t * chans
-    grad_spatial = summed[:n_s].reshape(taps_s, chans, chans)
-    grad_temporal = summed[n_s : n_s + n_t].reshape(taps_t, chans, chans)
-    grad_cond = summed[n_s + n_t :]
+    grad_spatial, grad_temporal, grad_cond = split_rows(
+        summed, [(0, n_s), (n_s, n_s + n_t), (n_s + n_t, n_s + n_t + chans)]
+    )
+    grad_spatial = grad_spatial.reshape(taps_s, chans, chans)
+    grad_temporal = grad_temporal.reshape(taps_t, chans, chans)
     return (output, grad_latents, grad_spatial, grad_temporal, grad_cond)
 
 

time: 172 us -> 172 us (level)
    ppermute x2 -> x1, waiting for transfers between devices: 4.07 us -> 3.95 us  [xor_doubling(): got = lax.ppermute(piece, axis, [(i, i ^ step) for i in range(count)])]
where the time goes in v13:
time: 172 us
  waiting for transfers between devices  93.8 us (55%)
  starting transfers between devices  38.8 us (23%)
  matrix products  24.4 us (14%)
  other arithmetic  9.97 us (6%)
  local copies, waits for them, and re-layouts  3.62 us (2%)
    ppermute x2, waiting for transfers between devices, tree_reduce(): value = value + lax.ppermute(value, axis, pairs)  37.7 us
    ppermute x3, waiting for transfers between devices, tree_broadcast(): got = lax.ppermute(value, axis, pairs)  23.1 us
    ppermute x3, starting transfers between devices, tree_broadcast(): got = lax.ppermute(value, axis, pairs)  14.4 us
    dot_general x18, matrix products, spatial_sum(): total = total + jnp.dot(piece, kernel, preferred_element_type=jnp.float32)  12.1 us
    ppermute x3, starting transfers between devices, direct_scatter(): total = total + lax.ppermute(send, axis, pairs)  11.6 us
    ppermute x3, waiting for transfers between devices, direct_gather(): got = lax.ppermute(piece, axis, pairs)  10.9 us
    ppermute x3, waiting for transfers between devices, direct_scatter(): total = total + lax.ppermute(send, axis, pairs)  10.2 us
    ppermute x2, waiting for transfers between devices, xor_halving(): flat = keep + lax.ppermute(send, axis, pairs)  6.6 us
  transfers between devices with their start and end apart: 19, of which 12 were waited for; matrix products, arithmetic and copies ran while one was open for 18% of the time, Pallas kernels for 0%

profile of v13, /device:TPU:0, one launch (start us, length us, event | category | flops | bytes accessed | tf_op | source)
XLA Modules:
  0.0 171.8 jit_solution(1322849606638339203)
XLA Ops:
  1.5 1.4 broadcast_multiply_fusion.1
  2.9 0.9 slice_select_fusion.1
  4.2 1.4 convert_reduce_fusion
  5.6 1.3 collective-permute-start.5
  7.7 8.3 %collective-permute-start.2 = (bf16[2,2,256,256]{3,2,1,0:T(8,128)(2,1)}, bf16[2,2,256,256]{3,2,1,0:T(8,128)(2,1)}, u32[]{:S(2)}, u32[]{:S(2)}) collective-permute-start(bf16[2,2,256,256]{3,2,1,0:T(8,128)(2,1)} %slice_bitcast_fusion), channel_id=1, source_target_pairs={{0,8},{1,9},{16,24},{17,25}} | collective-permute-start | bytes 1572872 | tf_op jit(solution)/shard_map/ppermute | solution.py:21
  16.0 1.4 fusion.87
  17.8 1.1 broadcast_select_fusion.8
  23.3 3.7 %collective-permute-done.2 = bf16[2,2,256,256]{3,2,1,0:T(8,128)(2,1)} collective-permute-done((bf16[2,2,256,256]{3,2,1,0:T(8,128)(2,1)}, bf16[2,2,256,256]{3,2,1,0:T(8,128)(2,1)}, u32[]{:S(2)}, u32[]{:S(2)}) %collective-permute-start.2) | collective-permute-done | bytes 524320 | tf_op jit(solution)/shard_map/ppermute | solution.py:21
  27.1 1.3 collective-permute-start.3
  28.4 1.6 multiply_convert_fusion.2
  30.0 1.5 collective-permute-start.1
  32.5 1.3 collective-permute-done.5
  34.2 1.1 multiply_convert_fusion
  39.5 4.8 %collective-permute-start.4 = (bf16[2,2,256,256]{3,2,1,0:T(8,128)(2,1)S(1)}, bf16[2,2,256,256]{3,2,1,0:T(8,128)(2,1)S(1)}, u32[]{:S(2)}, u32[]{:S(2)}) collective-permute-start(bf16[2,2,256,256]{3,2,1,0:T(8,128)(2,1)S(1)} %broadcast_select_fusion.3), channel_id=1, source_target_pairs={{0,2},{4,6},{8,10},{12,14},{1,3},{5,7},{9,11},{13,15},{16,18},{20,... | collective-permute-start | bytes 1572872 | tf_op jit(solution)/shard_map/ppermute | solution.py:21
  44.7 1.5 collective-permute-start.7
  48.2 19.4 %collective-permute-done.4 = bf16[2,2,256,256]{3,2,1,0:T(8,128)(2,1)S(1)} collective-permute-done((bf16[2,2,256,256]{3,2,1,0:T(8,128)(2,1)S(1)}, bf16[2,2,256,256]{3,2,1,0:T(8,128)(2,1)S(1)}, u32[]{:S(2)}, u32[]{:S(2)}) %collective-permute-start.4) | collective-permute-done | bytes 524320 | tf_op jit(solution)/shard_map/ppermute | solution.py:21
  69.0 0.9 select_maximum_fusion
  73.9 9.0 %collective-permute-start.10 = (f32[416,256]{1,0:T(8,128)S(1)}, f32[416,256]{1,0:T(8,128)S(1)}, u32[]{:S(2)}, u32[]{:S(2)}) collective-permute-start(f32[416,256]{1,0:T(8,128)S(1)} %get-tuple-element.11), channel_id=1, source_target_pairs={{0,4},{2,6},{4,8},{6,10},{8,12},{10,14},{12,0},{14,2},{1,5},{3,7},... | collective-permute-start | bytes 1277960 | tf_op jit(solution)/shard_map/ppermute | solution.py:71
  82.9 2.6 %collective-permute-start.11 = (f32[416,256]{1,0:T(8,128)S(1)}, f32[416,256]{1,0:T(8,128)S(1)}, u32[]{:S(2)}, u32[]{:S(2)}) collective-permute-start(f32[416,256]{1,0:T(8,128)S(1)} %get-tuple-element.13), channel_id=1, source_target_pairs={{0,8},{2,10},{4,12},{6,14},{8,0},{10,2},{12,4},{14,6},{1,9},{3,11}... | collective-permute-start | bytes 1277960 | tf_op jit(solution)/shard_map/ppermute | solution.py:71
  85.5 1.8 %multiply_convert_fusion.1 = bf16[2,2,2,256,256]{4,3,2,1,0:T(8,128)(2,1)} fusion(f32[2,2,2,256,256]{4,3,2,1,0:T(8,128)S(1)} %fusion.106, f32[2,2,2,256,256]{4,3,2,1,0:T(8,128)S(1)} %fusion.5, bf16[2,2,2,256,256]{4,3,2,1,0:T(8,128)(2,1)S(1)} %broadcast_multiply_fusion.1, f32[2,2]{1,0:T(2,128)S(1)} %get-tuple-element.7, f32[2,2,256,256]{3,2,1,0:T(8,128)S(1)} %fusion.70, ...), kind=kOutput, calls=%fused_computation.24 | convolution fusion | flops 272105472 | bytes 8520704 | tf_op jit(solution)/shard_map/dot_general | solution.py:166
  87.3 19.4 %collective-permute-done.7 = f32[2,2,256,256]{3,2,1,0:T(8,128)S(1)} collective-permute-done((f32[2,2,256,256]{3,2,1,0:T(8,128)S(1)}, f32[2,2,256,256]{3,2,1,0:T(8,128)S(1)}, u32[]{:S(2)}, u32[]{:S(2)}) %collective-permute-start.7) | collective-permute-done | bytes 1048608 | tf_op jit(solution)/shard_map/ppermute | solution.py:31
  106.8 1.3 collective-permute-start.8
  108.1 6.7 %collective-permute-done.11 = f32[416,256]{1,0:T(8,128)S(1)} collective-permute-done((f32[416,256]{1,0:T(8,128)S(1)}, f32[416,256]{1,0:T(8,128)S(1)}, u32[]{:S(2)}, u32[]{:S(2)}) %collective-permute-start.11) | collective-permute-done | bytes 426016 | tf_op jit(solution)/shard_map/ppermute | solution.py:71
  114.8 3.5 %collective-permute-done.12 = f32[416,256]{1,0:T(8,128)S(1)} collective-permute-done((f32[416,256]{1,0:T(8,128)S(1)}, f32[416,256]{1,0:T(8,128)S(1)}, u32[]{:S(2)}, u32[]{:S(2)}) %collective-permute-start.12) | collective-permute-done | bytes 426016 | tf_op jit(solution)/shard_map/ppermute | solution.py:71
  119.0 6.6 %collective-permute-done.13 = f32[208,256]{1,0:T(8,128)S(1)} collective-permute-done((f32[208,256]{1,0:T(8,128)S(1)}, f32[208,256]{1,0:T(8,128)S(1)}, u32[]{:S(2)}, u32[]{:S(2)}) %collective-permute-start.13) | collective-permute-done | bytes 213024 | tf_op jit(solution)/shard_map/ppermute | solution.py:45
  126.4 3.9 %collective-permute-done.14 = bf16[208,256]{1,0:T(8,128)(2,1)S(1)} collective-permute-done((bf16[208,256]{1,0:T(8,128)(2,1)S(1)}, bf16[208,256]{1,0:T(8,128)(2,1)S(1)}, u32[]{:S(2)}, u32[]{:S(2)}) %collective-permute-start.14) | collective-permute-done | bytes 106528 | tf_op jit(solution)/shard_map/ppermute | solution.py:53
  130.5 6.0 %collective-permute-start.15 = (bf16[416,256]{1,0:T(8,128)(2,1)S(1)}, bf16[416,256]{1,0:T(8,128)(2,1)S(1)}, u32[]{:S(2)}, u32[]{:S(2)}) collective-permute-start(bf16[416,256]{1,0:T(8,128)(2,1)S(1)} %maximum_select_fusion.1), channel_id=1, source_target_pairs={{0,4},{2,6},{4,8},{6,10},{8,12},{10,14},{12,0},{14,2},{1,5},{3,7},... | collective-permute-start | bytes 638984 | tf_op jit(solution)/shard_map/ppermute | solution.py:84
  136.4 18.3 %collective-permute-done.8 = f32[2,2,256,256]{3,2,1,0:T(8,128)S(1)} collective-permute-done((f32[2,2,256,256]{3,2,1,0:T(8,128)S(1)}, f32[2,2,256,256]{3,2,1,0:T(8,128)S(1)}, u32[]{:S(2)}, u32[]{:S(2)}) %collective-permute-start.8) | collective-permute-done | bytes 1048608 | tf_op jit(solution)/shard_map/ppermute | solution.py:31
  155.7 8.8 %collective-permute-done.16 = bf16[416,256]{1,0:T(8,128)(2,1)S(1)} collective-permute-done((bf16[416,256]{1,0:T(8,128)(2,1)S(1)}, bf16[416,256]{1,0:T(8,128)(2,1)S(1)}, u32[]{:S(2)}, u32[]{:S(2)}) %collective-permute-start.16) | collective-permute-done | bytes 213024 | tf_op jit(solution)/shard_map/ppermute | solution.py:84
  164.6 2.0 %collective-permute-done.17 = bf16[416,256]{1,0:T(8,128)(2,1)S(1)} collective-permute-done((bf16[416,256]{1,0:T(8,128)(2,1)S(1)}, bf16[416,256]{1,0:T(8,128)(2,1)S(1)}, u32[]{:S(2)}, u32[]{:S(2)}) %collective-permute-start.17) | collective-permute-done | bytes 213024 | tf_op jit(solution)/shard_map/ppermute | solution.py:84
  166.7 2.2 %fusion.4 = bf16[2,2,2,256,256]{4,3,2,1,0:T(8,128)(2,1)} fusion(bf16[2,2,2,256,256]{4,3,2,1,0:T(8,128)(2,1)S(1)} %get-tuple-element.6, f32[2,2,2,256,256]{4,3,2,1,0:T(8,128)S(1)} %fusion.17, f32[2,2,2,256,256]{4,3,2,1,0:T(8,128)S(1)} %fusion.35, f32[2,2,2,256,256]{4,3,2,1,0:T(8,128)S(1)} %fusion.37, f32[2,2,2,256,256]{4,3,2,1,0:T(8,128)S(1)} %fusion.85, ...), kind=kOutput, calls=%fused_computation.13 | convolution fusion | flops 275775488 | bytes 21104128 | tf_op jit(solution)/shard_map/dot_general | solution.py:159
  170.7 1.1 pad_maximum_fusion.3
  (95 shorter events, 24.5 us)
Async XLA Ops:
  0.6 70.2 %copy-start = (bf16[256,256]{1,0:T(8,128)(2,1)S(1)}, bf16[256,256]{1,0:T(8,128)(2,1)}, u32[]{:S(2)}) copy-start(bf16[256,256]{1,0:T(8,128)(2,1)} %param.11) | copy-start | bytes 393220
  0.6 3.5 %copy-start.6 = (bf16[2,2,2,256,256]{4,3,2,1,0:T(8,128)(2,1)S(1)}, bf16[2,2,2,256,256]{4,3,2,1,0:T(8,128)(2,1)}, u32[]{:S(2)}) copy-start(bf16[2,2,2,256,256]{4,3,2,1,0:T(8,128)(2,1)} %param.7) | copy-start | bytes 3145732
  3.7 14.1 %collective-permute-start = (bf16[2,2,1,256,256]{4,3,2,1,0:T(8,128)(2,1)}, bf16[2,2,1,256,256]{4,3,2,1,0:T(8,128)(2,1)}, u32[]{:S(2)}, u32[]{:S(2)}) collective-permute-start(bf16[2,2,1,256,256]{4,3,2,1,0:T(8,128)(2,1)} %slice_select_fusion.1), channel_id=1, source_target_pairs={{0,1},{1,0},{2,3},{3,2},{4,5},{5,4},{6,7},{7,6},{8,9},{9,8},{10,11... | collective-permute-start | bytes 1572872 | tf_op jit(solution)/shard_map/ppermute | solution.py:202
  5.6 28.2 %collective-permute-start.5 = (bf16[2,2,2,256,256]{4,3,2,1,0:T(8,128)(2,1)S(1)}, bf16[2,2,2,256,256]{4,3,2,1,0:T(8,128)(2,1)S(1)}, u32[]{:S(2)}, u32[]{:S(2)}) collective-permute-start(bf16[2,2,2,256,256]{4,3,2,1,0:T(8,128)(2,1)S(1)} %get-tuple-element.6), channel_id=1, source_target_pairs={{2,0},{4,2},{6,4},{8,6},{10,8},{12,10},{14,12},{3,1},{5,3},{7,5},{... | collective-permute-start | bytes 3145736 | tf_op jit(solution)/shard_map/ppermute | solution.py:10
  7.7 19.4 %collective-permute-start.2 = (bf16[2,2,256,256]{3,2,1,0:T(8,128)(2,1)}, bf16[2,2,256,256]{3,2,1,0:T(8,128)(2,1)}, u32[]{:S(2)}, u32[]{:S(2)}) collective-permute-start(bf16[2,2,256,256]{3,2,1,0:T(8,128)(2,1)} %slice_bitcast_fusion), channel_id=1, source_target_pairs={{0,8},{1,9},{16,24},{17,25}} | collective-permute-start | bytes 1572872 | tf_op jit(solution)/shard_map/ppermute | solution.py:21
  16.0 1.4 copy-start.5
  19.0 1.3 copy-start.4
  27.1 12.3 %collective-permute-start.3 = (bf16[2,2,256,256]{3,2,1,0:T(8,128)(2,1)S(1)}, bf16[2,2,256,256]{3,2,1,0:T(8,128)(2,1)S(1)}, u32[]{:S(2)}, u32[]{:S(2)}) collective-permute-start(bf16[2,2,256,256]{3,2,1,0:T(8,128)(2,1)S(1)} %broadcast_select_fusion.2), channel_id=1, source_target_pairs={{0,4},{8,12},{1,5},{9,13},{16,20},{24,28},{17,21},{25,29}} | collective-permute-start | bytes 1572872 | tf_op jit(solution)/shard_map/ppermute | solution.py:21
  30.0 39.8 %collective-permute-start.1 = (bf16[2,2,2,256,256]{4,3,2,1,0:T(8,128)(2,1)S(1)}, bf16[2,2,2,256,256]{4,3,2,1,0:T(8,128)(2,1)S(1)}, u32[]{:S(2)}, u32[]{:S(2)}) collective-permute-start(bf16[2,2,2,256,256]{4,3,2,1,0:T(8,128)(2,1)S(1)} %get-tuple-element.18), channel_id=1, source_target_pairs={{0,2},{2,4},{4,6},{6,8},{8,10},{10,12},{12,14},{1,3},{3,5},{5,7},{... | collective-permute-start | bytes 3145736 | tf_op jit(solution)/shard_map/ppermute | solution.py:10
  39.4 5.2 %copy-start.1 = (f32[2,2,256,256]{3,2,1,0:T(8,128)S(1)}, f32[2,2,256,256]{3,2,1,0:T(8,128)}, u32[]{:S(2)}) copy-start(f32[2,2,256,256]{3,2,1,0:T(8,128)} %get-tuple-element.5) | copy-start | bytes 3145732
  39.5 28.1 %collective-permute-start.4 = (bf16[2,2,256,256]{3,2,1,0:T(8,128)(2,1)S(1)}, bf16[2,2,256,256]{3,2,1,0:T(8,128)(2,1)S(1)}, u32[]{:S(2)}, u32[]{:S(2)}) collective-permute-start(bf16[2,2,256,256]{3,2,1,0:T(8,128)(2,1)S(1)} %broadcast_select_fusion.3), channel_id=1, source_target_pairs={{0,2},{4,6},{8,10},{12,14},{1,3},{5,7},{9,11},{13,15},{16,18},{20,... | collective-permute-start | bytes 1572872 | tf_op jit(solution)/shard_map/ppermute | solution.py:21
  44.3 24.6 %collective-permute-start.6 = (bf16[2,2,1,256,256]{4,3,2,1,0:T(8,128)(2,1)S(1)}, bf16[2,2,1,256,256]{4,3,2,1,0:T(8,128)(2,1)S(1)}, u32[]{:S(2)}, u32[]{:S(2)}) collective-permute-start(bf16[2,2,1,256,256]{4,3,2,1,0:T(8,128)(2,1)S(1)} %slice_select_fusion), channel_id=1, source_target_pairs={{0,1},{1,0},{2,3},{3,2},{4,5},{5,4},{6,7},{7,6},{8,9},{9,8},{10,11... | collective-permute-start | bytes 1572872 | tf_op jit(solution)/shard_map/ppermute | solution.py:202
  44.7 61.9 %collective-permute-start.7 = (f32[2,2,256,256]{3,2,1,0:T(8,128)S(1)}, f32[2,2,256,256]{3,2,1,0:T(8,128)S(1)}, u32[]{:S(2)}, u32[]{:S(2)}) collective-permute-start(f32[2,2,256,256]{3,2,1,0:T(8,128)S(1)} %add.243), channel_id=1, source_target_pairs={{4,0},{12,8},{5,1},{13,9},{20,16},{28,24},{21,17},{29,25}} | collective-permute-start | bytes 3145736 | tf_op jit(solution)/shard_map/ppermute | solution.py:31
  68.8 4.7 %collective-permute-start.9 = (f32[1664,256]{1,0:T(8,128)S(1)}, f32[1664,256]{1,0:T(8,128)S(1)}, u32[]{:S(2)}, u32[]{:S(2)}) collective-permute-start(f32[1664,256]{1,0:T(8,128)S(1)} %constant_dynamic-slice_fusion.4), channel_id=1, source_target_pairs={{0,1},{1,0},{2,3},{3,2},{4,5},{5,4},{6,7},{7,6},{8,9},{9,8},{10,11... | collective-permute-start | bytes 5111816 | tf_op jit(solution)/shard_map/ppermute | solution.py:45
  69.8 1.0 copy-start.2
  73.8 11.7 %copy-start.3 = (bf16[2,2,2,256,256]{4,3,2,1,0:T(8,128)(2,1)S(1)}, bf16[2,2,2,256,256]{4,3,2,1,0:T(8,128)(2,1)}, u32[]{:S(2)}) copy-start(bf16[2,2,2,256,256]{4,3,2,1,0:T(8,128)(2,1)} %copy-done.2) | copy-start | bytes 3145732
  73.9 34.2 %collective-permute-start.10 = (f32[416,256]{1,0:T(8,128)S(1)}, f32[416,256]{1,0:T(8,128)S(1)}, u32[]{:S(2)}, u32[]{:S(2)}) collective-permute-start(f32[416,256]{1,0:T(8,128)S(1)} %get-tuple-element.11), channel_id=1, source_target_pairs={{0,4},{2,6},{4,8},{6,10},{8,12},{10,14},{12,0},{14,2},{1,5},{3,7},... | collective-permute-start | bytes 1277960 | tf_op jit(solution)/shard_map/ppermute | solution.py:71
  82.9 31.9 %collective-permute-start.11 = (f32[416,256]{1,0:T(8,128)S(1)}, f32[416,256]{1,0:T(8,128)S(1)}, u32[]{:S(2)}, u32[]{:S(2)}) collective-permute-start(f32[416,256]{1,0:T(8,128)S(1)} %get-tuple-element.13), channel_id=1, source_target_pairs={{0,8},{2,10},{4,12},{6,14},{8,0},{10,2},{12,4},{14,6},{1,9},{3,11}... | collective-permute-start | bytes 1277960 | tf_op jit(solution)/shard_map/ppermute | solution.py:71
  85.5 32.8 %collective-permute-start.12 = (f32[416,256]{1,0:T(8,128)S(1)}, f32[416,256]{1,0:T(8,128)S(1)}, u32[]{:S(2)}, u32[]{:S(2)}) collective-permute-start(f32[416,256]{1,0:T(8,128)S(1)} %get-tuple-element.12), channel_id=1, source_target_pairs={{0,12},{2,14},{4,0},{6,2},{8,4},{10,6},{12,8},{14,10},{1,13},{3,15... | collective-permute-start | bytes 1277960 | tf_op jit(solution)/shard_map/ppermute | solution.py:71
  106.8 48.0 %collective-permute-start.8 = (f32[2,2,256,256]{3,2,1,0:T(8,128)S(1)}, f32[2,2,256,256]{3,2,1,0:T(8,128)S(1)}, u32[]{:S(2)}, u32[]{:S(2)}) collective-permute-start(f32[2,2,256,256]{3,2,1,0:T(8,128)S(1)} %add.244), channel_id=1, source_target_pairs={{8,0},{9,1},{24,16},{25,17}} | collective-permute-start | bytes 3145736 | tf_op jit(solution)/shard_map/ppermute | solution.py:31
  118.4 7.1 %collective-permute-start.13 = (f32[208,256]{1,0:T(8,128)S(1)}, f32[208,256]{1,0:T(8,128)S(1)}, u32[]{:S(2)}, u32[]{:S(2)}) collective-permute-start(f32[208,256]{1,0:T(8,128)S(1)} %constant_dynamic-slice_fusion), channel_id=1, source_target_pairs={{0,2},{2,0},{4,6},{6,4},{8,10},{10,8},{12,14},{14,12},{1,3},{3,1},... | collective-permute-start | bytes 638984 | tf_op jit(solution)/shard_map/ppermute | solution.py:45
  125.6 4.8 %collective-permute-start.14 = (bf16[208,256]{1,0:T(8,128)(2,1)S(1)}, bf16[208,256]{1,0:T(8,128)(2,1)S(1)}, u32[]{:S(2)}, u32[]{:S(2)}) collective-permute-start(bf16[208,256]{1,0:T(8,128)(2,1)S(1)} %multiply_convert_fusion.3), channel_id=1, source_target_pairs={{0,2},{2,0},{4,6},{6,4},{8,10},{10,8},{12,14},{14,12},{1,3},{3,1},... | collective-permute-start | bytes 319496 | tf_op jit(solution)/shard_map/ppermute | solution.py:53
  130.5 25.2 %collective-permute-start.15 = (bf16[416,256]{1,0:T(8,128)(2,1)S(1)}, bf16[416,256]{1,0:T(8,128)(2,1)S(1)}, u32[]{:S(2)}, u32[]{:S(2)}) collective-permute-start(bf16[416,256]{1,0:T(8,128)(2,1)S(1)} %maximum_select_fusion.1), channel_id=1, source_target_pairs={{0,4},{2,6},{4,8},{6,10},{8,12},{10,14},{12,0},{14,2},{1,5},{3,7},... | collective-permute-start | bytes 638984 | tf_op jit(solution)/shard_map/ppermute | solution.py:84
  155.4 9.2 %collective-permute-start.16 = (bf16[416,256]{1,0:T(8,128)(2,1)S(1)}, bf16[416,256]{1,0:T(8,128)(2,1)S(1)}, u32[]{:S(2)}, u32[]{:S(2)}) collective-permute-start(bf16[416,256]{1,0:T(8,128)(2,1)S(1)} %maximum_select_fusion.1), channel_id=1, source_target_pairs={{0,8},{2,10},{4,12},{6,14},{8,0},{10,2},{12,4},{14,6},{1,9},{3,11}... | collective-permute-start | bytes 638984 | tf_op jit(solution)/shard_map/ppermute | solution.py:84
  155.5 11.1 %collective-permute-start.17 = (bf16[416,256]{1,0:T(8,128)(2,1)S(1)}, bf16[416,256]{1,0:T(8,128)(2,1)S(1)}, u32[]{:S(2)}, u32[]{:S(2)}) collective-permute-start(bf16[416,256]{1,0:T(8,128)(2,1)S(1)} %maximum_select_fusion.1), channel_id=1, source_target_pairs={{0,12},{2,14},{4,0},{6,2},{8,4},{10,6},{12,8},{14,10},{1,13},{3,15... | collective-permute-start | bytes 638984 | tf_op jit(solution)/shard_map/ppermute | solution.py:84
  166.7 2.4 %collective-permute-start.18 = (bf16[1664,256]{1,0:T(8,128)(2,1)S(1)}, bf16[1664,256]{1,0:T(8,128)(2,1)S(1)}, u32[]{:S(2)}, u32[]{:S(2)}) collective-permute-start(bf16[1664,256]{1,0:T(8,128)(2,1)S(1)} %bitcast.256), channel_id=1, source_target_pairs={{0,1},{1,0},{2,3},{3,2},{4,5},{5,4},{6,7},{7,6},{8,9},{9,8},{10,11... | collective-permute-start | bytes 2555912 | tf_op jit(solution)/shard_map/ppermute | solution.py:130

commit v14 on v13

--- a/solution.py
+++ b/solution.py
@@ -30,6 +30,16 @@
         pairs = [(i + step, i) for i in range(0, count, 2 * step) if i + step < count]
         value = value + lax.ppermute(value, axis, pairs)
         step *= 2
+    return value
+
+
+def chain_reduce(value, axis, step):
+    count = lax.axis_size(axis)
+    holders = list(range(0, count, step))
+    if len(holders) > 4:
+        return tree_reduce(value, axis, step)
+    for k in range(len(holders) - 1, 0, -1):
+        value = value + lax.ppermute(value, axis, [(holders[k], holders[k - 1])])
     return value
 
 
@@ -222,7 +232,7 @@
     later = shifted(cot, "space", -1)
     if lax.axis_size("space") % 2 == 0:
         cot_pair = cot_local + jnp.sum(later, axis=1, dtype=jnp.float32)
-        cot_sum = tree_reduce(cot_pair, "space", 2)
+        cot_sum = chain_reduce(cot_pair, "space", 2)
     else:
         cot_sum = tree_reduce(cot_local, "space")
     rows_pad = row_halo(masked)

time: 172 us -> 187 us (1.087)
  starting transfers between devices: 38.8 us -> 56.9 us
  waiting for transfers between devices: 93.8 us -> 89.5 us
    ppermute x2 -> x3, waiting for transfers between devices: 37.7 us -> 4.86 us  [chain_reduce(): value = value + lax.ppermute(value, axis, [(holders[k], holders[k - 1])])]
    ppermute x3, waiting for transfers between devices: 10.2 us -> 42.9 us  [direct_scatter(): total = total + lax.ppermute(send, axis, pairs)]
    ppermute x3, starting transfers between devices: 11.6 us -> 23.4 us  [direct_scatter(): total = total + lax.ppermute(send, axis, pairs)]
    ppermute x3, starting transfers between devices: 6.09 us -> 12.2 us  [direct_gather(): got = lax.ppermute(piece, axis, pairs)]
    ppermute x3, waiting for transfers between devices: 10.9 us -> 5.91 us  [direct_gather(): got = lax.ppermute(piece, axis, pairs)]
  transfers between devices with their start and end apart: 19 -> 20, of which waited for: 12 -> 12; matrix products, arithmetic and copies ran while one was open for 18% -> 17% of each run, Pallas kernels for 0% -> 0%
where the time goes in v14:
time: 187 us; the launch traced here: 186 us
  waiting for transfers between devices  89.5 us (48%)
  starting transfers between devices  56.9 us (30%)
  matrix products  24.4 us (13%)
  other arithmetic  10.1 us (5%)
  local copies, waits for them, and re-layouts  3.62 us (2%)
    ppermute x3, waiting for transfers between devices, direct_scatter(): total = total + lax.ppermute(send, axis, pairs)  42.9 us
    ppermute x3, waiting for transfers between devices, tree_broadcast(): got = lax.ppermute(value, axis, pairs)  23.8 us
    ppermute x3, starting transfers between devices, direct_scatter(): total = total + lax.ppermute(send, axis, pairs)  23.4 us
    ppermute x3, starting transfers between devices, tree_broadcast(): got = lax.ppermute(value, axis, pairs)  14.4 us
    ppermute x3, starting transfers between devices, direct_gather(): got = lax.ppermute(piece, axis, pairs)  12.2 us
    dot_general x18, matrix products, spatial_sum(): total = total + jnp.dot(piece, kernel, preferred_element_type=jnp.float32)  12.1 us
    ppermute x2, waiting for transfers between devices, xor_halving(): flat = keep + lax.ppermute(send, axis, pairs)  6.64 us
    ppermute x3, waiting for transfers between devices, direct_gather(): got = lax.ppermute(piece, axis, pairs)  5.91 us
  transfers between devices with their start and end apart: 20, of which 12 were waited for; matrix products, arithmetic and copies ran while one was open for 17% of the time, Pallas kernels for 0%

profile of v14, /device:TPU:0, one launch (start us, length us, event | category | flops | bytes accessed | tf_op | source)
XLA Modules:
  0.0 185.6 jit_solution(4756423384013012153)
XLA Ops:
  1.5 1.4 broadcast_multiply_fusion.1
  4.2 1.4 convert_reduce_fusion
  5.6 1.3 collective-permute-start.5
  7.7 8.3 %collective-permute-start.2 = (bf16[2,2,256,256]{3,2,1,0:T(8,128)(2,1)}, bf16[2,2,256,256]{3,2,1,0:T(8,128)(2,1)}, u32[]{:S(2)}, u32[]{:S(2)}) collective-permute-start(bf16[2,2,256,256]{3,2,1,0:T(8,128)(2,1)} %slice_bitcast_fusion), channel_id=1, source_target_pairs={{0,8},{1,9},{16,24},{17,25}} | collective-permute-start | bytes 1572872 | tf_op jit(solution)/shard_map/ppermute | solution.py:21
  16.0 1.4 fusion.87
  17.8 1.1 broadcast_select_fusion.8
  23.3 3.7 %collective-permute-done.2 = bf16[2,2,256,256]{3,2,1,0:T(8,128)(2,1)} collective-permute-done((bf16[2,2,256,256]{3,2,1,0:T(8,128)(2,1)}, bf16[2,2,256,256]{3,2,1,0:T(8,128)(2,1)}, u32[]{:S(2)}, u32[]{:S(2)}) %collective-permute-start.2) | collective-permute-done | bytes 524320 | tf_op jit(solution)/shard_map/ppermute | solution.py:21
  27.1 1.3 collective-permute-start.3
  28.4 1.6 multiply_convert_fusion.2
  30.0 1.5 collective-permute-start.1
  32.5 1.3 collective-permute-done.5
  34.2 1.1 multiply_convert_fusion
  39.5 4.7 %collective-permute-start.4 = (bf16[2,2,256,256]{3,2,1,0:T(8,128)(2,1)S(1)}, bf16[2,2,256,256]{3,2,1,0:T(8,128)(2,1)S(1)}, u32[]{:S(2)}, u32[]{:S(2)}) collective-permute-start(bf16[2,2,256,256]{3,2,1,0:T(8,128)(2,1)S(1)} %broadcast_select_fusion.3), channel_id=1, source_target_pairs={{0,2},{4,6},{8,10},{12,14},{1,3},{5,7},{9,11},{13,15},{16,18},{20,... | collective-permute-start | bytes 1572872 | tf_op jit(solution)/shard_map/ppermute | solution.py:21
  44.6 0.9 collective-permute-start.7
  47.6 20.0 %collective-permute-done.4 = bf16[2,2,256,256]{3,2,1,0:T(8,128)(2,1)S(1)} collective-permute-done((bf16[2,2,256,256]{3,2,1,0:T(8,128)(2,1)S(1)}, bf16[2,2,256,256]{3,2,1,0:T(8,128)(2,1)S(1)}, u32[]{:S(2)}, u32[]{:S(2)}) %collective-permute-start.4) | collective-permute-done | bytes 524320 | tf_op jit(solution)/shard_map/ppermute | solution.py:21
  69.0 0.9 select_maximum_fusion
  74.8 9.4 %collective-permute-start.11 = (f32[416,256]{1,0:T(8,128)S(1)}, f32[416,256]{1,0:T(8,128)S(1)}, u32[]{:S(2)}, u32[]{:S(2)}) collective-permute-start(f32[416,256]{1,0:T(8,128)S(1)} %get-tuple-element.11), channel_id=1, source_target_pairs={{0,4},{2,6},{4,8},{6,10},{8,12},{10,14},{12,0},{14,2},{1,5},{3,7},... | collective-permute-start | bytes 1277960 | tf_op jit(solution)/shard_map/ppermute | solution.py:81
  84.2 11.1 %collective-permute-start.12 = (f32[416,256]{1,0:T(8,128)S(1)}, f32[416,256]{1,0:T(8,128)S(1)}, u32[]{:S(2)}, u32[]{:S(2)}) collective-permute-start(f32[416,256]{1,0:T(8,128)S(1)} %get-tuple-element.13), channel_id=1, source_target_pairs={{0,8},{2,10},{4,12},{6,14},{8,0},{10,2},{12,4},{14,6},{1,9},{3,11}... | collective-permute-start | bytes 1277960 | tf_op jit(solution)/shard_map/ppermute | solution.py:81
  95.4 2.8 %collective-permute-start.13 = (f32[416,256]{1,0:T(8,128)S(1)}, f32[416,256]{1,0:T(8,128)S(1)}, u32[]{:S(2)}, u32[]{:S(2)}) collective-permute-start(f32[416,256]{1,0:T(8,128)S(1)} %get-tuple-element.12), channel_id=1, source_target_pairs={{0,12},{2,14},{4,0},{6,2},{8,4},{10,6},{12,8},{14,10},{1,13},{3,15... | collective-permute-start | bytes 1277960 | tf_op jit(solution)/shard_map/ppermute | solution.py:81
  98.2 1.8 multiply_convert_fusion.1
  100.2 1.3 collective-permute-start.9
  101.5 2.9 %collective-permute-done.11 = f32[416,256]{1,0:T(8,128)S(1)} collective-permute-done((f32[416,256]{1,0:T(8,128)S(1)}, f32[416,256]{1,0:T(8,128)S(1)}, u32[]{:S(2)}, u32[]{:S(2)}) %collective-permute-start.11) | collective-permute-done | bytes 426016 | tf_op jit(solution)/shard_map/ppermute | solution.py:81
  104.4 40.0 %collective-permute-done.12 = f32[416,256]{1,0:T(8,128)S(1)} collective-permute-done((f32[416,256]{1,0:T(8,128)S(1)}, f32[416,256]{1,0:T(8,128)S(1)}, u32[]{:S(2)}, u32[]{:S(2)}) %collective-permute-start.12) | collective-permute-done | bytes 426016 | tf_op jit(solution)/shard_map/ppermute | solution.py:81
  145.1 6.6 %collective-permute-done.14 = f32[208,256]{1,0:T(8,128)S(1)} collective-permute-done((f32[208,256]{1,0:T(8,128)S(1)}, f32[208,256]{1,0:T(8,128)S(1)}, u32[]{:S(2)}, u32[]{:S(2)}) %collective-permute-start.14) | collective-permute-done | bytes 213024 | tf_op jit(solution)/shard_map/ppermute | solution.py:55
  152.6 4.0 %collective-permute-done.15 = bf16[208,256]{1,0:T(8,128)(2,1)S(1)} collective-permute-done((bf16[208,256]{1,0:T(8,128)(2,1)S(1)}, bf16[208,256]{1,0:T(8,128)(2,1)S(1)}, u32[]{:S(2)}, u32[]{:S(2)}) %collective-permute-start.15) | collective-permute-done | bytes 106528 | tf_op jit(solution)/shard_map/ppermute | solution.py:63
  156.6 9.7 %collective-permute-start.16 = (bf16[416,256]{1,0:T(8,128)(2,1)S(1)}, bf16[416,256]{1,0:T(8,128)(2,1)S(1)}, u32[]{:S(2)}, u32[]{:S(2)}) collective-permute-start(bf16[416,256]{1,0:T(8,128)(2,1)S(1)} %maximum_select_fusion.1), channel_id=1, source_target_pairs={{0,4},{2,6},{4,8},{6,10},{8,12},{10,14},{12,0},{14,2},{1,5},{3,7},... | collective-permute-start | bytes 638984 | tf_op jit(solution)/shard_map/ppermute | solution.py:94
  166.4 2.4 %collective-permute-start.18 = (bf16[416,256]{1,0:T(8,128)(2,1)S(1)}, bf16[416,256]{1,0:T(8,128)(2,1)S(1)}, u32[]{:S(2)}, u32[]{:S(2)}) collective-permute-start(bf16[416,256]{1,0:T(8,128)(2,1)S(1)} %maximum_select_fusion.1), channel_id=1, source_target_pairs={{0,12},{2,14},{4,0},{6,2},{8,4},{10,6},{12,8},{14,10},{1,13},{3,15... | collective-permute-start | bytes 638984 | tf_op jit(solution)/shard_map/ppermute | solution.py:94
  169.0 4.9 %collective-permute-done.9 = f32[2,2,256,256]{3,2,1,0:T(8,128)S(1)} collective-permute-done((f32[2,2,256,256]{3,2,1,0:T(8,128)S(1)}, f32[2,2,256,256]{3,2,1,0:T(8,128)S(1)}, u32[]{:S(2)}, u32[]{:S(2)}) %collective-permute-start.9) | collective-permute-done | bytes 1048608 | tf_op jit(solution)/shard_map/ppermute | solution.py:42
  174.5 3.0 %collective-permute-done.17 = bf16[416,256]{1,0:T(8,128)(2,1)S(1)} collective-permute-done((bf16[416,256]{1,0:T(8,128)(2,1)S(1)}, bf16[416,256]{1,0:T(8,128)(2,1)S(1)}, u32[]{:S(2)}, u32[]{:S(2)}) %collective-permute-start.17) | collective-permute-done | bytes 213024 | tf_op jit(solution)/shard_map/ppermute | solution.py:94
  177.6 2.9 %collective-permute-done.18 = bf16[416,256]{1,0:T(8,128)(2,1)S(1)} collective-permute-done((bf16[416,256]{1,0:T(8,128)(2,1)S(1)}, bf16[416,256]{1,0:T(8,128)(2,1)S(1)}, u32[]{:S(2)}, u32[]{:S(2)}) %collective-permute-start.18) | collective-permute-done | bytes 213024 | tf_op jit(solution)/shard_map/ppermute | solution.py:94
  180.6 2.2 %fusion.4 = bf16[2,2,2,256,256]{4,3,2,1,0:T(8,128)(2,1)} fusion(bf16[2,2,2,256,256]{4,3,2,1,0:T(8,128)(2,1)S(1)} %get-tuple-element.6, f32[2,2,2,256,256]{4,3,2,1,0:T(8,128)S(1)} %fusion.17, f32[2,2,2,256,256]{4,3,2,1,0:T(8,128)S(1)} %fusion.35, f32[2,2,2,256,256]{4,3,2,1,0:T(8,128)S(1)} %fusion.37, f32[2,2,2,256,256]{4,3,2,1,0:T(8,128)S(1)} %fusion.85, ...), kind=kOutput, calls=%fused_computation.13 | convolution fusion | flops 275775488 | bytes 21104128 | tf_op jit(solution)/shard_map/dot_general | solution.py:169
  184.6 1.1 pad_maximum_fusion.3
  (98 shorter events, 26.2 us)
Async XLA Ops:
  0.6 71.1 %copy-start = (bf16[256,256]{1,0:T(8,128)(2,1)S(1)}, bf16[256,256]{1,0:T(8,128)(2,1)}, u32[]{:S(2)}) copy-start(bf16[256,256]{1,0:T(8,128)(2,1)} %param.11) | copy-start | bytes 393220
  0.6 3.5 %copy-start.6 = (bf16[2,2,2,256,256]{4,3,2,1,0:T(8,128)(2,1)S(1)}, bf16[2,2,2,256,256]{4,3,2,1,0:T(8,128)(2,1)}, u32[]{:S(2)}) copy-start(bf16[2,2,2,256,256]{4,3,2,1,0:T(8,128)(2,1)} %param.7) | copy-start | bytes 3145732
  3.7 14.1 %collective-permute-start = (bf16[2,2,1,256,256]{4,3,2,1,0:T(8,128)(2,1)}, bf16[2,2,1,256,256]{4,3,2,1,0:T(8,128)(2,1)}, u32[]{:S(2)}, u32[]{:S(2)}) collective-permute-start(bf16[2,2,1,256,256]{4,3,2,1,0:T(8,128)(2,1)} %slice_select_fusion.1), channel_id=1, source_target_pairs={{0,1},{1,0},{2,3},{3,2},{4,5},{5,4},{6,7},{7,6},{8,9},{9,8},{10,11... | collective-permute-start | bytes 1572872 | tf_op jit(solution)/shard_map/ppermute | solution.py:212
  5.6 28.2 %collective-permute-start.5 = (bf16[2,2,2,256,256]{4,3,2,1,0:T(8,128)(2,1)S(1)}, bf16[2,2,2,256,256]{4,3,2,1,0:T(8,128)(2,1)S(1)}, u32[]{:S(2)}, u32[]{:S(2)}) collective-permute-start(bf16[2,2,2,256,256]{4,3,2,1,0:T(8,128)(2,1)S(1)} %get-tuple-element.6), channel_id=1, source_target_pairs={{2,0},{4,2},{6,4},{8,6},{10,8},{12,10},{14,12},{3,1},{5,3},{7,5},{... | collective-permute-start | bytes 3145736 | tf_op jit(solution)/shard_map/ppermute | solution.py:10
  7.7 19.4 %collective-permute-start.2 = (bf16[2,2,256,256]{3,2,1,0:T(8,128)(2,1)}, bf16[2,2,256,256]{3,2,1,0:T(8,128)(2,1)}, u32[]{:S(2)}, u32[]{:S(2)}) collective-permute-start(bf16[2,2,256,256]{3,2,1,0:T(8,128)(2,1)} %slice_bitcast_fusion), channel_id=1, source_target_pairs={{0,8},{1,9},{16,24},{17,25}} | collective-permute-start | bytes 1572872 | tf_op jit(solution)/shard_map/ppermute | solution.py:21
  16.0 1.4 copy-start.5
  19.0 1.3 copy-start.4
  27.1 12.3 %collective-permute-start.3 = (bf16[2,2,256,256]{3,2,1,0:T(8,128)(2,1)S(1)}, bf16[2,2,256,256]{3,2,1,0:T(8,128)(2,1)S(1)}, u32[]{:S(2)}, u32[]{:S(2)}) collective-permute-start(bf16[2,2,256,256]{3,2,1,0:T(8,128)(2,1)S(1)} %broadcast_select_fusion.2), channel_id=1, source_target_pairs={{0,4},{8,12},{1,5},{9,13},{16,20},{24,28},{17,21},{25,29}} | collective-permute-start | bytes 1572872 | tf_op jit(solution)/shard_map/ppermute | solution.py:21
  30.0 40.3 %collective-permute-start.1 = (bf16[2,2,2,256,256]{4,3,2,1,0:T(8,128)(2,1)S(1)}, bf16[2,2,2,256,256]{4,3,2,1,0:T(8,128)(2,1)S(1)}, u32[]{:S(2)}, u32[]{:S(2)}) collective-permute-start(bf16[2,2,2,256,256]{4,3,2,1,0:T(8,128)(2,1)S(1)} %get-tuple-element.18), channel_id=1, source_target_pairs={{0,2},{2,4},{4,6},{6,8},{8,10},{10,12},{12,14},{1,3},{3,5},{5,7},{... | collective-permute-start | bytes 3145736 | tf_op jit(solution)/shard_map/ppermute | solution.py:10
  39.3 5.2 %copy-start.1 = (f32[2,2,256,256]{3,2,1,0:T(8,128)S(1)}, f32[2,2,256,256]{3,2,1,0:T(8,128)}, u32[]{:S(2)}) copy-start(f32[2,2,256,256]{3,2,1,0:T(8,128)} %get-tuple-element.5) | copy-start | bytes 3145732
  39.5 28.1 %collective-permute-start.4 = (bf16[2,2,256,256]{3,2,1,0:T(8,128)(2,1)S(1)}, bf16[2,2,256,256]{3,2,1,0:T(8,128)(2,1)S(1)}, u32[]{:S(2)}, u32[]{:S(2)}) collective-permute-start(bf16[2,2,256,256]{3,2,1,0:T(8,128)(2,1)S(1)} %broadcast_select_fusion.3), channel_id=1, source_target_pairs={{0,2},{4,6},{8,10},{12,14},{1,3},{5,7},{9,11},{13,15},{16,18},{20,... | collective-permute-start | bytes 1572872 | tf_op jit(solution)/shard_map/ppermute | solution.py:21
  44.2 24.7 %collective-permute-start.6 = (bf16[2,2,1,256,256]{4,3,2,1,0:T(8,128)(2,1)S(1)}, bf16[2,2,1,256,256]{4,3,2,1,0:T(8,128)(2,1)S(1)}, u32[]{:S(2)}, u32[]{:S(2)}) collective-permute-start(bf16[2,2,1,256,256]{4,3,2,1,0:T(8,128)(2,1)S(1)} %slice_select_fusion), channel_id=1, source_target_pairs={{0,1},{1,0},{2,3},{3,2},{4,5},{5,4},{6,7},{7,6},{8,9},{9,8},{10,11... | collective-permute-start | bytes 1572872 | tf_op jit(solution)/shard_map/ppermute | solution.py:212
  44.6 28.9 %collective-permute-start.7 = (f32[2,2,256,256]{3,2,1,0:T(8,128)S(1)}, f32[2,2,256,256]{3,2,1,0:T(8,128)S(1)}, u32[]{:S(2)}, u32[]{:S(2)}) collective-permute-start(f32[2,2,256,256]{3,2,1,0:T(8,128)S(1)} %add.246), channel_id=1, source_target_pairs={{12,8},{13,9},{28,24},{29,25}} | collective-permute-start | bytes 3145736 | tf_op jit(solution)/shard_map/ppermute | solution.py:42
  68.8 5.6 %collective-permute-start.10 = (f32[1664,256]{1,0:T(8,128)S(1)}, f32[1664,256]{1,0:T(8,128)S(1)}, u32[]{:S(2)}, u32[]{:S(2)}) collective-permute-start(f32[1664,256]{1,0:T(8,128)S(1)} %constant_dynamic-slice_fusion.4), channel_id=1, source_target_pairs={{0,1},{1,0},{2,3},{3,2},{4,5},{5,4},{6,7},{7,6},{8,9},{9,8},{10,11... | collective-permute-start | bytes 5111816 | tf_op jit(solution)/shard_map/ppermute | solution.py:55
  70.3 1.0 copy-start.2
  73.7 26.4 %collective-permute-start.8 = (f32[2,2,256,256]{3,2,1,0:T(8,128)S(1)}, f32[2,2,256,256]{3,2,1,0:T(8,128)S(1)}, u32[]{:S(2)}, u32[]{:S(2)}) collective-permute-start(f32[2,2,256,256]{3,2,1,0:T(8,128)S(1)} %add.247), channel_id=1, source_target_pairs={{8,4},{9,5},{24,20},{25,21}} | collective-permute-start | bytes 3145736 | tf_op jit(solution)/shard_map/ppermute | solution.py:42
  74.7 23.6 %copy-start.3 = (bf16[2,2,2,256,256]{4,3,2,1,0:T(8,128)(2,1)S(1)}, bf16[2,2,2,256,256]{4,3,2,1,0:T(8,128)(2,1)}, u32[]{:S(2)}) copy-start(bf16[2,2,2,256,256]{4,3,2,1,0:T(8,128)(2,1)} %copy-done.2) | copy-start | bytes 3145732
  74.8 29.6 %collective-permute-start.11 = (f32[416,256]{1,0:T(8,128)S(1)}, f32[416,256]{1,0:T(8,128)S(1)}, u32[]{:S(2)}, u32[]{:S(2)}) collective-permute-start(f32[416,256]{1,0:T(8,128)S(1)} %get-tuple-element.11), channel_id=1, source_target_pairs={{0,4},{2,6},{4,8},{6,10},{8,12},{10,14},{12,0},{14,2},{1,5},{3,7},... | collective-permute-start | bytes 1277960 | tf_op jit(solution)/shard_map/ppermute | solution.py:81
  84.2 60.2 %collective-permute-start.12 = (f32[416,256]{1,0:T(8,128)S(1)}, f32[416,256]{1,0:T(8,128)S(1)}, u32[]{:S(2)}, u32[]{:S(2)}) collective-permute-start(f32[416,256]{1,0:T(8,128)S(1)} %get-tuple-element.13), channel_id=1, source_target_pairs={{0,8},{2,10},{4,12},{6,14},{8,0},{10,2},{12,4},{14,6},{1,9},{3,11}... | collective-permute-start | bytes 1277960 | tf_op jit(solution)/shard_map/ppermute | solution.py:81
  95.4 49.0 %collective-permute-start.13 = (f32[416,256]{1,0:T(8,128)S(1)}, f32[416,256]{1,0:T(8,128)S(1)}, u32[]{:S(2)}, u32[]{:S(2)}) collective-permute-start(f32[416,256]{1,0:T(8,128)S(1)} %get-tuple-element.12), channel_id=1, source_target_pairs={{0,12},{2,14},{4,0},{6,2},{8,4},{10,6},{12,8},{14,10},{1,13},{3,15... | collective-permute-start | bytes 1277960 | tf_op jit(solution)/shard_map/ppermute | solution.py:81
  100.2 73.6 %collective-permute-start.9 = (f32[2,2,256,256]{3,2,1,0:T(8,128)S(1)}, f32[2,2,256,256]{3,2,1,0:T(8,128)S(1)}, u32[]{:S(2)}, u32[]{:S(2)}) collective-permute-start(f32[2,2,256,256]{3,2,1,0:T(8,128)S(1)} %add.248), channel_id=1, source_target_pairs={{4,0},{5,1},{20,16},{21,17}} | collective-permute-start | bytes 3145736 | tf_op jit(solution)/shard_map/ppermute | solution.py:42
  144.6 7.2 %collective-permute-start.14 = (f32[208,256]{1,0:T(8,128)S(1)}, f32[208,256]{1,0:T(8,128)S(1)}, u32[]{:S(2)}, u32[]{:S(2)}) collective-permute-start(f32[208,256]{1,0:T(8,128)S(1)} %constant_dynamic-slice_fusion), channel_id=1, source_target_pairs={{0,2},{2,0},{4,6},{6,4},{8,10},{10,8},{12,14},{14,12},{1,3},{3,1},... | collective-permute-start | bytes 638984 | tf_op jit(solution)/shard_map/ppermute | solution.py:55
  151.8 4.8 %collective-permute-start.15 = (bf16[208,256]{1,0:T(8,128)(2,1)S(1)}, bf16[208,256]{1,0:T(8,128)(2,1)S(1)}, u32[]{:S(2)}, u32[]{:S(2)}) collective-permute-start(bf16[208,256]{1,0:T(8,128)(2,1)S(1)} %multiply_convert_fusion.3), channel_id=1, source_target_pairs={{0,2},{2,0},{4,6},{6,4},{8,10},{10,8},{12,14},{14,12},{1,3},{3,1},... | collective-permute-start | bytes 319496 | tf_op jit(solution)/shard_map/ppermute | solution.py:63
  156.6 17.9 %collective-permute-start.16 = (bf16[416,256]{1,0:T(8,128)(2,1)S(1)}, bf16[416,256]{1,0:T(8,128)(2,1)S(1)}, u32[]{:S(2)}, u32[]{:S(2)}) collective-permute-start(bf16[416,256]{1,0:T(8,128)(2,1)S(1)} %maximum_select_fusion.1), channel_id=1, source_target_pairs={{0,4},{2,6},{4,8},{6,10},{8,12},{10,14},{12,0},{14,2},{1,5},{3,7},... | collective-permute-start | bytes 638984 | tf_op jit(solution)/shard_map/ppermute | solution.py:94
  166.4 11.2 %collective-permute-start.17 = (bf16[416,256]{1,0:T(8,128)(2,1)S(1)}, bf16[416,256]{1,0:T(8,128)(2,1)S(1)}, u32[]{:S(2)}, u32[]{:S(2)}) collective-permute-start(bf16[416,256]{1,0:T(8,128)(2,1)S(1)} %maximum_select_fusion.1), channel_id=1, source_target_pairs={{0,8},{2,10},{4,12},{6,14},{8,0},{10,2},{12,4},{14,6},{1,9},{3,11}... | collective-permute-start | bytes 638984 | tf_op jit(solution)/shard_map/ppermute | solution.py:94
  166.4 14.1 %collective-permute-start.18 = (bf16[416,256]{1,0:T(8,128)(2,1)S(1)}, bf16[416,256]{1,0:T(8,128)(2,1)S(1)}, u32[]{:S(2)}, u32[]{:S(2)}) collective-permute-start(bf16[416,256]{1,0:T(8,128)(2,1)S(1)} %maximum_select_fusion.1), channel_id=1, source_target_pairs={{0,12},{2,14},{4,0},{6,2},{8,4},{10,6},{12,8},{14,10},{1,13},{3,15... | collective-permute-start | bytes 638984 | tf_op jit(solution)/shard_map/ppermute | solution.py:94
  180.5 2.4 %collective-permute-start.19 = (bf16[1664,256]{1,0:T(8,128)(2,1)S(1)}, bf16[1664,256]{1,0:T(8,128)(2,1)S(1)}, u32[]{:S(2)}, u32[]{:S(2)}) collective-permute-start(bf16[1664,256]{1,0:T(8,128)(2,1)S(1)} %bitcast.256), channel_id=1, source_target_pairs={{0,1},{1,0},{2,3},{3,2},{4,5},{5,4},{6,7},{7,6},{8,9},{9,8},{10,11... | collective-permute-start | bytes 2555912 | tf_op jit(solution)/shard_map/ppermute | solution.py:140

commit v15 on v13

--- a/solution.py
+++ b/solution.py
@@ -10,9 +10,28 @@
     return lax.ppermute(value, axis, pairs)
 
 
+def rounds_broadcast(value, axis, rounds):
+    me = lax.axis_index(axis)
+    for permutes in rounds:
+        for pairs in permutes:
+            got = lax.ppermute(value, axis, pairs)
+            takes = me == pairs[0][1]
+            for _, dst in pairs[1:]:
+                takes = takes | (me == dst)
+            value = jnp.where(takes, got, value)
+    return value
+
+
 def tree_broadcast(value, axis):
     count = lax.axis_size(axis)
     me = lax.axis_index(axis)
+    if count == 8:
+        rounds = [
+            [[(0, 1)], [(0, 4)]],
+            [[(0, 2), (4, 6), (1, 5)]],
+            [[(1, 3), (5, 7)]],
+        ]
+        return rounds_broadcast(value, axis, rounds)
     step = 1
     while step * 2 < count:
         step *= 2

time: 172 us -> 181 us (1.052)
  the two profiles are of different devices: /device:TPU:0 before, /device:TPU:25 now
where the time goes in v15:
time: 181 us; the launch traced here: 180 us
  waiting for transfers between devices  89.3 us (49%)
  starting transfers between devices  50 us (28%)
  matrix products  26.5 us (15%)
  other arithmetic  10.1 us (6%)
  local copies, waits for them, and re-layouts  3.08 us (2%)
    ppermute x2, waiting for transfers between devices, shifted(): return lax.ppermute(value, axis, pairs)  30.9 us
    ppermute x3, waiting for transfers between devices, direct_scatter(): total = total + lax.ppermute(send, axis, pairs)  29.8 us
    ppermute x2, starting transfers between devices, xor_halving(): flat = keep + lax.ppermute(send, axis, pairs)  23.5 us
    ppermute x3, waiting for transfers between devices, direct_gather(): got = lax.ppermute(piece, axis, pairs)  15.3 us
    dot_general x18, matrix products, spatial_sum(): total = total + jnp.dot(piece, kernel, preferred_element_type=jnp.float32)  12 us
    ppermute x4, waiting for transfers between devices, rounds_broadcast(): got = lax.ppermute(value, axis, pairs)  5.5 us
    ppermute x2, starting transfers between devices, shifted(): return lax.ppermute(value, axis, pairs)  5.34 us
    ppermute x2, starting transfers between devices, tree_reduce(): value = value + lax.ppermute(value, axis, pairs)  5.09 us
  transfers between devices with their start and end apart: 20, of which 8 were waited for; matrix products, arithmetic and copies ran while one was open for 19% of the time, Pallas kernels for 0%

profile of v15, /device:TPU:25, one launch (start us, length us, event | category | flops | bytes accessed | tf_op | source)
XLA Modules:
  0.0 180.1 jit_solution(17996240977893297779)
XLA Ops:
  1.5 1.4 broadcast_multiply_fusion.1
  2.9 0.9 slice_select_fusion.1
  4.4 1.4 convert_reduce_fusion
  5.8 3.0 %collective-permute-start.6 = (bf16[2,2,2,256,256]{4,3,2,1,0:T(8,128)(2,1)S(1)}, bf16[2,2,2,256,256]{4,3,2,1,0:T(8,128)(2,1)S(1)}, u32[]{:S(2)}, u32[]{:S(2)}) collective-permute-start(bf16[2,2,2,256,256]{4,3,2,1,0:T(8,128)(2,1)S(1)} %get-tuple-element.6), channel_id=1, source_target_pairs={{2,0},{4,2},{6,4},{8,6},{10,8},{12,10},{14,12},{3,1},{5,3},{7,5},{... | collective-permute-start | bytes 3145736 | tf_op jit(solution)/shard_map/ppermute | solution.py:10
  9.6 1.5 collective-permute-start.2
  11.1 1.4 fusion.87
  13.0 1.1 broadcast_select_fusion.9
  14.1 0.8 select_maximum_fusion.2
  19.2 1.5 multiply_convert_fusion.2
  20.7 2.3 %collective-permute-start.1 = (bf16[2,2,2,256,256]{4,3,2,1,0:T(8,128)(2,1)S(1)}, bf16[2,2,2,256,256]{4,3,2,1,0:T(8,128)(2,1)}, u32[]{:S(2)}, u32[]{:S(2)}) collective-permute-start(bf16[2,2,2,256,256]{4,3,2,1,0:T(8,128)(2,1)S(1)} %get-tuple-element.18), channel_id=1, source_target_pairs={{0,2},{2,4},{4,6},{6,8},{8,10},{10,12},{12,14},{1,3},{3,5},{5,7},{... | collective-permute-start | bytes 3145736 | tf_op jit(solution)/shard_map/ppermute | solution.py:10
  24.0 30.9 %collective-permute-done.6 = bf16[2,2,2,256,256]{4,3,2,1,0:T(8,128)(2,1)S(1)} collective-permute-done((bf16[2,2,2,256,256]{4,3,2,1,0:T(8,128)(2,1)S(1)}, bf16[2,2,2,256,256]{4,3,2,1,0:T(8,128)(2,1)S(1)}, u32[]{:S(2)}, u32[]{:S(2)}) %collective-permute-start.6) | collective-permute-done | bytes 1048608 | tf_op jit(solution)/shard_map/ppermute | solution.py:10
  55.4 1.1 multiply_convert_fusion
  60.5 1.6 collective-permute-start.4
  62.1 0.9 collective-permute-start.7
  63.3 4.4 %collective-permute-start.8 = (f32[2,2,256,256]{3,2,1,0:T(8,128)S(1)}, f32[2,2,256,256]{3,2,1,0:T(8,128)S(1)}, u32[]{:S(2)}, u32[]{:S(2)}) collective-permute-start(f32[2,2,256,256]{3,2,1,0:T(8,128)S(1)} %add.233), channel_id=1, source_target_pairs={{4,0},{12,8},{5,1},{13,9},{20,16},{28,24},{21,17},{29,25}} | collective-permute-start | bytes 3145736 | tf_op jit(solution)/shard_map/ppermute | solution.py:50
  69.7 5.5 %collective-permute-done.4 = bf16[2,2,256,256]{3,2,1,0:T(8,128)(2,1)S(1)} collective-permute-done((bf16[2,2,256,256]{3,2,1,0:T(8,128)(2,1)S(1)}, bf16[2,2,256,256]{3,2,1,0:T(8,128)(2,1)S(1)}, u32[]{:S(2)}, u32[]{:S(2)}) %collective-permute-start.4) | collective-permute-done | bytes 524320 | tf_op jit(solution)/shard_map/ppermute | solution.py:17
  78.1 1.7 collective-permute-start.10
  83.9 1.0 collective-permute-start.13
  84.9 1.5 fusion.5
  86.9 3.3 %collective-permute-done.8 = f32[2,2,256,256]{3,2,1,0:T(8,128)S(1)} collective-permute-done((f32[2,2,256,256]{3,2,1,0:T(8,128)S(1)}, f32[2,2,256,256]{3,2,1,0:T(8,128)S(1)}, u32[]{:S(2)}, u32[]{:S(2)}) %collective-permute-start.8) | collective-permute-done | bytes 1048608 | tf_op jit(solution)/shard_map/ppermute | solution.py:50
  91.0 8.3 %collective-permute-done.11 = f32[416,256]{1,0:T(8,128)S(1)} collective-permute-done((f32[416,256]{1,0:T(8,128)S(1)}, f32[416,256]{1,0:T(8,128)S(1)}, u32[]{:S(2)}, u32[]{:S(2)}) %collective-permute-start.11) | collective-permute-done | bytes 426016 | tf_op jit(solution)/shard_map/ppermute | solution.py:90
  99.3 21.5 %collective-permute-done.12 = f32[416,256]{1,0:T(8,128)S(1)} collective-permute-done((f32[416,256]{1,0:T(8,128)S(1)}, f32[416,256]{1,0:T(8,128)S(1)}, u32[]{:S(2)}, u32[]{:S(2)}) %collective-permute-start.12) | collective-permute-done | bytes 426016 | tf_op jit(solution)/shard_map/ppermute | solution.py:90
  121.0 21.8 %collective-permute-start.14 = (f32[208,256]{1,0:T(8,128)S(1)}, f32[208,256]{1,0:T(8,128)S(1)}, u32[]{:S(2)}, u32[]{:S(2)}) collective-permute-start(f32[208,256]{1,0:T(8,128)S(1)} %constant_dynamic-slice_fusion), channel_id=1, source_target_pairs={{0,2},{2,0},{4,6},{6,4},{8,10},{10,8},{12,14},{14,12},{1,3},{3,1},... | collective-permute-start | bytes 638984 | tf_op jit(solution)/shard_map/ppermute | solution.py:64
  143.1 4.1 %collective-permute-done.14 = f32[208,256]{1,0:T(8,128)S(1)} collective-permute-done((f32[208,256]{1,0:T(8,128)S(1)}, f32[208,256]{1,0:T(8,128)S(1)}, u32[]{:S(2)}, u32[]{:S(2)}) %collective-permute-start.14) | collective-permute-done | bytes 213024 | tf_op jit(solution)/shard_map/ppermute | solution.py:64
  147.2 1.2 collective-permute-start.15
  148.5 3.0 %multiply_convert_fusion.1 = bf16[2,2,2,256,256]{4,3,2,1,0:T(8,128)(2,1)} fusion(f32[2,2,2,256,256]{4,3,2,1,0:T(8,128)S(1)} %fusion.106, f32[2,2,2,256,256]{4,3,2,1,0:T(8,128)S(1)} %fusion.5, bf16[2,2,2,256,256]{4,3,2,1,0:T(8,128)(2,1)S(1)} %broadcast_multiply_fusion.1, f32[2,2]{1,0:T(2,128)S(1)} %get-tuple-element.7, f32[2,2,256,256]{3,2,1,0:T(8,128)S(1)} %fusion.70, ...), kind=kOutput, calls=%fused_computation.24 | convolution fusion | flops 272105472 | bytes 8520704 | tf_op jit(solution)/shard_map/dot_general | solution.py:185
  152.3 3.6 %collective-permute-start.17 = (bf16[416,256]{1,0:T(8,128)(2,1)S(1)}, bf16[416,256]{1,0:T(8,128)(2,1)S(1)}, u32[]{:S(2)}, u32[]{:S(2)}) collective-permute-start(bf16[416,256]{1,0:T(8,128)(2,1)S(1)} %maximum_select_fusion.1), channel_id=1, source_target_pairs={{0,8},{2,10},{4,12},{6,14},{8,0},{10,2},{12,4},{14,6},{1,9},{3,11}... | collective-permute-start | bytes 638984 | tf_op jit(solution)/shard_map/ppermute | solution.py:103
  155.9 1.4 collective-permute-start.18
  157.5 15.3 %collective-permute-done.17 = bf16[416,256]{1,0:T(8,128)(2,1)S(1)} collective-permute-done((bf16[416,256]{1,0:T(8,128)(2,1)S(1)}, bf16[416,256]{1,0:T(8,128)(2,1)S(1)}, u32[]{:S(2)}, u32[]{:S(2)}) %collective-permute-start.17) | collective-permute-done | bytes 213024 | tf_op jit(solution)/shard_map/ppermute | solution.py:103
  172.8 2.3 %collective-permute-start.19 = (bf16[1664,256]{1,0:T(8,128)(2,1)S(1)}, bf16[1664,256]{1,0:T(8,128)(2,1)S(1)}, u32[]{:S(2)}, u32[]{:S(2)}) collective-permute-start(bf16[1664,256]{1,0:T(8,128)(2,1)S(1)} %bitcast.256), channel_id=1, source_target_pairs={{0,1},{1,0},{2,3},{3,2},{4,5},{5,4},{6,7},{7,6},{8,9},{9,8},{10,11... | collective-permute-start | bytes 2555912 | tf_op jit(solution)/shard_map/ppermute | solution.py:149
  175.1 2.2 %fusion.4 = bf16[2,2,2,256,256]{4,3,2,1,0:T(8,128)(2,1)} fusion(bf16[2,2,2,256,256]{4,3,2,1,0:T(8,128)(2,1)S(1)} %get-tuple-element.6, f32[2,2,2,256,256]{4,3,2,1,0:T(8,128)S(1)} %fusion.17, f32[2,2,2,256,256]{4,3,2,1,0:T(8,128)S(1)} %fusion.35, f32[2,2,2,256,256]{4,3,2,1,0:T(8,128)S(1)} %fusion.37, f32[2,2,2,256,256]{4,3,2,1,0:T(8,128)S(1)} %fusion.85, ...), kind=kOutput, calls=%fused_computation.13 | convolution fusion | flops 275775488 | bytes 21104128 | tf_op jit(solution)/shard_map/dot_general | solution.py:178
  179.0 1.1 pad_maximum_fusion.3
  (94 shorter events, 26.0 us)
Async XLA Ops:
  0.6 142.2 %copy-start = (bf16[256,256]{1,0:T(8,128)(2,1)S(1)}, bf16[256,256]{1,0:T(8,128)(2,1)}, u32[]{:S(2)}) copy-start(bf16[256,256]{1,0:T(8,128)(2,1)} %param.11) | copy-start | bytes 393220
  0.6 3.7 %copy-start.4 = (bf16[2,2,2,256,256]{4,3,2,1,0:T(8,128)(2,1)S(1)}, bf16[2,2,2,256,256]{4,3,2,1,0:T(8,128)(2,1)}, u32[]{:S(2)}) copy-start(bf16[2,2,2,256,256]{4,3,2,1,0:T(8,128)(2,1)} %param.7) | copy-start | bytes 3145732
  3.7 9.2 %collective-permute-start = (bf16[2,2,1,256,256]{4,3,2,1,0:T(8,128)(2,1)}, bf16[2,2,1,256,256]{4,3,2,1,0:T(8,128)(2,1)}, u32[]{:S(2)}, u32[]{:S(2)}) collective-permute-start(bf16[2,2,1,256,256]{4,3,2,1,0:T(8,128)(2,1)} %slice_select_fusion.1), channel_id=1, source_target_pairs={{0,1},{1,0},{2,3},{3,2},{4,5},{5,4},{6,7},{7,6},{8,9},{9,8},{10,11... | collective-permute-start | bytes 1572872 | tf_op jit(solution)/shard_map/ppermute | solution.py:221
  5.8 49.1 %collective-permute-start.6 = (bf16[2,2,2,256,256]{4,3,2,1,0:T(8,128)(2,1)S(1)}, bf16[2,2,2,256,256]{4,3,2,1,0:T(8,128)(2,1)S(1)}, u32[]{:S(2)}, u32[]{:S(2)}) collective-permute-start(bf16[2,2,2,256,256]{4,3,2,1,0:T(8,128)(2,1)S(1)} %get-tuple-element.6), channel_id=1, source_target_pairs={{2,0},{4,2},{6,4},{8,6},{10,8},{12,10},{14,12},{3,1},{5,3},{7,5},{... | collective-permute-start | bytes 3145736 | tf_op jit(solution)/shard_map/ppermute | solution.py:10
  9.6 8.8 %collective-permute-start.2 = (bf16[2,2,256,256]{3,2,1,0:T(8,128)(2,1)}, bf16[2,2,256,256]{3,2,1,0:T(8,128)(2,1)}, u32[]{:S(2)}, u32[]{:S(2)}) collective-permute-start(bf16[2,2,256,256]{3,2,1,0:T(8,128)(2,1)} %slice_bitcast_fusion), channel_id=1, source_target_pairs={{0,2},{1,3},{16,18},{17,19}} | collective-permute-start | bytes 1572872 | tf_op jit(solution)/shard_map/ppermute | solution.py:17
  11.1 1.4 copy-start.3
  14.1 1.3 copy-start.2
  18.5 41.9 %collective-permute-start.3 = (bf16[2,2,256,256]{3,2,1,0:T(8,128)(2,1)S(1)}, bf16[2,2,256,256]{3,2,1,0:T(8,128)(2,1)S(1)}, u32[]{:S(2)}, u32[]{:S(2)}) collective-permute-start(bf16[2,2,256,256]{3,2,1,0:T(8,128)(2,1)S(1)} %broadcast_select_fusion.2), channel_id=1, source_target_pairs={{0,8},{1,9},{16,24},{17,25}} | collective-permute-start | bytes 1572872 | tf_op jit(solution)/shard_map/ppermute | solution.py:17
  20.7 64.2 %collective-permute-start.1 = (bf16[2,2,2,256,256]{4,3,2,1,0:T(8,128)(2,1)S(1)}, bf16[2,2,2,256,256]{4,3,2,1,0:T(8,128)(2,1)}, u32[]{:S(2)}, u32[]{:S(2)}) collective-permute-start(bf16[2,2,2,256,256]{4,3,2,1,0:T(8,128)(2,1)S(1)} %get-tuple-element.18), channel_id=1, source_target_pairs={{0,2},{2,4},{4,6},{6,8},{8,10},{10,12},{12,14},{1,3},{3,5},{5,7},{... | collective-permute-start | bytes 3145736 | tf_op jit(solution)/shard_map/ppermute | solution.py:10
  60.4 2.7 %copy-start.1 = (f32[2,2,256,256]{3,2,1,0:T(8,128)S(1)}, f32[2,2,256,256]{3,2,1,0:T(8,128)}, u32[]{:S(2)}) copy-start(f32[2,2,256,256]{3,2,1,0:T(8,128)} %get-tuple-element.5) | copy-start | bytes 3145732
  60.5 14.7 %collective-permute-start.4 = (bf16[2,2,256,256]{3,2,1,0:T(8,128)(2,1)S(1)}, bf16[2,2,256,256]{3,2,1,0:T(8,128)(2,1)S(1)}, u32[]{:S(2)}, u32[]{:S(2)}) collective-permute-start(bf16[2,2,256,256]{3,2,1,0:T(8,128)(2,1)S(1)} %broadcast_select_fusion.3), channel_id=1, source_target_pairs={{0,4},{8,12},{2,10},{1,5},{9,13},{3,11},{16,20},{24,28},{18,26},{1... | collective-permute-start | bytes 1572872 | tf_op jit(solution)/shard_map/ppermute | solution.py:17
  62.1 13.8 %collective-permute-start.7 = (bf16[2,2,1,256,256]{4,3,2,1,0:T(8,128)(2,1)S(1)}, bf16[2,2,1,256,256]{4,3,2,1,0:T(8,128)(2,1)S(1)}, u32[]{:S(2)}, u32[]{:S(2)}) collective-permute-start(bf16[2,2,1,256,256]{4,3,2,1,0:T(8,128)(2,1)S(1)} %slice_select_fusion), channel_id=1, source_target_pairs={{0,1},{1,0},{2,3},{3,2},{4,5},{5,4},{6,7},{7,6},{8,9},{9,8},{10,11... | collective-permute-start | bytes 1572872 | tf_op jit(solution)/shard_map/ppermute | solution.py:221
  63.3 26.9 %collective-permute-start.8 = (f32[2,2,256,256]{3,2,1,0:T(8,128)S(1)}, f32[2,2,256,256]{3,2,1,0:T(8,128)S(1)}, u32[]{:S(2)}, u32[]{:S(2)}) collective-permute-start(f32[2,2,256,256]{3,2,1,0:T(8,128)S(1)} %add.233), channel_id=1, source_target_pairs={{4,0},{12,8},{5,1},{13,9},{20,16},{28,24},{21,17},{29,25}} | collective-permute-start | bytes 3145736 | tf_op jit(solution)/shard_map/ppermute | solution.py:50
  75.3 1.6 collective-permute-start.5
  78.1 5.0 %collective-permute-start.10 = (f32[1664,256]{1,0:T(8,128)S(1)}, f32[1664,256]{1,0:T(8,128)S(1)}, u32[]{:S(2)}, u32[]{:S(2)}) collective-permute-start(f32[1664,256]{1,0:T(8,128)S(1)} %constant_dynamic-slice_fusion.4), channel_id=1, source_target_pairs={{0,1},{1,0},{2,3},{3,2},{4,5},{5,4},{6,7},{7,6},{8,9},{9,8},{10,11... | collective-permute-start | bytes 5111816 | tf_op jit(solution)/shard_map/ppermute | solution.py:64
  83.4 15.9 %collective-permute-start.11 = (f32[416,256]{1,0:T(8,128)S(1)}, f32[416,256]{1,0:T(8,128)S(1)}, u32[]{:S(2)}, u32[]{:S(2)}) collective-permute-start(f32[416,256]{1,0:T(8,128)S(1)} %get-tuple-element.11), channel_id=1, source_target_pairs={{0,4},{2,6},{4,8},{6,10},{8,12},{10,14},{12,0},{14,2},{1,5},{3,7},... | collective-permute-start | bytes 1277960 | tf_op jit(solution)/shard_map/ppermute | solution.py:90
  83.5 37.4 %collective-permute-start.12 = (f32[416,256]{1,0:T(8,128)S(1)}, f32[416,256]{1,0:T(8,128)S(1)}, u32[]{:S(2)}, u32[]{:S(2)}) collective-permute-start(f32[416,256]{1,0:T(8,128)S(1)} %get-tuple-element.13), channel_id=1, source_target_pairs={{0,8},{2,10},{4,12},{6,14},{8,0},{10,2},{12,4},{14,6},{1,9},{3,11}... | collective-permute-start | bytes 1277960 | tf_op jit(solution)/shard_map/ppermute | solution.py:90
  83.9 37.0 %collective-permute-start.13 = (f32[416,256]{1,0:T(8,128)S(1)}, f32[416,256]{1,0:T(8,128)S(1)}, u32[]{:S(2)}, u32[]{:S(2)}) collective-permute-start(f32[416,256]{1,0:T(8,128)S(1)} %get-tuple-element.12), channel_id=1, source_target_pairs={{0,12},{2,14},{4,0},{6,2},{8,4},{10,6},{12,8},{14,10},{1,13},{3,15... | collective-permute-start | bytes 1277960 | tf_op jit(solution)/shard_map/ppermute | solution.py:90
  90.3 61.3 %collective-permute-start.9 = (f32[2,2,256,256]{3,2,1,0:T(8,128)S(1)}, f32[2,2,256,256]{3,2,1,0:T(8,128)S(1)}, u32[]{:S(2)}, u32[]{:S(2)}) collective-permute-start(f32[2,2,256,256]{3,2,1,0:T(8,128)S(1)} %add.234), channel_id=1, source_target_pairs={{8,0},{9,1},{24,16},{25,17}} | collective-permute-start | bytes 3145736 | tf_op jit(solution)/shard_map/ppermute | solution.py:50
  121.0 26.2 %collective-permute-start.14 = (f32[208,256]{1,0:T(8,128)S(1)}, f32[208,256]{1,0:T(8,128)S(1)}, u32[]{:S(2)}, u32[]{:S(2)}) collective-permute-start(f32[208,256]{1,0:T(8,128)S(1)} %constant_dynamic-slice_fusion), channel_id=1, source_target_pairs={{0,2},{2,0},{4,6},{6,4},{8,10},{10,8},{12,14},{14,12},{1,3},{3,1},... | collective-permute-start | bytes 638984 | tf_op jit(solution)/shard_map/ppermute | solution.py:64
  147.2 4.3 %collective-permute-start.15 = (bf16[208,256]{1,0:T(8,128)(2,1)S(1)}, bf16[208,256]{1,0:T(8,128)(2,1)S(1)}, u32[]{:S(2)}, u32[]{:S(2)}) collective-permute-start(bf16[208,256]{1,0:T(8,128)(2,1)S(1)} %multiply_convert_fusion.3), channel_id=1, source_target_pairs={{0,2},{2,0},{4,6},{6,4},{8,10},{10,8},{12,14},{14,12},{1,3},{3,1},... | collective-permute-start | bytes 319496 | tf_op jit(solution)/shard_map/ppermute | solution.py:72
  151.6 5.9 %collective-permute-start.16 = (bf16[416,256]{1,0:T(8,128)(2,1)S(1)}, bf16[416,256]{1,0:T(8,128)(2,1)S(1)}, u32[]{:S(2)}, u32[]{:S(2)}) collective-permute-start(bf16[416,256]{1,0:T(8,128)(2,1)S(1)} %maximum_select_fusion.1), channel_id=1, source_target_pairs={{0,4},{2,6},{4,8},{6,10},{8,12},{10,14},{12,0},{14,2},{1,5},{3,7},... | collective-permute-start | bytes 638984 | tf_op jit(solution)/shard_map/ppermute | solution.py:103
  152.3 20.4 %collective-permute-start.17 = (bf16[416,256]{1,0:T(8,128)(2,1)S(1)}, bf16[416,256]{1,0:T(8,128)(2,1)S(1)}, u32[]{:S(2)}, u32[]{:S(2)}) collective-permute-start(bf16[416,256]{1,0:T(8,128)(2,1)S(1)} %maximum_select_fusion.1), channel_id=1, source_target_pairs={{0,8},{2,10},{4,12},{6,14},{8,0},{10,2},{12,4},{14,6},{1,9},{3,11}... | collective-permute-start | bytes 638984 | tf_op jit(solution)/shard_map/ppermute | solution.py:103
  155.9 16.9 %collective-permute-start.18 = (bf16[416,256]{1,0:T(8,128)(2,1)S(1)}, bf16[416,256]{1,0:T(8,128)(2,1)S(1)}, u32[]{:S(2)}, u32[]{:S(2)}) collective-permute-start(bf16[416,256]{1,0:T(8,128)(2,1)S(1)} %maximum_select_fusion.1), channel_id=1, source_target_pairs={{0,12},{2,14},{4,0},{6,2},{8,4},{10,6},{12,8},{14,10},{1,13},{3,15... | collective-permute-start | bytes 638984 | tf_op jit(solution)/shard_map/ppermute | solution.py:103
  172.8 4.6 %collective-permute-start.19 = (bf16[1664,256]{1,0:T(8,128)(2,1)S(1)}, bf16[1664,256]{1,0:T(8,128)(2,1)S(1)}, u32[]{:S(2)}, u32[]{:S(2)}) collective-permute-start(bf16[1664,256]{1,0:T(8,128)(2,1)S(1)} %bitcast.256), channel_id=1, source_target_pairs={{0,1},{1,0},{2,3},{3,2},{4,5},{5,4},{6,7},{7,6},{8,9},{9,8},{10,11... | collective-permute-start | bytes 2555912 | tf_op jit(solution)/shard_map/ppermute | solution.py:149

commit v16 on v13

--- a/solution.py
+++ b/solution.py
@@ -90,11 +90,11 @@
     return n >= 1 and (n & (n - 1)) == 0
 
 
-def all_sum_rounded(flat, scale):
+def all_sum_rounded(flat, scale, held=None):
     n_tm = lax.axis_size("tm")
     n_sp = lax.axis_size("space")
     if not (is_pow2(n_tm) and is_pow2(n_sp)):
-        return (lax.psum(flat, ("tm", "space")) * scale).astype(jnp.bfloat16), [], flat.shape[0]
+        return (lax.psum(flat, ("tm", "space")) * scale).astype(jnp.bfloat16), [], flat.shape[0], held
     high = min(4, n_sp)
     low = n_sp // high
     tm_steps = []
@@ -114,15 +114,16 @@
         flat = jnp.pad(flat, ((0, padded_rows - rows), (0, 0)))
     flat = xor_halving(flat, "tm", tm_steps)
     flat = direct_scatter(flat, "space", low, high)
+    flat, held = lax.optimization_barrier((flat, held))
     flat = xor_halving(flat, "space", sp_steps)
     piece = (flat * scale).astype(jnp.bfloat16)
     piece = xor_doubling(piece, "space", sp_steps)
     piece = direct_gather(piece, "space", low, high)
-    return piece, tm_steps, rows
+    return piece, tm_steps, rows, held
 
 
 def split_rows(gathered, cuts):
-    piece, tm_steps, rows = gathered
+    piece, tm_steps, rows, _ = gathered
     if len(tm_steps) != 1:
         whole = xor_doubling(piece, "tm", tm_steps)
         return [whole[a:b] for a, b in cuts]
@@ -222,9 +223,10 @@
     later = shifted(cot, "space", -1)
     if lax.axis_size("space") % 2 == 0:
         cot_pair = cot_local + jnp.sum(later, axis=1, dtype=jnp.float32)
-        cot_sum = tree_reduce(cot_pair, "space", 2)
+        cot_step = 2
     else:
-        cot_sum = tree_reduce(cot_local, "space")
+        cot_pair = cot_local
+        cot_step = 1
     rows_pad = row_halo(masked)
     padded = jnp.pad(rows_pad, ((0, 0), (0, 0), (0, 0), (1, 1), (0, 0)))
     pre = spatial_sum(padded, spatial_weight, False)
@@ -239,14 +241,9 @@
     output = ((masked.astype(jnp.float32) + mixed + cond[:, None]) * mask_f).astype(jnp.bfloat16)
     sig = jax.nn.sigmoid(pre)
     dpre = (dact * sig * (1.0 + pre * (1.0 - sig))).astype(jnp.bfloat16)
-    cond_back = jnp.dot(cot_sum, cond_weight.astype(jnp.float32).T, precision=lax.Precision.HIGHEST)
     dpre_rows = row_halo(dpre)
     dpre_pad = jnp.pad(dpre_rows, ((0, 0), (0, 0), (0, 0), (1, 1), (0, 0)))
     dmasked = spatial_sum(dpre_pad, spatial_weight, True)
-    is_first = (frame_ids == 0).astype(jnp.float32)[None, :, None, None, None]
-    grad_latents = (
-        (cot.astype(jnp.float32) + dmasked + is_first * cond_back[:, None]) * mask_f
-    ).astype(jnp.bfloat16)
     dims = (((0, 1, 2, 3), (0, 1, 2, 3)), ((), ()))
     spatial_terms = []
     for row_off in range(3):
@@ -273,7 +270,13 @@
         axis=0,
     )
     scale = (clips * frames * rows * cols * lax.axis_size("space") * lax.axis_size("tm")) ** (-0.5)
-    summed = all_sum_rounded(flat, scale)
+    summed = all_sum_rounded(flat, scale, cot_pair)
+    cot_sum = tree_reduce(summed[3], "space", cot_step)
+    cond_back = jnp.dot(cot_sum, cond_weight.astype(jnp.float32).T, precision=lax.Precision.HIGHEST)
+    is_first = (frame_ids == 0).astype(jnp.float32)[None, :, None, None, None]
+    grad_latents = (
+        (cot.astype(jnp.float32) + dmasked + is_first * cond_back[:, None]) * mask_f
+    ).astype(jnp.bfloat16)
     n_s = taps_s * chans
     n_t = taps_t * chans
     grad_spatial, grad_temporal, grad_cond = split_rows(

time: 172 us -> 204 us (1.19)
  waiting for transfers between devices: 93.8 us -> 125 us
    ppermute x3, waiting for transfers between devices: 10.2 us -> 35.1 us  [direct_scatter(): total = total + lax.ppermute(send, axis, pairs)]
    ppermute x3, waiting for transfers between devices: 10.9 us -> 31 us  [direct_gather(): got = lax.ppermute(piece, axis, pairs)]
    ppermute x2, waiting for transfers between devices: 37.7 us -> 23.6 us  [tree_reduce(): value = value + lax.ppermute(value, axis, pairs)]
    ppermute x3, waiting for transfers between devices: 23.1 us -> 26 us  [tree_broadcast(): got = lax.ppermute(value, axis, pairs)]
    ppermute x2, starting transfers between devices: 0.15 us -> 2.63 us  [xor_halving(): flat = keep + lax.ppermute(send, axis, pairs)]
  transfers between devices with their start and end apart: 19 -> 19, of which waited for: 12 -> 14; matrix products, arithmetic and copies ran while one was open for 18% -> 15% of each run, Pallas kernels for 0% -> 0%
where the time goes in v16:
time: 204 us
  waiting for transfers between devices  125 us (61%)
  starting transfers between devices  40.5 us (20%)
  matrix products  24.2 us (12%)
  other arithmetic  10 us (5%)
  local copies, waits for them, and re-layouts  3.09 us (2%)
    ppermute x3, waiting for transfers between devices, direct_scatter(): total = total + lax.ppermute(send, axis, pairs)  35.1 us
    ppermute x3, waiting for transfers between devices, direct_gather(): got = lax.ppermute(piece, axis, pairs)  31 us
    ppermute x3, waiting for transfers between devices, tree_broadcast(): got = lax.ppermute(value, axis, pairs)  26 us
    ppermute x2, waiting for transfers between devices, tree_reduce(): value = value + lax.ppermute(value, axis, pairs)  23.6 us
    ppermute x3, starting transfers between devices, tree_broadcast(): got = lax.ppermute(value, axis, pairs)  13.9 us
    dot_general x18, matrix products, spatial_sum(): total = total + jnp.dot(piece, kernel, preferred_element_type=jnp.float32)  11.9 us
    ppermute x3, starting transfers between devices, direct_scatter(): total = total + lax.ppermute(send, axis, pairs)  10.9 us
    ppermute x3, starting transfers between devices, direct_gather(): got = lax.ppermute(piece, axis, pairs)  5.2 us
  transfers between devices with their start and end apart: 19, of which 14 were waited for; matrix products, arithmetic and copies ran while one was open for 15% of the time, Pallas kernels for 0%

profile of v16, /device:TPU:0, one launch (start us, length us, event | category | flops | bytes accessed | tf_op | source)
XLA Modules:
  0.0 204.0 jit_solution(1319932518781596364)
XLA Ops:
  1.5 1.4 broadcast_multiply_fusion.1
  4.2 1.4 convert_reduce_fusion
  5.6 1.3 collective-permute-start.5
  7.7 8.3 %collective-permute-start.2 = (bf16[2,2,256,256]{3,2,1,0:T(8,128)(2,1)}, bf16[2,2,256,256]{3,2,1,0:T(8,128)(2,1)}, u32[]{:S(2)}, u32[]{:S(2)}) collective-permute-start(bf16[2,2,256,256]{3,2,1,0:T(8,128)(2,1)} %slice_bitcast_fusion), channel_id=1, source_target_pairs={{0,8},{1,9},{16,24},{17,25}} | collective-permute-start | bytes 1572872 | tf_op jit(solution)/shard_map/ppermute | solution.py:21
  16.0 1.4 fusion.87
  17.8 1.1 broadcast_select_fusion.8
  23.3 3.7 %collective-permute-done.2 = bf16[2,2,256,256]{3,2,1,0:T(8,128)(2,1)} collective-permute-done((bf16[2,2,256,256]{3,2,1,0:T(8,128)(2,1)}, bf16[2,2,256,256]{3,2,1,0:T(8,128)(2,1)}, u32[]{:S(2)}, u32[]{:S(2)}) %collective-permute-start.2) | collective-permute-done | bytes 524320 | tf_op jit(solution)/shard_map/ppermute | solution.py:21
  27.1 1.3 collective-permute-start.3
  28.4 1.3 multiply_convert_fusion.2
  29.7 1.4 collective-permute-start.1
  32.0 1.8 collective-permute-done.5
  34.2 1.1 multiply_convert_fusion
  39.5 4.3 %collective-permute-start.4 = (bf16[2,2,256,256]{3,2,1,0:T(8,128)(2,1)S(1)}, bf16[2,2,256,256]{3,2,1,0:T(8,128)(2,1)S(1)}, u32[]{:S(2)}, u32[]{:S(2)}) collective-permute-start(bf16[2,2,256,256]{3,2,1,0:T(8,128)(2,1)S(1)} %broadcast_select_fusion.3), channel_id=1, source_target_pairs={{0,2},{4,6},{8,10},{12,14},{1,3},{5,7},{9,11},{13,15},{16,18},{20,... | collective-permute-start | bytes 1572872 | tf_op jit(solution)/shard_map/ppermute | solution.py:21
  45.9 21.7 %collective-permute-done.4 = bf16[2,2,256,256]{3,2,1,0:T(8,128)(2,1)S(1)} collective-permute-done((bf16[2,2,256,256]{3,2,1,0:T(8,128)(2,1)S(1)}, bf16[2,2,256,256]{3,2,1,0:T(8,128)(2,1)S(1)}, u32[]{:S(2)}, u32[]{:S(2)}) %collective-permute-start.4) | collective-permute-done | bytes 524320 | tf_op jit(solution)/shard_map/ppermute | solution.py:21
  72.8 10.3 %collective-permute-start.10 = (f32[416,256]{1,0:T(8,128)S(1)}, f32[416,256]{1,0:T(8,128)S(1)}, u32[]{:S(2)}, u32[]{:S(2)}) collective-permute-start(f32[416,256]{1,0:T(8,128)S(1)} %get-tuple-element.16), channel_id=1, source_target_pairs={{0,12},{2,14},{4,0},{6,2},{8,4},{10,6},{12,8},{14,10},{1,13},{3,15... | collective-permute-start | bytes 1277960 | tf_op jit(solution)/shard_map/ppermute | solution.py:71
  84.7 8.6 %collective-permute-done.10 = f32[416,256]{1,0:T(8,128)S(1)} collective-permute-done((f32[416,256]{1,0:T(8,128)S(1)}, f32[416,256]{1,0:T(8,128)S(1)}, u32[]{:S(2)}, u32[]{:S(2)}) %collective-permute-start.10) | collective-permute-done | bytes 426016 | tf_op jit(solution)/shard_map/ppermute | solution.py:71
  93.3 9.6 %collective-permute-done.8 = f32[416,256]{1,0:T(8,128)S(1)} collective-permute-done((f32[416,256]{1,0:T(8,128)S(1)}, f32[416,256]{1,0:T(8,128)S(1)}, u32[]{:S(2)}, u32[]{:S(2)}) %collective-permute-start.8) | collective-permute-done | bytes 426016 | tf_op jit(solution)/shard_map/ppermute | solution.py:71
  102.9 16.8 %collective-permute-done.9 = f32[416,256]{1,0:T(8,128)S(1)} collective-permute-done((f32[416,256]{1,0:T(8,128)S(1)}, f32[416,256]{1,0:T(8,128)S(1)}, u32[]{:S(2)}, u32[]{:S(2)}) %collective-permute-start.9) | collective-permute-done | bytes 426016 | tf_op jit(solution)/shard_map/ppermute | solution.py:71
  119.9 2.5 %collective-permute-start.13 = (f32[208,256]{1,0:T(8,128)S(1)}, f32[208,256]{1,0:T(8,128)S(1)}, u32[]{:S(2)}, u32[]{:S(2)}) collective-permute-start(f32[208,256]{1,0:T(8,128)S(1)} %constant_dynamic-slice_fusion), channel_id=1, source_target_pairs={{0,2},{2,0},{4,6},{6,4},{8,10},{10,8},{12,14},{14,12},{1,3},{3,1},... | collective-permute-start | bytes 638984 | tf_op jit(solution)/shard_map/ppermute | solution.py:45
  122.9 4.2 %collective-permute-done.13 = f32[208,256]{1,0:T(8,128)S(1)} collective-permute-done((f32[208,256]{1,0:T(8,128)S(1)}, f32[208,256]{1,0:T(8,128)S(1)}, u32[]{:S(2)}, u32[]{:S(2)}) %collective-permute-start.13) | collective-permute-done | bytes 213024 | tf_op jit(solution)/shard_map/ppermute | solution.py:45
  127.2 1.8 collective-permute-start.14
  129.5 2.5 %collective-permute-done.14 = bf16[208,256]{1,0:T(8,128)(2,1)S(1)} collective-permute-done((bf16[208,256]{1,0:T(8,128)(2,1)S(1)}, bf16[208,256]{1,0:T(8,128)(2,1)S(1)}, u32[]{:S(2)}, u32[]{:S(2)}) %collective-permute-start.14) | collective-permute-done | bytes 106528 | tf_op jit(solution)/shard_map/ppermute | solution.py:53
  132.5 1.3 collective-permute-start.11
  133.8 2.9 %collective-permute-start.16 = (bf16[416,256]{1,0:T(8,128)(2,1)S(1)}, bf16[416,256]{1,0:T(8,128)(2,1)S(1)}, u32[]{:S(2)}, u32[]{:S(2)}) collective-permute-start(bf16[416,256]{1,0:T(8,128)(2,1)S(1)} %maximum_select_fusion.1), channel_id=1, source_target_pairs={{0,8},{2,10},{4,12},{6,14},{8,0},{10,2},{12,4},{14,6},{1,9},{3,11}... | collective-permute-start | bytes 638984 | tf_op jit(solution)/shard_map/ppermute | solution.py:84
  136.8 2.2 %collective-permute-start.17 = (bf16[416,256]{1,0:T(8,128)(2,1)S(1)}, bf16[416,256]{1,0:T(8,128)(2,1)S(1)}, u32[]{:S(2)}, u32[]{:S(2)}) collective-permute-start(bf16[416,256]{1,0:T(8,128)(2,1)S(1)} %maximum_select_fusion.1), channel_id=1, source_target_pairs={{0,12},{2,14},{4,0},{6,2},{8,4},{10,6},{12,8},{14,10},{1,13},{3,15... | collective-permute-start | bytes 638984 | tf_op jit(solution)/shard_map/ppermute | solution.py:84
  139.1 3.0 %collective-permute-done.15 = bf16[416,256]{1,0:T(8,128)(2,1)S(1)} collective-permute-done((bf16[416,256]{1,0:T(8,128)(2,1)S(1)}, bf16[416,256]{1,0:T(8,128)(2,1)S(1)}, u32[]{:S(2)}, u32[]{:S(2)}) %collective-permute-start.15) | collective-permute-done | bytes 213024 | tf_op jit(solution)/shard_map/ppermute | solution.py:84
  142.1 2.7 %collective-permute-done.16 = bf16[416,256]{1,0:T(8,128)(2,1)S(1)} collective-permute-done((bf16[416,256]{1,0:T(8,128)(2,1)S(1)}, bf16[416,256]{1,0:T(8,128)(2,1)S(1)}, u32[]{:S(2)}, u32[]{:S(2)}) %collective-permute-start.16) | collective-permute-done | bytes 213024 | tf_op jit(solution)/shard_map/ppermute | solution.py:84
  144.9 25.3 %collective-permute-done.17 = bf16[416,256]{1,0:T(8,128)(2,1)S(1)} collective-permute-done((bf16[416,256]{1,0:T(8,128)(2,1)S(1)}, bf16[416,256]{1,0:T(8,128)(2,1)S(1)}, u32[]{:S(2)}, u32[]{:S(2)}) %collective-permute-start.17) | collective-permute-done | bytes 213024 | tf_op jit(solution)/shard_map/ppermute | solution.py:84
  170.6 1.8 multiply_convert_fusion.1
  172.6 1.5 collective-permute-start.12
  177.3 23.6 %collective-permute-done.12 = f32[2,2,256,256]{3,2,1,0:T(8,128)S(1)} collective-permute-done((f32[2,2,256,256]{3,2,1,0:T(8,128)S(1)}, f32[2,2,256,256]{3,2,1,0:T(8,128)S(1)}, u32[]{:S(2)}, u32[]{:S(2)}) %collective-permute-start.12) | collective-permute-done | bytes 1048608 | tf_op jit(solution)/shard_map/ppermute | solution.py:31
  201.6 2.4 %fusion.4 = bf16[2,2,2,256,256]{4,3,2,1,0:T(8,128)(2,1)} fusion(bf16[2,2,2,256,256]{4,3,2,1,0:T(8,128)(2,1)S(1)} %get-tuple-element.10, f32[2,2,2,256,256]{4,3,2,1,0:T(8,128)S(1)} %fusion.17, f32[2,2,2,256,256]{4,3,2,1,0:T(8,128)S(1)} %fusion.35, f32[2,2,2,256,256]{4,3,2,1,0:T(8,128)S(1)} %fusion.37, f32[2,2,2,256,256]{4,3,2,1,0:T(8,128)S(1)} %fusion.85, ...), kind=kOutput, calls=%fused_computation.13 | convolution fusion | flops 275775488 | bytes 21104128 | tf_op jit(solution)/shard_map/dot_general | solution.py:160
  (91 shorter events, 28.3 us)
Async XLA Ops:
  0.6 169.7 %copy-start = (bf16[256,256]{1,0:T(8,128)(2,1)S(1)}, bf16[256,256]{1,0:T(8,128)(2,1)}, u32[]{:S(2)}) copy-start(bf16[256,256]{1,0:T(8,128)(2,1)} %param.11) | copy-start | bytes 393220
  0.6 3.5 %copy-start.4 = (bf16[2,2,2,256,256]{4,3,2,1,0:T(8,128)(2,1)S(1)}, bf16[2,2,2,256,256]{4,3,2,1,0:T(8,128)(2,1)}, u32[]{:S(2)}) copy-start(bf16[2,2,2,256,256]{4,3,2,1,0:T(8,128)(2,1)} %param.7) | copy-start | bytes 3145732
  3.7 14.1 %collective-permute-start = (bf16[2,2,1,256,256]{4,3,2,1,0:T(8,128)(2,1)}, bf16[2,2,1,256,256]{4,3,2,1,0:T(8,128)(2,1)}, u32[]{:S(2)}, u32[]{:S(2)}) collective-permute-start(bf16[2,2,1,256,256]{4,3,2,1,0:T(8,128)(2,1)} %slice_select_fusion.1), channel_id=1, source_target_pairs={{0,1},{1,0},{2,3},{3,2},{4,5},{5,4},{6,7},{7,6},{8,9},{9,8},{10,11... | collective-permute-start | bytes 1572872 | tf_op jit(solution)/shard_map/ppermute | solution.py:203
  5.6 28.2 %collective-permute-start.5 = (bf16[2,2,2,256,256]{4,3,2,1,0:T(8,128)(2,1)S(1)}, bf16[2,2,2,256,256]{4,3,2,1,0:T(8,128)(2,1)S(1)}, u32[]{:S(2)}, u32[]{:S(2)}) collective-permute-start(bf16[2,2,2,256,256]{4,3,2,1,0:T(8,128)(2,1)S(1)} %get-tuple-element.10), channel_id=1, source_target_pairs={{2,0},{4,2},{6,4},{8,6},{10,8},{12,10},{14,12},{3,1},{5,3},{7,5},{... | collective-permute-start | bytes 3145736 | tf_op jit(solution)/shard_map/ppermute | solution.py:10
  7.7 19.4 %collective-permute-start.2 = (bf16[2,2,256,256]{3,2,1,0:T(8,128)(2,1)}, bf16[2,2,256,256]{3,2,1,0:T(8,128)(2,1)}, u32[]{:S(2)}, u32[]{:S(2)}) collective-permute-start(bf16[2,2,256,256]{3,2,1,0:T(8,128)(2,1)} %slice_bitcast_fusion), channel_id=1, source_target_pairs={{0,8},{1,9},{16,24},{17,25}} | collective-permute-start | bytes 1572872 | tf_op jit(solution)/shard_map/ppermute | solution.py:21
  16.0 1.4 copy-start.3
  19.0 1.3 copy-start.2
  27.1 12.3 %collective-permute-start.3 = (bf16[2,2,256,256]{3,2,1,0:T(8,128)(2,1)S(1)}, bf16[2,2,256,256]{3,2,1,0:T(8,128)(2,1)S(1)}, u32[]{:S(2)}, u32[]{:S(2)}) collective-permute-start(bf16[2,2,256,256]{3,2,1,0:T(8,128)(2,1)S(1)} %broadcast_select_fusion.2), channel_id=1, source_target_pairs={{0,4},{8,12},{1,5},{9,13},{16,20},{24,28},{17,21},{25,29}} | collective-permute-start | bytes 1572872 | tf_op jit(solution)/shard_map/ppermute | solution.py:21
  29.7 102.4 %collective-permute-start.1 = (bf16[2,2,2,256,256]{4,3,2,1,0:T(8,128)(2,1)S(1)}, bf16[2,2,2,256,256]{4,3,2,1,0:T(8,128)(2,1)S(1)}, u32[]{:S(2)}, u32[]{:S(2)}) collective-permute-start(bf16[2,2,2,256,256]{4,3,2,1,0:T(8,128)(2,1)S(1)} %get-tuple-element.22), channel_id=1, source_target_pairs={{0,2},{2,4},{4,6},{6,8},{8,10},{10,12},{12,14},{1,3},{3,5},{5,7},{... | collective-permute-start | bytes 3145736 | tf_op jit(solution)/shard_map/ppermute | solution.py:10
  39.5 28.2 %collective-permute-start.4 = (bf16[2,2,256,256]{3,2,1,0:T(8,128)(2,1)S(1)}, bf16[2,2,256,256]{3,2,1,0:T(8,128)(2,1)S(1)}, u32[]{:S(2)}, u32[]{:S(2)}) collective-permute-start(bf16[2,2,256,256]{3,2,1,0:T(8,128)(2,1)S(1)} %broadcast_select_fusion.3), channel_id=1, source_target_pairs={{0,2},{4,6},{8,10},{12,14},{1,3},{5,7},{9,11},{13,15},{16,18},{20,... | collective-permute-start | bytes 1572872 | tf_op jit(solution)/shard_map/ppermute | solution.py:21
  43.8 25.9 %collective-permute-start.6 = (bf16[2,2,1,256,256]{4,3,2,1,0:T(8,128)(2,1)S(1)}, bf16[2,2,1,256,256]{4,3,2,1,0:T(8,128)(2,1)S(1)}, u32[]{:S(2)}, u32[]{:S(2)}) collective-permute-start(bf16[2,2,1,256,256]{4,3,2,1,0:T(8,128)(2,1)S(1)} %slice_select_fusion), channel_id=1, source_target_pairs={{0,1},{1,0},{2,3},{3,2},{4,5},{5,4},{6,7},{7,6},{8,9},{9,8},{10,11... | collective-permute-start | bytes 1572872 | tf_op jit(solution)/shard_map/ppermute | solution.py:203
  45.4 22.2 %copy-start.1 = (f32[2,2,256,256]{3,2,1,0:T(8,128)S(1)}, f32[2,2,256,256]{3,2,1,0:T(8,128)}, u32[]{:S(2)}) copy-start(f32[2,2,256,256]{3,2,1,0:T(8,128)} %get-tuple-element.9) | copy-start | bytes 3145732
  68.8 3.7 %collective-permute-start.7 = (f32[1664,256]{1,0:T(8,128)S(1)}, f32[1664,256]{1,0:T(8,128)S(1)}, u32[]{:S(2)}, u32[]{:S(2)}) collective-permute-start(f32[1664,256]{1,0:T(8,128)S(1)} %constant_dynamic-slice_fusion.4), channel_id=1, source_target_pairs={{0,1},{1,0},{2,3},{3,2},{4,5},{5,4},{6,7},{7,6},{8,9},{9,8},{10,11... | collective-permute-start | bytes 5111816 | tf_op jit(solution)/shard_map/ppermute | solution.py:45
  72.8 20.5 %collective-permute-start.10 = (f32[416,256]{1,0:T(8,128)S(1)}, f32[416,256]{1,0:T(8,128)S(1)}, u32[]{:S(2)}, u32[]{:S(2)}) collective-permute-start(f32[416,256]{1,0:T(8,128)S(1)} %get-tuple-element.16), channel_id=1, source_target_pairs={{0,12},{2,14},{4,0},{6,2},{8,4},{10,6},{12,8},{14,10},{1,13},{3,15... | collective-permute-start | bytes 1277960 | tf_op jit(solution)/shard_map/ppermute | solution.py:71
  83.1 19.8 %collective-permute-start.8 = (f32[416,256]{1,0:T(8,128)S(1)}, f32[416,256]{1,0:T(8,128)S(1)}, u32[]{:S(2)}, u32[]{:S(2)}) collective-permute-start(f32[416,256]{1,0:T(8,128)S(1)} %get-tuple-element.15), channel_id=1, source_target_pairs={{0,4},{2,6},{4,8},{6,10},{8,12},{10,14},{12,0},{14,2},{1,5},{3,7},... | collective-permute-start | bytes 1277960 | tf_op jit(solution)/shard_map/ppermute | solution.py:71
  83.1 36.6 %collective-permute-start.9 = (f32[416,256]{1,0:T(8,128)S(1)}, f32[416,256]{1,0:T(8,128)S(1)}, u32[]{:S(2)}, u32[]{:S(2)}) collective-permute-start(f32[416,256]{1,0:T(8,128)S(1)} %get-tuple-element.17), channel_id=1, source_target_pairs={{0,8},{2,10},{4,12},{6,14},{8,0},{10,2},{12,4},{14,6},{1,9},{3,11}... | collective-permute-start | bytes 1277960 | tf_op jit(solution)/shard_map/ppermute | solution.py:71
  119.9 7.3 %collective-permute-start.13 = (f32[208,256]{1,0:T(8,128)S(1)}, f32[208,256]{1,0:T(8,128)S(1)}, u32[]{:S(2)}, u32[]{:S(2)}) collective-permute-start(f32[208,256]{1,0:T(8,128)S(1)} %constant_dynamic-slice_fusion), channel_id=1, source_target_pairs={{0,2},{2,0},{4,6},{6,4},{8,10},{10,8},{12,14},{14,12},{1,3},{3,1},... | collective-permute-start | bytes 638984 | tf_op jit(solution)/shard_map/ppermute | solution.py:45
  127.2 4.8 %collective-permute-start.14 = (bf16[208,256]{1,0:T(8,128)(2,1)S(1)}, bf16[208,256]{1,0:T(8,128)(2,1)S(1)}, u32[]{:S(2)}, u32[]{:S(2)}) collective-permute-start(bf16[208,256]{1,0:T(8,128)(2,1)S(1)} %multiply_convert_fusion.3), channel_id=1, source_target_pairs={{0,2},{2,0},{4,6},{6,4},{8,10},{10,8},{12,14},{14,12},{1,3},{3,1},... | collective-permute-start | bytes 319496 | tf_op jit(solution)/shard_map/ppermute | solution.py:53
  132.0 10.0 %collective-permute-start.15 = (bf16[416,256]{1,0:T(8,128)(2,1)S(1)}, bf16[416,256]{1,0:T(8,128)(2,1)S(1)}, u32[]{:S(2)}, u32[]{:S(2)}) collective-permute-start(bf16[416,256]{1,0:T(8,128)(2,1)S(1)} %maximum_select_fusion.1), channel_id=1, source_target_pairs={{0,4},{2,6},{4,8},{6,10},{8,12},{10,14},{12,0},{14,2},{1,5},{3,7},... | collective-permute-start | bytes 638984 | tf_op jit(solution)/shard_map/ppermute | solution.py:84
  132.5 39.8 %collective-permute-start.11 = (f32[2,2,256,256]{3,2,1,0:T(8,128)S(1)}, f32[2,2,256,256]{3,2,1,0:T(8,128)S(1)}, u32[]{:S(2)}, u32[]{:S(2)}) collective-permute-start(f32[2,2,256,256]{3,2,1,0:T(8,128)S(1)} %add.260), channel_id=1, source_target_pairs={{4,0},{12,8},{5,1},{13,9},{20,16},{28,24},{21,17},{29,25}} | collective-permute-start | bytes 3145736 | tf_op jit(solution)/shard_map/ppermute | solution.py:31
  133.8 11.0 %collective-permute-start.16 = (bf16[416,256]{1,0:T(8,128)(2,1)S(1)}, bf16[416,256]{1,0:T(8,128)(2,1)S(1)}, u32[]{:S(2)}, u32[]{:S(2)}) collective-permute-start(bf16[416,256]{1,0:T(8,128)(2,1)S(1)} %maximum_select_fusion.1), channel_id=1, source_target_pairs={{0,8},{2,10},{4,12},{6,14},{8,0},{10,2},{12,4},{14,6},{1,9},{3,11}... | collective-permute-start | bytes 638984 | tf_op jit(solution)/shard_map/ppermute | solution.py:84
  136.8 33.4 %collective-permute-start.17 = (bf16[416,256]{1,0:T(8,128)(2,1)S(1)}, bf16[416,256]{1,0:T(8,128)(2,1)S(1)}, u32[]{:S(2)}, u32[]{:S(2)}) collective-permute-start(bf16[416,256]{1,0:T(8,128)(2,1)S(1)} %maximum_select_fusion.1), channel_id=1, source_target_pairs={{0,12},{2,14},{4,0},{6,2},{8,4},{10,6},{12,8},{14,10},{1,13},{3,15... | collective-permute-start | bytes 638984 | tf_op jit(solution)/shard_map/ppermute | solution.py:84
  170.2 4.3 %collective-permute-start.18 = (bf16[1664,256]{1,0:T(8,128)(2,1)S(1)}, bf16[1664,256]{1,0:T(8,128)(2,1)S(1)}, u32[]{:S(2)}, u32[]{:S(2)}) collective-permute-start(bf16[1664,256]{1,0:T(8,128)(2,1)S(1)} %bitcast.256), channel_id=1, source_target_pairs={{0,1},{1,0},{2,3},{3,2},{4,5},{5,4},{6,7},{7,6},{8,9},{9,8},{10,11... | collective-permute-start | bytes 2555912 | tf_op jit(solution)/shard_map/ppermute | solution.py:131
  172.6 28.4 %collective-permute-start.12 = (f32[2,2,256,256]{3,2,1,0:T(8,128)S(1)}, f32[2,2,256,256]{3,2,1,0:T(8,128)S(1)}, u32[]{:S(2)}, u32[]{:S(2)}) collective-permute-start(f32[2,2,256,256]{3,2,1,0:T(8,128)S(1)} %add.261), channel_id=1, source_target_pairs={{8,0},{9,1},{24,16},{25,17}} | collective-permute-start | bytes 3145736 | tf_op jit(solution)/shard_map/ppermute | solution.py:31

commit v17 on v13

--- a/solution.py
+++ b/solution.py
@@ -17,6 +17,20 @@
     while step * 2 < count:
         step *= 2
     while step >= 1 and count > 1:
+        pairs = [(i, i + step) for i in range(0, count, 2 * step) if i + step < count]
+        got = lax.ppermute(value, axis, pairs)
+        value = jnp.where(me % (2 * step) == step, got, value)
+        step //= 2
+    return value
+
+
+def tree_broadcast_from(value, axis, unit):
+    count = lax.axis_size(axis)
+    me = lax.axis_index(axis)
+    step = unit
+    while step * 2 < count:
+        step *= 2
+    while step >= unit:
         pairs = [(i, i + step) for i in range(0, count, 2 * step) if i + step < count]
         got = lax.ppermute(value, axis, pairs)
         value = jnp.where(me % (2 * step) == step, got, value)
@@ -217,7 +231,11 @@
     mask_f = mask.astype(jnp.float32)
     masked = latents * mask
     cot = cotangent * mask
-    first = tree_broadcast(masked[:, 0], "space")
+    pair_first = lax.axis_size("space") % 2 == 0
+    if pair_first:
+        first = tree_broadcast_from(masked[:, 0], "space", 2)
+    else:
+        first = tree_broadcast(masked[:, 0], "space")
     cot_local = jnp.sum(cot, axis=1, dtype=jnp.float32)
     later = shifted(cot, "space", -1)
     if lax.axis_size("space") % 2 == 0:
@@ -229,7 +247,12 @@
     padded = jnp.pad(rows_pad, ((0, 0), (0, 0), (0, 0), (1, 1), (0, 0)))
     pre = spatial_sum(padded, spatial_weight, False)
     act = jax.nn.silu(pre).astype(jnp.bfloat16)
-    earlier = shifted(act, "space", 1)
+    if pair_first:
+        sent = shifted(jnp.concatenate([act, first[:, None]], axis=1), "space", 1)
+        earlier = sent[:, :frames]
+        first = jnp.where(slab % 2 == 1, sent[:, frames], first)
+    else:
+        earlier = shifted(act, "space", 1)
     act_pad = jnp.concatenate([earlier, act], axis=1)
     mixed = lag_forward(act_pad, temporal_weight, frames)
     cot_pad = jnp.concatenate([cot, later], axis=1)

time: 172 us -> 177 us (1.029)
  waiting for transfers between devices: 93.8 us -> 88 us
  other arithmetic: 9.97 us -> 14.6 us
  matrix products: 24.4 us -> 28.5 us
  local copies, waits for them, and re-layouts: 3.62 us -> 5.82 us
    ppermute x2, waiting for transfers between devices: 1.3 us -> 25.3 us  [shifted(): return lax.ppermute(value, axis, pairs)]
    ppermute x3 -> x2, waiting for transfers between devices: 23.1 us -> 2.2 us  [tree_broadcast_from(): got = lax.ppermute(value, axis, pairs)]
    ppermute x2, waiting for transfers between devices: 37.7 us -> 18.5 us  [tree_reduce(): value = value + lax.ppermute(value, axis, pairs)]
    ppermute x3, waiting for transfers between devices: 10.2 us -> 23.5 us  [direct_scatter(): total = total + lax.ppermute(send, axis, pairs)]
    ppermute x3, starting transfers between devices: 11.6 us -> 5.57 us  [direct_scatter(): total = total + lax.ppermute(send, axis, pairs)]
    ppermute x3 -> x2, starting transfers between devices: 14.4 us -> 10.2 us  [tree_broadcast_from(): got = lax.ppermute(value, axis, pairs)]
    ppermute x3, starting transfers between devices: 6.09 us -> 9.64 us  [direct_gather(): got = lax.ppermute(piece, axis, pairs)]
    ppermute x2, starting transfers between devices: 2.82 us -> 5.92 us  [shifted(): return lax.ppermute(value, axis, pairs)]
  transfers between devices with their start and end apart: 19 -> 18, of which waited for: 12 -> 12; matrix products, arithmetic and copies ran while one was open for 18% -> 23% of each run, Pallas kernels for 0% -> 0%
where the time goes in v17:
time: 177 us; the launch traced here: 176 us
  waiting for transfers between devices  88 us (50%)
  starting transfers between devices  37.9 us (21%)
  matrix products  28.5 us (16%)
  other arithmetic  14.6 us (8%)
  local copies, waits for them, and re-layouts  5.82 us (3%)
    ppermute x2, waiting for transfers between devices, shifted(): return lax.ppermute(value, axis, pairs)  25.3 us
    ppermute x3, waiting for transfers between devices, direct_scatter(): total = total + lax.ppermute(send, axis, pairs)  23.5 us
    ppermute x2, waiting for transfers between devices, tree_reduce(): value = value + lax.ppermute(value, axis, pairs)  18.5 us
    dot_general x18, matrix products, spatial_sum(): total = total + jnp.dot(piece, kernel, preferred_element_type=jnp.float32)  11.9 us
    ppermute x3, waiting for transfers between devices, direct_gather(): got = lax.ppermute(piece, axis, pairs)  11.1 us
    ppermute x2, starting transfers between devices, tree_broadcast_from(): got = lax.ppermute(value, axis, pairs)  10.2 us
    ppermute x3, starting transfers between devices, direct_gather(): got = lax.ppermute(piece, axis, pairs)  9.64 us
    ppermute x2, starting transfers between devices, shifted(): return lax.ppermute(value, axis, pairs)  5.92 us
  transfers between devices with their start and end apart: 18, of which 12 were waited for; matrix products, arithmetic and copies ran while one was open for 23% of the time, Pallas kernels for 0%

profile of v17, /device:TPU:0, one launch (start us, length us, event | category | flops | bytes accessed | tf_op | source)
XLA Modules:
  0.0 176.1 jit_solution(15229696358789424734)
XLA Ops:
  1.4 1.4 broadcast_multiply_fusion.1
  6.8 8.7 %collective-permute-start.1 = (bf16[2,2,256,256]{3,2,1,0:T(8,128)(2,1)}, bf16[2,2,256,256]{3,2,1,0:T(8,128)(2,1)}, u32[]{:S(2)}, u32[]{:S(2)}) collective-permute-start(bf16[2,2,256,256]{3,2,1,0:T(8,128)(2,1)} %slice_bitcast_fusion.1), channel_id=1, source_target_pairs={{0,8},{1,9},{16,24},{17,25}} | collective-permute-start | bytes 1572872 | tf_op jit(solution)/shard_map/ppermute | solution.py:35
  15.5 1.4 fusion.54
  23.8 2.2 %collective-permute-done.1 = bf16[2,2,256,256]{3,2,1,0:T(8,128)(2,1)} collective-permute-done((bf16[2,2,256,256]{3,2,1,0:T(8,128)(2,1)}, bf16[2,2,256,256]{3,2,1,0:T(8,128)(2,1)}, u32[]{:S(2)}, u32[]{:S(2)}) %collective-permute-start.1) | collective-permute-done | bytes 524320 | tf_op jit(solution)/shard_map/ppermute | solution.py:35
  26.1 1.5 collective-permute-start.2
  27.6 1.5 multiply_convert_fusion.2
  30.0 2.8 %collective-permute-done.4 = bf16[2,2,2,256,256]{4,3,2,1,0:T(8,128)(2,1)} collective-permute-done((bf16[2,2,2,256,256]{4,3,2,1,0:T(8,128)(2,1)S(1)}, bf16[2,2,2,256,256]{4,3,2,1,0:T(8,128)(2,1)}, u32[]{:S(2)}, u32[]{:S(2)}) %collective-permute-start.4) | collective-permute-done | bytes 1048608 | tf_op jit(solution)/shard_map/ppermute | solution.py:10
  32.9 1.5 fusion.43
  34.4 2.3 %multiply_convert_fusion = bf16[2,2,2,256,256]{4,3,2,0,1:T(8,128)(2,1)S(1)} fusion(f32[2,2,2,256,256]{4,3,2,0,1:T(8,128)S(1)} %get-tuple-element.35, f32[2,2,2,256,256]{4,3,2,0,1:T(8,128)S(1)} %fusion.45, f32[2,2,2,256,256]{4,3,2,0,1:T(8,128)S(1)} %fusion.43, bf16[2,2,2,256,256]{4,3,2,1,0:T(8,128)(2,1)} %collective-permute-done.4, ...), kind=kOutput, calls=%fused_computation.23 | convolution fusion | flops 274202624 | bytes 8519680 | tf_op jit(solution)/shard_map/dot_general | solution.py:191
  41.2 1.4 pad_maximum_fusion.1
  43.0 4.6 %collective-permute-start.3 = (bf16[2,3,2,256,256]{4,3,2,0,1:T(8,128)(2,1)}, bf16[2,3,2,256,256]{4,3,2,0,1:T(8,128)(2,1)S(1)}, u32[]{:S(2)}, u32[]{:S(2)}) collective-permute-start(bf16[2,3,2,256,256]{4,3,2,0,1:T(8,128)(2,1)} %pad_maximum_fusion.1), channel_id=1, source_target_pairs={{0,2},{2,4},{4,6},{6,8},{8,10},{10,12},{12,14},{1,3},{3,5},{5,7},{... | collective-permute-start | bytes 4718600 | tf_op jit(solution)/shard_map/ppermute | solution.py:10
  47.8 1.5 convert_reduce_fusion.1
  50.4 1.5 collective-permute-start.6
  51.9 1.7 convolution_bitcast_fusion.1
  53.6 1.5 convolution_bitcast_fusion.2
  56.5 1.3 fusion.173
  58.3 22.4 %collective-permute-done.3 = bf16[2,3,2,256,256]{4,3,2,0,1:T(8,128)(2,1)S(1)} collective-permute-done((bf16[2,3,2,256,256]{4,3,2,0,1:T(8,128)(2,1)}, bf16[2,3,2,256,256]{4,3,2,0,1:T(8,128)(2,1)S(1)}, u32[]{:S(2)}, u32[]{:S(2)}) %collective-permute-start.3) | collective-permute-done | bytes 1572896 | tf_op jit(solution)/shard_map/ppermute | solution.py:10
  86.0 3.5 %collective-permute-start.10 = (f32[416,256]{1,0:T(8,128)S(1)}, f32[416,256]{1,0:T(8,128)S(1)}, u32[]{:S(2)}, u32[]{:S(2)}) collective-permute-start(f32[416,256]{1,0:T(8,128)S(1)} %get-tuple-element.25), channel_id=1, source_target_pairs={{0,8},{2,10},{4,12},{6,14},{8,0},{10,2},{12,4},{14,6},{1,9},{3,11}... | collective-permute-start | bytes 1277960 | tf_op jit(solution)/shard_map/ppermute | solution.py:85
  89.6 1.4 collective-permute-start.11
  92.1 1.7 add.244
  95.6 13.9 %collective-permute-done.10 = f32[416,256]{1,0:T(8,128)S(1)} collective-permute-done((f32[416,256]{1,0:T(8,128)S(1)}, f32[416,256]{1,0:T(8,128)S(1)}, u32[]{:S(2)}, u32[]{:S(2)}) %collective-permute-start.10) | collective-permute-done | bytes 426016 | tf_op jit(solution)/shard_map/ppermute | solution.py:85
  109.5 9.6 %collective-permute-done.9 = f32[416,256]{1,0:T(8,128)S(1)} collective-permute-done((f32[416,256]{1,0:T(8,128)S(1)}, f32[416,256]{1,0:T(8,128)S(1)}, u32[]{:S(2)}, u32[]{:S(2)}) %collective-permute-start.9) | collective-permute-done | bytes 426016 | tf_op jit(solution)/shard_map/ppermute | solution.py:85
  119.3 1.6 collective-permute-start.12
  121.2 4.6 %collective-permute-done.12 = f32[208,256]{1,0:T(8,128)S(1)} collective-permute-done((f32[208,256]{1,0:T(8,128)S(1)}, f32[208,256]{1,0:T(8,128)S(1)}, u32[]{:S(2)}, u32[]{:S(2)}) %collective-permute-start.12) | collective-permute-done | bytes 213024 | tf_op jit(solution)/shard_map/ppermute | solution.py:59
  125.8 1.6 collective-permute-start.13
  127.4 1.7 multiply_convert_fusion.1
  129.1 1.5 collective-permute-done.13
  130.7 9.5 %collective-permute-start.14 = (bf16[416,256]{1,0:T(8,128)(2,1)S(1)}, bf16[416,256]{1,0:T(8,128)(2,1)S(1)}, u32[]{:S(2)}, u32[]{:S(2)}) collective-permute-start(bf16[416,256]{1,0:T(8,128)(2,1)S(1)} %maximum_select_fusion.1), channel_id=1, source_target_pairs={{0,4},{2,6},{4,8},{6,10},{8,12},{10,14},{12,0},{14,2},{1,5},{3,7},... | collective-permute-start | bytes 638984 | tf_op jit(solution)/shard_map/ppermute | solution.py:98
  140.2 18.5 %collective-permute-done.7 = f32[2,2,256,256]{3,2,1,0:T(8,128)S(1)} collective-permute-done((f32[2,2,256,256]{3,2,1,0:T(8,128)S(1)}, f32[2,2,256,256]{3,2,1,0:T(8,128)S(1)}, u32[]{:S(2)}, u32[]{:S(2)}) %collective-permute-start.7) | collective-permute-done | bytes 1048608 | tf_op jit(solution)/shard_map/ppermute | solution.py:45
  159.7 8.8 %collective-permute-done.15 = bf16[416,256]{1,0:T(8,128)(2,1)S(1)} collective-permute-done((bf16[416,256]{1,0:T(8,128)(2,1)S(1)}, bf16[416,256]{1,0:T(8,128)(2,1)S(1)}, u32[]{:S(2)}, u32[]{:S(2)}) %collective-permute-start.15) | collective-permute-done | bytes 213024 | tf_op jit(solution)/shard_map/ppermute | solution.py:98
  168.5 2.3 %collective-permute-done.16 = bf16[416,256]{1,0:T(8,128)(2,1)S(1)} collective-permute-done((bf16[416,256]{1,0:T(8,128)(2,1)S(1)}, bf16[416,256]{1,0:T(8,128)(2,1)S(1)}, u32[]{:S(2)}, u32[]{:S(2)}) %collective-permute-start.16) | collective-permute-done | bytes 213024 | tf_op jit(solution)/shard_map/ppermute | solution.py:98
  171.0 2.2 %fusion.14 = bf16[2,2,2,256,256]{4,3,2,1,0:T(8,128)(2,1)} fusion(bf16[2,2,2,256,256]{4,3,2,1,0:T(8,128)(2,1)S(1)} %get-tuple-element.6, f32[2,2,2,256,256]{4,3,2,1,0:T(8,128)S(1)} %fusion.66, f32[2,2,2,256,256]{4,3,2,1,0:T(8,128)S(1)} %fusion.68, f32[2,2,2,256,256]{4,3,2,1,0:T(8,128)S(1)} %fusion.70, f32[2,2,2,256,256]{4,3,2,1,0:T(8,128)S(1)} %fusion.102, ...), kind=kOutput, calls=%fused_computation.21 | convolution fusion | flops 275775488 | bytes 21104128 | tf_op jit(solution)/shard_map/dot_general | solution.py:173
  (101 shorter events, 32.9 us)
Async XLA Ops:
  0.6 120.3 %copy-start = (bf16[256,256]{1,0:T(8,128)(2,1)S(1)}, bf16[256,256]{1,0:T(8,128)(2,1)}, u32[]{:S(2)}) copy-start(bf16[256,256]{1,0:T(8,128)(2,1)} %param.11) | copy-start | bytes 393220
  2.8 1.4 copy-start.6
  3.7 13.7 %collective-permute-start = (bf16[2,2,1,256,256]{4,3,2,1,0:T(8,128)(2,1)}, bf16[2,2,1,256,256]{4,3,2,1,0:T(8,128)(2,1)}, u32[]{:S(2)}, u32[]{:S(2)}) collective-permute-start(bf16[2,2,1,256,256]{4,3,2,1,0:T(8,128)(2,1)} %slice_select_fusion.1), channel_id=1, source_target_pairs={{0,1},{1,0},{2,3},{3,2},{4,5},{5,4},{6,7},{7,6},{8,9},{9,8},{10,11... | collective-permute-start | bytes 1572872 | tf_op jit(solution)/shard_map/ppermute | solution.py:216
  4.6 28.2 %collective-permute-start.4 = (bf16[2,2,2,256,256]{4,3,2,1,0:T(8,128)(2,1)S(1)}, bf16[2,2,2,256,256]{4,3,2,1,0:T(8,128)(2,1)}, u32[]{:S(2)}, u32[]{:S(2)}) collective-permute-start(bf16[2,2,2,256,256]{4,3,2,1,0:T(8,128)(2,1)S(1)} %get-tuple-element.6), channel_id=1, source_target_pairs={{2,0},{4,2},{6,4},{8,6},{10,8},{12,10},{14,12},{3,1},{5,3},{7,5},{... | collective-permute-start | bytes 3145736 | tf_op jit(solution)/shard_map/ppermute | solution.py:10
  6.8 19.3 %collective-permute-start.1 = (bf16[2,2,256,256]{3,2,1,0:T(8,128)(2,1)}, bf16[2,2,256,256]{3,2,1,0:T(8,128)(2,1)}, u32[]{:S(2)}, u32[]{:S(2)}) collective-permute-start(bf16[2,2,256,256]{3,2,1,0:T(8,128)(2,1)} %slice_bitcast_fusion.1), channel_id=1, source_target_pairs={{0,8},{1,9},{16,24},{17,25}} | collective-permute-start | bytes 1572872 | tf_op jit(solution)/shard_map/ppermute | solution.py:35
  15.5 1.4 copy-start.4
  19.5 1.3 copy-start.1
  26.1 15.1 %collective-permute-start.2 = (bf16[2,2,256,256]{3,2,1,0:T(8,128)(2,1)S(1)}, bf16[2,2,256,256]{3,2,1,0:T(8,128)(2,1)S(1)}, u32[]{:S(2)}, u32[]{:S(2)}) collective-permute-start(bf16[2,2,256,256]{3,2,1,0:T(8,128)(2,1)S(1)} %broadcast_select_fusion.4), channel_id=1, source_target_pairs={{0,4},{8,12},{1,5},{9,13},{16,20},{24,28},{17,21},{25,29}} | collective-permute-start | bytes 1572872 | tf_op jit(solution)/shard_map/ppermute | solution.py:35
  41.1 1.9 %copy-start.2 = (f32[9,256,256]{2,1,0:T(8,128)}, f32[9,256,256]{2,1,0:T(8,128)S(1)}, u32[]{:S(2)}) copy-start(f32[9,256,256]{2,1,0:T(8,128)S(1)} %fusion.35) | copy-start | bytes 7077892
  43.0 37.8 %collective-permute-start.3 = (bf16[2,3,2,256,256]{4,3,2,0,1:T(8,128)(2,1)}, bf16[2,3,2,256,256]{4,3,2,0,1:T(8,128)(2,1)S(1)}, u32[]{:S(2)}, u32[]{:S(2)}) collective-permute-start(bf16[2,3,2,256,256]{4,3,2,0,1:T(8,128)(2,1)} %pad_maximum_fusion.1), channel_id=1, source_target_pairs={{0,2},{2,4},{4,6},{6,8},{8,10},{10,12},{12,14},{1,3},{3,5},{5,7},{... | collective-permute-start | bytes 4718600 | tf_op jit(solution)/shard_map/ppermute | solution.py:10
  47.7 8.0 %collective-permute-start.5 = (bf16[2,2,1,256,256]{4,3,2,1,0:T(8,128)(2,1)S(1)}, bf16[2,2,1,256,256]{4,3,2,1,0:T(8,128)(2,1)S(1)}, u32[]{:S(2)}, u32[]{:S(2)}) collective-permute-start(bf16[2,2,1,256,256]{4,3,2,1,0:T(8,128)(2,1)S(1)} %copy.28), channel_id=1, source_target_pairs={{0,1},{1,0},{2,3},{3,2},{4,5},{5,4},{6,7},{7,6},{8,9},{9,8},{10,11... | collective-permute-start | bytes 1572872 | tf_op jit(solution)/shard_map/ppermute | solution.py:216
  50.4 41.6 %collective-permute-start.6 = (f32[2,2,256,256]{3,2,1,0:T(8,128)}, f32[2,2,256,256]{3,2,1,0:T(8,128)}, u32[]{:S(2)}, u32[]{:S(2)}) collective-permute-start(f32[2,2,256,256]{3,2,1,0:T(8,128)} %add.243), channel_id=1, source_target_pairs={{4,0},{12,8},{5,1},{13,9},{20,16},{28,24},{21,17},{29,25}} | collective-permute-start | bytes 3145736 | tf_op jit(solution)/shard_map/ppermute | solution.py:45
  58.3 23.3 %copy-start.3 = (f32[9,256,256]{2,1,0:T(8,128)S(1)}, f32[9,256,256]{2,1,0:T(8,128)}, u32[]{:S(2)}) copy-start(f32[9,256,256]{2,1,0:T(8,128)} %copy-done.2) | copy-start | bytes 7077892
  82.0 3.7 %collective-permute-start.8 = (f32[1664,256]{1,0:T(8,128)S(1)}, f32[1664,256]{1,0:T(8,128)S(1)}, u32[]{:S(2)}, u32[]{:S(2)}) collective-permute-start(f32[1664,256]{1,0:T(8,128)S(1)} %constant_dynamic-slice_fusion.4), channel_id=1, source_target_pairs={{0,1},{1,0},{2,3},{3,2},{4,5},{5,4},{6,7},{7,6},{8,9},{9,8},{10,11... | collective-permute-start | bytes 5111816 | tf_op jit(solution)/shard_map/ppermute | solution.py:59
  86.0 23.5 %collective-permute-start.10 = (f32[416,256]{1,0:T(8,128)S(1)}, f32[416,256]{1,0:T(8,128)S(1)}, u32[]{:S(2)}, u32[]{:S(2)}) collective-permute-start(f32[416,256]{1,0:T(8,128)S(1)} %get-tuple-element.25), channel_id=1, source_target_pairs={{0,8},{2,10},{4,12},{6,14},{8,0},{10,2},{12,4},{14,6},{1,9},{3,11}... | collective-permute-start | bytes 1277960 | tf_op jit(solution)/shard_map/ppermute | solution.py:85
  89.6 20.0 %collective-permute-start.11 = (f32[416,256]{1,0:T(8,128)S(1)}, f32[416,256]{1,0:T(8,128)S(1)}, u32[]{:S(2)}, u32[]{:S(2)}) collective-permute-start(f32[416,256]{1,0:T(8,128)S(1)} %get-tuple-element.24), channel_id=1, source_target_pairs={{0,12},{2,14},{4,0},{6,2},{8,4},{10,6},{12,8},{14,10},{1,13},{3,15... | collective-permute-start | bytes 1277960 | tf_op jit(solution)/shard_map/ppermute | solution.py:85
  90.9 28.2 %collective-permute-start.9 = (f32[416,256]{1,0:T(8,128)S(1)}, f32[416,256]{1,0:T(8,128)S(1)}, u32[]{:S(2)}, u32[]{:S(2)}) collective-permute-start(f32[416,256]{1,0:T(8,128)S(1)} %get-tuple-element.23), channel_id=1, source_target_pairs={{0,4},{2,6},{4,8},{6,10},{8,12},{10,14},{12,0},{14,2},{1,5},{3,7},... | collective-permute-start | bytes 1277960 | tf_op jit(solution)/shard_map/ppermute | solution.py:85
  92.0 3.1 %copy-start.5 = (bf16[3,256,256]{2,1,0:T(8,128)(2,1)S(1)}, bf16[3,256,256]{2,1,0:T(8,128)(2,1)}, u32[]{:S(2)}) copy-start(bf16[3,256,256]{2,1,0:T(8,128)(2,1)} %param.10) | copy-start | bytes 1179652
  93.8 64.9 %collective-permute-start.7 = (f32[2,2,256,256]{3,2,1,0:T(8,128)S(1)}, f32[2,2,256,256]{3,2,1,0:T(8,128)S(1)}, u32[]{:S(2)}, u32[]{:S(2)}) collective-permute-start(f32[2,2,256,256]{3,2,1,0:T(8,128)S(1)} %add.244), channel_id=1, source_target_pairs={{8,0},{9,1},{24,16},{25,17}} | collective-permute-start | bytes 3145736 | tf_op jit(solution)/shard_map/ppermute | solution.py:45
  119.3 6.5 %collective-permute-start.12 = (f32[208,256]{1,0:T(8,128)S(1)}, f32[208,256]{1,0:T(8,128)S(1)}, u32[]{:S(2)}, u32[]{:S(2)}) collective-permute-start(f32[208,256]{1,0:T(8,128)S(1)} %constant_dynamic-slice_fusion), channel_id=1, source_target_pairs={{0,2},{2,0},{4,6},{6,4},{8,10},{10,8},{12,14},{14,12},{1,3},{3,1},... | collective-permute-start | bytes 638984 | tf_op jit(solution)/shard_map/ppermute | solution.py:59
  125.8 4.8 %collective-permute-start.13 = (bf16[208,256]{1,0:T(8,128)(2,1)S(1)}, bf16[208,256]{1,0:T(8,128)(2,1)S(1)}, u32[]{:S(2)}, u32[]{:S(2)}) collective-permute-start(bf16[208,256]{1,0:T(8,128)(2,1)S(1)} %multiply_convert_fusion.3), channel_id=1, source_target_pairs={{0,2},{2,0},{4,6},{6,4},{8,10},{10,8},{12,14},{14,12},{1,3},{3,1},... | collective-permute-start | bytes 319496 | tf_op jit(solution)/shard_map/ppermute | solution.py:67
  130.7 29.0 %collective-permute-start.14 = (bf16[416,256]{1,0:T(8,128)(2,1)S(1)}, bf16[416,256]{1,0:T(8,128)(2,1)S(1)}, u32[]{:S(2)}, u32[]{:S(2)}) collective-permute-start(bf16[416,256]{1,0:T(8,128)(2,1)S(1)} %maximum_select_fusion.1), channel_id=1, source_target_pairs={{0,4},{2,6},{4,8},{6,10},{8,12},{10,14},{12,0},{14,2},{1,5},{3,7},... | collective-permute-start | bytes 638984 | tf_op jit(solution)/shard_map/ppermute | solution.py:98
  159.4 9.1 %collective-permute-start.15 = (bf16[416,256]{1,0:T(8,128)(2,1)S(1)}, bf16[416,256]{1,0:T(8,128)(2,1)S(1)}, u32[]{:S(2)}, u32[]{:S(2)}) collective-permute-start(bf16[416,256]{1,0:T(8,128)(2,1)S(1)} %maximum_select_fusion.1), channel_id=1, source_target_pairs={{0,8},{2,10},{4,12},{6,14},{8,0},{10,2},{12,4},{14,6},{1,9},{3,11}... | collective-permute-start | bytes 638984 | tf_op jit(solution)/shard_map/ppermute | solution.py:98
  159.5 11.4 %collective-permute-start.16 = (bf16[416,256]{1,0:T(8,128)(2,1)S(1)}, bf16[416,256]{1,0:T(8,128)(2,1)S(1)}, u32[]{:S(2)}, u32[]{:S(2)}) collective-permute-start(bf16[416,256]{1,0:T(8,128)(2,1)S(1)} %maximum_select_fusion.1), channel_id=1, source_target_pairs={{0,12},{2,14},{4,0},{6,2},{8,4},{10,6},{12,8},{14,10},{1,13},{3,15... | collective-permute-start | bytes 638984 | tf_op jit(solution)/shard_map/ppermute | solution.py:98
  170.9 2.4 %collective-permute-start.17 = (bf16[1664,256]{1,0:T(8,128)(2,1)S(1)}, bf16[1664,256]{1,0:T(8,128)(2,1)S(1)}, u32[]{:S(2)}, u32[]{:S(2)}) collective-permute-start(bf16[1664,256]{1,0:T(8,128)(2,1)S(1)} %bitcast.271), channel_id=1, source_target_pairs={{0,1},{1,0},{2,3},{3,2},{4,5},{5,4},{6,7},{7,6},{8,9},{9,8},{10,11... | collective-permute-start | bytes 2555912 | tf_op jit(solution)/shard_map/ppermute | solution.py:144

commit v18 on v13

--- a/solution.py
+++ b/solution.py
@@ -31,6 +31,27 @@
         value = value + lax.ppermute(value, axis, pairs)
         step *= 2
     return value
+
+
+def two_column_sum(pair, local, axis):
+    count = lax.axis_size(axis)
+    me = lax.axis_index(axis)
+    half = pair.shape[0] // 2
+    odd = me % 2 == 1
+    value = jnp.where(odd, pair[half:], pair[:half])
+    n = count // 2
+    step = 1
+    while step < n:
+        pairs = []
+        for i in range(0, n, 2 * step):
+            if i + step < n:
+                pairs.append((2 * (i + step), 2 * i))
+                if 2 * (i + step) + 1 < count:
+                    pairs.append((2 * (i + step) + 1, 2 * i + 1))
+        value = value + lax.ppermute(value, axis, pairs)
+        step *= 2
+    got = lax.ppermute(value, axis, [(1, 0)])
+    return jnp.concatenate([value, got + local[half:]], axis=0)
 
 
 def xor_halving(flat, axis, steps):
@@ -222,7 +243,10 @@
     later = shifted(cot, "space", -1)
     if lax.axis_size("space") % 2 == 0:
         cot_pair = cot_local + jnp.sum(later, axis=1, dtype=jnp.float32)
-        cot_sum = tree_reduce(cot_pair, "space", 2)
+        if clips % 2 == 0 and lax.axis_size("space") >= 4:
+            cot_sum = two_column_sum(cot_pair, cot_local, "space")
+        else:
+            cot_sum = tree_reduce(cot_pair, "space", 2)
     else:
         cot_sum = tree_reduce(cot_local, "space")
     rows_pad = row_halo(masked)

time: 172 us -> 162 us (0.942); the launches traced: 172 us -> 160 us
  waiting for transfers between devices: 93.8 us -> 83.5 us
    ppermute x2 -> x3, waiting for transfers between devices: 37.7 us -> 30.3 us  [the longest x2 30.3 us: two_column_sum(): value = value + lax.ppermute(value, axis, pairs)]
    ppermute x3, starting transfers between devices: 11.6 us -> 6.55 us  [direct_scatter(): total = total + lax.ppermute(send, axis, pairs)]
    ppermute x3, waiting for transfers between devices: 10.2 us -> 7.75 us  [direct_scatter(): total = total + lax.ppermute(send, axis, pairs)]
    ppermute x3, starting transfers between devices: 6.09 us -> 8.4 us  [direct_gather(): got = lax.ppermute(piece, axis, pairs)]
    ppermute x3, waiting for transfers between devices: 10.9 us -> 8.59 us  [direct_gather(): got = lax.ppermute(piece, axis, pairs)]
    ppermute x2 -> x3, starting transfers between devices: 2.8 us -> 4.1 us  [the longest x2 2.8 us: two_column_sum(): value = value + lax.ppermute(value, axis, pairs)]
  transfers between devices with their start and end apart: 19 -> 20, of which waited for: 12 -> 12; matrix products, arithmetic and copies ran while one was open for 18% -> 20% of each run, Pallas kernels for 0% -> 0%
where the time goes in v18:
time: 162 us; the launch traced here: 160 us
  waiting for transfers between devices  83.5 us (52%)
  starting transfers between devices  37.1 us (23%)
  matrix products  24.4 us (15%)
  other arithmetic  10.2 us (6%)
  local copies, waits for them, and re-layouts  3.62 us (2%)
    ppermute x2, waiting for transfers between devices, two_column_sum(): value = value + lax.ppermute(value, axis, pairs)  30.3 us
    ppermute x3, waiting for transfers between devices, tree_broadcast(): got = lax.ppermute(value, axis, pairs)  23.4 us
    ppermute x3, starting transfers between devices, tree_broadcast(): got = lax.ppermute(value, axis, pairs)  14.4 us
    dot_general x18, matrix products, spatial_sum(): total = total + jnp.dot(piece, kernel, preferred_element_type=jnp.float32)  12.1 us
    ppermute x3, waiting for transfers between devices, direct_gather(): got = lax.ppermute(piece, axis, pairs)  8.59 us
    ppermute x3, starting transfers between devices, direct_gather(): got = lax.ppermute(piece, axis, pairs)  8.4 us
    ppermute x3, waiting for transfers between devices, direct_scatter(): total = total + lax.ppermute(send, axis, pairs)  7.75 us
    ppermute x2, waiting for transfers between devices, xor_halving(): flat = keep + lax.ppermute(send, axis, pairs)  7.41 us
  transfers between devices with their start and end apart: 20, of which 12 were waited for; matrix products, arithmetic and copies ran while one was open for 20% of the time, Pallas kernels for 0%

profile of v18, /device:TPU:0, one launch (start us, length us, event | category | flops | bytes accessed | tf_op | source)
XLA Modules:
  0.0 159.9 jit_solution(3274098371982254515)
XLA Ops:
  1.5 1.4 broadcast_multiply_fusion.1
  2.9 0.9 slice_select_fusion.2
  4.2 1.4 convert_reduce_fusion
  5.6 1.3 collective-permute-start.5
  7.7 8.3 %collective-permute-start.2 = (bf16[2,2,256,256]{3,2,1,0:T(8,128)(2,1)}, bf16[2,2,256,256]{3,2,1,0:T(8,128)(2,1)}, u32[]{:S(2)}, u32[]{:S(2)}) collective-permute-start(bf16[2,2,256,256]{3,2,1,0:T(8,128)(2,1)} %slice_bitcast_fusion), channel_id=1, source_target_pairs={{0,8},{1,9},{16,24},{17,25}} | collective-permute-start | bytes 1572872 | tf_op jit(solution)/shard_map/ppermute | solution.py:21
  16.0 1.4 fusion.89
  17.8 1.1 broadcast_select_fusion.8
  23.3 3.7 %collective-permute-done.2 = bf16[2,2,256,256]{3,2,1,0:T(8,128)(2,1)} collective-permute-done((bf16[2,2,256,256]{3,2,1,0:T(8,128)(2,1)}, bf16[2,2,256,256]{3,2,1,0:T(8,128)(2,1)}, u32[]{:S(2)}, u32[]{:S(2)}) %collective-permute-start.2) | collective-permute-done | bytes 524320 | tf_op jit(solution)/shard_map/ppermute | solution.py:21
  27.1 1.3 collective-permute-start.3
  28.4 1.6 multiply_convert_fusion.2
  30.0 1.5 collective-permute-start.1
  32.5 1.3 collective-permute-done.5
  34.2 1.1 multiply_convert_fusion
  39.5 4.8 %collective-permute-start.4 = (bf16[2,2,256,256]{3,2,1,0:T(8,128)(2,1)S(1)}, bf16[2,2,256,256]{3,2,1,0:T(8,128)(2,1)S(1)}, u32[]{:S(2)}, u32[]{:S(2)}) collective-permute-start(bf16[2,2,256,256]{3,2,1,0:T(8,128)(2,1)S(1)} %broadcast_select_fusion.3), channel_id=1, source_target_pairs={{0,2},{4,6},{8,10},{12,14},{1,3},{5,7},{9,11},{13,15},{16,18},{20,... | collective-permute-start | bytes 1572872 | tf_op jit(solution)/shard_map/ppermute | solution.py:21
  44.6 1.3 collective-permute-start.7
  48.0 19.6 %collective-permute-done.4 = bf16[2,2,256,256]{3,2,1,0:T(8,128)(2,1)S(1)} collective-permute-done((bf16[2,2,256,256]{3,2,1,0:T(8,128)(2,1)S(1)}, bf16[2,2,256,256]{3,2,1,0:T(8,128)(2,1)S(1)}, u32[]{:S(2)}, u32[]{:S(2)}) %collective-permute-start.4) | collective-permute-done | bytes 524320 | tf_op jit(solution)/shard_map/ppermute | solution.py:21
  68.9 9.8 %collective-permute-done.7 = f32[1,2,256,256]{3,2,1,0:T(8,128)S(1)} collective-permute-done((f32[1,2,256,256]{3,2,1,0:T(8,128)S(1)}, f32[1,2,256,256]{3,2,1,0:T(8,128)S(1)}, u32[]{:S(2)}, u32[]{:S(2)}) %collective-permute-start.7) | collective-permute-done | bytes 524320 | tf_op jit(solution)/shard_map/ppermute | solution.py:51
  78.8 1.5 collective-permute-start.8
  85.8 3.6 %collective-permute-start.12 = (f32[416,256]{1,0:T(8,128)S(1)}, f32[416,256]{1,0:T(8,128)S(1)}, u32[]{:S(2)}, u32[]{:S(2)}) collective-permute-start(f32[416,256]{1,0:T(8,128)S(1)} %get-tuple-element.13), channel_id=1, source_target_pairs={{0,8},{2,10},{4,12},{6,14},{8,0},{10,2},{12,4},{14,6},{1,9},{3,11}... | collective-permute-start | bytes 1277960 | tf_op jit(solution)/shard_map/ppermute | solution.py:92
  89.5 2.8 %collective-permute-start.13 = (f32[416,256]{1,0:T(8,128)S(1)}, f32[416,256]{1,0:T(8,128)S(1)}, u32[]{:S(2)}, u32[]{:S(2)}) collective-permute-start(f32[416,256]{1,0:T(8,128)S(1)} %get-tuple-element.12), channel_id=1, source_target_pairs={{0,12},{2,14},{4,0},{6,2},{8,4},{10,6},{12,8},{14,10},{1,13},{3,15... | collective-permute-start | bytes 1277960 | tf_op jit(solution)/shard_map/ppermute | solution.py:92
  92.3 1.8 %multiply_convert_fusion.1 = bf16[2,2,2,256,256]{4,3,2,1,0:T(8,128)(2,1)} fusion(f32[2,2,2,256,256]{4,3,2,1,0:T(8,128)S(1)} %fusion.108, f32[2,2,2,256,256]{4,3,2,1,0:T(8,128)S(1)} %fusion.5, bf16[2,2,2,256,256]{4,3,2,1,0:T(8,128)(2,1)S(1)} %broadcast_multiply_fusion.1, f32[2,2]{1,0:T(2,128)S(1)} %get-tuple-element.7, f32[2,2,256,256]{3,2,1,0:T(8,128)S(1)} %fusion.72, ...), kind=kOutput, calls=%fused_computation.24 | convolution fusion | flops 272105472 | bytes 8520704 | tf_op jit(solution)/shard_map/dot_general | solution.py:187
  94.1 20.6 %collective-permute-done.8 = f32[1,2,256,256]{3,2,1,0:T(8,128)S(1)} collective-permute-done((f32[1,2,256,256]{3,2,1,0:T(8,128)S(1)}, f32[1,2,256,256]{3,2,1,0:T(8,128)S(1)}, u32[]{:S(2)}, u32[]{:S(2)}) %collective-permute-start.8) | collective-permute-done | bytes 524320 | tf_op jit(solution)/shard_map/ppermute | solution.py:51
  114.8 1.3 collective-permute-start.9
  116.1 7.7 %collective-permute-done.12 = f32[416,256]{1,0:T(8,128)S(1)} collective-permute-done((f32[416,256]{1,0:T(8,128)S(1)}, f32[416,256]{1,0:T(8,128)S(1)}, u32[]{:S(2)}, u32[]{:S(2)}) %collective-permute-start.12) | collective-permute-done | bytes 426016 | tf_op jit(solution)/shard_map/ppermute | solution.py:92
  124.5 7.4 %collective-permute-done.14 = f32[208,256]{1,0:T(8,128)S(1)} collective-permute-done((f32[208,256]{1,0:T(8,128)S(1)}, f32[208,256]{1,0:T(8,128)S(1)}, u32[]{:S(2)}, u32[]{:S(2)}) %collective-permute-start.14) | collective-permute-done | bytes 213024 | tf_op jit(solution)/shard_map/ppermute | solution.py:66
  132.2 4.6 %collective-permute-done.15 = bf16[208,256]{1,0:T(8,128)(2,1)S(1)} collective-permute-done((bf16[208,256]{1,0:T(8,128)(2,1)S(1)}, bf16[208,256]{1,0:T(8,128)(2,1)S(1)}, u32[]{:S(2)}, u32[]{:S(2)}) %collective-permute-start.15) | collective-permute-done | bytes 106528 | tf_op jit(solution)/shard_map/ppermute | solution.py:74
  136.8 6.0 %collective-permute-start.16 = (bf16[416,256]{1,0:T(8,128)(2,1)S(1)}, bf16[416,256]{1,0:T(8,128)(2,1)S(1)}, u32[]{:S(2)}, u32[]{:S(2)}) collective-permute-start(bf16[416,256]{1,0:T(8,128)(2,1)S(1)} %maximum_select_fusion.1), channel_id=1, source_target_pairs={{0,4},{2,6},{4,8},{6,10},{8,12},{10,14},{12,0},{14,2},{1,5},{3,7},... | collective-permute-start | bytes 638984 | tf_op jit(solution)/shard_map/ppermute | solution.py:105
  143.5 2.4 %collective-permute-start.18 = (bf16[416,256]{1,0:T(8,128)(2,1)S(1)}, bf16[416,256]{1,0:T(8,128)(2,1)S(1)}, u32[]{:S(2)}, u32[]{:S(2)}) collective-permute-start(bf16[416,256]{1,0:T(8,128)(2,1)S(1)} %maximum_select_fusion.1), channel_id=1, source_target_pairs={{0,12},{2,14},{4,0},{6,2},{8,4},{10,6},{12,8},{14,10},{1,13},{3,15... | collective-permute-start | bytes 638984 | tf_op jit(solution)/shard_map/ppermute | solution.py:105
  146.0 1.9 %collective-permute-done.16 = bf16[416,256]{1,0:T(8,128)(2,1)S(1)} collective-permute-done((bf16[416,256]{1,0:T(8,128)(2,1)S(1)}, bf16[416,256]{1,0:T(8,128)(2,1)S(1)}, u32[]{:S(2)}, u32[]{:S(2)}) %collective-permute-start.16) | collective-permute-done | bytes 213024 | tf_op jit(solution)/shard_map/ppermute | solution.py:105
  147.9 6.7 %collective-permute-done.17 = bf16[416,256]{1,0:T(8,128)(2,1)S(1)} collective-permute-done((bf16[416,256]{1,0:T(8,128)(2,1)S(1)}, bf16[416,256]{1,0:T(8,128)(2,1)S(1)}, u32[]{:S(2)}, u32[]{:S(2)}) %collective-permute-start.17) | collective-permute-done | bytes 213024 | tf_op jit(solution)/shard_map/ppermute | solution.py:105
  154.8 2.3 %fusion.4 = bf16[2,2,2,256,256]{4,3,2,1,0:T(8,128)(2,1)} fusion(bf16[2,2,2,256,256]{4,3,2,1,0:T(8,128)(2,1)S(1)} %get-tuple-element.6, f32[2,2,2,256,256]{4,3,2,1,0:T(8,128)S(1)} %fusion.17, f32[2,2,2,256,256]{4,3,2,1,0:T(8,128)S(1)} %fusion.35, f32[2,2,2,256,256]{4,3,2,1,0:T(8,128)S(1)} %fusion.37, f32[2,2,2,256,256]{4,3,2,1,0:T(8,128)S(1)} %fusion.87, ...), kind=kOutput, calls=%fused_computation.13 | convolution fusion | flops 275775488 | bytes 21104128 | tf_op jit(solution)/shard_map/dot_general | solution.py:180
  158.8 1.1 pad_maximum_fusion.3
  (100 shorter events, 25.3 us)
Async XLA Ops:
  0.6 82.1 %copy-start = (bf16[256,256]{1,0:T(8,128)(2,1)S(1)}, bf16[256,256]{1,0:T(8,128)(2,1)}, u32[]{:S(2)}) copy-start(bf16[256,256]{1,0:T(8,128)(2,1)} %param.11) | copy-start | bytes 393220
  0.6 3.5 %copy-start.6 = (bf16[2,2,2,256,256]{4,3,2,1,0:T(8,128)(2,1)S(1)}, bf16[2,2,2,256,256]{4,3,2,1,0:T(8,128)(2,1)}, u32[]{:S(2)}) copy-start(bf16[2,2,2,256,256]{4,3,2,1,0:T(8,128)(2,1)} %param.7) | copy-start | bytes 3145732
  3.7 14.1 %collective-permute-start = (bf16[2,2,1,256,256]{4,3,2,1,0:T(8,128)(2,1)}, bf16[2,2,1,256,256]{4,3,2,1,0:T(8,128)(2,1)}, u32[]{:S(2)}, u32[]{:S(2)}) collective-permute-start(bf16[2,2,1,256,256]{4,3,2,1,0:T(8,128)(2,1)} %slice_select_fusion.2), channel_id=1, source_target_pairs={{0,1},{1,0},{2,3},{3,2},{4,5},{5,4},{6,7},{7,6},{8,9},{9,8},{10,11... | collective-permute-start | bytes 1572872 | tf_op jit(solution)/shard_map/ppermute | solution.py:223
  5.6 28.2 %collective-permute-start.5 = (bf16[2,2,2,256,256]{4,3,2,1,0:T(8,128)(2,1)S(1)}, bf16[2,2,2,256,256]{4,3,2,1,0:T(8,128)(2,1)S(1)}, u32[]{:S(2)}, u32[]{:S(2)}) collective-permute-start(bf16[2,2,2,256,256]{4,3,2,1,0:T(8,128)(2,1)S(1)} %get-tuple-element.6), channel_id=1, source_target_pairs={{2,0},{4,2},{6,4},{8,6},{10,8},{12,10},{14,12},{3,1},{5,3},{7,5},{... | collective-permute-start | bytes 3145736 | tf_op jit(solution)/shard_map/ppermute | solution.py:10
  7.7 19.4 %collective-permute-start.2 = (bf16[2,2,256,256]{3,2,1,0:T(8,128)(2,1)}, bf16[2,2,256,256]{3,2,1,0:T(8,128)(2,1)}, u32[]{:S(2)}, u32[]{:S(2)}) collective-permute-start(bf16[2,2,256,256]{3,2,1,0:T(8,128)(2,1)} %slice_bitcast_fusion), channel_id=1, source_target_pairs={{0,8},{1,9},{16,24},{17,25}} | collective-permute-start | bytes 1572872 | tf_op jit(solution)/shard_map/ppermute | solution.py:21
  16.0 1.4 copy-start.5
  19.0 1.3 copy-start.4
  27.1 12.3 %collective-permute-start.3 = (bf16[2,2,256,256]{3,2,1,0:T(8,128)(2,1)S(1)}, bf16[2,2,256,256]{3,2,1,0:T(8,128)(2,1)S(1)}, u32[]{:S(2)}, u32[]{:S(2)}) collective-permute-start(bf16[2,2,256,256]{3,2,1,0:T(8,128)(2,1)S(1)} %broadcast_select_fusion.2), channel_id=1, source_target_pairs={{0,4},{8,12},{1,5},{9,13},{16,20},{24,28},{17,21},{25,29}} | collective-permute-start | bytes 1572872 | tf_op jit(solution)/shard_map/ppermute | solution.py:21
  30.0 51.7 %collective-permute-start.1 = (bf16[2,2,2,256,256]{4,3,2,1,0:T(8,128)(2,1)S(1)}, bf16[2,2,2,256,256]{4,3,2,1,0:T(8,128)(2,1)S(1)}, u32[]{:S(2)}, u32[]{:S(2)}) collective-permute-start(bf16[2,2,2,256,256]{4,3,2,1,0:T(8,128)(2,1)S(1)} %get-tuple-element.18), channel_id=1, source_target_pairs={{0,2},{2,4},{4,6},{6,8},{8,10},{10,12},{12,14},{1,3},{3,5},{5,7},{... | collective-permute-start | bytes 3145736 | tf_op jit(solution)/shard_map/ppermute | solution.py:10
  39.3 5.1 %copy-start.1 = (f32[2,2,256,256]{3,2,1,0:T(8,128)S(1)}, f32[2,2,256,256]{3,2,1,0:T(8,128)}, u32[]{:S(2)}) copy-start(f32[2,2,256,256]{3,2,1,0:T(8,128)} %get-tuple-element.5) | copy-start | bytes 3145732
  39.5 28.2 %collective-permute-start.4 = (bf16[2,2,256,256]{3,2,1,0:T(8,128)(2,1)S(1)}, bf16[2,2,256,256]{3,2,1,0:T(8,128)(2,1)S(1)}, u32[]{:S(2)}, u32[]{:S(2)}) collective-permute-start(bf16[2,2,256,256]{3,2,1,0:T(8,128)(2,1)S(1)} %broadcast_select_fusion.3), channel_id=1, source_target_pairs={{0,2},{4,6},{8,10},{12,14},{1,3},{5,7},{9,11},{13,15},{16,18},{20,... | collective-permute-start | bytes 1572872 | tf_op jit(solution)/shard_map/ppermute | solution.py:21
  44.6 34.0 %collective-permute-start.7 = (f32[1,2,256,256]{3,2,1,0:T(8,128)S(1)}, f32[1,2,256,256]{3,2,1,0:T(8,128)S(1)}, u32[]{:S(2)}, u32[]{:S(2)}) collective-permute-start(f32[1,2,256,256]{3,2,1,0:T(8,128)S(1)} %slice_select_fusion), channel_id=1, source_target_pairs={{4,0},{6,2},{12,8},{14,10},{5,1},{7,3},{13,9},{15,11},{20,16},{22,... | collective-permute-start | bytes 1572872 | tf_op jit(solution)/shard_map/ppermute | solution.py:51
  45.9 34.3 %collective-permute-start.6 = (bf16[2,2,1,256,256]{4,3,2,1,0:T(8,128)(2,1)S(1)}, bf16[2,2,1,256,256]{4,3,2,1,0:T(8,128)(2,1)S(1)}, u32[]{:S(2)}, u32[]{:S(2)}) collective-permute-start(bf16[2,2,1,256,256]{4,3,2,1,0:T(8,128)(2,1)S(1)} %slice_select_fusion.1), channel_id=1, source_target_pairs={{0,1},{1,0},{2,3},{3,2},{4,5},{5,4},{6,7},{7,6},{8,9},{9,8},{10,11... | collective-permute-start | bytes 1572872 | tf_op jit(solution)/shard_map/ppermute | solution.py:223
  68.8 16.6 %collective-permute-start.10 = (f32[1664,256]{1,0:T(8,128)S(1)}, f32[1664,256]{1,0:T(8,128)S(1)}, u32[]{:S(2)}, u32[]{:S(2)}) collective-permute-start(f32[1664,256]{1,0:T(8,128)S(1)} %constant_dynamic-slice_fusion.4), channel_id=1, source_target_pairs={{0,1},{1,0},{2,3},{3,2},{4,5},{5,4},{6,7},{7,6},{8,9},{9,8},{10,11... | collective-permute-start | bytes 5111816 | tf_op jit(solution)/shard_map/ppermute | solution.py:66
  78.8 36.0 %collective-permute-start.8 = (f32[1,2,256,256]{3,2,1,0:T(8,128)S(1)}, f32[1,2,256,256]{3,2,1,0:T(8,128)S(1)}, u32[]{:S(2)}, u32[]{:S(2)}) collective-permute-start(f32[1,2,256,256]{3,2,1,0:T(8,128)S(1)} %fusion.167), channel_id=1, source_target_pairs={{8,0},{10,2},{9,1},{11,3},{24,16},{26,18},{25,17},{27,19}} | collective-permute-start | bytes 1572872 | tf_op jit(solution)/shard_map/ppermute | solution.py:51
  81.7 1.0 copy-start.2
  85.6 6.7 %copy-start.3 = (bf16[2,2,2,256,256]{4,3,2,1,0:T(8,128)(2,1)S(1)}, bf16[2,2,2,256,256]{4,3,2,1,0:T(8,128)(2,1)}, u32[]{:S(2)}) copy-start(bf16[2,2,2,256,256]{4,3,2,1,0:T(8,128)(2,1)} %copy-done.2) | copy-start | bytes 3145732
  85.7 30.4 %collective-permute-start.11 = (f32[416,256]{1,0:T(8,128)S(1)}, f32[416,256]{1,0:T(8,128)S(1)}, u32[]{:S(2)}, u32[]{:S(2)}) collective-permute-start(f32[416,256]{1,0:T(8,128)S(1)} %get-tuple-element.11), channel_id=1, source_target_pairs={{0,4},{2,6},{4,8},{6,10},{8,12},{10,14},{12,0},{14,2},{1,5},{3,7},... | collective-permute-start | bytes 1277960 | tf_op jit(solution)/shard_map/ppermute | solution.py:92
  85.8 38.0 %collective-permute-start.12 = (f32[416,256]{1,0:T(8,128)S(1)}, f32[416,256]{1,0:T(8,128)S(1)}, u32[]{:S(2)}, u32[]{:S(2)}) collective-permute-start(f32[416,256]{1,0:T(8,128)S(1)} %get-tuple-element.13), channel_id=1, source_target_pairs={{0,8},{2,10},{4,12},{6,14},{8,0},{10,2},{12,4},{14,6},{1,9},{3,11}... | collective-permute-start | bytes 1277960 | tf_op jit(solution)/shard_map/ppermute | solution.py:92
  89.5 34.4 %collective-permute-start.13 = (f32[416,256]{1,0:T(8,128)S(1)}, f32[416,256]{1,0:T(8,128)S(1)}, u32[]{:S(2)}, u32[]{:S(2)}) collective-permute-start(f32[416,256]{1,0:T(8,128)S(1)} %get-tuple-element.12), channel_id=1, source_target_pairs={{0,12},{2,14},{4,0},{6,2},{8,4},{10,6},{12,8},{14,10},{1,13},{3,15... | collective-permute-start | bytes 1277960 | tf_op jit(solution)/shard_map/ppermute | solution.py:92
  114.8 17.3 %collective-permute-start.9 = (f32[1,2,256,256]{3,2,1,0:T(8,128)S(1)}, f32[1,2,256,256]{3,2,1,0:T(8,128)S(1)}, u32[]{:S(2)}, u32[]{:S(2)}) collective-permute-start(f32[1,2,256,256]{3,2,1,0:T(8,128)S(1)} %add.249), channel_id=1, source_target_pairs={{2,0},{3,1},{18,16},{19,17}} | collective-permute-start | bytes 1572872 | tf_op jit(solution)/shard_map/ppermute | solution.py:53
  124.0 8.0 %collective-permute-start.14 = (f32[208,256]{1,0:T(8,128)S(1)}, f32[208,256]{1,0:T(8,128)S(1)}, u32[]{:S(2)}, u32[]{:S(2)}) collective-permute-start(f32[208,256]{1,0:T(8,128)S(1)} %constant_dynamic-slice_fusion), channel_id=1, source_target_pairs={{0,2},{2,0},{4,6},{6,4},{8,10},{10,8},{12,14},{14,12},{1,3},{3,1},... | collective-permute-start | bytes 638984 | tf_op jit(solution)/shard_map/ppermute | solution.py:66
  132.0 4.8 %collective-permute-start.15 = (bf16[208,256]{1,0:T(8,128)(2,1)S(1)}, bf16[208,256]{1,0:T(8,128)(2,1)S(1)}, u32[]{:S(2)}, u32[]{:S(2)}) collective-permute-start(bf16[208,256]{1,0:T(8,128)(2,1)S(1)} %multiply_convert_fusion.3), channel_id=1, source_target_pairs={{0,2},{2,0},{4,6},{6,4},{8,10},{10,8},{12,14},{14,12},{1,3},{3,1},... | collective-permute-start | bytes 319496 | tf_op jit(solution)/shard_map/ppermute | solution.py:74
  136.8 11.1 %collective-permute-start.16 = (bf16[416,256]{1,0:T(8,128)(2,1)S(1)}, bf16[416,256]{1,0:T(8,128)(2,1)S(1)}, u32[]{:S(2)}, u32[]{:S(2)}) collective-permute-start(bf16[416,256]{1,0:T(8,128)(2,1)S(1)} %maximum_select_fusion.1), channel_id=1, source_target_pairs={{0,4},{2,6},{4,8},{6,10},{8,12},{10,14},{12,0},{14,2},{1,5},{3,7},... | collective-permute-start | bytes 638984 | tf_op jit(solution)/shard_map/ppermute | solution.py:105
  143.5 11.2 %collective-permute-start.17 = (bf16[416,256]{1,0:T(8,128)(2,1)S(1)}, bf16[416,256]{1,0:T(8,128)(2,1)S(1)}, u32[]{:S(2)}, u32[]{:S(2)}) collective-permute-start(bf16[416,256]{1,0:T(8,128)(2,1)S(1)} %maximum_select_fusion.1), channel_id=1, source_target_pairs={{0,8},{2,10},{4,12},{6,14},{8,0},{10,2},{12,4},{14,6},{1,9},{3,11}... | collective-permute-start | bytes 638984 | tf_op jit(solution)/shard_map/ppermute | solution.py:105
  143.5 11.1 %collective-permute-start.18 = (bf16[416,256]{1,0:T(8,128)(2,1)S(1)}, bf16[416,256]{1,0:T(8,128)(2,1)S(1)}, u32[]{:S(2)}, u32[]{:S(2)}) collective-permute-start(bf16[416,256]{1,0:T(8,128)(2,1)S(1)} %maximum_select_fusion.1), channel_id=1, source_target_pairs={{0,12},{2,14},{4,0},{6,2},{8,4},{10,6},{12,8},{14,10},{1,13},{3,15... | collective-permute-start | bytes 638984 | tf_op jit(solution)/shard_map/ppermute | solution.py:105
  154.7 2.4 %collective-permute-start.19 = (bf16[1664,256]{1,0:T(8,128)(2,1)S(1)}, bf16[1664,256]{1,0:T(8,128)(2,1)S(1)}, u32[]{:S(2)}, u32[]{:S(2)}) collective-permute-start(bf16[1664,256]{1,0:T(8,128)(2,1)S(1)} %bitcast.256), channel_id=1, source_target_pairs={{0,1},{1,0},{2,3},{3,2},{4,5},{5,4},{6,7},{7,6},{8,9},{9,8},{10,11... | collective-permute-start | bytes 2555912 | tf_op jit(solution)/shard_map/ppermute | solution.py:151

commit v19 on v18

--- a/solution.py
+++ b/solution.py
@@ -31,6 +31,33 @@
         value = value + lax.ppermute(value, axis, pairs)
         step *= 2
     return value
+
+
+def two_column_broadcast(value, axis):
+    count = lax.axis_size(axis)
+    me = lax.axis_index(axis)
+    half = value.shape[0] // 2
+    odd = me % 2 == 1
+    hop = lax.ppermute(value[half:], axis, [(0, 1)])
+    part = jnp.where(odd, hop, value[:half])
+    n = count // 2
+    step = 1
+    while step * 2 < n:
+        step *= 2
+    while step >= 1:
+        pairs = []
+        for i in range(0, n, 2 * step):
+            if i + step < n:
+                pairs.append((2 * i, 2 * (i + step)))
+                if 2 * (i + step) + 1 < count:
+                    pairs.append((2 * i + 1, 2 * (i + step) + 1))
+        got = lax.ppermute(part, axis, pairs)
+        part = jnp.where((me // 2) % (2 * step) == step, got, part)
+        step //= 2
+    other = lax.ppermute(part, axis, [(i, i ^ 1) for i in range(count)])
+    return jnp.where(
+        odd, jnp.concatenate([other, part], 0), jnp.concatenate([part, other], 0)
+    )
 
 
 def two_column_sum(pair, local, axis):
@@ -238,7 +265,10 @@
     mask_f = mask.astype(jnp.float32)
     masked = latents * mask
     cot = cotangent * mask
-    first = tree_broadcast(masked[:, 0], "space")
+    if clips % 2 == 0 and lax.axis_size("space") >= 4 and lax.axis_size("space") % 2 == 0:
+        first = two_column_broadcast(masked[:, 0], "space")
+    else:
+        first = tree_broadcast(masked[:, 0], "space")
     cot_local = jnp.sum(cot, axis=1, dtype=jnp.float32)
     later = shifted(cot, "space", -1)
     if lax.axis_size("space") % 2 == 0:

time: 162 us -> 173 us (1.068)
  the two profiles are of different devices: /device:TPU:0 before, /device:TPU:25 now
where the time goes in v19:
time: 173 us; the launch traced here: 172 us
  waiting for transfers between devices  93.8 us (54%)
  starting transfers between devices  37.1 us (21%)
  matrix products  26.4 us (15%)
  other arithmetic  10.1 us (6%)
  local copies, waits for them, and re-layouts  3.81 us (2%)
    ppermute x3, waiting for transfers between devices, direct_scatter(): total = total + lax.ppermute(send, axis, pairs)  32.6 us
    ppermute x2, waiting for transfers between devices, two_column_broadcast(): got = lax.ppermute(part, axis, pairs)  25.5 us
    ppermute x1, waiting for transfers between devices, two_column_broadcast(): other = lax.ppermute(part, axis, [(i, i ^ 1) for i in range(count)])  14.9 us
    ppermute x3, waiting for transfers between devices, direct_gather(): got = lax.ppermute(piece, axis, pairs)  14.2 us
    dot_general x18, matrix products, spatial_sum(): total = total + jnp.dot(piece, kernel, preferred_element_type=jnp.float32)  13.2 us
    ppermute x3, starting transfers between devices, direct_gather(): got = lax.ppermute(piece, axis, pairs)  7.68 us
    ppermute x2, starting transfers between devices, shifted(): return lax.ppermute(value, axis, pairs)  6.44 us
    dot_general x9, matrix products, on_device(): lax.dot_general(piece, dpre, dims, preferred_element_type=jnp.float32)  4.41 us
  transfers between devices with their start and end apart: 21, of which 7 were waited for; matrix products, arithmetic and copies ran while one was open for 19% of the time, Pallas kernels for 0%

profile of v19, /device:TPU:25, one launch (start us, length us, event | category | flops | bytes accessed | tf_op | source)
XLA Modules:
  0.0 172.4 jit_solution(1475578479495979615)
XLA Ops:
  1.5 1.4 broadcast_multiply_fusion.1
  4.4 1.4 convert_reduce_fusion
  5.8 3.0 %collective-permute-start.6 = (bf16[2,2,2,256,256]{4,3,2,1,0:T(8,128)(2,1)S(1)}, bf16[2,2,2,256,256]{4,3,2,1,0:T(8,128)(2,1)S(1)}, u32[]{:S(2)}, u32[]{:S(2)}) collective-permute-start(bf16[2,2,2,256,256]{4,3,2,1,0:T(8,128)(2,1)S(1)} %get-tuple-element.6), channel_id=1, source_target_pairs={{2,0},{4,2},{6,4},{8,6},{10,8},{12,10},{14,12},{3,1},{5,3},{7,5},{... | collective-permute-start | bytes 3145736 | tf_op jit(solution)/shard_map/ppermute | solution.py:10
  8.8 1.4 collective-permute-start.2
  10.2 2.7 %fusion.90 = f32[2,2,2,256,256]{4,3,2,1,0:T(8,128)} fusion(bf16[2,2,2,256,256]{4,3,2,1,0:T(8,128)(2,1)S(1)} %broadcast_multiply_fusion.1, bf16[9,256,256]{2,1,0:T(8,128)(2,1)} %param.9), kind=kOutput, calls=%fused_computation.141 | convolution fusion | flops 268435456 | bytes 3276800 | tf_op jit(solution)/shard_map/dot_general | solution.py:207
  12.9 1.4 fusion.107
  15.0 1.1 broadcast_select_fusion.5
  20.5 1.4 collective-permute-start.4
  22.0 1.4 multiply_convert_fusion.2
  23.4 3.4 %collective-permute-start.1 = (bf16[2,2,2,256,256]{4,3,2,1,0:T(8,128)(2,1)S(1)}, bf16[2,2,2,256,256]{4,3,2,1,0:T(8,128)(2,1)S(1)}, u32[]{:S(2)}, u32[]{:S(2)}) collective-permute-start(bf16[2,2,2,256,256]{4,3,2,1,0:T(8,128)(2,1)S(1)} %get-tuple-element.18), channel_id=1, source_target_pairs={{0,2},{2,4},{4,6},{6,8},{8,10},{10,12},{12,14},{1,3},{3,5},{5,7},{... | collective-permute-start | bytes 3145736 | tf_op jit(solution)/shard_map/ppermute | solution.py:10
  27.8 25.5 %collective-permute-done.4 = bf16[1,2,256,256]{3,2,1,0:T(8,128)(2,1)S(1)} collective-permute-done((bf16[1,2,256,256]{3,2,1,0:T(8,128)(2,1)S(1)}, bf16[1,2,256,256]{3,2,1,0:T(8,128)(2,1)S(1)}, u32[]{:S(2)}, u32[]{:S(2)}) %collective-permute-start.4) | collective-permute-done | bytes 262176 | tf_op jit(solution)/shard_map/ppermute | solution.py:54
  53.3 3.4 %collective-permute-start.5 = (bf16[1,2,256,256]{3,2,1,0:T(8,128)(2,1)S(1)}, bf16[1,2,256,256]{3,2,1,0:T(8,128)(2,1)S(1)}, u32[]{:S(2)}, u32[]{:S(2)}) collective-permute-start(bf16[1,2,256,256]{3,2,1,0:T(8,128)(2,1)S(1)} %broadcast_select_fusion.7), channel_id=1, source_target_pairs={{0,2},{2,0},{4,6},{6,4},{8,10},{10,8},{12,14},{14,12},{1,3},{3,1},... | collective-permute-start | bytes 786440 | tf_op jit(solution)/shard_map/ppermute | solution.py:57
  57.1 1.1 multiply_convert_fusion
  63.7 1.3 collective-permute-start.8
  65.1 3.2 %collective-permute-start.7 = (bf16[2,2,1,256,256]{4,3,2,1,0:T(8,128)(2,1)S(1)}, bf16[2,2,1,256,256]{4,3,2,1,0:T(8,128)(2,1)S(1)}, u32[]{:S(2)}, u32[]{:S(2)}) collective-permute-start(bf16[2,2,1,256,256]{4,3,2,1,0:T(8,128)(2,1)S(1)} %slice_select_fusion.1), channel_id=1, source_target_pairs={{0,1},{1,0},{2,3},{3,2},{4,5},{5,4},{6,7},{7,6},{8,9},{9,8},{10,11... | collective-permute-start | bytes 1572872 | tf_op jit(solution)/shard_map/ppermute | solution.py:250
  69.8 14.9 %collective-permute-done.5 = bf16[1,2,256,256]{3,2,1,0:T(8,128)(2,1)S(1)} collective-permute-done((bf16[1,2,256,256]{3,2,1,0:T(8,128)(2,1)S(1)}, bf16[1,2,256,256]{3,2,1,0:T(8,128)(2,1)S(1)}, u32[]{:S(2)}, u32[]{:S(2)}) %collective-permute-start.5) | collective-permute-done | bytes 262176 | tf_op jit(solution)/shard_map/ppermute | solution.py:57
  85.9 1.0 collective-permute-start.11
  89.6 1.0 copy-done.3
  94.0 1.4 collective-permute-start.14
  95.3 1.7 %multiply_convert_fusion.1 = bf16[2,2,2,256,256]{4,3,2,1,0:T(8,128)(2,1)} fusion(f32[2,2,2,256,256]{4,3,2,1,0:T(8,128)S(1)} %fusion.109, f32[2,2,2,256,256]{4,3,2,1,0:T(8,128)S(1)} %fusion.5, bf16[2,2,2,256,256]{4,3,2,1,0:T(8,128)(2,1)S(1)} %broadcast_multiply_fusion.1, f32[2,2]{1,0:T(2,128)S(1)} %get-tuple-element.7, f32[2,2,256,256]{3,2,1,0:T(8,128)S(1)} %fusion.74, ...), kind=kOutput, calls=%fused_computation.24 | convolution fusion | flops 272105472 | bytes 8520704 | tf_op jit(solution)/shard_map/dot_general | solution.py:214
  97.8 8.6 %collective-permute-done.12 = f32[416,256]{1,0:T(8,128)S(1)} collective-permute-done((f32[416,256]{1,0:T(8,128)S(1)}, f32[416,256]{1,0:T(8,128)S(1)}, u32[]{:S(2)}, u32[]{:S(2)}) %collective-permute-start.12) | collective-permute-done | bytes 426016 | tf_op jit(solution)/shard_map/ppermute | solution.py:119
  106.4 24.1 %collective-permute-done.13 = f32[416,256]{1,0:T(8,128)S(1)} collective-permute-done((f32[416,256]{1,0:T(8,128)S(1)}, f32[416,256]{1,0:T(8,128)S(1)}, u32[]{:S(2)}, u32[]{:S(2)}) %collective-permute-start.13) | collective-permute-done | bytes 426016 | tf_op jit(solution)/shard_map/ppermute | solution.py:119
  130.6 2.2 %collective-permute-start.15 = (f32[208,256]{1,0:T(8,128)S(1)}, f32[208,256]{1,0:T(8,128)S(1)}, u32[]{:S(2)}, u32[]{:S(2)}) collective-permute-start(f32[208,256]{1,0:T(8,128)S(1)} %constant_dynamic-slice_fusion), channel_id=1, source_target_pairs={{0,2},{2,0},{4,6},{6,4},{8,10},{10,8},{12,14},{14,12},{1,3},{3,1},... | collective-permute-start | bytes 638984 | tf_op jit(solution)/shard_map/ppermute | solution.py:93
  133.3 4.1 %collective-permute-done.15 = f32[208,256]{1,0:T(8,128)S(1)} collective-permute-done((f32[208,256]{1,0:T(8,128)S(1)}, f32[208,256]{1,0:T(8,128)S(1)}, u32[]{:S(2)}, u32[]{:S(2)}) %collective-permute-start.15) | collective-permute-done | bytes 213024 | tf_op jit(solution)/shard_map/ppermute | solution.py:93
  137.5 1.2 collective-permute-start.16
  138.8 2.3 %collective-permute-done.16 = bf16[208,256]{1,0:T(8,128)(2,1)S(1)} collective-permute-done((bf16[208,256]{1,0:T(8,128)(2,1)S(1)}, bf16[208,256]{1,0:T(8,128)(2,1)S(1)}, u32[]{:S(2)}, u32[]{:S(2)}) %collective-permute-start.16) | collective-permute-done | bytes 106528 | tf_op jit(solution)/shard_map/ppermute | solution.py:101
  142.5 5.5 %collective-permute-start.18 = (bf16[416,256]{1,0:T(8,128)(2,1)S(1)}, bf16[416,256]{1,0:T(8,128)(2,1)S(1)}, u32[]{:S(2)}, u32[]{:S(2)}) collective-permute-start(bf16[416,256]{1,0:T(8,128)(2,1)S(1)} %maximum_select_fusion.2), channel_id=1, source_target_pairs={{0,8},{2,10},{4,12},{6,14},{8,0},{10,2},{12,4},{14,6},{1,9},{3,11}... | collective-permute-start | bytes 638984 | tf_op jit(solution)/shard_map/ppermute | solution.py:132
  148.1 1.4 collective-permute-start.19
  149.7 14.2 %collective-permute-done.18 = bf16[416,256]{1,0:T(8,128)(2,1)S(1)} collective-permute-done((bf16[416,256]{1,0:T(8,128)(2,1)S(1)}, bf16[416,256]{1,0:T(8,128)(2,1)S(1)}, u32[]{:S(2)}, u32[]{:S(2)}) %collective-permute-start.18) | collective-permute-done | bytes 213024 | tf_op jit(solution)/shard_map/ppermute | solution.py:132
  164.0 3.4 %collective-permute-start.20 = (bf16[1664,256]{1,0:T(8,128)(2,1)S(1)}, bf16[1664,256]{1,0:T(8,128)(2,1)S(1)}, u32[]{:S(2)}, u32[]{:S(2)}) collective-permute-start(bf16[1664,256]{1,0:T(8,128)(2,1)S(1)} %bitcast.258), channel_id=1, source_target_pairs={{0,1},{1,0},{2,3},{3,2},{4,5},{5,4},{6,7},{7,6},{8,9},{9,8},{10,11... | collective-permute-start | bytes 2555912 | tf_op jit(solution)/shard_map/ppermute | solution.py:178
  167.4 2.3 %fusion.4 = bf16[2,2,2,256,256]{4,3,2,1,0:T(8,128)(2,1)} fusion(bf16[2,2,2,256,256]{4,3,2,1,0:T(8,128)(2,1)S(1)} %get-tuple-element.6, f32[2,2,2,256,256]{4,3,2,1,0:T(8,128)S(1)} %fusion.17, f32[2,2,2,256,256]{4,3,2,1,0:T(8,128)S(1)} %fusion.35, f32[2,2,2,256,256]{4,3,2,1,0:T(8,128)S(1)} %fusion.37, f32[2,2,2,256,256]{4,3,2,1,0:T(8,128)S(1)} %fusion.88, ...), kind=kOutput, calls=%fused_computation.13 | convolution fusion | flops 275775488 | bytes 21104128 | tf_op jit(solution)/shard_map/dot_general | solution.py:207
  171.3 1.1 pad_maximum_fusion.3
  (105 shorter events, 27.6 us)
Async XLA Ops:
  0.6 86.2 %copy-start = (bf16[256,256]{1,0:T(8,128)(2,1)S(1)}, bf16[256,256]{1,0:T(8,128)(2,1)}, u32[]{:S(2)}) copy-start(bf16[256,256]{1,0:T(8,128)(2,1)} %param.11) | copy-start | bytes 393220
  0.6 3.7 %copy-start.7 = (bf16[2,2,2,256,256]{4,3,2,1,0:T(8,128)(2,1)S(1)}, bf16[2,2,2,256,256]{4,3,2,1,0:T(8,128)(2,1)}, u32[]{:S(2)}) copy-start(bf16[2,2,2,256,256]{4,3,2,1,0:T(8,128)(2,1)} %param.7) | copy-start | bytes 3145732
  3.7 11.3 %collective-permute-start = (bf16[2,2,1,256,256]{4,3,2,1,0:T(8,128)(2,1)}, bf16[2,2,1,256,256]{4,3,2,1,0:T(8,128)(2,1)}, u32[]{:S(2)}, u32[]{:S(2)}) collective-permute-start(bf16[2,2,1,256,256]{4,3,2,1,0:T(8,128)(2,1)} %slice_select_fusion.2), channel_id=1, source_target_pairs={{0,1},{1,0},{2,3},{3,2},{4,5},{5,4},{6,7},{7,6},{8,9},{9,8},{10,11... | collective-permute-start | bytes 1572872 | tf_op jit(solution)/shard_map/ppermute | solution.py:250
  5.8 50.9 %collective-permute-start.6 = (bf16[2,2,2,256,256]{4,3,2,1,0:T(8,128)(2,1)S(1)}, bf16[2,2,2,256,256]{4,3,2,1,0:T(8,128)(2,1)S(1)}, u32[]{:S(2)}, u32[]{:S(2)}) collective-permute-start(bf16[2,2,2,256,256]{4,3,2,1,0:T(8,128)(2,1)S(1)} %get-tuple-element.6), channel_id=1, source_target_pairs={{2,0},{4,2},{6,4},{8,6},{10,8},{12,10},{14,12},{3,1},{5,3},{7,5},{... | collective-permute-start | bytes 3145736 | tf_op jit(solution)/shard_map/ppermute | solution.py:10
  8.8 5.5 %collective-permute-start.2 = (bf16[1,2,256,256]{3,2,1,0:T(8,128)(2,1)S(1)}, bf16[1,2,256,256]{3,2,1,0:T(8,128)(2,1)}, u32[]{:S(2)}, u32[]{:S(2)}) collective-permute-start(bf16[1,2,256,256]{3,2,1,0:T(8,128)(2,1)S(1)} %slice_bitcast_fusion.1), channel_id=1, source_target_pairs={{0,2},{1,3},{16,18},{17,19}} | collective-permute-start | bytes 786440 | tf_op jit(solution)/shard_map/ppermute | solution.py:41
  14.3 6.2 %collective-permute-start.3 = (bf16[1,2,256,256]{3,2,1,0:T(8,128)(2,1)S(1)}, bf16[1,2,256,256]{3,2,1,0:T(8,128)(2,1)S(1)}, u32[]{:S(2)}, u32[]{:S(2)}) collective-permute-start(bf16[1,2,256,256]{3,2,1,0:T(8,128)(2,1)S(1)} %fusion.71), channel_id=1, source_target_pairs={{0,8},{2,10},{1,9},{3,11},{16,24},{18,26},{17,25},{19,27}} | collective-permute-start | bytes 786440 | tf_op jit(solution)/shard_map/ppermute | solution.py:54
  16.1 1.3 copy-start.5
  20.0 1.9 %copy-start.1 = (f32[2,2,2,256,256]{4,3,2,1,0:T(8,128)S(1)}, f32[2,2,2,256,256]{4,3,2,1,0:T(8,128)}, u32[]{:S(2)}) copy-start(f32[2,2,2,256,256]{4,3,2,1,0:T(8,128)} %fusion.90) | copy-start | bytes 6291460
  20.5 6.3 %copy-start.6 = (bf16[3,256,256]{2,1,0:T(8,128)(2,1)S(1)}, bf16[3,256,256]{2,1,0:T(8,128)(2,1)}, u32[]{:S(2)}) copy-start(bf16[3,256,256]{2,1,0:T(8,128)(2,1)} %param.10) | copy-start | bytes 1179652
  20.5 32.7 %collective-permute-start.4 = (bf16[1,2,256,256]{3,2,1,0:T(8,128)(2,1)S(1)}, bf16[1,2,256,256]{3,2,1,0:T(8,128)(2,1)S(1)}, u32[]{:S(2)}, u32[]{:S(2)}) collective-permute-start(bf16[1,2,256,256]{3,2,1,0:T(8,128)(2,1)S(1)} %broadcast_select_fusion.6), channel_id=1, source_target_pairs={{0,4},{2,6},{8,12},{10,14},{1,5},{3,7},{9,13},{11,15},{16,20},{18,... | collective-permute-start | bytes 786440 | tf_op jit(solution)/shard_map/ppermute | solution.py:54
  23.4 66.2 %collective-permute-start.1 = (bf16[2,2,2,256,256]{4,3,2,1,0:T(8,128)(2,1)S(1)}, bf16[2,2,2,256,256]{4,3,2,1,0:T(8,128)(2,1)S(1)}, u32[]{:S(2)}, u32[]{:S(2)}) collective-permute-start(bf16[2,2,2,256,256]{4,3,2,1,0:T(8,128)(2,1)S(1)} %get-tuple-element.18), channel_id=1, source_target_pairs={{0,2},{2,4},{4,6},{6,8},{8,10},{10,12},{12,14},{1,3},{3,5},{5,7},{... | collective-permute-start | bytes 3145736 | tf_op jit(solution)/shard_map/ppermute | solution.py:10
  53.3 31.4 %collective-permute-start.5 = (bf16[1,2,256,256]{3,2,1,0:T(8,128)(2,1)S(1)}, bf16[1,2,256,256]{3,2,1,0:T(8,128)(2,1)S(1)}, u32[]{:S(2)}, u32[]{:S(2)}) collective-permute-start(bf16[1,2,256,256]{3,2,1,0:T(8,128)(2,1)S(1)} %broadcast_select_fusion.7), channel_id=1, source_target_pairs={{0,2},{2,0},{4,6},{6,4},{8,10},{10,8},{12,14},{14,12},{1,3},{3,1},... | collective-permute-start | bytes 786440 | tf_op jit(solution)/shard_map/ppermute | solution.py:57
  62.3 1.2 copy-start.2
  63.7 23.4 %collective-permute-start.8 = (f32[1,2,256,256]{3,2,1,0:T(8,128)S(1)}, f32[1,2,256,256]{3,2,1,0:T(8,128)S(1)}, u32[]{:S(2)}, u32[]{:S(2)}) collective-permute-start(f32[1,2,256,256]{3,2,1,0:T(8,128)S(1)} %slice_select_fusion), channel_id=1, source_target_pairs={{4,0},{6,2},{12,8},{14,10},{5,1},{7,3},{13,9},{15,11},{20,16},{22,... | collective-permute-start | bytes 1572872 | tf_op jit(solution)/shard_map/ppermute | solution.py:78
  65.1 23.1 %collective-permute-start.7 = (bf16[2,2,1,256,256]{4,3,2,1,0:T(8,128)(2,1)S(1)}, bf16[2,2,1,256,256]{4,3,2,1,0:T(8,128)(2,1)S(1)}, u32[]{:S(2)}, u32[]{:S(2)}) collective-permute-start(bf16[2,2,1,256,256]{4,3,2,1,0:T(8,128)(2,1)S(1)} %slice_select_fusion.1), channel_id=1, source_target_pairs={{0,1},{1,0},{2,3},{3,2},{4,5},{5,4},{6,7},{7,6},{8,9},{9,8},{10,11... | collective-permute-start | bytes 1572872 | tf_op jit(solution)/shard_map/ppermute | solution.py:250
  85.9 7.6 %collective-permute-start.11 = (f32[1664,256]{1,0:T(8,128)S(1)}, f32[1664,256]{1,0:T(8,128)S(1)}, u32[]{:S(2)}, u32[]{:S(2)}) collective-permute-start(f32[1664,256]{1,0:T(8,128)S(1)} %constant_dynamic-slice_fusion.4), channel_id=1, source_target_pairs={{0,1},{1,0},{2,3},{3,2},{4,5},{5,4},{6,7},{7,6},{8,9},{9,8},{10,11... | collective-permute-start | bytes 5111816 | tf_op jit(solution)/shard_map/ppermute | solution.py:93
  87.3 9.8 %collective-permute-start.9 = (f32[1,2,256,256]{3,2,1,0:T(8,128)S(1)}, f32[1,2,256,256]{3,2,1,0:T(8,128)S(1)}, u32[]{:S(2)}, u32[]{:S(2)}) collective-permute-start(f32[1,2,256,256]{3,2,1,0:T(8,128)S(1)} %fusion.170), channel_id=1, source_target_pairs={{8,0},{10,2},{9,1},{11,3},{24,16},{26,18},{25,17},{27,19}} | collective-permute-start | bytes 1572872 | tf_op jit(solution)/shard_map/ppermute | solution.py:78
  89.6 1.0 copy-start.3
  93.7 1.6 copy-start.4
  93.8 12.6 %collective-permute-start.12 = (f32[416,256]{1,0:T(8,128)S(1)}, f32[416,256]{1,0:T(8,128)S(1)}, u32[]{:S(2)}, u32[]{:S(2)}) collective-permute-start(f32[416,256]{1,0:T(8,128)S(1)} %get-tuple-element.11), channel_id=1, source_target_pairs={{0,4},{2,6},{4,8},{6,10},{8,12},{10,14},{12,0},{14,2},{1,5},{3,7},... | collective-permute-start | bytes 1277960 | tf_op jit(solution)/shard_map/ppermute | solution.py:119
  93.9 36.6 %collective-permute-start.13 = (f32[416,256]{1,0:T(8,128)S(1)}, f32[416,256]{1,0:T(8,128)S(1)}, u32[]{:S(2)}, u32[]{:S(2)}) collective-permute-start(f32[416,256]{1,0:T(8,128)S(1)} %get-tuple-element.13), channel_id=1, source_target_pairs={{0,8},{2,10},{4,12},{6,14},{8,0},{10,2},{12,4},{14,6},{1,9},{3,11}... | collective-permute-start | bytes 1277960 | tf_op jit(solution)/shard_map/ppermute | solution.py:119
  94.0 36.5 %collective-permute-start.14 = (f32[416,256]{1,0:T(8,128)S(1)}, f32[416,256]{1,0:T(8,128)S(1)}, u32[]{:S(2)}, u32[]{:S(2)}) collective-permute-start(f32[416,256]{1,0:T(8,128)S(1)} %get-tuple-element.12), channel_id=1, source_target_pairs={{0,12},{2,14},{4,0},{6,2},{8,4},{10,6},{12,8},{14,10},{1,13},{3,15... | collective-permute-start | bytes 1277960 | tf_op jit(solution)/shard_map/ppermute | solution.py:119
  97.1 41.6 %collective-permute-start.10 = (f32[1,2,256,256]{3,2,1,0:T(8,128)S(1)}, f32[1,2,256,256]{3,2,1,0:T(8,128)S(1)}, u32[]{:S(2)}, u32[]{:S(2)}) collective-permute-start(f32[1,2,256,256]{3,2,1,0:T(8,128)S(1)} %add.249), channel_id=1, source_target_pairs={{2,0},{3,1},{18,16},{19,17}} | collective-permute-start | bytes 1572872 | tf_op jit(solution)/shard_map/ppermute | solution.py:80
  130.6 6.8 %collective-permute-start.15 = (f32[208,256]{1,0:T(8,128)S(1)}, f32[208,256]{1,0:T(8,128)S(1)}, u32[]{:S(2)}, u32[]{:S(2)}) collective-permute-start(f32[208,256]{1,0:T(8,128)S(1)} %constant_dynamic-slice_fusion), channel_id=1, source_target_pairs={{0,2},{2,0},{4,6},{6,4},{8,10},{10,8},{12,14},{14,12},{1,3},{3,1},... | collective-permute-start | bytes 638984 | tf_op jit(solution)/shard_map/ppermute | solution.py:93
  137.5 3.6 %collective-permute-start.16 = (bf16[208,256]{1,0:T(8,128)(2,1)S(1)}, bf16[208,256]{1,0:T(8,128)(2,1)S(1)}, u32[]{:S(2)}, u32[]{:S(2)}) collective-permute-start(bf16[208,256]{1,0:T(8,128)(2,1)S(1)} %multiply_convert_fusion.3), channel_id=1, source_target_pairs={{0,2},{2,0},{4,6},{6,4},{8,10},{10,8},{12,14},{14,12},{1,3},{3,1},... | collective-permute-start | bytes 319496 | tf_op jit(solution)/shard_map/ppermute | solution.py:101
  141.2 8.5 %collective-permute-start.17 = (bf16[416,256]{1,0:T(8,128)(2,1)S(1)}, bf16[416,256]{1,0:T(8,128)(2,1)S(1)}, u32[]{:S(2)}, u32[]{:S(2)}) collective-permute-start(bf16[416,256]{1,0:T(8,128)(2,1)S(1)} %maximum_select_fusion.2), channel_id=1, source_target_pairs={{0,4},{2,6},{4,8},{6,10},{8,12},{10,14},{12,0},{14,2},{1,5},{3,7},... | collective-permute-start | bytes 638984 | tf_op jit(solution)/shard_map/ppermute | solution.py:132
  142.5 21.4 %collective-permute-start.18 = (bf16[416,256]{1,0:T(8,128)(2,1)S(1)}, bf16[416,256]{1,0:T(8,128)(2,1)S(1)}, u32[]{:S(2)}, u32[]{:S(2)}) collective-permute-start(bf16[416,256]{1,0:T(8,128)(2,1)S(1)} %maximum_select_fusion.2), channel_id=1, source_target_pairs={{0,8},{2,10},{4,12},{6,14},{8,0},{10,2},{12,4},{14,6},{1,9},{3,11}... | collective-permute-start | bytes 638984 | tf_op jit(solution)/shard_map/ppermute | solution.py:132
  148.1 15.9 %collective-permute-start.19 = (bf16[416,256]{1,0:T(8,128)(2,1)S(1)}, bf16[416,256]{1,0:T(8,128)(2,1)S(1)}, u32[]{:S(2)}, u32[]{:S(2)}) collective-permute-start(bf16[416,256]{1,0:T(8,128)(2,1)S(1)} %maximum_select_fusion.2), channel_id=1, source_target_pairs={{0,12},{2,14},{4,0},{6,2},{8,4},{10,6},{12,8},{14,10},{1,13},{3,15... | collective-permute-start | bytes 638984 | tf_op jit(solution)/shard_map/ppermute | solution.py:132
  164.0 5.6 %collective-permute-start.20 = (bf16[1664,256]{1,0:T(8,128)(2,1)S(1)}, bf16[1664,256]{1,0:T(8,128)(2,1)S(1)}, u32[]{:S(2)}, u32[]{:S(2)}) collective-permute-start(bf16[1664,256]{1,0:T(8,128)(2,1)S(1)} %bitcast.258), channel_id=1, source_target_pairs={{0,1},{1,0},{2,3},{3,2},{4,5},{5,4},{6,7},{7,6},{8,9},{9,8},{10,11... | collective-permute-start | bytes 2555912 | tf_op jit(solution)/shard_map/ppermute | solution.py:178

commit v20 on v18

--- a/solution.py
+++ b/solution.py
@@ -134,11 +134,11 @@
     if padded_rows != rows:
         flat = jnp.pad(flat, ((0, padded_rows - rows), (0, 0)))
     flat = xor_halving(flat, "tm", tm_steps)
+    flat = xor_halving(flat, "space", sp_steps)
     flat = direct_scatter(flat, "space", low, high)
-    flat = xor_halving(flat, "space", sp_steps)
     piece = (flat * scale).astype(jnp.bfloat16)
+    piece = direct_gather(piece, "space", low, high)
     piece = xor_doubling(piece, "space", sp_steps)
-    piece = direct_gather(piece, "space", low, high)
     return piece, tm_steps, rows
 
 

time: 162 us -> 157 us (0.969); the launches traced: 160 us -> 157 us
  waiting for transfers between devices: 83.5 us -> 81.1 us
    ppermute x2, waiting for transfers between devices: 30.3 us -> 9.76 us  [two_column_sum(): value = value + lax.ppermute(value, axis, pairs)]
    ppermute x2, waiting for transfers between devices: 7.41 us -> 17.2 us  [xor_halving(): flat = keep + lax.ppermute(send, axis, pairs)]
    ppermute x1, waiting for transfers between devices: 0.01 us -> 5.64 us  [two_column_sum(): got = lax.ppermute(value, axis, [(1, 0)])]
    ppermute x3, waiting for transfers between devices: 8.59 us -> 5.55 us  [direct_gather(): got = lax.ppermute(piece, axis, pairs)]
    ppermute x3, waiting for transfers between devices: 7.75 us -> 10.6 us  [direct_scatter(): total = total + lax.ppermute(send, axis, pairs)]
    ppermute x1, waiting for transfers between devices: 4.58 us -> 7.15 us  [xor_doubling(): got = lax.ppermute(piece, axis, [(i, i ^ step) for i in range(count)])]
    ppermute x1, starting transfers between devices: 0.07 us -> 2.35 us  [xor_doubling(): got = lax.ppermute(piece, axis, [(i, i ^ step) for i in range(count)])]
  transfers between devices with their start and end apart: 20 -> 20, of which waited for: 12 -> 13; matrix products, arithmetic and copies ran while one was open for 20% -> 20% of each run, Pallas kernels for 0% -> 0%
where the time goes in v20:
time: 157 us
  waiting for transfers between devices  81.1 us (52%)
  starting transfers between devices  37.6 us (24%)
  matrix products  24 us (15%)
  other arithmetic  10.2 us (6%)
  local copies, waits for them, and re-layouts  3.03 us (2%)
    ppermute x3, waiting for transfers between devices, tree_broadcast(): got = lax.ppermute(value, axis, pairs)  23.4 us
    ppermute x2, waiting for transfers between devices, xor_halving(): flat = keep + lax.ppermute(send, axis, pairs)  17.2 us
    ppermute x3, starting transfers between devices, tree_broadcast(): got = lax.ppermute(value, axis, pairs)  14.4 us
    dot_general x18, matrix products, spatial_sum(): total = total + jnp.dot(piece, kernel, preferred_element_type=jnp.float32)  11.8 us
    ppermute x3, waiting for transfers between devices, direct_scatter(): total = total + lax.ppermute(send, axis, pairs)  10.6 us
    ppermute x2, waiting for transfers between devices, two_column_sum(): value = value + lax.ppermute(value, axis, pairs)  9.76 us
    ppermute x1, waiting for transfers between devices, xor_doubling(): got = lax.ppermute(piece, axis, [(i, i ^ step) for i in range(count)])  7.15 us
    ppermute x3, starting transfers between devices, direct_gather(): got = lax.ppermute(piece, axis, pairs)  6.92 us
  transfers between devices with their start and end apart: 20, of which 13 were waited for; matrix products, arithmetic and copies ran while one was open for 20% of the time, Pallas kernels for 0%

profile of v20, /device:TPU:0, one launch (start us, length us, event | category | flops | bytes accessed | tf_op | source)
XLA Modules:
  0.0 157.1 jit_solution(11497188471874591677)
XLA Ops:
  1.5 1.4 broadcast_multiply_fusion.1
  4.2 1.4 convert_reduce_fusion
  5.6 1.3 collective-permute-start.5
  7.7 8.3 %collective-permute-start.2 = (bf16[2,2,256,256]{3,2,1,0:T(8,128)(2,1)}, bf16[2,2,256,256]{3,2,1,0:T(8,128)(2,1)}, u32[]{:S(2)}, u32[]{:S(2)}) collective-permute-start(bf16[2,2,256,256]{3,2,1,0:T(8,128)(2,1)} %slice_bitcast_fusion), channel_id=1, source_target_pairs={{0,8},{1,9},{16,24},{17,25}} | collective-permute-start | bytes 1572872 | tf_op jit(solution)/shard_map/ppermute | solution.py:21
  16.0 1.4 fusion.88
  17.8 1.1 broadcast_select_fusion.8
  23.3 3.7 %collective-permute-done.2 = bf16[2,2,256,256]{3,2,1,0:T(8,128)(2,1)} collective-permute-done((bf16[2,2,256,256]{3,2,1,0:T(8,128)(2,1)}, bf16[2,2,256,256]{3,2,1,0:T(8,128)(2,1)}, u32[]{:S(2)}, u32[]{:S(2)}) %collective-permute-start.2) | collective-permute-done | bytes 524320 | tf_op jit(solution)/shard_map/ppermute | solution.py:21
  27.1 1.3 collective-permute-start.3
  28.4 1.3 multiply_convert_fusion.2
  29.7 1.5 collective-permute-start.1
  32.2 1.6 %collective-permute-done.5 = bf16[2,2,2,256,256]{4,3,2,1,0:T(8,128)(2,1)S(1)} collective-permute-done((bf16[2,2,2,256,256]{4,3,2,1,0:T(8,128)(2,1)S(1)}, bf16[2,2,2,256,256]{4,3,2,1,0:T(8,128)(2,1)S(1)}, u32[]{:S(2)}, u32[]{:S(2)}) %collective-permute-start.5) | collective-permute-done | bytes 1048608 | tf_op jit(solution)/shard_map/ppermute | solution.py:10
  34.2 1.1 multiply_convert_fusion
  39.5 4.8 %collective-permute-start.4 = (bf16[2,2,256,256]{3,2,1,0:T(8,128)(2,1)S(1)}, bf16[2,2,256,256]{3,2,1,0:T(8,128)(2,1)S(1)}, u32[]{:S(2)}, u32[]{:S(2)}) collective-permute-start(bf16[2,2,256,256]{3,2,1,0:T(8,128)(2,1)S(1)} %broadcast_select_fusion.3), channel_id=1, source_target_pairs={{0,2},{4,6},{8,10},{12,14},{1,3},{5,7},{9,11},{13,15},{16,18},{20,... | collective-permute-start | bytes 1572872 | tf_op jit(solution)/shard_map/ppermute | solution.py:21
  44.6 1.3 collective-permute-start.7
  48.0 19.6 %collective-permute-done.4 = bf16[2,2,256,256]{3,2,1,0:T(8,128)(2,1)S(1)} collective-permute-done((bf16[2,2,256,256]{3,2,1,0:T(8,128)(2,1)S(1)}, bf16[2,2,256,256]{3,2,1,0:T(8,128)(2,1)S(1)}, u32[]{:S(2)}, u32[]{:S(2)}) %collective-permute-start.4) | collective-permute-done | bytes 524320 | tf_op jit(solution)/shard_map/ppermute | solution.py:21
  68.9 9.8 %collective-permute-done.7 = f32[1,2,256,256]{3,2,1,0:T(8,128)S(1)} collective-permute-done((f32[1,2,256,256]{3,2,1,0:T(8,128)S(1)}, f32[1,2,256,256]{3,2,1,0:T(8,128)S(1)}, u32[]{:S(2)}, u32[]{:S(2)}) %collective-permute-start.7) | collective-permute-done | bytes 524320 | tf_op jit(solution)/shard_map/ppermute | solution.py:51
  78.8 1.5 collective-permute-start.8
  84.8 1.8 %multiply_convert_fusion.1 = bf16[2,2,2,256,256]{4,3,2,1,0:T(8,128)(2,1)} fusion(f32[2,2,2,256,256]{4,3,2,1,0:T(8,128)S(1)} %fusion.107, f32[2,2,2,256,256]{4,3,2,1,0:T(8,128)S(1)} %fusion.5, bf16[2,2,2,256,256]{4,3,2,1,0:T(8,128)(2,1)S(1)} %broadcast_multiply_fusion.1, f32[2,2]{1,0:T(2,128)S(1)} %get-tuple-element.9, f32[2,2,256,256]{3,2,1,0:T(8,128)S(1)} %fusion.71, ...), kind=kOutput, calls=%fused_computation.24 | convolution fusion | flops 272105472 | bytes 8520704 | tf_op jit(solution)/shard_map/dot_general | solution.py:187
  86.6 17.2 %collective-permute-done.11 = f32[832,256]{1,0:T(8,128)S(1)} collective-permute-done((f32[832,256]{1,0:T(8,128)S(1)}, f32[832,256]{1,0:T(8,128)S(1)}, u32[]{:S(2)}, u32[]{:S(2)}) %collective-permute-start.11) | collective-permute-done | bytes 852000 | tf_op jit(solution)/shard_map/ppermute | solution.py:66
  104.8 2.6 %collective-permute-start.13 = (f32[208,256]{1,0:T(8,128)S(1)}, f32[208,256]{1,0:T(8,128)S(1)}, u32[]{:S(2)}, u32[]{:S(2)}) collective-permute-start(f32[208,256]{1,0:T(8,128)S(1)} %get-tuple-element.15), channel_id=1, source_target_pairs={{0,8},{2,10},{4,12},{6,14},{8,0},{10,2},{12,4},{14,6},{1,9},{3,11}... | collective-permute-start | bytes 638984 | tf_op jit(solution)/shard_map/ppermute | solution.py:92
  107.4 2.8 %collective-permute-start.14 = (f32[208,256]{1,0:T(8,128)S(1)}, f32[208,256]{1,0:T(8,128)S(1)}, u32[]{:S(2)}, u32[]{:S(2)}) collective-permute-start(f32[208,256]{1,0:T(8,128)S(1)} %get-tuple-element.14), channel_id=1, source_target_pairs={{0,12},{2,14},{4,0},{6,2},{8,4},{10,6},{12,8},{14,10},{1,13},{3,15... | collective-permute-start | bytes 638984 | tf_op jit(solution)/shard_map/ppermute | solution.py:92
  110.7 3.4 %collective-permute-done.12 = f32[208,256]{1,0:T(8,128)S(1)} collective-permute-done((f32[208,256]{1,0:T(8,128)S(1)}, f32[208,256]{1,0:T(8,128)S(1)}, u32[]{:S(2)}, u32[]{:S(2)}) %collective-permute-start.12) | collective-permute-done | bytes 213024 | tf_op jit(solution)/shard_map/ppermute | solution.py:92
  114.1 7.2 %collective-permute-done.13 = f32[208,256]{1,0:T(8,128)S(1)} collective-permute-done((f32[208,256]{1,0:T(8,128)S(1)}, f32[208,256]{1,0:T(8,128)S(1)}, u32[]{:S(2)}, u32[]{:S(2)}) %collective-permute-start.13) | collective-permute-done | bytes 213024 | tf_op jit(solution)/shard_map/ppermute | solution.py:92
  121.5 5.1 %collective-permute-start.15 = (bf16[208,256]{1,0:T(8,128)(2,1)S(1)}, bf16[208,256]{1,0:T(8,128)(2,1)S(1)}, u32[]{:S(2)}, u32[]{:S(2)}) collective-permute-start(bf16[208,256]{1,0:T(8,128)(2,1)S(1)} %get-tuple-element.6), channel_id=1, source_target_pairs={{0,4},{2,6},{4,8},{6,10},{8,12},{10,14},{12,0},{14,2},{1,5},{3,7},... | collective-permute-start | bytes 319496 | tf_op jit(solution)/shard_map/ppermute | solution.py:105
  127.1 1.3 collective-permute-start.9
  128.9 1.3 collective-permute-start.17
  130.3 5.3 %collective-permute-done.16 = bf16[208,256]{1,0:T(8,128)(2,1)S(1)} collective-permute-done((bf16[208,256]{1,0:T(8,128)(2,1)S(1)}, bf16[208,256]{1,0:T(8,128)(2,1)S(1)}, u32[]{:S(2)}, u32[]{:S(2)}) %collective-permute-start.16) | collective-permute-done | bytes 106528 | tf_op jit(solution)/shard_map/ppermute | solution.py:105
  135.8 2.4 %collective-permute-start.18 = (bf16[832,256]{1,0:T(8,128)(2,1)S(1)}, bf16[832,256]{1,0:T(8,128)(2,1)S(1)}, u32[]{:S(2)}, u32[]{:S(2)}) collective-permute-start(bf16[832,256]{1,0:T(8,128)(2,1)S(1)} %bitcast.256), channel_id=1, source_target_pairs={{0,2},{2,0},{4,6},{6,4},{8,10},{10,8},{12,14},{14,12},{1,3},{3,1},... | collective-permute-start | bytes 1277960 | tf_op jit(solution)/shard_map/ppermute | solution.py:74
  138.2 5.6 %collective-permute-done.9 = f32[1,2,256,256]{3,2,1,0:T(8,128)S(1)} collective-permute-done((f32[1,2,256,256]{3,2,1,0:T(8,128)S(1)}, f32[1,2,256,256]{3,2,1,0:T(8,128)S(1)}, u32[]{:S(2)}, u32[]{:S(2)}) %collective-permute-start.9) | collective-permute-done | bytes 524320 | tf_op jit(solution)/shard_map/ppermute | solution.py:53
  144.5 7.1 %collective-permute-done.18 = bf16[832,256]{1,0:T(8,128)(2,1)S(1)} collective-permute-done((bf16[832,256]{1,0:T(8,128)(2,1)S(1)}, bf16[832,256]{1,0:T(8,128)(2,1)S(1)}, u32[]{:S(2)}, u32[]{:S(2)}) %collective-permute-start.18) | collective-permute-done | bytes 426016 | tf_op jit(solution)/shard_map/ppermute | solution.py:74
  152.0 2.3 %fusion.4 = bf16[2,2,2,256,256]{4,3,2,1,0:T(8,128)(2,1)} fusion(bf16[2,2,2,256,256]{4,3,2,1,0:T(8,128)(2,1)S(1)} %get-tuple-element.8, f32[2,2,2,256,256]{4,3,2,1,0:T(8,128)S(1)} %fusion.17, f32[2,2,2,256,256]{4,3,2,1,0:T(8,128)S(1)} %fusion.35, f32[2,2,2,256,256]{4,3,2,1,0:T(8,128)S(1)} %fusion.37, f32[2,2,2,256,256]{4,3,2,1,0:T(8,128)S(1)} %fusion.86, ...), kind=kOutput, calls=%fused_computation.13 | convolution fusion | flops 275775488 | bytes 21104128 | tf_op jit(solution)/shard_map/dot_general | solution.py:180
  156.0 1.1 pad_maximum_fusion.3
  (95 shorter events, 27.0 us)
Async XLA Ops:
  0.6 83.4 %copy-start = (bf16[256,256]{1,0:T(8,128)(2,1)S(1)}, bf16[256,256]{1,0:T(8,128)(2,1)}, u32[]{:S(2)}) copy-start(bf16[256,256]{1,0:T(8,128)(2,1)} %param.11) | copy-start | bytes 393220
  0.6 3.5 %copy-start.4 = (bf16[2,2,2,256,256]{4,3,2,1,0:T(8,128)(2,1)S(1)}, bf16[2,2,2,256,256]{4,3,2,1,0:T(8,128)(2,1)}, u32[]{:S(2)}) copy-start(bf16[2,2,2,256,256]{4,3,2,1,0:T(8,128)(2,1)} %param.7) | copy-start | bytes 3145732
  3.7 14.1 %collective-permute-start = (bf16[2,2,1,256,256]{4,3,2,1,0:T(8,128)(2,1)}, bf16[2,2,1,256,256]{4,3,2,1,0:T(8,128)(2,1)}, u32[]{:S(2)}, u32[]{:S(2)}) collective-permute-start(bf16[2,2,1,256,256]{4,3,2,1,0:T(8,128)(2,1)} %slice_select_fusion.2), channel_id=1, source_target_pairs={{0,1},{1,0},{2,3},{3,2},{4,5},{5,4},{6,7},{7,6},{8,9},{9,8},{10,11... | collective-permute-start | bytes 1572872 | tf_op jit(solution)/shard_map/ppermute | solution.py:223
  5.6 28.2 %collective-permute-start.5 = (bf16[2,2,2,256,256]{4,3,2,1,0:T(8,128)(2,1)S(1)}, bf16[2,2,2,256,256]{4,3,2,1,0:T(8,128)(2,1)S(1)}, u32[]{:S(2)}, u32[]{:S(2)}) collective-permute-start(bf16[2,2,2,256,256]{4,3,2,1,0:T(8,128)(2,1)S(1)} %get-tuple-element.8), channel_id=1, source_target_pairs={{2,0},{4,2},{6,4},{8,6},{10,8},{12,10},{14,12},{3,1},{5,3},{7,5},{... | collective-permute-start | bytes 3145736 | tf_op jit(solution)/shard_map/ppermute | solution.py:10
  7.7 19.4 %collective-permute-start.2 = (bf16[2,2,256,256]{3,2,1,0:T(8,128)(2,1)}, bf16[2,2,256,256]{3,2,1,0:T(8,128)(2,1)}, u32[]{:S(2)}, u32[]{:S(2)}) collective-permute-start(bf16[2,2,256,256]{3,2,1,0:T(8,128)(2,1)} %slice_bitcast_fusion), channel_id=1, source_target_pairs={{0,8},{1,9},{16,24},{17,25}} | collective-permute-start | bytes 1572872 | tf_op jit(solution)/shard_map/ppermute | solution.py:21
  16.0 1.4 copy-start.3
  19.0 1.3 copy-start.2
  27.1 12.3 %collective-permute-start.3 = (bf16[2,2,256,256]{3,2,1,0:T(8,128)(2,1)S(1)}, bf16[2,2,256,256]{3,2,1,0:T(8,128)(2,1)S(1)}, u32[]{:S(2)}, u32[]{:S(2)}) collective-permute-start(bf16[2,2,256,256]{3,2,1,0:T(8,128)(2,1)S(1)} %broadcast_select_fusion.2), channel_id=1, source_target_pairs={{0,4},{8,12},{1,5},{9,13},{16,20},{24,28},{17,21},{25,29}} | collective-permute-start | bytes 1572872 | tf_op jit(solution)/shard_map/ppermute | solution.py:21
  29.7 50.6 %collective-permute-start.1 = (bf16[2,2,2,256,256]{4,3,2,1,0:T(8,128)(2,1)S(1)}, bf16[2,2,2,256,256]{4,3,2,1,0:T(8,128)(2,1)S(1)}, u32[]{:S(2)}, u32[]{:S(2)}) collective-permute-start(bf16[2,2,2,256,256]{4,3,2,1,0:T(8,128)(2,1)S(1)} %get-tuple-element.20), channel_id=1, source_target_pairs={{0,2},{2,4},{4,6},{6,8},{8,10},{10,12},{12,14},{1,3},{3,5},{5,7},{... | collective-permute-start | bytes 3145736 | tf_op jit(solution)/shard_map/ppermute | solution.py:10
  39.3 5.1 %copy-start.1 = (f32[2,2,256,256]{3,2,1,0:T(8,128)S(1)}, f32[2,2,256,256]{3,2,1,0:T(8,128)}, u32[]{:S(2)}) copy-start(f32[2,2,256,256]{3,2,1,0:T(8,128)} %get-tuple-element.7) | copy-start | bytes 3145732
  39.5 28.2 %collective-permute-start.4 = (bf16[2,2,256,256]{3,2,1,0:T(8,128)(2,1)S(1)}, bf16[2,2,256,256]{3,2,1,0:T(8,128)(2,1)S(1)}, u32[]{:S(2)}, u32[]{:S(2)}) collective-permute-start(bf16[2,2,256,256]{3,2,1,0:T(8,128)(2,1)S(1)} %broadcast_select_fusion.3), channel_id=1, source_target_pairs={{0,2},{4,6},{8,10},{12,14},{1,3},{5,7},{9,11},{13,15},{16,18},{20,... | collective-permute-start | bytes 1572872 | tf_op jit(solution)/shard_map/ppermute | solution.py:21
  44.6 34.0 %collective-permute-start.7 = (f32[1,2,256,256]{3,2,1,0:T(8,128)S(1)}, f32[1,2,256,256]{3,2,1,0:T(8,128)S(1)}, u32[]{:S(2)}, u32[]{:S(2)}) collective-permute-start(f32[1,2,256,256]{3,2,1,0:T(8,128)S(1)} %slice_select_fusion), channel_id=1, source_target_pairs={{4,0},{6,2},{12,8},{14,10},{5,1},{7,3},{13,9},{15,11},{20,16},{22,... | collective-permute-start | bytes 1572872 | tf_op jit(solution)/shard_map/ppermute | solution.py:51
  45.9 34.8 %collective-permute-start.6 = (bf16[2,2,1,256,256]{4,3,2,1,0:T(8,128)(2,1)S(1)}, bf16[2,2,1,256,256]{4,3,2,1,0:T(8,128)(2,1)S(1)}, u32[]{:S(2)}, u32[]{:S(2)}) collective-permute-start(bf16[2,2,1,256,256]{4,3,2,1,0:T(8,128)(2,1)S(1)} %slice_select_fusion.1), channel_id=1, source_target_pairs={{0,1},{1,0},{2,3},{3,2},{4,5},{5,4},{6,7},{7,6},{8,9},{9,8},{10,11... | collective-permute-start | bytes 1572872 | tf_op jit(solution)/shard_map/ppermute | solution.py:223
  68.8 14.8 %collective-permute-start.10 = (f32[1664,256]{1,0:T(8,128)S(1)}, f32[1664,256]{1,0:T(8,128)S(1)}, u32[]{:S(2)}, u32[]{:S(2)}) collective-permute-start(f32[1664,256]{1,0:T(8,128)S(1)} %constant_dynamic-slice_fusion.4), channel_id=1, source_target_pairs={{0,1},{1,0},{2,3},{3,2},{4,5},{5,4},{6,7},{7,6},{8,9},{9,8},{10,11... | collective-permute-start | bytes 5111816 | tf_op jit(solution)/shard_map/ppermute | solution.py:66
  78.8 48.3 %collective-permute-start.8 = (f32[1,2,256,256]{3,2,1,0:T(8,128)S(1)}, f32[1,2,256,256]{3,2,1,0:T(8,128)S(1)}, u32[]{:S(2)}, u32[]{:S(2)}) collective-permute-start(f32[1,2,256,256]{3,2,1,0:T(8,128)S(1)} %fusion.166), channel_id=1, source_target_pairs={{8,0},{10,2},{9,1},{11,3},{24,16},{26,18},{25,17},{27,19}} | collective-permute-start | bytes 1572872 | tf_op jit(solution)/shard_map/ppermute | solution.py:51
  83.9 19.9 %collective-permute-start.11 = (f32[832,256]{1,0:T(8,128)S(1)}, f32[832,256]{1,0:T(8,128)S(1)}, u32[]{:S(2)}, u32[]{:S(2)}) collective-permute-start(f32[832,256]{1,0:T(8,128)S(1)} %constant_dynamic-slice_fusion.3), channel_id=1, source_target_pairs={{0,2},{2,0},{4,6},{6,4},{8,10},{10,8},{12,14},{14,12},{1,3},{3,1},... | collective-permute-start | bytes 2555912 | tf_op jit(solution)/shard_map/ppermute | solution.py:66
  104.0 10.1 %collective-permute-start.12 = (f32[208,256]{1,0:T(8,128)S(1)}, f32[208,256]{1,0:T(8,128)S(1)}, u32[]{:S(2)}, u32[]{:S(2)}) collective-permute-start(f32[208,256]{1,0:T(8,128)S(1)} %get-tuple-element.13), channel_id=1, source_target_pairs={{0,4},{2,6},{4,8},{6,10},{8,12},{10,14},{12,0},{14,2},{1,5},{3,7},... | collective-permute-start | bytes 638984 | tf_op jit(solution)/shard_map/ppermute | solution.py:92
  104.8 16.6 %collective-permute-start.13 = (f32[208,256]{1,0:T(8,128)S(1)}, f32[208,256]{1,0:T(8,128)S(1)}, u32[]{:S(2)}, u32[]{:S(2)}) collective-permute-start(f32[208,256]{1,0:T(8,128)S(1)} %get-tuple-element.15), channel_id=1, source_target_pairs={{0,8},{2,10},{4,12},{6,14},{8,0},{10,2},{12,4},{14,6},{1,9},{3,11}... | collective-permute-start | bytes 638984 | tf_op jit(solution)/shard_map/ppermute | solution.py:92
  107.4 14.0 %collective-permute-start.14 = (f32[208,256]{1,0:T(8,128)S(1)}, f32[208,256]{1,0:T(8,128)S(1)}, u32[]{:S(2)}, u32[]{:S(2)}) collective-permute-start(f32[208,256]{1,0:T(8,128)S(1)} %get-tuple-element.14), channel_id=1, source_target_pairs={{0,12},{2,14},{4,0},{6,2},{8,4},{10,6},{12,8},{14,10},{1,13},{3,15... | collective-permute-start | bytes 638984 | tf_op jit(solution)/shard_map/ppermute | solution.py:92
  121.5 8.8 %collective-permute-start.15 = (bf16[208,256]{1,0:T(8,128)(2,1)S(1)}, bf16[208,256]{1,0:T(8,128)(2,1)S(1)}, u32[]{:S(2)}, u32[]{:S(2)}) collective-permute-start(bf16[208,256]{1,0:T(8,128)(2,1)S(1)} %get-tuple-element.6), channel_id=1, source_target_pairs={{0,4},{2,6},{4,8},{6,10},{8,12},{10,14},{12,0},{14,2},{1,5},{3,7},... | collective-permute-start | bytes 319496 | tf_op jit(solution)/shard_map/ppermute | solution.py:105
  127.1 16.7 %collective-permute-start.9 = (f32[1,2,256,256]{3,2,1,0:T(8,128)S(1)}, f32[1,2,256,256]{3,2,1,0:T(8,128)S(1)}, u32[]{:S(2)}, u32[]{:S(2)}) collective-permute-start(f32[1,2,256,256]{3,2,1,0:T(8,128)S(1)} %add.249), channel_id=1, source_target_pairs={{2,0},{3,1},{18,16},{19,17}} | collective-permute-start | bytes 1572872 | tf_op jit(solution)/shard_map/ppermute | solution.py:53
  128.4 7.1 %collective-permute-start.16 = (bf16[208,256]{1,0:T(8,128)(2,1)S(1)}, bf16[208,256]{1,0:T(8,128)(2,1)S(1)}, u32[]{:S(2)}, u32[]{:S(2)}) collective-permute-start(bf16[208,256]{1,0:T(8,128)(2,1)S(1)} %get-tuple-element.6), channel_id=1, source_target_pairs={{0,8},{2,10},{4,12},{6,14},{8,0},{10,2},{12,4},{14,6},{1,9},{3,11}... | collective-permute-start | bytes 319496 | tf_op jit(solution)/shard_map/ppermute | solution.py:105
  128.9 6.9 %collective-permute-start.17 = (bf16[208,256]{1,0:T(8,128)(2,1)S(1)}, bf16[208,256]{1,0:T(8,128)(2,1)S(1)}, u32[]{:S(2)}, u32[]{:S(2)}) collective-permute-start(bf16[208,256]{1,0:T(8,128)(2,1)S(1)} %get-tuple-element.6), channel_id=1, source_target_pairs={{0,12},{2,14},{4,0},{6,2},{8,4},{10,6},{12,8},{14,10},{1,13},{3,15... | collective-permute-start | bytes 319496 | tf_op jit(solution)/shard_map/ppermute | solution.py:105
  135.8 15.8 %collective-permute-start.18 = (bf16[832,256]{1,0:T(8,128)(2,1)S(1)}, bf16[832,256]{1,0:T(8,128)(2,1)S(1)}, u32[]{:S(2)}, u32[]{:S(2)}) collective-permute-start(bf16[832,256]{1,0:T(8,128)(2,1)S(1)} %bitcast.256), channel_id=1, source_target_pairs={{0,2},{2,0},{4,6},{6,4},{8,10},{10,8},{12,14},{14,12},{1,3},{3,1},... | collective-permute-start | bytes 1277960 | tf_op jit(solution)/shard_map/ppermute | solution.py:74
  151.9 2.4 %collective-permute-start.19 = (bf16[1664,256]{1,0:T(8,128)(2,1)S(1)}, bf16[1664,256]{1,0:T(8,128)(2,1)S(1)}, u32[]{:S(2)}, u32[]{:S(2)}) collective-permute-start(bf16[1664,256]{1,0:T(8,128)(2,1)S(1)} %maximum_select_fusion), channel_id=1, source_target_pairs={{0,1},{1,0},{2,3},{3,2},{4,5},{5,4},{6,7},{7,6},{8,9},{9,8},{10,11... | collective-permute-start | bytes 2555912 | tf_op jit(solution)/shard_map/ppermute | solution.py:151

commit v21 on v20

--- a/solution.py
+++ b/solution.py
@@ -41,15 +41,17 @@
     value = jnp.where(odd, pair[half:], pair[:half])
     n = count // 2
     step = 1
-    while step < n:
+    while step * 2 < n:
+        step *= 2
+    while step >= 1:
         pairs = []
-        for i in range(0, n, 2 * step):
-            if i + step < n:
+        for i in range(n):
+            if i < step and i + step < n:
                 pairs.append((2 * (i + step), 2 * i))
                 if 2 * (i + step) + 1 < count:
                     pairs.append((2 * (i + step) + 1, 2 * i + 1))
         value = value + lax.ppermute(value, axis, pairs)
-        step *= 2
+        step //= 2
     got = lax.ppermute(value, axis, [(1, 0)])
     return jnp.concatenate([value, got + local[half:]], axis=0)
 

time: 157 us -> 157 us (level)
  waiting for transfers between devices: 81.1 us -> 71.2 us
  starting transfers between devices: 37.6 us -> 46.8 us
    ppermute x2, waiting for transfers between devices: 9.76 us -> 0.01 us  [two_column_sum(): value = value + lax.ppermute(value, axis, pairs)]
    ppermute x3, starting transfers between devices: 6.27 us -> 12.9 us  [direct_scatter(): total = total + lax.ppermute(send, axis, pairs)]
    ppermute x2, starting transfers between devices: 0.15 us -> 2.62 us  [xor_halving(): flat = keep + lax.ppermute(send, axis, pairs)]
  transfers between devices with their start and end apart: 20 -> 20, of which waited for: 13 -> 12; matrix products, arithmetic and copies ran while one was open for 20% -> 20% of each run, Pallas kernels for 0% -> 0%
where the time goes in v21:
time: 157 us; the launch traced here: 156 us
  waiting for transfers between devices  71.2 us (45%)
  starting transfers between devices  46.8 us (30%)
  matrix products  24 us (15%)
  other arithmetic  10.2 us (6%)
  local copies, waits for them, and re-layouts  3.03 us (2%)
    ppermute x3, waiting for transfers between devices, tree_broadcast(): got = lax.ppermute(value, axis, pairs)  23.4 us
    ppermute x2, waiting for transfers between devices, xor_halving(): flat = keep + lax.ppermute(send, axis, pairs)  17 us
    ppermute x3, starting transfers between devices, tree_broadcast(): got = lax.ppermute(value, axis, pairs)  14.4 us
    ppermute x3, starting transfers between devices, direct_scatter(): total = total + lax.ppermute(send, axis, pairs)  12.9 us
    dot_general x18, matrix products, spatial_sum(): total = total + jnp.dot(piece, kernel, preferred_element_type=jnp.float32)  11.8 us
    ppermute x3, waiting for transfers between devices, direct_scatter(): total = total + lax.ppermute(send, axis, pairs)  10.8 us
    ppermute x1, waiting for transfers between devices, xor_doubling(): got = lax.ppermute(piece, axis, [(i, i ^ step) for i in range(count)])  7.15 us
    ppermute x3, starting transfers between devices, direct_gather(): got = lax.ppermute(piece, axis, pairs)  6.94 us
  transfers between devices with their start and end apart: 20, of which 12 were waited for; matrix products, arithmetic and copies ran while one was open for 20% of the time, Pallas kernels for 0%

profile of v21, /device:TPU:0, one launch (start us, length us, event | category | flops | bytes accessed | tf_op | source)
XLA Modules:
  0.0 156.4 jit_solution(16431755082358590888)
XLA Ops:
  1.5 1.4 broadcast_multiply_fusion.1
  4.2 1.4 convert_reduce_fusion
  5.6 1.3 collective-permute-start.5
  7.7 8.3 %collective-permute-start.2 = (bf16[2,2,256,256]{3,2,1,0:T(8,128)(2,1)}, bf16[2,2,256,256]{3,2,1,0:T(8,128)(2,1)}, u32[]{:S(2)}, u32[]{:S(2)}) collective-permute-start(bf16[2,2,256,256]{3,2,1,0:T(8,128)(2,1)} %slice_bitcast_fusion), channel_id=1, source_target_pairs={{0,8},{1,9},{16,24},{17,25}} | collective-permute-start | bytes 1572872 | tf_op jit(solution)/shard_map/ppermute | solution.py:21
  16.0 1.4 fusion.88
  17.8 1.1 broadcast_select_fusion.8
  23.3 3.7 %collective-permute-done.2 = bf16[2,2,256,256]{3,2,1,0:T(8,128)(2,1)} collective-permute-done((bf16[2,2,256,256]{3,2,1,0:T(8,128)(2,1)}, bf16[2,2,256,256]{3,2,1,0:T(8,128)(2,1)}, u32[]{:S(2)}, u32[]{:S(2)}) %collective-permute-start.2) | collective-permute-done | bytes 524320 | tf_op jit(solution)/shard_map/ppermute | solution.py:21
  27.1 1.3 collective-permute-start.3
  28.4 1.3 multiply_convert_fusion.2
  29.7 1.5 collective-permute-start.1
  32.2 1.6 %collective-permute-done.5 = bf16[2,2,2,256,256]{4,3,2,1,0:T(8,128)(2,1)S(1)} collective-permute-done((bf16[2,2,2,256,256]{4,3,2,1,0:T(8,128)(2,1)S(1)}, bf16[2,2,2,256,256]{4,3,2,1,0:T(8,128)(2,1)S(1)}, u32[]{:S(2)}, u32[]{:S(2)}) %collective-permute-start.5) | collective-permute-done | bytes 1048608 | tf_op jit(solution)/shard_map/ppermute | solution.py:10
  34.2 1.1 multiply_convert_fusion
  39.5 4.8 %collective-permute-start.4 = (bf16[2,2,256,256]{3,2,1,0:T(8,128)(2,1)S(1)}, bf16[2,2,256,256]{3,2,1,0:T(8,128)(2,1)S(1)}, u32[]{:S(2)}, u32[]{:S(2)}) collective-permute-start(bf16[2,2,256,256]{3,2,1,0:T(8,128)(2,1)S(1)} %broadcast_select_fusion.3), channel_id=1, source_target_pairs={{0,2},{4,6},{8,10},{12,14},{1,3},{5,7},{9,11},{13,15},{16,18},{20,... | collective-permute-start | bytes 1572872 | tf_op jit(solution)/shard_map/ppermute | solution.py:21
  44.6 1.3 collective-permute-start.7
  48.0 19.6 %collective-permute-done.4 = bf16[2,2,256,256]{3,2,1,0:T(8,128)(2,1)S(1)} collective-permute-done((bf16[2,2,256,256]{3,2,1,0:T(8,128)(2,1)S(1)}, bf16[2,2,256,256]{3,2,1,0:T(8,128)(2,1)S(1)}, u32[]{:S(2)}, u32[]{:S(2)}) %collective-permute-start.4) | collective-permute-done | bytes 524320 | tf_op jit(solution)/shard_map/ppermute | solution.py:21
  69.0 1.5 collective-permute-start.8
  74.2 2.5 %collective-permute-start.11 = (f32[832,256]{1,0:T(8,128)S(1)}, f32[832,256]{1,0:T(8,128)S(1)}, u32[]{:S(2)}, u32[]{:S(2)}) collective-permute-start(f32[832,256]{1,0:T(8,128)S(1)} %constant_dynamic-slice_fusion.3), channel_id=1, source_target_pairs={{0,2},{2,0},{4,6},{6,4},{8,10},{10,8},{12,14},{14,12},{1,3},{3,1},... | collective-permute-start | bytes 2555912 | tf_op jit(solution)/shard_map/ppermute | solution.py:68
  77.5 1.8 %multiply_convert_fusion.1 = bf16[2,2,2,256,256]{4,3,2,1,0:T(8,128)(2,1)} fusion(f32[2,2,2,256,256]{4,3,2,1,0:T(8,128)S(1)} %fusion.107, f32[2,2,2,256,256]{4,3,2,1,0:T(8,128)S(1)} %fusion.5, bf16[2,2,2,256,256]{4,3,2,1,0:T(8,128)(2,1)S(1)} %broadcast_multiply_fusion.1, f32[2,2]{1,0:T(2,128)S(1)} %get-tuple-element.9, f32[2,2,256,256]{3,2,1,0:T(8,128)S(1)} %fusion.71, ...), kind=kOutput, calls=%fused_computation.24 | convolution fusion | flops 272105472 | bytes 8520704 | tf_op jit(solution)/shard_map/dot_general | solution.py:189
  79.3 17.0 %collective-permute-done.11 = f32[832,256]{1,0:T(8,128)S(1)} collective-permute-done((f32[832,256]{1,0:T(8,128)S(1)}, f32[832,256]{1,0:T(8,128)S(1)}, u32[]{:S(2)}, u32[]{:S(2)}) %collective-permute-start.11) | collective-permute-done | bytes 852000 | tf_op jit(solution)/shard_map/ppermute | solution.py:68
  96.5 10.5 %collective-permute-start.12 = (f32[208,256]{1,0:T(8,128)S(1)}, f32[208,256]{1,0:T(8,128)S(1)}, u32[]{:S(2)}, u32[]{:S(2)}) collective-permute-start(f32[208,256]{1,0:T(8,128)S(1)} %get-tuple-element.13), channel_id=1, source_target_pairs={{0,4},{2,6},{4,8},{6,10},{8,12},{10,14},{12,0},{14,2},{1,5},{3,7},... | collective-permute-start | bytes 638984 | tf_op jit(solution)/shard_map/ppermute | solution.py:94
  107.4 2.1 %collective-permute-start.14 = (f32[208,256]{1,0:T(8,128)S(1)}, f32[208,256]{1,0:T(8,128)S(1)}, u32[]{:S(2)}, u32[]{:S(2)}) collective-permute-start(f32[208,256]{1,0:T(8,128)S(1)} %get-tuple-element.14), channel_id=1, source_target_pairs={{0,12},{2,14},{4,0},{6,2},{8,4},{10,6},{12,8},{14,10},{1,13},{3,15... | collective-permute-start | bytes 638984 | tf_op jit(solution)/shard_map/ppermute | solution.py:94
  109.9 3.2 %collective-permute-done.12 = f32[208,256]{1,0:T(8,128)S(1)} collective-permute-done((f32[208,256]{1,0:T(8,128)S(1)}, f32[208,256]{1,0:T(8,128)S(1)}, u32[]{:S(2)}, u32[]{:S(2)}) %collective-permute-start.12) | collective-permute-done | bytes 213024 | tf_op jit(solution)/shard_map/ppermute | solution.py:94
  113.0 7.7 %collective-permute-done.13 = f32[208,256]{1,0:T(8,128)S(1)} collective-permute-done((f32[208,256]{1,0:T(8,128)S(1)}, f32[208,256]{1,0:T(8,128)S(1)}, u32[]{:S(2)}, u32[]{:S(2)}) %collective-permute-start.13) | collective-permute-done | bytes 213024 | tf_op jit(solution)/shard_map/ppermute | solution.py:94
  120.8 5.1 %collective-permute-start.15 = (bf16[208,256]{1,0:T(8,128)(2,1)S(1)}, bf16[208,256]{1,0:T(8,128)(2,1)S(1)}, u32[]{:S(2)}, u32[]{:S(2)}) collective-permute-start(bf16[208,256]{1,0:T(8,128)(2,1)S(1)} %get-tuple-element.6), channel_id=1, source_target_pairs={{0,4},{2,6},{4,8},{6,10},{8,12},{10,14},{12,0},{14,2},{1,5},{3,7},... | collective-permute-start | bytes 319496 | tf_op jit(solution)/shard_map/ppermute | solution.py:107
  126.5 1.3 collective-permute-start.9
  128.2 1.4 collective-permute-start.17
  129.7 5.3 %collective-permute-done.16 = bf16[208,256]{1,0:T(8,128)(2,1)S(1)} collective-permute-done((bf16[208,256]{1,0:T(8,128)(2,1)S(1)}, bf16[208,256]{1,0:T(8,128)(2,1)S(1)}, u32[]{:S(2)}, u32[]{:S(2)}) %collective-permute-start.16) | collective-permute-done | bytes 106528 | tf_op jit(solution)/shard_map/ppermute | solution.py:107
  135.2 2.4 %collective-permute-start.18 = (bf16[832,256]{1,0:T(8,128)(2,1)S(1)}, bf16[832,256]{1,0:T(8,128)(2,1)S(1)}, u32[]{:S(2)}, u32[]{:S(2)}) collective-permute-start(bf16[832,256]{1,0:T(8,128)(2,1)S(1)} %bitcast.256), channel_id=1, source_target_pairs={{0,2},{2,0},{4,6},{6,4},{8,10},{10,8},{12,14},{14,12},{1,3},{3,1},... | collective-permute-start | bytes 1277960 | tf_op jit(solution)/shard_map/ppermute | solution.py:76
  137.6 5.6 %collective-permute-done.9 = f32[1,2,256,256]{3,2,1,0:T(8,128)S(1)} collective-permute-done((f32[1,2,256,256]{3,2,1,0:T(8,128)S(1)}, f32[1,2,256,256]{3,2,1,0:T(8,128)S(1)}, u32[]{:S(2)}, u32[]{:S(2)}) %collective-permute-start.9) | collective-permute-done | bytes 524320 | tf_op jit(solution)/shard_map/ppermute | solution.py:55
  143.9 7.2 %collective-permute-done.18 = bf16[832,256]{1,0:T(8,128)(2,1)S(1)} collective-permute-done((bf16[832,256]{1,0:T(8,128)(2,1)S(1)}, bf16[832,256]{1,0:T(8,128)(2,1)S(1)}, u32[]{:S(2)}, u32[]{:S(2)}) %collective-permute-start.18) | collective-permute-done | bytes 426016 | tf_op jit(solution)/shard_map/ppermute | solution.py:76
  151.4 2.3 %fusion.4 = bf16[2,2,2,256,256]{4,3,2,1,0:T(8,128)(2,1)} fusion(bf16[2,2,2,256,256]{4,3,2,1,0:T(8,128)(2,1)S(1)} %get-tuple-element.8, f32[2,2,2,256,256]{4,3,2,1,0:T(8,128)S(1)} %fusion.17, f32[2,2,2,256,256]{4,3,2,1,0:T(8,128)S(1)} %fusion.35, f32[2,2,2,256,256]{4,3,2,1,0:T(8,128)S(1)} %fusion.37, f32[2,2,2,256,256]{4,3,2,1,0:T(8,128)S(1)} %fusion.86, ...), kind=kOutput, calls=%fused_computation.13 | convolution fusion | flops 275775488 | bytes 21104128 | tf_op jit(solution)/shard_map/dot_general | solution.py:182
  155.3 1.1 pad_maximum_fusion.3
  (95 shorter events, 26.4 us)
Async XLA Ops:
  0.6 76.1 %copy-start = (bf16[256,256]{1,0:T(8,128)(2,1)S(1)}, bf16[256,256]{1,0:T(8,128)(2,1)}, u32[]{:S(2)}) copy-start(bf16[256,256]{1,0:T(8,128)(2,1)} %param.11) | copy-start | bytes 393220
  0.6 3.5 %copy-start.4 = (bf16[2,2,2,256,256]{4,3,2,1,0:T(8,128)(2,1)S(1)}, bf16[2,2,2,256,256]{4,3,2,1,0:T(8,128)(2,1)}, u32[]{:S(2)}) copy-start(bf16[2,2,2,256,256]{4,3,2,1,0:T(8,128)(2,1)} %param.7) | copy-start | bytes 3145732
  3.7 14.1 %collective-permute-start = (bf16[2,2,1,256,256]{4,3,2,1,0:T(8,128)(2,1)}, bf16[2,2,1,256,256]{4,3,2,1,0:T(8,128)(2,1)}, u32[]{:S(2)}, u32[]{:S(2)}) collective-permute-start(bf16[2,2,1,256,256]{4,3,2,1,0:T(8,128)(2,1)} %slice_select_fusion.2), channel_id=1, source_target_pairs={{0,1},{1,0},{2,3},{3,2},{4,5},{5,4},{6,7},{7,6},{8,9},{9,8},{10,11... | collective-permute-start | bytes 1572872 | tf_op jit(solution)/shard_map/ppermute | solution.py:225
  5.6 28.2 %collective-permute-start.5 = (bf16[2,2,2,256,256]{4,3,2,1,0:T(8,128)(2,1)S(1)}, bf16[2,2,2,256,256]{4,3,2,1,0:T(8,128)(2,1)S(1)}, u32[]{:S(2)}, u32[]{:S(2)}) collective-permute-start(bf16[2,2,2,256,256]{4,3,2,1,0:T(8,128)(2,1)S(1)} %get-tuple-element.8), channel_id=1, source_target_pairs={{2,0},{4,2},{6,4},{8,6},{10,8},{12,10},{14,12},{3,1},{5,3},{7,5},{... | collective-permute-start | bytes 3145736 | tf_op jit(solution)/shard_map/ppermute | solution.py:10
  7.7 19.4 %collective-permute-start.2 = (bf16[2,2,256,256]{3,2,1,0:T(8,128)(2,1)}, bf16[2,2,256,256]{3,2,1,0:T(8,128)(2,1)}, u32[]{:S(2)}, u32[]{:S(2)}) collective-permute-start(bf16[2,2,256,256]{3,2,1,0:T(8,128)(2,1)} %slice_bitcast_fusion), channel_id=1, source_target_pairs={{0,8},{1,9},{16,24},{17,25}} | collective-permute-start | bytes 1572872 | tf_op jit(solution)/shard_map/ppermute | solution.py:21
  16.0 1.4 copy-start.3
  19.0 1.3 copy-start.2
  27.1 12.3 %collective-permute-start.3 = (bf16[2,2,256,256]{3,2,1,0:T(8,128)(2,1)S(1)}, bf16[2,2,256,256]{3,2,1,0:T(8,128)(2,1)S(1)}, u32[]{:S(2)}, u32[]{:S(2)}) collective-permute-start(bf16[2,2,256,256]{3,2,1,0:T(8,128)(2,1)S(1)} %broadcast_select_fusion.2), channel_id=1, source_target_pairs={{0,4},{8,12},{1,5},{9,13},{16,20},{24,28},{17,21},{25,29}} | collective-permute-start | bytes 1572872 | tf_op jit(solution)/shard_map/ppermute | solution.py:21
  29.7 40.8 %collective-permute-start.1 = (bf16[2,2,2,256,256]{4,3,2,1,0:T(8,128)(2,1)S(1)}, bf16[2,2,2,256,256]{4,3,2,1,0:T(8,128)(2,1)S(1)}, u32[]{:S(2)}, u32[]{:S(2)}) collective-permute-start(bf16[2,2,2,256,256]{4,3,2,1,0:T(8,128)(2,1)S(1)} %get-tuple-element.20), channel_id=1, source_target_pairs={{0,2},{2,4},{4,6},{6,8},{8,10},{10,12},{12,14},{1,3},{3,5},{5,7},{... | collective-permute-start | bytes 3145736 | tf_op jit(solution)/shard_map/ppermute | solution.py:10
  39.3 5.1 %copy-start.1 = (f32[2,2,256,256]{3,2,1,0:T(8,128)S(1)}, f32[2,2,256,256]{3,2,1,0:T(8,128)}, u32[]{:S(2)}) copy-start(f32[2,2,256,256]{3,2,1,0:T(8,128)} %get-tuple-element.7) | copy-start | bytes 3145732
  39.5 28.2 %collective-permute-start.4 = (bf16[2,2,256,256]{3,2,1,0:T(8,128)(2,1)S(1)}, bf16[2,2,256,256]{3,2,1,0:T(8,128)(2,1)S(1)}, u32[]{:S(2)}, u32[]{:S(2)}) collective-permute-start(bf16[2,2,256,256]{3,2,1,0:T(8,128)(2,1)S(1)} %broadcast_select_fusion.3), channel_id=1, source_target_pairs={{0,2},{4,6},{8,10},{12,14},{1,3},{5,7},{9,11},{13,15},{16,18},{20,... | collective-permute-start | bytes 1572872 | tf_op jit(solution)/shard_map/ppermute | solution.py:21
  44.6 24.3 %collective-permute-start.7 = (f32[1,2,256,256]{3,2,1,0:T(8,128)S(1)}, f32[1,2,256,256]{3,2,1,0:T(8,128)S(1)}, u32[]{:S(2)}, u32[]{:S(2)}) collective-permute-start(f32[1,2,256,256]{3,2,1,0:T(8,128)S(1)} %slice_select_fusion), channel_id=1, source_target_pairs={{8,0},{10,2},{12,4},{14,6},{9,1},{11,3},{13,5},{15,7},{24,16},{26,... | collective-permute-start | bytes 1572872 | tf_op jit(solution)/shard_map/ppermute | solution.py:53
  45.9 25.1 %collective-permute-start.6 = (bf16[2,2,1,256,256]{4,3,2,1,0:T(8,128)(2,1)S(1)}, bf16[2,2,1,256,256]{4,3,2,1,0:T(8,128)(2,1)S(1)}, u32[]{:S(2)}, u32[]{:S(2)}) collective-permute-start(bf16[2,2,1,256,256]{4,3,2,1,0:T(8,128)(2,1)S(1)} %slice_select_fusion.1), channel_id=1, source_target_pairs={{0,1},{1,0},{2,3},{3,2},{4,5},{5,4},{6,7},{7,6},{8,9},{9,8},{10,11... | collective-permute-start | bytes 1572872 | tf_op jit(solution)/shard_map/ppermute | solution.py:225
  68.8 5.0 %collective-permute-start.10 = (f32[1664,256]{1,0:T(8,128)S(1)}, f32[1664,256]{1,0:T(8,128)S(1)}, u32[]{:S(2)}, u32[]{:S(2)}) collective-permute-start(f32[1664,256]{1,0:T(8,128)S(1)} %constant_dynamic-slice_fusion.4), channel_id=1, source_target_pairs={{0,1},{1,0},{2,3},{3,2},{4,5},{5,4},{6,7},{7,6},{8,9},{9,8},{10,11... | collective-permute-start | bytes 5111816 | tf_op jit(solution)/shard_map/ppermute | solution.py:68
  69.0 57.4 %collective-permute-start.8 = (f32[1,2,256,256]{3,2,1,0:T(8,128)S(1)}, f32[1,2,256,256]{3,2,1,0:T(8,128)S(1)}, u32[]{:S(2)}, u32[]{:S(2)}) collective-permute-start(f32[1,2,256,256]{3,2,1,0:T(8,128)S(1)} %fusion.166), channel_id=1, source_target_pairs={{4,0},{6,2},{5,1},{7,3},{20,16},{22,18},{21,17},{23,19}} | collective-permute-start | bytes 1572872 | tf_op jit(solution)/shard_map/ppermute | solution.py:53
  74.2 22.1 %collective-permute-start.11 = (f32[832,256]{1,0:T(8,128)S(1)}, f32[832,256]{1,0:T(8,128)S(1)}, u32[]{:S(2)}, u32[]{:S(2)}) collective-permute-start(f32[832,256]{1,0:T(8,128)S(1)} %constant_dynamic-slice_fusion.3), channel_id=1, source_target_pairs={{0,2},{2,0},{4,6},{6,4},{8,10},{10,8},{12,14},{14,12},{1,3},{3,1},... | collective-permute-start | bytes 2555912 | tf_op jit(solution)/shard_map/ppermute | solution.py:68
  96.5 16.6 %collective-permute-start.12 = (f32[208,256]{1,0:T(8,128)S(1)}, f32[208,256]{1,0:T(8,128)S(1)}, u32[]{:S(2)}, u32[]{:S(2)}) collective-permute-start(f32[208,256]{1,0:T(8,128)S(1)} %get-tuple-element.13), channel_id=1, source_target_pairs={{0,4},{2,6},{4,8},{6,10},{8,12},{10,14},{12,0},{14,2},{1,5},{3,7},... | collective-permute-start | bytes 638984 | tf_op jit(solution)/shard_map/ppermute | solution.py:94
  107.0 13.7 %collective-permute-start.13 = (f32[208,256]{1,0:T(8,128)S(1)}, f32[208,256]{1,0:T(8,128)S(1)}, u32[]{:S(2)}, u32[]{:S(2)}) collective-permute-start(f32[208,256]{1,0:T(8,128)S(1)} %get-tuple-element.15), channel_id=1, source_target_pairs={{0,8},{2,10},{4,12},{6,14},{8,0},{10,2},{12,4},{14,6},{1,9},{3,11}... | collective-permute-start | bytes 638984 | tf_op jit(solution)/shard_map/ppermute | solution.py:94
  107.4 13.4 %collective-permute-start.14 = (f32[208,256]{1,0:T(8,128)S(1)}, f32[208,256]{1,0:T(8,128)S(1)}, u32[]{:S(2)}, u32[]{:S(2)}) collective-permute-start(f32[208,256]{1,0:T(8,128)S(1)} %get-tuple-element.14), channel_id=1, source_target_pairs={{0,12},{2,14},{4,0},{6,2},{8,4},{10,6},{12,8},{14,10},{1,13},{3,15... | collective-permute-start | bytes 638984 | tf_op jit(solution)/shard_map/ppermute | solution.py:94
  120.8 8.8 %collective-permute-start.15 = (bf16[208,256]{1,0:T(8,128)(2,1)S(1)}, bf16[208,256]{1,0:T(8,128)(2,1)S(1)}, u32[]{:S(2)}, u32[]{:S(2)}) collective-permute-start(bf16[208,256]{1,0:T(8,128)(2,1)S(1)} %get-tuple-element.6), channel_id=1, source_target_pairs={{0,4},{2,6},{4,8},{6,10},{8,12},{10,14},{12,0},{14,2},{1,5},{3,7},... | collective-permute-start | bytes 319496 | tf_op jit(solution)/shard_map/ppermute | solution.py:107
  126.5 16.7 %collective-permute-start.9 = (f32[1,2,256,256]{3,2,1,0:T(8,128)S(1)}, f32[1,2,256,256]{3,2,1,0:T(8,128)S(1)}, u32[]{:S(2)}, u32[]{:S(2)}) collective-permute-start(f32[1,2,256,256]{3,2,1,0:T(8,128)S(1)} %add.249), channel_id=1, source_target_pairs={{2,0},{3,1},{18,16},{19,17}} | collective-permute-start | bytes 1572872 | tf_op jit(solution)/shard_map/ppermute | solution.py:55
  127.8 7.1 %collective-permute-start.16 = (bf16[208,256]{1,0:T(8,128)(2,1)S(1)}, bf16[208,256]{1,0:T(8,128)(2,1)S(1)}, u32[]{:S(2)}, u32[]{:S(2)}) collective-permute-start(bf16[208,256]{1,0:T(8,128)(2,1)S(1)} %get-tuple-element.6), channel_id=1, source_target_pairs={{0,8},{2,10},{4,12},{6,14},{8,0},{10,2},{12,4},{14,6},{1,9},{3,11}... | collective-permute-start | bytes 319496 | tf_op jit(solution)/shard_map/ppermute | solution.py:107
  128.2 6.9 %collective-permute-start.17 = (bf16[208,256]{1,0:T(8,128)(2,1)S(1)}, bf16[208,256]{1,0:T(8,128)(2,1)S(1)}, u32[]{:S(2)}, u32[]{:S(2)}) collective-permute-start(bf16[208,256]{1,0:T(8,128)(2,1)S(1)} %get-tuple-element.6), channel_id=1, source_target_pairs={{0,12},{2,14},{4,0},{6,2},{8,4},{10,6},{12,8},{14,10},{1,13},{3,15... | collective-permute-start | bytes 319496 | tf_op jit(solution)/shard_map/ppermute | solution.py:107
  135.2 15.9 %collective-permute-start.18 = (bf16[832,256]{1,0:T(8,128)(2,1)S(1)}, bf16[832,256]{1,0:T(8,128)(2,1)S(1)}, u32[]{:S(2)}, u32[]{:S(2)}) collective-permute-start(bf16[832,256]{1,0:T(8,128)(2,1)S(1)} %bitcast.256), channel_id=1, source_target_pairs={{0,2},{2,0},{4,6},{6,4},{8,10},{10,8},{12,14},{14,12},{1,3},{3,1},... | collective-permute-start | bytes 1277960 | tf_op jit(solution)/shard_map/ppermute | solution.py:76
  151.3 2.4 %collective-permute-start.19 = (bf16[1664,256]{1,0:T(8,128)(2,1)S(1)}, bf16[1664,256]{1,0:T(8,128)(2,1)S(1)}, u32[]{:S(2)}, u32[]{:S(2)}) collective-permute-start(bf16[1664,256]{1,0:T(8,128)(2,1)S(1)} %maximum_select_fusion), channel_id=1, source_target_pairs={{0,1},{1,0},{2,3},{3,2},{4,5},{5,4},{6,7},{7,6},{8,9},{9,8},{10,11... | collective-permute-start | bytes 2555912 | tf_op jit(solution)/shard_map/ppermute | solution.py:153

commit v22 on v21

--- a/solution.py
+++ b/solution.py
@@ -17,6 +17,20 @@
     while step * 2 < count:
         step *= 2
     while step >= 1 and count > 1:
+        pairs = [(i, i + step) for i in range(0, count, 2 * step) if i + step < count]
+        got = lax.ppermute(value, axis, pairs)
+        value = jnp.where(me % (2 * step) == step, got, value)
+        step //= 2
+    return value
+
+
+def tree_broadcast_from(value, axis, unit):
+    count = lax.axis_size(axis)
+    me = lax.axis_index(axis)
+    step = unit
+    while step * 2 < count:
+        step *= 2
+    while step >= unit:
         pairs = [(i, i + step) for i in range(0, count, 2 * step) if i + step < count]
         got = lax.ppermute(value, axis, pairs)
         value = jnp.where(me % (2 * step) == step, got, value)
@@ -240,7 +254,15 @@
     mask_f = mask.astype(jnp.float32)
     masked = latents * mask
     cot = cotangent * mask
-    first = tree_broadcast(masked[:, 0], "space")
+    paired = lax.axis_size("space") % 2 == 0
+    if paired:
+        first_even = tree_broadcast_from(masked[:, 0], "space", 2)
+        hop = lax.ppermute(
+            first_even, "space", [(i, i + 1) for i in range(0, lax.axis_size("space"), 2)]
+        )
+        first = jnp.where(slab % 2 == 1, hop, first_even)
+    else:
+        first = tree_broadcast(masked[:, 0], "space")
     cot_local = jnp.sum(cot, axis=1, dtype=jnp.float32)
     later = shifted(cot, "space", -1)
     if lax.axis_size("space") % 2 == 0:
@@ -282,9 +304,15 @@
                 lax.dot_general(piece, dpre, dims, preferred_element_type=jnp.float32)
             )
     spatial_terms = jnp.stack(spatial_terms)
+    if paired:
+        cond_lhs = first_even.astype(jnp.float32)
+        cond_rhs = cot_pair * (slab % 2 == 0).astype(jnp.float32)
+    else:
+        cond_lhs = first.astype(jnp.float32)
+        cond_rhs = cot_local
     cond_terms = lax.dot_general(
-        first.astype(jnp.float32),
-        cot_local,
+        cond_lhs,
+        cond_rhs,
         (((0, 1, 2), (0, 1, 2)), ((), ())),
         precision=lax.Precision.HIGHEST,
     )

time: 157 us -> 160 us (1.019)
  starting transfers between devices: 46.8 us -> 54.6 us
  waiting for transfers between devices: 71.2 us -> 66.2 us
    ppermute x3, waiting for transfers between devices: 23.4 us -> 3.73 us  [the longest x2 3.72 us: tree_broadcast_from(): got = lax.ppermute(value, axis, pairs)]
    ppermute x2, waiting for transfers between devices: 0.01 us -> 14.7 us  [two_column_sum(): value = value + lax.ppermute(value, axis, pairs)]
    ppermute x3, starting transfers between devices: 12.9 us -> 23.6 us  [direct_scatter(): total = total + lax.ppermute(send, axis, pairs)]
    ppermute x2, starting transfers between devices: 2.62 us -> 0.14 us  [xor_halving(): flat = keep + lax.ppermute(send, axis, pairs)]
    ppermute x1, starting transfers between devices: 2.42 us -> 0.71 us  [xor_doubling(): got = lax.ppermute(piece, axis, [(i, i ^ step) for i in range(count)])]
  transfers between devices with their start and end apart: 20 -> 20, of which waited for: 12 -> 13; matrix products, arithmetic and copies ran while one was open for 20% -> 19% of each run, Pallas kernels for 0% -> 0%
where the time goes in v22:
time: 160 us; the launch traced here: 159 us
  waiting for transfers between devices  66.2 us (41%)
  starting transfers between devices  54.6 us (34%)
  matrix products  24 us (15%)
  other arithmetic  10.2 us (6%)
  local copies, waits for them, and re-layouts  3.03 us (2%)
    ppermute x3, starting transfers between devices, direct_scatter(): total = total + lax.ppermute(send, axis, pairs)  23.6 us
    ppermute x2, waiting for transfers between devices, xor_halving(): flat = keep + lax.ppermute(send, axis, pairs)  18 us
    ppermute x2, waiting for transfers between devices, two_column_sum(): value = value + lax.ppermute(value, axis, pairs)  14.7 us
    dot_general x18, matrix products, spatial_sum(): total = total + jnp.dot(piece, kernel, preferred_element_type=jnp.float32)  11.8 us
    ppermute x3, waiting for transfers between devices, direct_scatter(): total = total + lax.ppermute(send, axis, pairs)  9.75 us
    ppermute x2, starting transfers between devices, tree_broadcast_from(): got = lax.ppermute(value, axis, pairs)  9.61 us
    ppermute x3, starting transfers between devices, direct_gather(): got = lax.ppermute(piece, axis, pairs)  7.71 us
    ppermute x1, waiting for transfers between devices, xor_doubling(): got = lax.ppermute(piece, axis, [(i, i ^ step) for i in range(count)])  6.53 us
  transfers between devices with their start and end apart: 20, of which 13 were waited for; matrix products, arithmetic and copies ran while one was open for 19% of the time, Pallas kernels for 0%

profile of v22, /device:TPU:0, one launch (start us, length us, event | category | flops | bytes accessed | tf_op | source)
XLA Modules:
  0.0 159.3 jit_solution(12795270116472014139)
XLA Ops:
  1.5 1.4 broadcast_multiply_fusion.1
  4.2 1.4 convert_reduce_fusion
  5.6 1.3 collective-permute-start.5
  7.7 8.3 %collective-permute-start.2 = (bf16[2,2,256,256]{3,2,1,0:T(8,128)(2,1)}, bf16[2,2,256,256]{3,2,1,0:T(8,128)(2,1)}, u32[]{:S(2)}, u32[]{:S(2)}) collective-permute-start(bf16[2,2,256,256]{3,2,1,0:T(8,128)(2,1)} %slice_bitcast_fusion), channel_id=1, source_target_pairs={{0,8},{1,9},{16,24},{17,25}} | collective-permute-start | bytes 1572872 | tf_op jit(solution)/shard_map/ppermute | solution.py:35
  16.0 1.4 fusion.92
  17.8 1.1 broadcast_select_fusion.7
  23.3 3.7 %collective-permute-done.2 = bf16[2,2,256,256]{3,2,1,0:T(8,128)(2,1)} collective-permute-done((bf16[2,2,256,256]{3,2,1,0:T(8,128)(2,1)}, bf16[2,2,256,256]{3,2,1,0:T(8,128)(2,1)}, u32[]{:S(2)}, u32[]{:S(2)}) %collective-permute-start.2) | collective-permute-done | bytes 524320 | tf_op jit(solution)/shard_map/ppermute | solution.py:35
  27.1 1.3 collective-permute-start.3
  28.4 1.3 multiply_convert_fusion.2
  29.7 1.5 collective-permute-start.1
  32.2 1.6 collective-permute-done.5
  34.2 1.1 multiply_convert_fusion
  39.8 4.8 %collective-permute-start.4 = (bf16[2,2,256,256]{3,2,1,0:T(8,128)(2,1)S(1)}, bf16[2,2,256,256]{3,2,1,0:T(8,128)(2,1)S(1)}, u32[]{:S(2)}, u32[]{:S(2)}) collective-permute-start(bf16[2,2,256,256]{3,2,1,0:T(8,128)(2,1)S(1)} %broadcast_select_fusion.3), channel_id=1, source_target_pairs={{0,2},{4,6},{8,10},{12,14},{1,3},{5,7},{9,11},{13,15},{16,18},{20,... | collective-permute-start | bytes 1572872 | tf_op jit(solution)/shard_map/ppermute | solution.py:260
  47.4 1.3 collective-permute-start.7
  49.8 14.7 %collective-permute-done.7 = f32[1,2,256,256]{3,2,1,0:T(8,128)S(1)} collective-permute-done((f32[1,2,256,256]{3,2,1,0:T(8,128)S(1)}, f32[1,2,256,256]{3,2,1,0:T(8,128)S(1)}, u32[]{:S(2)}, u32[]{:S(2)}) %collective-permute-start.7) | collective-permute-done | bytes 524320 | tf_op jit(solution)/shard_map/ppermute | solution.py:67
  64.6 1.5 collective-permute-start.8
  66.6 0.9 select_maximum_fusion
  70.6 1.8 %multiply_convert_fusion.1 = bf16[2,2,2,256,256]{4,3,2,1,0:T(8,128)(2,1)} fusion(f32[2,2,2,256,256]{4,3,2,1,0:T(8,128)S(1)} %fusion.111, f32[2,2,2,256,256]{4,3,2,1,0:T(8,128)S(1)} %fusion.5, bf16[2,2,2,256,256]{4,3,2,1,0:T(8,128)(2,1)S(1)} %broadcast_multiply_fusion.1, f32[2,2]{1,0:T(2,128)S(1)} %get-tuple-element.9, f32[2,2,256,256]{3,2,1,0:T(8,128)S(1)} %fusion.73, ...), kind=kOutput, calls=%fused_computation.24 | convolution fusion | flops 272105472 | bytes 8520704 | tf_op jit(solution)/shard_map/dot_general | solution.py:203
  72.4 18.0 %collective-permute-done.11 = f32[832,256]{1,0:T(8,128)S(1)} collective-permute-done((f32[832,256]{1,0:T(8,128)S(1)}, f32[832,256]{1,0:T(8,128)S(1)}, u32[]{:S(2)}, u32[]{:S(2)}) %collective-permute-start.11) | collective-permute-done | bytes 852000 | tf_op jit(solution)/shard_map/ppermute | solution.py:82
  90.5 21.2 %collective-permute-start.12 = (f32[208,256]{1,0:T(8,128)S(1)}, f32[208,256]{1,0:T(8,128)S(1)}, u32[]{:S(2)}, u32[]{:S(2)}) collective-permute-start(f32[208,256]{1,0:T(8,128)S(1)} %get-tuple-element.13), channel_id=1, source_target_pairs={{0,4},{2,6},{4,8},{6,10},{8,12},{10,14},{12,0},{14,2},{1,5},{3,7},... | collective-permute-start | bytes 638984 | tf_op jit(solution)/shard_map/ppermute | solution.py:108
  111.7 2.4 %collective-permute-start.14 = (f32[208,256]{1,0:T(8,128)S(1)}, f32[208,256]{1,0:T(8,128)S(1)}, u32[]{:S(2)}, u32[]{:S(2)}) collective-permute-start(f32[208,256]{1,0:T(8,128)S(1)} %get-tuple-element.14), channel_id=1, source_target_pairs={{0,12},{2,14},{4,0},{6,2},{8,4},{10,6},{12,8},{14,10},{1,13},{3,15... | collective-permute-start | bytes 638984 | tf_op jit(solution)/shard_map/ppermute | solution.py:108
  114.6 2.8 %collective-permute-done.12 = f32[208,256]{1,0:T(8,128)S(1)} collective-permute-done((f32[208,256]{1,0:T(8,128)S(1)}, f32[208,256]{1,0:T(8,128)S(1)}, u32[]{:S(2)}, u32[]{:S(2)}) %collective-permute-start.12) | collective-permute-done | bytes 213024 | tf_op jit(solution)/shard_map/ppermute | solution.py:108
  117.4 6.1 %collective-permute-done.13 = f32[208,256]{1,0:T(8,128)S(1)} collective-permute-done((f32[208,256]{1,0:T(8,128)S(1)}, f32[208,256]{1,0:T(8,128)S(1)}, u32[]{:S(2)}, u32[]{:S(2)}) %collective-permute-start.13) | collective-permute-done | bytes 213024 | tf_op jit(solution)/shard_map/ppermute | solution.py:108
  124.5 4.9 %collective-permute-start.15 = (bf16[208,256]{1,0:T(8,128)(2,1)S(1)}, bf16[208,256]{1,0:T(8,128)(2,1)S(1)}, u32[]{:S(2)}, u32[]{:S(2)}) collective-permute-start(bf16[208,256]{1,0:T(8,128)(2,1)S(1)} %get-tuple-element.6), channel_id=1, source_target_pairs={{0,4},{2,6},{4,8},{6,10},{8,12},{10,14},{12,0},{14,2},{1,5},{3,7},... | collective-permute-start | bytes 319496 | tf_op jit(solution)/shard_map/ppermute | solution.py:121
  129.9 1.3 collective-permute-start.9
  131.2 2.8 %collective-permute-start.16 = (bf16[208,256]{1,0:T(8,128)(2,1)S(1)}, bf16[208,256]{1,0:T(8,128)(2,1)S(1)}, u32[]{:S(2)}, u32[]{:S(2)}) collective-permute-start(bf16[208,256]{1,0:T(8,128)(2,1)S(1)} %get-tuple-element.6), channel_id=1, source_target_pairs={{0,8},{2,10},{4,12},{6,14},{8,0},{10,2},{12,4},{14,6},{1,9},{3,11}... | collective-permute-start | bytes 319496 | tf_op jit(solution)/shard_map/ppermute | solution.py:121
  134.0 1.5 collective-permute-done.15
  135.6 3.5 %collective-permute-done.16 = bf16[208,256]{1,0:T(8,128)(2,1)S(1)} collective-permute-done((bf16[208,256]{1,0:T(8,128)(2,1)S(1)}, bf16[208,256]{1,0:T(8,128)(2,1)S(1)}, u32[]{:S(2)}, u32[]{:S(2)}) %collective-permute-start.16) | collective-permute-done | bytes 106528 | tf_op jit(solution)/shard_map/ppermute | solution.py:121
  140.6 6.0 %collective-permute-done.9 = f32[1,2,256,256]{3,2,1,0:T(8,128)S(1)} collective-permute-done((f32[1,2,256,256]{3,2,1,0:T(8,128)S(1)}, f32[1,2,256,256]{3,2,1,0:T(8,128)S(1)}, u32[]{:S(2)}, u32[]{:S(2)}) %collective-permute-start.9) | collective-permute-done | bytes 524320 | tf_op jit(solution)/shard_map/ppermute | solution.py:69
  147.4 6.5 %collective-permute-done.18 = bf16[832,256]{1,0:T(8,128)(2,1)S(1)} collective-permute-done((bf16[832,256]{1,0:T(8,128)(2,1)S(1)}, bf16[832,256]{1,0:T(8,128)(2,1)S(1)}, u32[]{:S(2)}, u32[]{:S(2)}) %collective-permute-start.18) | collective-permute-done | bytes 426016 | tf_op jit(solution)/shard_map/ppermute | solution.py:90
  154.2 2.3 %fusion.4 = bf16[2,2,2,256,256]{4,3,2,1,0:T(8,128)(2,1)} fusion(bf16[2,2,2,256,256]{4,3,2,1,0:T(8,128)(2,1)S(1)} %get-tuple-element.8, f32[2,2,2,256,256]{4,3,2,1,0:T(8,128)S(1)} %fusion.17, f32[2,2,2,256,256]{4,3,2,1,0:T(8,128)S(1)} %fusion.35, f32[2,2,2,256,256]{4,3,2,1,0:T(8,128)S(1)} %fusion.37, f32[2,2,2,256,256]{4,3,2,1,0:T(8,128)S(1)} %fusion.90, ...), kind=kOutput, calls=%fused_computation.13 | convolution fusion | flops 275775488 | bytes 21104128 | tf_op jit(solution)/shard_map/dot_general | solution.py:196
  158.2 1.1 pad_maximum_fusion.3
  (95 shorter events, 27.4 us)
Async XLA Ops:
  0.6 69.2 %copy-start = (bf16[256,256]{1,0:T(8,128)(2,1)S(1)}, bf16[256,256]{1,0:T(8,128)(2,1)}, u32[]{:S(2)}) copy-start(bf16[256,256]{1,0:T(8,128)(2,1)} %param.11) | copy-start | bytes 393220
  0.6 3.5 %copy-start.4 = (bf16[2,2,2,256,256]{4,3,2,1,0:T(8,128)(2,1)S(1)}, bf16[2,2,2,256,256]{4,3,2,1,0:T(8,128)(2,1)}, u32[]{:S(2)}) copy-start(bf16[2,2,2,256,256]{4,3,2,1,0:T(8,128)(2,1)} %param.7) | copy-start | bytes 3145732
  3.7 14.1 %collective-permute-start = (bf16[2,2,1,256,256]{4,3,2,1,0:T(8,128)(2,1)}, bf16[2,2,1,256,256]{4,3,2,1,0:T(8,128)(2,1)}, u32[]{:S(2)}, u32[]{:S(2)}) collective-permute-start(bf16[2,2,1,256,256]{4,3,2,1,0:T(8,128)(2,1)} %slice_select_fusion.2), channel_id=1, source_target_pairs={{0,1},{1,0},{2,3},{3,2},{4,5},{5,4},{6,7},{7,6},{8,9},{9,8},{10,11... | collective-permute-start | bytes 1572872 | tf_op jit(solution)/shard_map/ppermute | solution.py:239
  5.6 28.2 %collective-permute-start.5 = (bf16[2,2,2,256,256]{4,3,2,1,0:T(8,128)(2,1)S(1)}, bf16[2,2,2,256,256]{4,3,2,1,0:T(8,128)(2,1)S(1)}, u32[]{:S(2)}, u32[]{:S(2)}) collective-permute-start(bf16[2,2,2,256,256]{4,3,2,1,0:T(8,128)(2,1)S(1)} %get-tuple-element.8), channel_id=1, source_target_pairs={{2,0},{4,2},{6,4},{8,6},{10,8},{12,10},{14,12},{3,1},{5,3},{7,5},{... | collective-permute-start | bytes 3145736 | tf_op jit(solution)/shard_map/ppermute | solution.py:10
  7.7 19.4 %collective-permute-start.2 = (bf16[2,2,256,256]{3,2,1,0:T(8,128)(2,1)}, bf16[2,2,256,256]{3,2,1,0:T(8,128)(2,1)}, u32[]{:S(2)}, u32[]{:S(2)}) collective-permute-start(bf16[2,2,256,256]{3,2,1,0:T(8,128)(2,1)} %slice_bitcast_fusion), channel_id=1, source_target_pairs={{0,8},{1,9},{16,24},{17,25}} | collective-permute-start | bytes 1572872 | tf_op jit(solution)/shard_map/ppermute | solution.py:35
  16.0 1.4 copy-start.3
  19.0 1.3 copy-start.2
  27.1 12.7 %collective-permute-start.3 = (bf16[2,2,256,256]{3,2,1,0:T(8,128)(2,1)S(1)}, bf16[2,2,256,256]{3,2,1,0:T(8,128)(2,1)S(1)}, u32[]{:S(2)}, u32[]{:S(2)}) collective-permute-start(bf16[2,2,256,256]{3,2,1,0:T(8,128)(2,1)S(1)} %broadcast_select_fusion.2), channel_id=1, source_target_pairs={{0,4},{8,12},{1,5},{9,13},{16,20},{24,28},{17,21},{25,29}} | collective-permute-start | bytes 1572872 | tf_op jit(solution)/shard_map/ppermute | solution.py:35
  29.7 36.4 %collective-permute-start.1 = (bf16[2,2,2,256,256]{4,3,2,1,0:T(8,128)(2,1)S(1)}, bf16[2,2,2,256,256]{4,3,2,1,0:T(8,128)(2,1)S(1)}, u32[]{:S(2)}, u32[]{:S(2)}) collective-permute-start(bf16[2,2,2,256,256]{4,3,2,1,0:T(8,128)(2,1)S(1)} %get-tuple-element.20), channel_id=1, source_target_pairs={{0,2},{2,4},{4,6},{6,8},{8,10},{10,12},{12,14},{1,3},{3,5},{5,7},{... | collective-permute-start | bytes 3145736 | tf_op jit(solution)/shard_map/ppermute | solution.py:10
  39.7 5.1 %copy-start.1 = (f32[2,2,256,256]{3,2,1,0:T(8,128)S(1)}, f32[2,2,256,256]{3,2,1,0:T(8,128)}, u32[]{:S(2)}) copy-start(f32[2,2,256,256]{3,2,1,0:T(8,128)} %get-tuple-element.7) | copy-start | bytes 3145732
  39.8 30.0 %collective-permute-start.4 = (bf16[2,2,256,256]{3,2,1,0:T(8,128)(2,1)S(1)}, bf16[2,2,256,256]{3,2,1,0:T(8,128)(2,1)S(1)}, u32[]{:S(2)}, u32[]{:S(2)}) collective-permute-start(bf16[2,2,256,256]{3,2,1,0:T(8,128)(2,1)S(1)} %broadcast_select_fusion.3), channel_id=1, source_target_pairs={{0,2},{4,6},{8,10},{12,14},{1,3},{5,7},{9,11},{13,15},{16,18},{20,... | collective-permute-start | bytes 1572872 | tf_op jit(solution)/shard_map/ppermute | solution.py:260
  47.2 22.2 %collective-permute-start.10 = (f32[1664,256]{1,0:T(8,128)S(1)}, f32[1664,256]{1,0:T(8,128)S(1)}, u32[]{:S(2)}, u32[]{:S(2)}) collective-permute-start(f32[1664,256]{1,0:T(8,128)S(1)} %constant_dynamic-slice_fusion.4), channel_id=1, source_target_pairs={{0,1},{1,0},{2,3},{3,2},{4,5},{5,4},{6,7},{7,6},{8,9},{9,8},{10,11... | collective-permute-start | bytes 5111816 | tf_op jit(solution)/shard_map/ppermute | solution.py:82
  47.4 17.1 %collective-permute-start.7 = (f32[1,2,256,256]{3,2,1,0:T(8,128)S(1)}, f32[1,2,256,256]{3,2,1,0:T(8,128)S(1)}, u32[]{:S(2)}, u32[]{:S(2)}) collective-permute-start(f32[1,2,256,256]{3,2,1,0:T(8,128)S(1)} %slice_select_fusion), channel_id=1, source_target_pairs={{8,0},{10,2},{12,4},{14,6},{9,1},{11,3},{13,5},{15,7},{24,16},{26,... | collective-permute-start | bytes 1572872 | tf_op jit(solution)/shard_map/ppermute | solution.py:67
  48.7 17.8 %collective-permute-start.6 = (bf16[2,2,1,256,256]{4,3,2,1,0:T(8,128)(2,1)S(1)}, bf16[2,2,1,256,256]{4,3,2,1,0:T(8,128)(2,1)S(1)}, u32[]{:S(2)}, u32[]{:S(2)}) collective-permute-start(bf16[2,2,1,256,256]{4,3,2,1,0:T(8,128)(2,1)S(1)} %slice_select_fusion.1), channel_id=1, source_target_pairs={{0,1},{1,0},{2,3},{3,2},{4,5},{5,4},{6,7},{7,6},{8,9},{9,8},{10,11... | collective-permute-start | bytes 1572872 | tf_op jit(solution)/shard_map/ppermute | solution.py:239
  64.6 65.2 %collective-permute-start.8 = (f32[1,2,256,256]{3,2,1,0:T(8,128)S(1)}, f32[1,2,256,256]{3,2,1,0:T(8,128)S(1)}, u32[]{:S(2)}, u32[]{:S(2)}) collective-permute-start(f32[1,2,256,256]{3,2,1,0:T(8,128)S(1)} %fusion.170), channel_id=1, source_target_pairs={{4,0},{6,2},{5,1},{7,3},{20,16},{22,18},{21,17},{23,19}} | collective-permute-start | bytes 1572872 | tf_op jit(solution)/shard_map/ppermute | solution.py:67
  69.7 20.6 %collective-permute-start.11 = (f32[832,256]{1,0:T(8,128)S(1)}, f32[832,256]{1,0:T(8,128)S(1)}, u32[]{:S(2)}, u32[]{:S(2)}) collective-permute-start(f32[832,256]{1,0:T(8,128)S(1)} %constant_dynamic-slice_fusion.3), channel_id=1, source_target_pairs={{0,2},{2,0},{4,6},{6,4},{8,10},{10,8},{12,14},{14,12},{1,3},{3,1},... | collective-permute-start | bytes 2555912 | tf_op jit(solution)/shard_map/ppermute | solution.py:82
  90.5 26.9 %collective-permute-start.12 = (f32[208,256]{1,0:T(8,128)S(1)}, f32[208,256]{1,0:T(8,128)S(1)}, u32[]{:S(2)}, u32[]{:S(2)}) collective-permute-start(f32[208,256]{1,0:T(8,128)S(1)} %get-tuple-element.13), channel_id=1, source_target_pairs={{0,4},{2,6},{4,8},{6,10},{8,12},{10,14},{12,0},{14,2},{1,5},{3,7},... | collective-permute-start | bytes 638984 | tf_op jit(solution)/shard_map/ppermute | solution.py:108
  111.7 11.8 %collective-permute-start.13 = (f32[208,256]{1,0:T(8,128)S(1)}, f32[208,256]{1,0:T(8,128)S(1)}, u32[]{:S(2)}, u32[]{:S(2)}) collective-permute-start(f32[208,256]{1,0:T(8,128)S(1)} %get-tuple-element.15), channel_id=1, source_target_pairs={{0,8},{2,10},{4,12},{6,14},{8,0},{10,2},{12,4},{14,6},{1,9},{3,11}... | collective-permute-start | bytes 638984 | tf_op jit(solution)/shard_map/ppermute | solution.py:108
  111.7 12.6 %collective-permute-start.14 = (f32[208,256]{1,0:T(8,128)S(1)}, f32[208,256]{1,0:T(8,128)S(1)}, u32[]{:S(2)}, u32[]{:S(2)}) collective-permute-start(f32[208,256]{1,0:T(8,128)S(1)} %get-tuple-element.14), channel_id=1, source_target_pairs={{0,12},{2,14},{4,0},{6,2},{8,4},{10,6},{12,8},{14,10},{1,13},{3,15... | collective-permute-start | bytes 638984 | tf_op jit(solution)/shard_map/ppermute | solution.py:108
  124.5 11.1 %collective-permute-start.15 = (bf16[208,256]{1,0:T(8,128)(2,1)S(1)}, bf16[208,256]{1,0:T(8,128)(2,1)S(1)}, u32[]{:S(2)}, u32[]{:S(2)}) collective-permute-start(bf16[208,256]{1,0:T(8,128)(2,1)S(1)} %get-tuple-element.6), channel_id=1, source_target_pairs={{0,4},{2,6},{4,8},{6,10},{8,12},{10,14},{12,0},{14,2},{1,5},{3,7},... | collective-permute-start | bytes 319496 | tf_op jit(solution)/shard_map/ppermute | solution.py:121
  129.9 16.8 %collective-permute-start.9 = (f32[1,2,256,256]{3,2,1,0:T(8,128)S(1)}, f32[1,2,256,256]{3,2,1,0:T(8,128)S(1)}, u32[]{:S(2)}, u32[]{:S(2)}) collective-permute-start(f32[1,2,256,256]{3,2,1,0:T(8,128)S(1)} %add.250), channel_id=1, source_target_pairs={{2,0},{3,1},{18,16},{19,17}} | collective-permute-start | bytes 1572872 | tf_op jit(solution)/shard_map/ppermute | solution.py:69
  131.2 7.8 %collective-permute-start.16 = (bf16[208,256]{1,0:T(8,128)(2,1)S(1)}, bf16[208,256]{1,0:T(8,128)(2,1)S(1)}, u32[]{:S(2)}, u32[]{:S(2)}) collective-permute-start(bf16[208,256]{1,0:T(8,128)(2,1)S(1)} %get-tuple-element.6), channel_id=1, source_target_pairs={{0,8},{2,10},{4,12},{6,14},{8,0},{10,2},{12,4},{14,6},{1,9},{3,11}... | collective-permute-start | bytes 319496 | tf_op jit(solution)/shard_map/ppermute | solution.py:121
  134.0 5.8 %collective-permute-start.17 = (bf16[208,256]{1,0:T(8,128)(2,1)S(1)}, bf16[208,256]{1,0:T(8,128)(2,1)S(1)}, u32[]{:S(2)}, u32[]{:S(2)}) collective-permute-start(bf16[208,256]{1,0:T(8,128)(2,1)S(1)} %get-tuple-element.6), channel_id=1, source_target_pairs={{0,12},{2,14},{4,0},{6,2},{8,4},{10,6},{12,8},{14,10},{1,13},{3,15... | collective-permute-start | bytes 319496 | tf_op jit(solution)/shard_map/ppermute | solution.py:121
  139.9 14.0 %collective-permute-start.18 = (bf16[832,256]{1,0:T(8,128)(2,1)S(1)}, bf16[832,256]{1,0:T(8,128)(2,1)S(1)}, u32[]{:S(2)}, u32[]{:S(2)}) collective-permute-start(bf16[832,256]{1,0:T(8,128)(2,1)S(1)} %bitcast.256), channel_id=1, source_target_pairs={{0,2},{2,0},{4,6},{6,4},{8,10},{10,8},{12,14},{14,12},{1,3},{3,1},... | collective-permute-start | bytes 1277960 | tf_op jit(solution)/shard_map/ppermute | solution.py:90
  154.1 2.4 %collective-permute-start.19 = (bf16[1664,256]{1,0:T(8,128)(2,1)S(1)}, bf16[1664,256]{1,0:T(8,128)(2,1)S(1)}, u32[]{:S(2)}, u32[]{:S(2)}) collective-permute-start(bf16[1664,256]{1,0:T(8,128)(2,1)S(1)} %maximum_select_fusion), channel_id=1, source_target_pairs={{0,1},{1,0},{2,3},{3,2},{4,5},{5,4},{6,7},{7,6},{8,9},{9,8},{10,11... | collective-permute-start | bytes 2555912 | tf_op jit(solution)/shard_map/ppermute | solution.py:167

commit v23 on v21

--- a/solution.py
+++ b/solution.py
@@ -22,6 +22,19 @@
         value = jnp.where(me % (2 * step) == step, got, value)
         step //= 2
     return value
+
+
+def even_first_broadcast(value, axis):
+    count = lax.axis_size(axis)
+    me = lax.axis_index(axis)
+    step = 2
+    while step < count:
+        pairs = [(i, i + step) for i in range(0, step, 2) if i + step < count]
+        got = lax.ppermute(value, axis, pairs)
+        value = jnp.where((me >= step) & (me < 2 * step) & (me % 2 == 0), got, value)
+        step *= 2
+    got = lax.ppermute(value, axis, [(i, i + 1) for i in range(0, count, 2)])
+    return jnp.where(me % 2 == 1, got, value)
 
 
 def tree_reduce(value, axis, step=1):
@@ -240,7 +253,10 @@
     mask_f = mask.astype(jnp.float32)
     masked = latents * mask
     cot = cotangent * mask
-    first = tree_broadcast(masked[:, 0], "space")
+    if lax.axis_size("space") % 2 == 0:
+        first = even_first_broadcast(masked[:, 0], "space")
+    else:
+        first = tree_broadcast(masked[:, 0], "space")
     cot_local = jnp.sum(cot, axis=1, dtype=jnp.float32)
     later = shifted(cot, "space", -1)
     if lax.axis_size("space") % 2 == 0:

time: 157 us -> 169 us (1.076)
  waiting for transfers between devices: 71.2 us -> 94.6 us
  starting transfers between devices: 46.8 us -> 35.3 us
    ppermute x2, waiting for transfers between devices: 0.01 us -> 22 us  [two_column_sum(): value = value + lax.ppermute(value, axis, pairs)]
    ppermute x3, starting transfers between devices: 12.9 us -> 4.89 us  [direct_scatter(): total = total + lax.ppermute(send, axis, pairs)]
    ppermute x2, starting transfers between devices: 2.62 us -> 0.15 us  [xor_halving(): flat = keep + lax.ppermute(send, axis, pairs)]
  transfers between devices with their start and end apart: 20 -> 20, of which waited for: 12 -> 12; matrix products, arithmetic and copies ran while one was open for 20% -> 18% of each run, Pallas kernels for 0% -> 0%
where the time goes in v23:
time: 169 us; the launch traced here: 168 us
  waiting for transfers between devices  94.6 us (56%)
  starting transfers between devices  35.3 us (21%)
  matrix products  24 us (14%)
  other arithmetic  10.2 us (6%)
  local copies, waits for them, and re-layouts  3.03 us (2%)
    ppermute x2, waiting for transfers between devices, two_column_sum(): value = value + lax.ppermute(value, axis, pairs)  22 us
    ppermute x1, waiting for transfers between devices, even_first_broadcast(): got = lax.ppermute(value, axis, [(i, i + 1) for i in range(0, count, 2)])  19.4 us
    ppermute x2, waiting for transfers between devices, xor_halving(): flat = keep + lax.ppermute(send, axis, pairs)  17.2 us
    dot_general x18, matrix products, spatial_sum(): total = total + jnp.dot(piece, kernel, preferred_element_type=jnp.float32)  11.8 us
    ppermute x3, waiting for transfers between devices, direct_scatter(): total = total + lax.ppermute(send, axis, pairs)  11 us
    ppermute x2, starting transfers between devices, even_first_broadcast(): got = lax.ppermute(value, axis, pairs)  8.6 us
    ppermute x1, waiting for transfers between devices, xor_doubling(): got = lax.ppermute(piece, axis, [(i, i ^ step) for i in range(count)])  7.16 us
    ppermute x3, starting transfers between devices, direct_gather(): got = lax.ppermute(piece, axis, pairs)  6.93 us
  transfers between devices with their start and end apart: 20, of which 12 were waited for; matrix products, arithmetic and copies ran while one was open for 18% of the time, Pallas kernels for 0%

profile of v23, /device:TPU:0, one launch (start us, length us, event | category | flops | bytes accessed | tf_op | source)
XLA Modules:
  0.0 168.4 jit_solution(9575499087954835857)
XLA Ops:
  1.5 1.4 broadcast_multiply_fusion.1
  4.2 1.4 convert_reduce_fusion
  5.6 1.3 collective-permute-start.5
  7.7 7.3 %collective-permute-start.2 = (bf16[2,2,256,256]{3,2,1,0:T(8,128)(2,1)}, bf16[2,2,256,256]{3,2,1,0:T(8,128)(2,1)}, u32[]{:S(2)}, u32[]{:S(2)}) collective-permute-start(bf16[2,2,256,256]{3,2,1,0:T(8,128)(2,1)} %slice_bitcast_fusion), channel_id=1, source_target_pairs={{0,4},{1,5},{16,20},{17,21}} | collective-permute-start | bytes 1572872 | tf_op jit(solution)/shard_map/ppermute | solution.py:33
  15.0 1.4 fusion.88
  16.8 1.1 broadcast_select_fusion.8
  22.3 3.7 %collective-permute-done.2 = bf16[2,2,256,256]{3,2,1,0:T(8,128)(2,1)} collective-permute-done((bf16[2,2,256,256]{3,2,1,0:T(8,128)(2,1)}, bf16[2,2,256,256]{3,2,1,0:T(8,128)(2,1)}, u32[]{:S(2)}, u32[]{:S(2)}) %collective-permute-start.2) | collective-permute-done | bytes 524320 | tf_op jit(solution)/shard_map/ppermute | solution.py:33
  26.1 1.3 collective-permute-start.3
  27.4 1.3 multiply_convert_fusion.2
  28.7 1.5 collective-permute-start.1
  31.2 2.6 %collective-permute-done.5 = bf16[2,2,2,256,256]{4,3,2,1,0:T(8,128)(2,1)S(1)} collective-permute-done((bf16[2,2,2,256,256]{4,3,2,1,0:T(8,128)(2,1)S(1)}, bf16[2,2,2,256,256]{4,3,2,1,0:T(8,128)(2,1)S(1)}, u32[]{:S(2)}, u32[]{:S(2)}) %collective-permute-start.5) | collective-permute-done | bytes 1048608 | tf_op jit(solution)/shard_map/ppermute | solution.py:10
  34.2 1.1 multiply_convert_fusion
  39.4 5.0 %collective-permute-start.4 = (bf16[2,2,256,256]{3,2,1,0:T(8,128)(2,1)S(1)}, bf16[2,2,256,256]{3,2,1,0:T(8,128)(2,1)S(1)}, u32[]{:S(2)}, u32[]{:S(2)}) collective-permute-start(bf16[2,2,256,256]{3,2,1,0:T(8,128)(2,1)S(1)} %broadcast_select_fusion.3), channel_id=1, source_target_pairs={{0,2},{4,6},{8,10},{12,14},{1,3},{5,7},{9,11},{13,15},{16,18},{20,... | collective-permute-start | bytes 1572872 | tf_op jit(solution)/shard_map/ppermute | solution.py:36
  44.8 1.3 collective-permute-start.7
  48.2 19.4 %collective-permute-done.4 = bf16[2,2,256,256]{3,2,1,0:T(8,128)(2,1)S(1)} collective-permute-done((bf16[2,2,256,256]{3,2,1,0:T(8,128)(2,1)S(1)}, bf16[2,2,256,256]{3,2,1,0:T(8,128)(2,1)S(1)}, u32[]{:S(2)}, u32[]{:S(2)}) %collective-permute-start.4) | collective-permute-done | bytes 524320 | tf_op jit(solution)/shard_map/ppermute | solution.py:36
  68.9 22.0 %collective-permute-done.7 = f32[1,2,256,256]{3,2,1,0:T(8,128)S(1)} collective-permute-done((f32[1,2,256,256]{3,2,1,0:T(8,128)S(1)}, f32[1,2,256,256]{3,2,1,0:T(8,128)S(1)}, u32[]{:S(2)}, u32[]{:S(2)}) %collective-permute-start.7) | collective-permute-done | bytes 524320 | tf_op jit(solution)/shard_map/ppermute | solution.py:66
  91.0 1.5 collective-permute-start.8
  97.1 1.8 %multiply_convert_fusion.1 = bf16[2,2,2,256,256]{4,3,2,1,0:T(8,128)(2,1)} fusion(f32[2,2,2,256,256]{4,3,2,1,0:T(8,128)S(1)} %fusion.107, f32[2,2,2,256,256]{4,3,2,1,0:T(8,128)S(1)} %fusion.5, bf16[2,2,2,256,256]{4,3,2,1,0:T(8,128)(2,1)S(1)} %broadcast_multiply_fusion.1, f32[2,2]{1,0:T(2,128)S(1)} %get-tuple-element.9, f32[2,2,256,256]{3,2,1,0:T(8,128)S(1)} %fusion.71, ...), kind=kOutput, calls=%fused_computation.24 | convolution fusion | flops 272105472 | bytes 8520704 | tf_op jit(solution)/shard_map/dot_general | solution.py:202
  98.8 17.2 %collective-permute-done.11 = f32[832,256]{1,0:T(8,128)S(1)} collective-permute-done((f32[832,256]{1,0:T(8,128)S(1)}, f32[832,256]{1,0:T(8,128)S(1)}, u32[]{:S(2)}, u32[]{:S(2)}) %collective-permute-start.11) | collective-permute-done | bytes 852000 | tf_op jit(solution)/shard_map/ppermute | solution.py:81
  116.2 2.4 %collective-permute-start.12 = (f32[208,256]{1,0:T(8,128)S(1)}, f32[208,256]{1,0:T(8,128)S(1)}, u32[]{:S(2)}, u32[]{:S(2)}) collective-permute-start(f32[208,256]{1,0:T(8,128)S(1)} %get-tuple-element.13), channel_id=1, source_target_pairs={{0,4},{2,6},{4,8},{6,10},{8,12},{10,14},{12,0},{14,2},{1,5},{3,7},... | collective-permute-start | bytes 638984 | tf_op jit(solution)/shard_map/ppermute | solution.py:107
  118.7 2.4 %collective-permute-start.14 = (f32[208,256]{1,0:T(8,128)S(1)}, f32[208,256]{1,0:T(8,128)S(1)}, u32[]{:S(2)}, u32[]{:S(2)}) collective-permute-start(f32[208,256]{1,0:T(8,128)S(1)} %get-tuple-element.14), channel_id=1, source_target_pairs={{0,12},{2,14},{4,0},{6,2},{8,4},{10,6},{12,8},{14,10},{1,13},{3,15... | collective-permute-start | bytes 638984 | tf_op jit(solution)/shard_map/ppermute | solution.py:107
  121.6 4.8 %collective-permute-done.12 = f32[208,256]{1,0:T(8,128)S(1)} collective-permute-done((f32[208,256]{1,0:T(8,128)S(1)}, f32[208,256]{1,0:T(8,128)S(1)}, u32[]{:S(2)}, u32[]{:S(2)}) %collective-permute-start.12) | collective-permute-done | bytes 213024 | tf_op jit(solution)/shard_map/ppermute | solution.py:107
  126.4 6.3 %collective-permute-done.13 = f32[208,256]{1,0:T(8,128)S(1)} collective-permute-done((f32[208,256]{1,0:T(8,128)S(1)}, f32[208,256]{1,0:T(8,128)S(1)}, u32[]{:S(2)}, u32[]{:S(2)}) %collective-permute-start.13) | collective-permute-done | bytes 213024 | tf_op jit(solution)/shard_map/ppermute | solution.py:107
  132.7 5.1 %collective-permute-start.15 = (bf16[208,256]{1,0:T(8,128)(2,1)S(1)}, bf16[208,256]{1,0:T(8,128)(2,1)S(1)}, u32[]{:S(2)}, u32[]{:S(2)}) collective-permute-start(bf16[208,256]{1,0:T(8,128)(2,1)S(1)} %get-tuple-element.6), channel_id=1, source_target_pairs={{0,4},{2,6},{4,8},{6,10},{8,12},{10,14},{12,0},{14,2},{1,5},{3,7},... | collective-permute-start | bytes 319496 | tf_op jit(solution)/shard_map/ppermute | solution.py:120
  138.4 1.3 collective-permute-start.9
  140.0 1.5 collective-permute-start.17
  141.6 5.3 %collective-permute-done.16 = bf16[208,256]{1,0:T(8,128)(2,1)S(1)} collective-permute-done((bf16[208,256]{1,0:T(8,128)(2,1)S(1)}, bf16[208,256]{1,0:T(8,128)(2,1)S(1)}, u32[]{:S(2)}, u32[]{:S(2)}) %collective-permute-start.16) | collective-permute-done | bytes 106528 | tf_op jit(solution)/shard_map/ppermute | solution.py:120
  147.0 2.2 %collective-permute-start.18 = (bf16[832,256]{1,0:T(8,128)(2,1)S(1)}, bf16[832,256]{1,0:T(8,128)(2,1)S(1)}, u32[]{:S(2)}, u32[]{:S(2)}) collective-permute-start(bf16[832,256]{1,0:T(8,128)(2,1)S(1)} %bitcast.256), channel_id=1, source_target_pairs={{0,2},{2,0},{4,6},{6,4},{8,10},{10,8},{12,14},{14,12},{1,3},{3,1},... | collective-permute-start | bytes 1277960 | tf_op jit(solution)/shard_map/ppermute | solution.py:89
  149.2 5.9 %collective-permute-done.9 = f32[1,2,256,256]{3,2,1,0:T(8,128)S(1)} collective-permute-done((f32[1,2,256,256]{3,2,1,0:T(8,128)S(1)}, f32[1,2,256,256]{3,2,1,0:T(8,128)S(1)}, u32[]{:S(2)}, u32[]{:S(2)}) %collective-permute-start.9) | collective-permute-done | bytes 524320 | tf_op jit(solution)/shard_map/ppermute | solution.py:68
  155.8 7.2 %collective-permute-done.18 = bf16[832,256]{1,0:T(8,128)(2,1)S(1)} collective-permute-done((bf16[832,256]{1,0:T(8,128)(2,1)S(1)}, bf16[832,256]{1,0:T(8,128)(2,1)S(1)}, u32[]{:S(2)}, u32[]{:S(2)}) %collective-permute-start.18) | collective-permute-done | bytes 426016 | tf_op jit(solution)/shard_map/ppermute | solution.py:89
  163.3 2.3 %fusion.4 = bf16[2,2,2,256,256]{4,3,2,1,0:T(8,128)(2,1)} fusion(bf16[2,2,2,256,256]{4,3,2,1,0:T(8,128)(2,1)S(1)} %get-tuple-element.8, f32[2,2,2,256,256]{4,3,2,1,0:T(8,128)S(1)} %fusion.17, f32[2,2,2,256,256]{4,3,2,1,0:T(8,128)S(1)} %fusion.35, f32[2,2,2,256,256]{4,3,2,1,0:T(8,128)S(1)} %fusion.37, f32[2,2,2,256,256]{4,3,2,1,0:T(8,128)S(1)} %fusion.86, ...), kind=kOutput, calls=%fused_computation.13 | convolution fusion | flops 275775488 | bytes 21104128 | tf_op jit(solution)/shard_map/dot_general | solution.py:195
  167.3 1.1 pad_maximum_fusion.3
  (95 shorter events, 25.9 us)
Async XLA Ops:
  0.6 95.6 %copy-start = (bf16[256,256]{1,0:T(8,128)(2,1)S(1)}, bf16[256,256]{1,0:T(8,128)(2,1)}, u32[]{:S(2)}) copy-start(bf16[256,256]{1,0:T(8,128)(2,1)} %param.11) | copy-start | bytes 393220
  0.6 3.5 %copy-start.4 = (bf16[2,2,2,256,256]{4,3,2,1,0:T(8,128)(2,1)S(1)}, bf16[2,2,2,256,256]{4,3,2,1,0:T(8,128)(2,1)}, u32[]{:S(2)}) copy-start(bf16[2,2,2,256,256]{4,3,2,1,0:T(8,128)(2,1)} %param.7) | copy-start | bytes 3145732
  3.7 13.1 %collective-permute-start = (bf16[2,2,1,256,256]{4,3,2,1,0:T(8,128)(2,1)}, bf16[2,2,1,256,256]{4,3,2,1,0:T(8,128)(2,1)}, u32[]{:S(2)}, u32[]{:S(2)}) collective-permute-start(bf16[2,2,1,256,256]{4,3,2,1,0:T(8,128)(2,1)} %slice_select_fusion.2), channel_id=1, source_target_pairs={{0,1},{1,0},{2,3},{3,2},{4,5},{5,4},{6,7},{7,6},{8,9},{9,8},{10,11... | collective-permute-start | bytes 1572872 | tf_op jit(solution)/shard_map/ppermute | solution.py:238
  5.6 28.2 %collective-permute-start.5 = (bf16[2,2,2,256,256]{4,3,2,1,0:T(8,128)(2,1)S(1)}, bf16[2,2,2,256,256]{4,3,2,1,0:T(8,128)(2,1)S(1)}, u32[]{:S(2)}, u32[]{:S(2)}) collective-permute-start(bf16[2,2,2,256,256]{4,3,2,1,0:T(8,128)(2,1)S(1)} %get-tuple-element.8), channel_id=1, source_target_pairs={{2,0},{4,2},{6,4},{8,6},{10,8},{12,10},{14,12},{3,1},{5,3},{7,5},{... | collective-permute-start | bytes 3145736 | tf_op jit(solution)/shard_map/ppermute | solution.py:10
  7.7 18.3 %collective-permute-start.2 = (bf16[2,2,256,256]{3,2,1,0:T(8,128)(2,1)}, bf16[2,2,256,256]{3,2,1,0:T(8,128)(2,1)}, u32[]{:S(2)}, u32[]{:S(2)}) collective-permute-start(bf16[2,2,256,256]{3,2,1,0:T(8,128)(2,1)} %slice_bitcast_fusion), channel_id=1, source_target_pairs={{0,4},{1,5},{16,20},{17,21}} | collective-permute-start | bytes 1572872 | tf_op jit(solution)/shard_map/ppermute | solution.py:33
  15.0 1.4 copy-start.3
  17.9 1.3 copy-start.2
  26.1 13.3 %collective-permute-start.3 = (bf16[2,2,256,256]{3,2,1,0:T(8,128)(2,1)S(1)}, bf16[2,2,256,256]{3,2,1,0:T(8,128)(2,1)S(1)}, u32[]{:S(2)}, u32[]{:S(2)}) collective-permute-start(bf16[2,2,256,256]{3,2,1,0:T(8,128)(2,1)S(1)} %broadcast_select_fusion.2), channel_id=1, source_target_pairs={{0,8},{4,12},{1,9},{5,13},{16,24},{20,28},{17,25},{21,29}} | collective-permute-start | bytes 1572872 | tf_op jit(solution)/shard_map/ppermute | solution.py:33
  28.7 63.8 %collective-permute-start.1 = (bf16[2,2,2,256,256]{4,3,2,1,0:T(8,128)(2,1)S(1)}, bf16[2,2,2,256,256]{4,3,2,1,0:T(8,128)(2,1)S(1)}, u32[]{:S(2)}, u32[]{:S(2)}) collective-permute-start(bf16[2,2,2,256,256]{4,3,2,1,0:T(8,128)(2,1)S(1)} %get-tuple-element.20), channel_id=1, source_target_pairs={{0,2},{2,4},{4,6},{6,8},{8,10},{10,12},{12,14},{1,3},{3,5},{5,7},{... | collective-permute-start | bytes 3145736 | tf_op jit(solution)/shard_map/ppermute | solution.py:10
  39.3 5.3 %copy-start.1 = (f32[2,2,256,256]{3,2,1,0:T(8,128)S(1)}, f32[2,2,256,256]{3,2,1,0:T(8,128)}, u32[]{:S(2)}) copy-start(f32[2,2,256,256]{3,2,1,0:T(8,128)} %get-tuple-element.7) | copy-start | bytes 3145732
  39.4 28.2 %collective-permute-start.4 = (bf16[2,2,256,256]{3,2,1,0:T(8,128)(2,1)S(1)}, bf16[2,2,256,256]{3,2,1,0:T(8,128)(2,1)S(1)}, u32[]{:S(2)}, u32[]{:S(2)}) collective-permute-start(bf16[2,2,256,256]{3,2,1,0:T(8,128)(2,1)S(1)} %broadcast_select_fusion.3), channel_id=1, source_target_pairs={{0,2},{4,6},{8,10},{12,14},{1,3},{5,7},{9,11},{13,15},{16,18},{20,... | collective-permute-start | bytes 1572872 | tf_op jit(solution)/shard_map/ppermute | solution.py:36
  44.8 46.1 %collective-permute-start.7 = (f32[1,2,256,256]{3,2,1,0:T(8,128)S(1)}, f32[1,2,256,256]{3,2,1,0:T(8,128)S(1)}, u32[]{:S(2)}, u32[]{:S(2)}) collective-permute-start(f32[1,2,256,256]{3,2,1,0:T(8,128)S(1)} %slice_select_fusion), channel_id=1, source_target_pairs={{8,0},{10,2},{12,4},{14,6},{9,1},{11,3},{13,5},{15,7},{24,16},{26,... | collective-permute-start | bytes 1572872 | tf_op jit(solution)/shard_map/ppermute | solution.py:66
  46.1 46.9 %collective-permute-start.6 = (bf16[2,2,1,256,256]{4,3,2,1,0:T(8,128)(2,1)S(1)}, bf16[2,2,1,256,256]{4,3,2,1,0:T(8,128)(2,1)S(1)}, u32[]{:S(2)}, u32[]{:S(2)}) collective-permute-start(bf16[2,2,1,256,256]{4,3,2,1,0:T(8,128)(2,1)S(1)} %slice_select_fusion.1), channel_id=1, source_target_pairs={{0,1},{1,0},{2,3},{3,2},{4,5},{5,4},{6,7},{7,6},{8,9},{9,8},{10,11... | collective-permute-start | bytes 1572872 | tf_op jit(solution)/shard_map/ppermute | solution.py:238
  68.8 27.0 %collective-permute-start.10 = (f32[1664,256]{1,0:T(8,128)S(1)}, f32[1664,256]{1,0:T(8,128)S(1)}, u32[]{:S(2)}, u32[]{:S(2)}) collective-permute-start(f32[1664,256]{1,0:T(8,128)S(1)} %constant_dynamic-slice_fusion.4), channel_id=1, source_target_pairs={{0,1},{1,0},{2,3},{3,2},{4,5},{5,4},{6,7},{7,6},{8,9},{9,8},{10,11... | collective-permute-start | bytes 5111816 | tf_op jit(solution)/shard_map/ppermute | solution.py:81
  91.0 47.3 %collective-permute-start.8 = (f32[1,2,256,256]{3,2,1,0:T(8,128)S(1)}, f32[1,2,256,256]{3,2,1,0:T(8,128)S(1)}, u32[]{:S(2)}, u32[]{:S(2)}) collective-permute-start(f32[1,2,256,256]{3,2,1,0:T(8,128)S(1)} %fusion.166), channel_id=1, source_target_pairs={{4,0},{6,2},{5,1},{7,3},{20,16},{22,18},{21,17},{23,19}} | collective-permute-start | bytes 1572872 | tf_op jit(solution)/shard_map/ppermute | solution.py:66
  96.2 19.9 %collective-permute-start.11 = (f32[832,256]{1,0:T(8,128)S(1)}, f32[832,256]{1,0:T(8,128)S(1)}, u32[]{:S(2)}, u32[]{:S(2)}) collective-permute-start(f32[832,256]{1,0:T(8,128)S(1)} %constant_dynamic-slice_fusion.3), channel_id=1, source_target_pairs={{0,2},{2,0},{4,6},{6,4},{8,10},{10,8},{12,14},{14,12},{1,3},{3,1},... | collective-permute-start | bytes 2555912 | tf_op jit(solution)/shard_map/ppermute | solution.py:81
  116.2 10.1 %collective-permute-start.12 = (f32[208,256]{1,0:T(8,128)S(1)}, f32[208,256]{1,0:T(8,128)S(1)}, u32[]{:S(2)}, u32[]{:S(2)}) collective-permute-start(f32[208,256]{1,0:T(8,128)S(1)} %get-tuple-element.13), channel_id=1, source_target_pairs={{0,4},{2,6},{4,8},{6,10},{8,12},{10,14},{12,0},{14,2},{1,5},{3,7},... | collective-permute-start | bytes 638984 | tf_op jit(solution)/shard_map/ppermute | solution.py:107
  118.7 13.9 %collective-permute-start.13 = (f32[208,256]{1,0:T(8,128)S(1)}, f32[208,256]{1,0:T(8,128)S(1)}, u32[]{:S(2)}, u32[]{:S(2)}) collective-permute-start(f32[208,256]{1,0:T(8,128)S(1)} %get-tuple-element.15), channel_id=1, source_target_pairs={{0,8},{2,10},{4,12},{6,14},{8,0},{10,2},{12,4},{14,6},{1,9},{3,11}... | collective-permute-start | bytes 638984 | tf_op jit(solution)/shard_map/ppermute | solution.py:107
  118.7 13.9 %collective-permute-start.14 = (f32[208,256]{1,0:T(8,128)S(1)}, f32[208,256]{1,0:T(8,128)S(1)}, u32[]{:S(2)}, u32[]{:S(2)}) collective-permute-start(f32[208,256]{1,0:T(8,128)S(1)} %get-tuple-element.14), channel_id=1, source_target_pairs={{0,12},{2,14},{4,0},{6,2},{8,4},{10,6},{12,8},{14,10},{1,13},{3,15... | collective-permute-start | bytes 638984 | tf_op jit(solution)/shard_map/ppermute | solution.py:107
  132.7 8.8 %collective-permute-start.15 = (bf16[208,256]{1,0:T(8,128)(2,1)S(1)}, bf16[208,256]{1,0:T(8,128)(2,1)S(1)}, u32[]{:S(2)}, u32[]{:S(2)}) collective-permute-start(bf16[208,256]{1,0:T(8,128)(2,1)S(1)} %get-tuple-element.6), channel_id=1, source_target_pairs={{0,4},{2,6},{4,8},{6,10},{8,12},{10,14},{12,0},{14,2},{1,5},{3,7},... | collective-permute-start | bytes 319496 | tf_op jit(solution)/shard_map/ppermute | solution.py:120
  138.4 16.7 %collective-permute-start.9 = (f32[1,2,256,256]{3,2,1,0:T(8,128)S(1)}, f32[1,2,256,256]{3,2,1,0:T(8,128)S(1)}, u32[]{:S(2)}, u32[]{:S(2)}) collective-permute-start(f32[1,2,256,256]{3,2,1,0:T(8,128)S(1)} %add.243), channel_id=1, source_target_pairs={{2,0},{3,1},{18,16},{19,17}} | collective-permute-start | bytes 1572872 | tf_op jit(solution)/shard_map/ppermute | solution.py:68
  139.7 7.1 %collective-permute-start.16 = (bf16[208,256]{1,0:T(8,128)(2,1)S(1)}, bf16[208,256]{1,0:T(8,128)(2,1)S(1)}, u32[]{:S(2)}, u32[]{:S(2)}) collective-permute-start(bf16[208,256]{1,0:T(8,128)(2,1)S(1)} %get-tuple-element.6), channel_id=1, source_target_pairs={{0,8},{2,10},{4,12},{6,14},{8,0},{10,2},{12,4},{14,6},{1,9},{3,11}... | collective-permute-start | bytes 319496 | tf_op jit(solution)/shard_map/ppermute | solution.py:120
  140.0 6.9 %collective-permute-start.17 = (bf16[208,256]{1,0:T(8,128)(2,1)S(1)}, bf16[208,256]{1,0:T(8,128)(2,1)S(1)}, u32[]{:S(2)}, u32[]{:S(2)}) collective-permute-start(bf16[208,256]{1,0:T(8,128)(2,1)S(1)} %get-tuple-element.6), channel_id=1, source_target_pairs={{0,12},{2,14},{4,0},{6,2},{8,4},{10,6},{12,8},{14,10},{1,13},{3,15... | collective-permute-start | bytes 319496 | tf_op jit(solution)/shard_map/ppermute | solution.py:120
  147.0 16.0 %collective-permute-start.18 = (bf16[832,256]{1,0:T(8,128)(2,1)S(1)}, bf16[832,256]{1,0:T(8,128)(2,1)S(1)}, u32[]{:S(2)}, u32[]{:S(2)}) collective-permute-start(bf16[832,256]{1,0:T(8,128)(2,1)S(1)} %bitcast.256), channel_id=1, source_target_pairs={{0,2},{2,0},{4,6},{6,4},{8,10},{10,8},{12,14},{14,12},{1,3},{3,1},... | collective-permute-start | bytes 1277960 | tf_op jit(solution)/shard_map/ppermute | solution.py:89
  163.2 2.4 %collective-permute-start.19 = (bf16[1664,256]{1,0:T(8,128)(2,1)S(1)}, bf16[1664,256]{1,0:T(8,128)(2,1)S(1)}, u32[]{:S(2)}, u32[]{:S(2)}) collective-permute-start(bf16[1664,256]{1,0:T(8,128)(2,1)S(1)} %maximum_select_fusion), channel_id=1, source_target_pairs={{0,1},{1,0},{2,3},{3,2},{4,5},{5,4},{6,7},{7,6},{8,9},{9,8},{10,11... | collective-permute-start | bytes 2555912 | tf_op jit(solution)/shard_map/ppermute | solution.py:166

commit v24 on v21

--- a/solution.py
+++ b/solution.py
@@ -86,7 +86,7 @@
     j = me // low
     blk = flat.shape[0] // high
     total = lax.dynamic_slice_in_dim(flat, j * blk, blk, 0)
-    for d in range(1, high):
+    for d in sorted(range(1, high), key=lambda d: -min(d, high - d)):
         send = lax.dynamic_slice_in_dim(flat, ((j + d) % high) * blk, blk, 0)
         pairs = [
             (a * low + b, ((a + d) % high) * low + b) for a in range(high) for b in range(low)
@@ -100,7 +100,7 @@
     j = me // low
     out = jnp.zeros((high,) + piece.shape, piece.dtype)
     out = lax.dynamic_update_index_in_dim(out, piece, j, 0)
-    for d in range(1, high):
+    for d in sorted(range(1, high), key=lambda d: -min(d, high - d)):
         pairs = [
             (a * low + b, ((a + d) % high) * low + b) for a in range(high) for b in range(low)
         ]

time: 157 us -> 152 us (0.968)
  waiting for transfers between devices: 71.2 us -> 66.4 us
    ppermute x3, waiting for transfers between devices: 5.48 us -> 3.15 us  [direct_gather(): got = lax.ppermute(piece, axis, pairs)]
where the time goes in v24:
time: 152 us
  waiting for transfers between devices  66.4 us (44%)
  starting transfers between devices  46.9 us (31%)
  matrix products  24 us (16%)
  other arithmetic  10.2 us (7%)
  local copies, waits for them, and re-layouts  3.03 us (2%)
    ppermute x3, waiting for transfers between devices, tree_broadcast(): got = lax.ppermute(value, axis, pairs)  23.4 us
    ppermute x2, waiting for transfers between devices, xor_halving(): flat = keep + lax.ppermute(send, axis, pairs)  17 us
    ppermute x3, starting transfers between devices, tree_broadcast(): got = lax.ppermute(value, axis, pairs)  14.4 us
    ppermute x3, starting transfers between devices, direct_scatter(): total = total + lax.ppermute(send, axis, pairs)  12.9 us
    dot_general x18, matrix products, spatial_sum(): total = total + jnp.dot(piece, kernel, preferred_element_type=jnp.float32)  11.8 us
    ppermute x3, waiting for transfers between devices, direct_scatter(): total = total + lax.ppermute(send, axis, pairs)  9.36 us
    ppermute x3, starting transfers between devices, direct_gather(): got = lax.ppermute(piece, axis, pairs)  7.19 us
    ppermute x1, waiting for transfers between devices, two_column_sum(): got = lax.ppermute(value, axis, [(1, 0)])  6.01 us
  transfers between devices with their start and end apart: 20, of which 12 were waited for; matrix products, arithmetic and copies ran while one was open for 20% of the time, Pallas kernels for 0%

profile of v24, /device:TPU:0, one launch (start us, length us, event | category | flops | bytes accessed | tf_op | source)
XLA Modules:
  0.0 151.7 jit_solution(16888948668047005252)
XLA Ops:
  1.5 1.4 broadcast_multiply_fusion.1
  4.2 1.4 convert_reduce_fusion
  5.6 1.3 collective-permute-start.5
  7.7 8.3 %collective-permute-start.2 = (bf16[2,2,256,256]{3,2,1,0:T(8,128)(2,1)}, bf16[2,2,256,256]{3,2,1,0:T(8,128)(2,1)}, u32[]{:S(2)}, u32[]{:S(2)}) collective-permute-start(bf16[2,2,256,256]{3,2,1,0:T(8,128)(2,1)} %slice_bitcast_fusion), channel_id=1, source_target_pairs={{0,8},{1,9},{16,24},{17,25}} | collective-permute-start | bytes 1572872 | tf_op jit(solution)/shard_map/ppermute | solution.py:21
  16.0 1.4 fusion.88
  17.8 1.1 broadcast_select_fusion.8
  23.3 3.7 %collective-permute-done.2 = bf16[2,2,256,256]{3,2,1,0:T(8,128)(2,1)} collective-permute-done((bf16[2,2,256,256]{3,2,1,0:T(8,128)(2,1)}, bf16[2,2,256,256]{3,2,1,0:T(8,128)(2,1)}, u32[]{:S(2)}, u32[]{:S(2)}) %collective-permute-start.2) | collective-permute-done | bytes 524320 | tf_op jit(solution)/shard_map/ppermute | solution.py:21
  27.1 1.3 collective-permute-start.3
  28.4 1.3 multiply_convert_fusion.2
  29.7 1.5 %collective-permute-start.1 = (bf16[2,2,2,256,256]{4,3,2,1,0:T(8,128)(2,1)S(1)}, bf16[2,2,2,256,256]{4,3,2,1,0:T(8,128)(2,1)S(1)}, u32[]{:S(2)}, u32[]{:S(2)}) collective-permute-start(bf16[2,2,2,256,256]{4,3,2,1,0:T(8,128)(2,1)S(1)} %get-tuple-element.20), channel_id=1, source_target_pairs={{0,2},{2,4},{4,6},{6,8},{8,10},{10,12},{12,14},{1,3},{3,5},{5,7},{... | collective-permute-start | bytes 3145736 | tf_op jit(solution)/shard_map/ppermute | solution.py:10
  32.2 1.6 %collective-permute-done.5 = bf16[2,2,2,256,256]{4,3,2,1,0:T(8,128)(2,1)S(1)} collective-permute-done((bf16[2,2,2,256,256]{4,3,2,1,0:T(8,128)(2,1)S(1)}, bf16[2,2,2,256,256]{4,3,2,1,0:T(8,128)(2,1)S(1)}, u32[]{:S(2)}, u32[]{:S(2)}) %collective-permute-start.5) | collective-permute-done | bytes 1048608 | tf_op jit(solution)/shard_map/ppermute | solution.py:10
  34.2 1.1 multiply_convert_fusion
  39.5 4.8 %collective-permute-start.4 = (bf16[2,2,256,256]{3,2,1,0:T(8,128)(2,1)S(1)}, bf16[2,2,256,256]{3,2,1,0:T(8,128)(2,1)S(1)}, u32[]{:S(2)}, u32[]{:S(2)}) collective-permute-start(bf16[2,2,256,256]{3,2,1,0:T(8,128)(2,1)S(1)} %broadcast_select_fusion.3), channel_id=1, source_target_pairs={{0,2},{4,6},{8,10},{12,14},{1,3},{5,7},{9,11},{13,15},{16,18},{20,... | collective-permute-start | bytes 1572872 | tf_op jit(solution)/shard_map/ppermute | solution.py:21
  44.6 1.3 collective-permute-start.7
  48.0 19.6 %collective-permute-done.4 = bf16[2,2,256,256]{3,2,1,0:T(8,128)(2,1)S(1)} collective-permute-done((bf16[2,2,256,256]{3,2,1,0:T(8,128)(2,1)S(1)}, bf16[2,2,256,256]{3,2,1,0:T(8,128)(2,1)S(1)}, u32[]{:S(2)}, u32[]{:S(2)}) %collective-permute-start.4) | collective-permute-done | bytes 524320 | tf_op jit(solution)/shard_map/ppermute | solution.py:21
  69.0 1.5 collective-permute-start.8
  74.2 2.5 %collective-permute-start.11 = (f32[832,256]{1,0:T(8,128)S(1)}, f32[832,256]{1,0:T(8,128)S(1)}, u32[]{:S(2)}, u32[]{:S(2)}) collective-permute-start(f32[832,256]{1,0:T(8,128)S(1)} %constant_dynamic-slice_fusion.3), channel_id=1, source_target_pairs={{0,2},{2,0},{4,6},{6,4},{8,10},{10,8},{12,14},{14,12},{1,3},{3,1},... | collective-permute-start | bytes 2555912 | tf_op jit(solution)/shard_map/ppermute | solution.py:68
  77.5 1.8 %multiply_convert_fusion.1 = bf16[2,2,2,256,256]{4,3,2,1,0:T(8,128)(2,1)} fusion(f32[2,2,2,256,256]{4,3,2,1,0:T(8,128)S(1)} %fusion.107, f32[2,2,2,256,256]{4,3,2,1,0:T(8,128)S(1)} %fusion.5, bf16[2,2,2,256,256]{4,3,2,1,0:T(8,128)(2,1)S(1)} %broadcast_multiply_fusion.1, f32[2,2]{1,0:T(2,128)S(1)} %get-tuple-element.9, f32[2,2,256,256]{3,2,1,0:T(8,128)S(1)} %fusion.71, ...), kind=kOutput, calls=%fused_computation.24 | convolution fusion | flops 272105472 | bytes 8520704 | tf_op jit(solution)/shard_map/dot_general | solution.py:189
  79.3 17.0 %collective-permute-done.11 = f32[832,256]{1,0:T(8,128)S(1)} collective-permute-done((f32[832,256]{1,0:T(8,128)S(1)}, f32[832,256]{1,0:T(8,128)S(1)}, u32[]{:S(2)}, u32[]{:S(2)}) %collective-permute-start.11) | collective-permute-done | bytes 852000 | tf_op jit(solution)/shard_map/ppermute | solution.py:68
  96.5 2.0 %collective-permute-start.12 = (f32[208,256]{1,0:T(8,128)S(1)}, f32[208,256]{1,0:T(8,128)S(1)}, u32[]{:S(2)}, u32[]{:S(2)}) collective-permute-start(f32[208,256]{1,0:T(8,128)S(1)} %get-tuple-element.13), channel_id=1, source_target_pairs={{0,8},{2,10},{4,12},{6,14},{8,0},{10,2},{12,4},{14,6},{1,9},{3,11}... | collective-permute-start | bytes 638984 | tf_op jit(solution)/shard_map/ppermute | solution.py:94
  98.5 8.9 %collective-permute-start.13 = (f32[208,256]{1,0:T(8,128)S(1)}, f32[208,256]{1,0:T(8,128)S(1)}, u32[]{:S(2)}, u32[]{:S(2)}) collective-permute-start(f32[208,256]{1,0:T(8,128)S(1)} %get-tuple-element.15), channel_id=1, source_target_pairs={{0,4},{2,6},{4,8},{6,10},{8,12},{10,14},{12,0},{14,2},{1,5},{3,7},... | collective-permute-start | bytes 638984 | tf_op jit(solution)/shard_map/ppermute | solution.py:94
  107.4 2.0 %collective-permute-start.14 = (f32[208,256]{1,0:T(8,128)S(1)}, f32[208,256]{1,0:T(8,128)S(1)}, u32[]{:S(2)}, u32[]{:S(2)}) collective-permute-start(f32[208,256]{1,0:T(8,128)S(1)} %get-tuple-element.14), channel_id=1, source_target_pairs={{0,12},{2,14},{4,0},{6,2},{8,4},{10,6},{12,8},{14,10},{1,13},{3,15... | collective-permute-start | bytes 638984 | tf_op jit(solution)/shard_map/ppermute | solution.py:94
  109.8 9.4 %collective-permute-done.13 = f32[208,256]{1,0:T(8,128)S(1)} collective-permute-done((f32[208,256]{1,0:T(8,128)S(1)}, f32[208,256]{1,0:T(8,128)S(1)}, u32[]{:S(2)}, u32[]{:S(2)}) %collective-permute-start.13) | collective-permute-done | bytes 213024 | tf_op jit(solution)/shard_map/ppermute | solution.py:94
  119.3 3.3 %collective-permute-start.15 = (bf16[208,256]{1,0:T(8,128)(2,1)S(1)}, bf16[208,256]{1,0:T(8,128)(2,1)S(1)}, u32[]{:S(2)}, u32[]{:S(2)}) collective-permute-start(bf16[208,256]{1,0:T(8,128)(2,1)S(1)} %get-tuple-element.6), channel_id=1, source_target_pairs={{0,8},{2,10},{4,12},{6,14},{8,0},{10,2},{12,4},{14,6},{1,9},{3,11}... | collective-permute-start | bytes 319496 | tf_op jit(solution)/shard_map/ppermute | solution.py:107
  123.2 1.3 collective-permute-start.9
  125.1 3.2 %collective-permute-start.17 = (bf16[208,256]{1,0:T(8,128)(2,1)S(1)}, bf16[208,256]{1,0:T(8,128)(2,1)S(1)}, u32[]{:S(2)}, u32[]{:S(2)}) collective-permute-start(bf16[208,256]{1,0:T(8,128)(2,1)S(1)} %get-tuple-element.6), channel_id=1, source_target_pairs={{0,12},{2,14},{4,0},{6,2},{8,4},{10,6},{12,8},{14,10},{1,13},{3,15... | collective-permute-start | bytes 319496 | tf_op jit(solution)/shard_map/ppermute | solution.py:107
  128.9 2.2 %collective-permute-done.16 = bf16[208,256]{1,0:T(8,128)(2,1)S(1)} collective-permute-done((bf16[208,256]{1,0:T(8,128)(2,1)S(1)}, bf16[208,256]{1,0:T(8,128)(2,1)S(1)}, u32[]{:S(2)}, u32[]{:S(2)}) %collective-permute-start.16) | collective-permute-done | bytes 106528 | tf_op jit(solution)/shard_map/ppermute | solution.py:107
  131.6 2.4 %collective-permute-start.18 = (bf16[832,256]{1,0:T(8,128)(2,1)S(1)}, bf16[832,256]{1,0:T(8,128)(2,1)S(1)}, u32[]{:S(2)}, u32[]{:S(2)}) collective-permute-start(bf16[832,256]{1,0:T(8,128)(2,1)S(1)} %bitcast.256), channel_id=1, source_target_pairs={{0,2},{2,0},{4,6},{6,4},{8,10},{10,8},{12,14},{14,12},{1,3},{3,1},... | collective-permute-start | bytes 1277960 | tf_op jit(solution)/shard_map/ppermute | solution.py:76
  133.9 6.0 %collective-permute-done.9 = f32[1,2,256,256]{3,2,1,0:T(8,128)S(1)} collective-permute-done((f32[1,2,256,256]{3,2,1,0:T(8,128)S(1)}, f32[1,2,256,256]{3,2,1,0:T(8,128)S(1)}, u32[]{:S(2)}, u32[]{:S(2)}) %collective-permute-start.9) | collective-permute-done | bytes 524320 | tf_op jit(solution)/shard_map/ppermute | solution.py:55
  140.6 5.7 %collective-permute-done.18 = bf16[832,256]{1,0:T(8,128)(2,1)S(1)} collective-permute-done((bf16[832,256]{1,0:T(8,128)(2,1)S(1)}, bf16[832,256]{1,0:T(8,128)(2,1)S(1)}, u32[]{:S(2)}, u32[]{:S(2)}) %collective-permute-start.18) | collective-permute-done | bytes 426016 | tf_op jit(solution)/shard_map/ppermute | solution.py:76
  146.7 2.3 %fusion.4 = bf16[2,2,2,256,256]{4,3,2,1,0:T(8,128)(2,1)} fusion(bf16[2,2,2,256,256]{4,3,2,1,0:T(8,128)(2,1)S(1)} %get-tuple-element.8, f32[2,2,2,256,256]{4,3,2,1,0:T(8,128)S(1)} %fusion.17, f32[2,2,2,256,256]{4,3,2,1,0:T(8,128)S(1)} %fusion.35, f32[2,2,2,256,256]{4,3,2,1,0:T(8,128)S(1)} %fusion.37, f32[2,2,2,256,256]{4,3,2,1,0:T(8,128)S(1)} %fusion.86, ...), kind=kOutput, calls=%fused_computation.13 | convolution fusion | flops 275775488 | bytes 21104128 | tf_op jit(solution)/shard_map/dot_general | solution.py:182
  150.6 1.1 pad_maximum_fusion.3
  (95 shorter events, 27.0 us)
Async XLA Ops:
  0.6 76.1 %copy-start = (bf16[256,256]{1,0:T(8,128)(2,1)S(1)}, bf16[256,256]{1,0:T(8,128)(2,1)}, u32[]{:S(2)}) copy-start(bf16[256,256]{1,0:T(8,128)(2,1)} %param.11) | copy-start | bytes 393220
  0.6 3.5 %copy-start.4 = (bf16[2,2,2,256,256]{4,3,2,1,0:T(8,128)(2,1)S(1)}, bf16[2,2,2,256,256]{4,3,2,1,0:T(8,128)(2,1)}, u32[]{:S(2)}) copy-start(bf16[2,2,2,256,256]{4,3,2,1,0:T(8,128)(2,1)} %param.7) | copy-start | bytes 3145732
  3.7 14.1 %collective-permute-start = (bf16[2,2,1,256,256]{4,3,2,1,0:T(8,128)(2,1)}, bf16[2,2,1,256,256]{4,3,2,1,0:T(8,128)(2,1)}, u32[]{:S(2)}, u32[]{:S(2)}) collective-permute-start(bf16[2,2,1,256,256]{4,3,2,1,0:T(8,128)(2,1)} %slice_select_fusion.2), channel_id=1, source_target_pairs={{0,1},{1,0},{2,3},{3,2},{4,5},{5,4},{6,7},{7,6},{8,9},{9,8},{10,11... | collective-permute-start | bytes 1572872 | tf_op jit(solution)/shard_map/ppermute | solution.py:225
  5.6 28.2 %collective-permute-start.5 = (bf16[2,2,2,256,256]{4,3,2,1,0:T(8,128)(2,1)S(1)}, bf16[2,2,2,256,256]{4,3,2,1,0:T(8,128)(2,1)S(1)}, u32[]{:S(2)}, u32[]{:S(2)}) collective-permute-start(bf16[2,2,2,256,256]{4,3,2,1,0:T(8,128)(2,1)S(1)} %get-tuple-element.8), channel_id=1, source_target_pairs={{2,0},{4,2},{6,4},{8,6},{10,8},{12,10},{14,12},{3,1},{5,3},{7,5},{... | collective-permute-start | bytes 3145736 | tf_op jit(solution)/shard_map/ppermute | solution.py:10
  7.7 19.4 %collective-permute-start.2 = (bf16[2,2,256,256]{3,2,1,0:T(8,128)(2,1)}, bf16[2,2,256,256]{3,2,1,0:T(8,128)(2,1)}, u32[]{:S(2)}, u32[]{:S(2)}) collective-permute-start(bf16[2,2,256,256]{3,2,1,0:T(8,128)(2,1)} %slice_bitcast_fusion), channel_id=1, source_target_pairs={{0,8},{1,9},{16,24},{17,25}} | collective-permute-start | bytes 1572872 | tf_op jit(solution)/shard_map/ppermute | solution.py:21
  16.0 1.4 copy-start.3
  19.0 1.3 copy-start.2
  27.1 12.3 %collective-permute-start.3 = (bf16[2,2,256,256]{3,2,1,0:T(8,128)(2,1)S(1)}, bf16[2,2,256,256]{3,2,1,0:T(8,128)(2,1)S(1)}, u32[]{:S(2)}, u32[]{:S(2)}) collective-permute-start(bf16[2,2,256,256]{3,2,1,0:T(8,128)(2,1)S(1)} %broadcast_select_fusion.2), channel_id=1, source_target_pairs={{0,4},{8,12},{1,5},{9,13},{16,20},{24,28},{17,21},{25,29}} | collective-permute-start | bytes 1572872 | tf_op jit(solution)/shard_map/ppermute | solution.py:21
  29.7 40.8 %collective-permute-start.1 = (bf16[2,2,2,256,256]{4,3,2,1,0:T(8,128)(2,1)S(1)}, bf16[2,2,2,256,256]{4,3,2,1,0:T(8,128)(2,1)S(1)}, u32[]{:S(2)}, u32[]{:S(2)}) collective-permute-start(bf16[2,2,2,256,256]{4,3,2,1,0:T(8,128)(2,1)S(1)} %get-tuple-element.20), channel_id=1, source_target_pairs={{0,2},{2,4},{4,6},{6,8},{8,10},{10,12},{12,14},{1,3},{3,5},{5,7},{... | collective-permute-start | bytes 3145736 | tf_op jit(solution)/shard_map/ppermute | solution.py:10
  39.3 5.1 %copy-start.1 = (f32[2,2,256,256]{3,2,1,0:T(8,128)S(1)}, f32[2,2,256,256]{3,2,1,0:T(8,128)}, u32[]{:S(2)}) copy-start(f32[2,2,256,256]{3,2,1,0:T(8,128)} %get-tuple-element.7) | copy-start | bytes 3145732
  39.5 28.2 %collective-permute-start.4 = (bf16[2,2,256,256]{3,2,1,0:T(8,128)(2,1)S(1)}, bf16[2,2,256,256]{3,2,1,0:T(8,128)(2,1)S(1)}, u32[]{:S(2)}, u32[]{:S(2)}) collective-permute-start(bf16[2,2,256,256]{3,2,1,0:T(8,128)(2,1)S(1)} %broadcast_select_fusion.3), channel_id=1, source_target_pairs={{0,2},{4,6},{8,10},{12,14},{1,3},{5,7},{9,11},{13,15},{16,18},{20,... | collective-permute-start | bytes 1572872 | tf_op jit(solution)/shard_map/ppermute | solution.py:21
  44.6 24.3 %collective-permute-start.7 = (f32[1,2,256,256]{3,2,1,0:T(8,128)S(1)}, f32[1,2,256,256]{3,2,1,0:T(8,128)S(1)}, u32[]{:S(2)}, u32[]{:S(2)}) collective-permute-start(f32[1,2,256,256]{3,2,1,0:T(8,128)S(1)} %slice_select_fusion), channel_id=1, source_target_pairs={{8,0},{10,2},{12,4},{14,6},{9,1},{11,3},{13,5},{15,7},{24,16},{26,... | collective-permute-start | bytes 1572872 | tf_op jit(solution)/shard_map/ppermute | solution.py:53
  45.9 25.1 %collective-permute-start.6 = (bf16[2,2,1,256,256]{4,3,2,1,0:T(8,128)(2,1)S(1)}, bf16[2,2,1,256,256]{4,3,2,1,0:T(8,128)(2,1)S(1)}, u32[]{:S(2)}, u32[]{:S(2)}) collective-permute-start(bf16[2,2,1,256,256]{4,3,2,1,0:T(8,128)(2,1)S(1)} %slice_select_fusion.1), channel_id=1, source_target_pairs={{0,1},{1,0},{2,3},{3,2},{4,5},{5,4},{6,7},{7,6},{8,9},{9,8},{10,11... | collective-permute-start | bytes 1572872 | tf_op jit(solution)/shard_map/ppermute | solution.py:225
  68.8 5.0 %collective-permute-start.10 = (f32[1664,256]{1,0:T(8,128)S(1)}, f32[1664,256]{1,0:T(8,128)S(1)}, u32[]{:S(2)}, u32[]{:S(2)}) collective-permute-start(f32[1664,256]{1,0:T(8,128)S(1)} %constant_dynamic-slice_fusion.4), channel_id=1, source_target_pairs={{0,1},{1,0},{2,3},{3,2},{4,5},{5,4},{6,7},{7,6},{8,9},{9,8},{10,11... | collective-permute-start | bytes 5111816 | tf_op jit(solution)/shard_map/ppermute | solution.py:68
  69.0 54.1 %collective-permute-start.8 = (f32[1,2,256,256]{3,2,1,0:T(8,128)S(1)}, f32[1,2,256,256]{3,2,1,0:T(8,128)S(1)}, u32[]{:S(2)}, u32[]{:S(2)}) collective-permute-start(f32[1,2,256,256]{3,2,1,0:T(8,128)S(1)} %fusion.166), channel_id=1, source_target_pairs={{4,0},{6,2},{5,1},{7,3},{20,16},{22,18},{21,17},{23,19}} | collective-permute-start | bytes 1572872 | tf_op jit(solution)/shard_map/ppermute | solution.py:53
  74.2 22.1 %collective-permute-start.11 = (f32[832,256]{1,0:T(8,128)S(1)}, f32[832,256]{1,0:T(8,128)S(1)}, u32[]{:S(2)}, u32[]{:S(2)}) collective-permute-start(f32[832,256]{1,0:T(8,128)S(1)} %constant_dynamic-slice_fusion.3), channel_id=1, source_target_pairs={{0,2},{2,0},{4,6},{6,4},{8,10},{10,8},{12,14},{14,12},{1,3},{3,1},... | collective-permute-start | bytes 2555912 | tf_op jit(solution)/shard_map/ppermute | solution.py:68
  96.5 13.4 %collective-permute-start.12 = (f32[208,256]{1,0:T(8,128)S(1)}, f32[208,256]{1,0:T(8,128)S(1)}, u32[]{:S(2)}, u32[]{:S(2)}) collective-permute-start(f32[208,256]{1,0:T(8,128)S(1)} %get-tuple-element.13), channel_id=1, source_target_pairs={{0,8},{2,10},{4,12},{6,14},{8,0},{10,2},{12,4},{14,6},{1,9},{3,11}... | collective-permute-start | bytes 638984 | tf_op jit(solution)/shard_map/ppermute | solution.py:94
  98.5 20.7 %collective-permute-start.13 = (f32[208,256]{1,0:T(8,128)S(1)}, f32[208,256]{1,0:T(8,128)S(1)}, u32[]{:S(2)}, u32[]{:S(2)}) collective-permute-start(f32[208,256]{1,0:T(8,128)S(1)} %get-tuple-element.15), channel_id=1, source_target_pairs={{0,4},{2,6},{4,8},{6,10},{8,12},{10,14},{12,0},{14,2},{1,5},{3,7},... | collective-permute-start | bytes 638984 | tf_op jit(solution)/shard_map/ppermute | solution.py:94
  107.4 11.8 %collective-permute-start.14 = (f32[208,256]{1,0:T(8,128)S(1)}, f32[208,256]{1,0:T(8,128)S(1)}, u32[]{:S(2)}, u32[]{:S(2)}) collective-permute-start(f32[208,256]{1,0:T(8,128)S(1)} %get-tuple-element.14), channel_id=1, source_target_pairs={{0,12},{2,14},{4,0},{6,2},{8,4},{10,6},{12,8},{14,10},{1,13},{3,15... | collective-permute-start | bytes 638984 | tf_op jit(solution)/shard_map/ppermute | solution.py:94
  119.3 9.6 %collective-permute-start.15 = (bf16[208,256]{1,0:T(8,128)(2,1)S(1)}, bf16[208,256]{1,0:T(8,128)(2,1)S(1)}, u32[]{:S(2)}, u32[]{:S(2)}) collective-permute-start(bf16[208,256]{1,0:T(8,128)(2,1)S(1)} %get-tuple-element.6), channel_id=1, source_target_pairs={{0,8},{2,10},{4,12},{6,14},{8,0},{10,2},{12,4},{14,6},{1,9},{3,11}... | collective-permute-start | bytes 319496 | tf_op jit(solution)/shard_map/ppermute | solution.py:107
  123.2 16.8 %collective-permute-start.9 = (f32[1,2,256,256]{3,2,1,0:T(8,128)S(1)}, f32[1,2,256,256]{3,2,1,0:T(8,128)S(1)}, u32[]{:S(2)}, u32[]{:S(2)}) collective-permute-start(f32[1,2,256,256]{3,2,1,0:T(8,128)S(1)} %add.249), channel_id=1, source_target_pairs={{2,0},{3,1},{18,16},{19,17}} | collective-permute-start | bytes 1572872 | tf_op jit(solution)/shard_map/ppermute | solution.py:55
  124.5 6.7 %collective-permute-start.16 = (bf16[208,256]{1,0:T(8,128)(2,1)S(1)}, bf16[208,256]{1,0:T(8,128)(2,1)S(1)}, u32[]{:S(2)}, u32[]{:S(2)}) collective-permute-start(bf16[208,256]{1,0:T(8,128)(2,1)S(1)} %get-tuple-element.6), channel_id=1, source_target_pairs={{0,4},{2,6},{4,8},{6,10},{8,12},{10,14},{12,0},{14,2},{1,5},{3,7},... | collective-permute-start | bytes 319496 | tf_op jit(solution)/shard_map/ppermute | solution.py:107
  125.1 6.4 %collective-permute-start.17 = (bf16[208,256]{1,0:T(8,128)(2,1)S(1)}, bf16[208,256]{1,0:T(8,128)(2,1)S(1)}, u32[]{:S(2)}, u32[]{:S(2)}) collective-permute-start(bf16[208,256]{1,0:T(8,128)(2,1)S(1)} %get-tuple-element.6), channel_id=1, source_target_pairs={{0,12},{2,14},{4,0},{6,2},{8,4},{10,6},{12,8},{14,10},{1,13},{3,15... | collective-permute-start | bytes 319496 | tf_op jit(solution)/shard_map/ppermute | solution.py:107
  131.6 14.8 %collective-permute-start.18 = (bf16[832,256]{1,0:T(8,128)(2,1)S(1)}, bf16[832,256]{1,0:T(8,128)(2,1)S(1)}, u32[]{:S(2)}, u32[]{:S(2)}) collective-permute-start(bf16[832,256]{1,0:T(8,128)(2,1)S(1)} %bitcast.256), channel_id=1, source_target_pairs={{0,2},{2,0},{4,6},{6,4},{8,10},{10,8},{12,14},{14,12},{1,3},{3,1},... | collective-permute-start | bytes 1277960 | tf_op jit(solution)/shard_map/ppermute | solution.py:76
  146.6 2.4 %collective-permute-start.19 = (bf16[1664,256]{1,0:T(8,128)(2,1)S(1)}, bf16[1664,256]{1,0:T(8,128)(2,1)S(1)}, u32[]{:S(2)}, u32[]{:S(2)}) collective-permute-start(bf16[1664,256]{1,0:T(8,128)(2,1)S(1)} %maximum_select_fusion), channel_id=1, source_target_pairs={{0,1},{1,0},{2,3},{3,2},{4,5},{5,4},{6,7},{7,6},{8,9},{9,8},{10,11... | collective-permute-start | bytes 2555912 | tf_op jit(solution)/shard_map/ppermute | solution.py:153
